TPU v7x, 32 devices: a whole 2x2x4 slice. The times are simulated.
32 devices in a mesh: vis: 2 (over x), ctx: 8 (over z, y), tp: 2 (over core).
Axes of the slice: x: 2, y: 2, z: 4, core: 2. Of those that a mesh axis runs over, the one named last changes fastest.
Arguments:
- patch_rows: bfloat16 [1024, 1280], P('ctx'), may hold values from -6 to 6
- vit_gain: float32 [1280], replicated, may hold values from 0.25 to 1.75
- vit_bias: float32 [1280], replicated, may hold values from -3 to 3
- vit_qkv: bfloat16 [1280, 3, 16, 80], P(None, None, ('vis', 'tp')), as said below
- vit_out: bfloat16 [16, 80, 1280], P(('vis', 'tp')), may hold values from -0.15625 to 0.15625
- merge_gain: float32 [1280], replicated, may hold values from 0.25 to 1.75
- merge_bias: float32 [1280], replicated, may hold values from -3 to 3
- merge_weight: bfloat16 [5120, 4096], P('ctx', ('vis', 'tp')), may hold values from -0.078125 to 0.078125
- image_patches: int32 [8, 2], replicated, may hold values from 4 to 64, as said below
- window_ids: int32 [1024], P('ctx'), may hold values from 0 to 1023, as said below
- image_pos: int32 [256], replicated, may hold values from 0 to 1023, as said below
- slice_order: int32 [8], replicated, may hold values from 0 to 7, as said below
- doc_ids: int32 [1024], replicated, may hold values from 0 to 3, never falling along the last dimension, each value on 1 to 512 neighbouring positions
- text_rows: bfloat16 [1024, 4096], P('ctx', ('vis', 'tp')), may hold values from -6 to 6
- norm_gain: float32 [4096], replicated, may hold values from 0.25 to 1.75
- w_query: bfloat16 [4096, 8, 4, 128], P(None, 'vis', 'tp'), as said below
- w_keyval: bfloat16 [2, 4096, 8, 128], P('tp', None, 'vis'), as said below
Outputs:
- attention_out: bfloat16 [1024, 8, 512], P('ctx', 'vis', 'tp')
Inputs may be any that keep to these rules, and one draw needn't show every extreme that they name: `image_patches`: each is h * w for an image of h by w patches, h and w even and at most 32; the images of one ctx shard hold at most 128 patches together, exactly 128 on some shard. `window_ids`: equal ids mark one attention window: consecutive slots of one ctx shard, a multiple of 4 of them and at most 64, never in two images; slots after a shard's live patches form windows of 4. `slice_order`: a permutation; ctx shard c holds the sequence slices slice_order[c] and 15 - slice_order[c] of 64 positions, in that order, as its 128 rows. `image_pos`: distinct positions, one for every merged slot, live or not; the 32 slots of any one ctx shard put exactly 4 positions into the rows of each ctx shard. `doc_ids`: never falling along positions; each document holds 1 to 512 positions. `vit_qkv`: independent centred entries. `w_query`: independent centred entries. `w_keyval`: independent centred entries.
All inputs are finite; a program needn't handle non-finite values.
Results may differ from a plain program's by a relative error of at most 0.022.
The roundings to bfloat16 on the way count: a program that leaves them out, or rounds other values in their place, can miss the bound.
Values may be sent and summed in bfloat16 or wider, within the bound.
No kernel may reach another device: no remote copies, remote signals or barrier semaphores. Data moves between devices by JAX's collectives and lax.ppermute only.
A program may use at most 64 MiB of HBM per device.

v0:
```python
import math

import jax
import jax.numpy as jnp
from jax import lax
from jax.sharding import PartitionSpec as P

D = 4096
HD = 128
VD = 1280
VHD = 80
TOK = 128
PCAP = 128
ICAP = 32


norm_eps = 1e-06
rope_base = 1000000.0
big_negative = -1e30


def swapped(value, axis, stride):
    return lax.ppermute(value, axis, [(i, i ^ 1 << stride) for i in range(lax.axis_size(axis))])


def layer_norm(values, scale_vec, shift_vec):
    centre = jnp.mean(values, axis=-1, keepdims=True)
    offset = values - centre
    spread = jnp.mean(offset * offset, axis=-1, keepdims=True)
    return offset * lax.rsqrt(spread + norm_eps) * scale_vec + shift_vec


def rotate(values, positions):
    half_dim = values.shape[-1] // 2
    exponent = jnp.arange(half_dim, dtype=jnp.float32) * (-2.0 / values.shape[-1])
    frequency = jnp.power(jnp.float32(rope_base), exponent)
    angles = positions.astype(jnp.float32)[:, None] * frequency[None, :]
    shape_out = (values.shape[0],) + (1,) * (values.ndim - 2) + (half_dim,)
    cosine = jnp.cos(angles).reshape(shape_out)
    sine_part = jnp.sin(angles).reshape(shape_out)
    lead_half = values[..., :half_dim]
    tail_half = values[..., half_dim:]
    return jnp.concatenate(
        [lead_half * cosine - tail_half * sine_part, tail_half * cosine + lead_half * sine_part],
        axis=-1,
    )


def row_positions(row_ids, slice_order, tokens_dev):
    shards = slice_order.shape[0]
    device_of = row_ids // tokens_dev
    local_row = row_ids % tokens_dev
    half_tok = tokens_dev // 2
    matches = device_of[:, None] == jnp.arange(shards, dtype=jnp.int32)[None, :]
    first_slice = jnp.sum(jnp.where(matches, slice_order[None, :], 0), axis=1)
    slice_ids = jnp.where(local_row < half_tok, first_slice, 2 * shards - 1 - first_slice)
    return slice_ids * half_tok + local_row % half_tok


def place_of(positions, slice_order, tokens_dev):
    shards = slice_order.shape[0]
    half_tok = tokens_dev // 2
    slice_ids = positions // half_tok
    paired = jnp.minimum(slice_ids, 2 * shards - 1 - slice_ids)
    owner_hot = (paired[..., None] == slice_order).astype(jnp.int32)
    owner_dev = jnp.sum(owner_hot * jnp.arange(shards, dtype=jnp.int32), axis=-1)
    local_row = jnp.where(slice_ids < shards, 0, half_tok) + positions % half_tok
    return (owner_dev, local_row, owner_hot)


def local(
    patch_rows,
    vit_gain,
    vit_bias,
    vit_qkv,
    vit_out,
    merge_gain,
    merge_bias,
    merge_weight,
    image_patches,
    window_ids,
    image_pos,
    slice_order,
    doc_ids,
    text_rows,
    norm_gain,
    w_query,
    w_keyval,
):
    shards = lax.axis_size("ctx")
    ctx_index = lax.axis_index("ctx")
    tp_index = lax.axis_index("tp")
    vit_heads = vit_qkv.shape[2]
    slab_width = merge_weight.shape[1]
    normed = layer_norm(patch_rows.astype(jnp.float32), vit_gain, vit_bias).astype(jnp.bfloat16)
    projected = jnp.dot(
        normed, vit_qkv.reshape(VD, 3 * vit_heads * VHD), preferred_element_type=jnp.float32
    )
    projected = projected.astype(jnp.bfloat16).reshape(PCAP, 3, vit_heads, VHD)
    scores = jnp.einsum(
        "qhd,khd->hqk", projected[:, 0], projected[:, 1], preferred_element_type=jnp.float32
    ) / math.sqrt(VHD)
    allowed = window_ids[:, None] == window_ids[None, :]
    scores = jnp.where(allowed[None], scores, big_negative)
    powers = jnp.exp(scores - jnp.max(scores, axis=-1, keepdims=True))
    totals = jnp.sum(powers, axis=-1)
    blended = jnp.einsum(
        "hqk,khd->qhd",
        powers.astype(jnp.bfloat16),
        projected[:, 2],
        preferred_element_type=jnp.float32,
    )
    blended = (
        (blended / jnp.transpose(totals)[:, :, None])
        .astype(jnp.bfloat16)
        .reshape(PCAP, vit_heads * VHD)
    )
    out_flat = vit_out.reshape(vit_heads * VHD, VD)
    branch_part = jnp.dot(blended, out_flat, preferred_element_type=jnp.float32)
    branch_sum = lax.psum(branch_part, ("vis", "tp"))
    hidden = patch_rows.astype(jnp.float32) + branch_sum
    merged = layer_norm(hidden, merge_gain, merge_bias).astype(jnp.bfloat16).reshape(ICAP, 4 * VD)
    image_emb = jnp.dot(
        merged,
        lax.all_gather(merge_weight, "ctx", axis=0, tiled=True),
        preferred_element_type=jnp.float32,
    ).astype(jnp.bfloat16)
    send_each = ICAP // shards
    slot_ids = jnp.arange(ICAP, dtype=jnp.int32)
    shard_ids = jnp.arange(shards, dtype=jnp.int32)
    live_count = jnp.sum(image_patches, axis=1) // 4
    all_pos = image_pos.reshape(shards, ICAP)
    owner_dev, local_row, owner_hot = place_of(all_pos, slice_order, TOK)
    before = jnp.cumsum(owner_hot, axis=1) - owner_hot
    rank_in = jnp.sum(before * owner_hot, axis=-1)
    is_live = slot_ids[None, :] < live_count[:, None]
    own_hot = (shard_ids == ctx_index)[:, None]
    own_owner = jnp.sum(jnp.where(own_hot, owner_dev, 0), axis=0)
    own_rank = jnp.sum(jnp.where(own_hot, rank_in, 0), axis=0)
    own_live = jnp.any(own_hot & is_live, axis=0)
    target_slot = own_owner * send_each + own_rank
    picker = ((target_slot[None, :] == slot_ids[:, None]) & own_live[None, :]).astype(jnp.bfloat16)
    outgoing = jnp.dot(picker, image_emb, preferred_element_type=jnp.float32).astype(jnp.bfloat16)
    incoming = lax.all_to_all(
        outgoing.reshape(shards, send_each, slab_width),
        "ctx",
        split_axis=0,
        concat_axis=0,
        tiled=True,
    )
    mine_live = ((owner_dev == ctx_index) & is_live).reshape(-1)
    column_of = (shard_ids[:, None] * send_each + rank_in).reshape(-1)
    row_hot = (
        (local_row.reshape(-1)[None, :] == jnp.arange(TOK, dtype=jnp.int32)[:, None])
        & mine_live[None, :]
    ).astype(jnp.bfloat16)
    column_hot = (column_of[:, None] == slot_ids[None, :]).astype(jnp.bfloat16)
    placing = jnp.dot(row_hot, column_hot, preferred_element_type=jnp.float32)
    is_image = jnp.sum(placing, axis=1) > 0.5
    image_part = jnp.dot(
        placing.astype(jnp.bfloat16),
        incoming.reshape(ICAP, slab_width),
        preferred_element_type=jnp.float32,
    )
    embeds = jnp.where(is_image[:, None], image_part.astype(jnp.bfloat16), text_rows)
    full_rows = lax.all_gather(embeds, ("vis", "tp"), axis=1, tiled=True)
    widened = full_rows.astype(jnp.float32)
    normed_rows = (
        widened
        * lax.rsqrt(jnp.mean(widened * widened, axis=1, keepdims=True) + norm_eps)
        * norm_gain
    ).astype(jnp.bfloat16)
    own_positions = row_positions(
        ctx_index * TOK + jnp.arange(TOK, dtype=jnp.int32), slice_order, TOK
    )
    own_doc = jnp.take(doc_ids, own_positions)
    kv_heads = w_query.shape[1]
    groups = w_query.shape[2]
    queries = jnp.dot(
        normed_rows, w_query.reshape(D, kv_heads * groups * HD), preferred_element_type=jnp.float32
    ).reshape(TOK, kv_heads, groups, HD)
    queries = rotate(queries, own_positions).astype(jnp.bfloat16)
    projected_half = jnp.dot(
        normed_rows, w_keyval[0].reshape(D, kv_heads * HD), preferred_element_type=jnp.float32
    ).reshape(TOK, kv_heads, HD)
    own_half = jnp.where(
        tp_index == 0, rotate(projected_half, own_positions), projected_half
    ).astype(jnp.bfloat16)
    initial = (
        jnp.full((kv_heads, groups, TOK), big_negative, jnp.float32),
        jnp.zeros((kv_heads, groups, TOK), jnp.float32),
        jnp.zeros((kv_heads, groups, TOK, HD), jnp.float32),
    )
    gathered = lax.all_gather(own_half, "ctx", axis=0, tiled=True)
    partner_all = swapped(gathered, "tp", 0)
    keys_every = jnp.where(tp_index == 0, gathered, partner_all)
    values_every = jnp.where(tp_index == 0, partner_all, gathered)
    carry_state = initial
    key_count = keys_every.shape[0]
    block_rows = key_count if key_count <= 1024 else math.gcd(key_count, 1024)
    block_count = key_count // block_rows
    key_pos = row_positions(jnp.arange(key_count, dtype=jnp.int32), slice_order, TOK)
    key_doc = jnp.take(doc_ids, key_pos)
    stacked = (
        keys_every.reshape(block_count, block_rows, kv_heads, HD),
        values_every.reshape(block_count, block_rows, kv_heads, HD),
        key_pos.reshape(block_count, block_rows),
        key_doc.reshape(block_count, block_rows),
    )

    def key_block(state_now, inputs_now):
        keys_blk, values_blk, pos_blk, doc_blk = inputs_now
        best_old, total_old, accum_old = state_now
        allowed_now = (pos_blk[None, :] <= own_positions[:, None]) & (
            doc_blk[None, :] == own_doc[:, None]
        )
        scores_now = jnp.einsum(
            "qkgd,nkd->kgqn", queries, keys_blk, preferred_element_type=jnp.float32
        ) / math.sqrt(HD)
        scores_now = jnp.where(allowed_now[None, None], scores_now, big_negative)
        best_new = jnp.maximum(best_old, jnp.max(scores_now, axis=-1))
        factor = jnp.exp(best_old - best_new)
        powers_now = jnp.where(
            allowed_now[None, None], jnp.exp(scores_now - best_new[..., None]), 0.0
        )
        total_new = total_old * factor + jnp.sum(powers_now, axis=-1)
        accum_new = accum_old * factor[..., None] + jnp.einsum(
            "kgqn,nkd->kgqd",
            powers_now.astype(jnp.bfloat16),
            values_blk,
            preferred_element_type=jnp.float32,
        )
        return ((best_new, total_new, accum_new), None)

    carry_state, unused = lax.scan(key_block, carry_state, stacked)
    best_final, total_final, accum_final = carry_state
    result = accum_final / total_final[..., None]
    return (
        jnp.transpose(result, (2, 0, 1, 3)).reshape(TOK, kv_heads, groups * HD).astype(jnp.bfloat16)
    )


def solution(mesh):
    placed = (
        P("ctx", None),
        P(),
        P(),
        P(None, None, ("vis", "tp"), None),
        P(("vis", "tp"), None, None),
        P(),
        P(),
        P("ctx", ("vis", "tp")),
        P(),
        P("ctx"),
        P(),
        P(),
        P(),
        P("ctx", ("vis", "tp")),
        P(),
        P(None, "vis", "tp", None),
        P("tp", None, "vis", None),
    )
    return jax.shard_map(
        local, mesh=mesh, in_specs=placed, out_specs=P("ctx", "vis", "tp"), check_vma=False
    )
```

profile of v0, /device:TPU:0, one launch (start us, length us, event | category | flops | bytes accessed | tf_op | source)
XLA Modules:
  0.0 267.5 jit_solution(11337003461193074470)
XLA Ops:
  7.4 0.0 all-reduce.2.cloned.1.call-start
  7.4 1.2 convert_reduce_fusion
  8.6 0.0 copy-start.2
  8.7 1.3 fusion.43
  9.9 0.8 broadcast_compare_fusion
  10.8 1.9 convolution_convert_fusion.1
  12.7 0.0 copy-start.7
  12.7 0.0 copy-start.8
  12.7 0.3 fusion.109
  12.9 0.1 fusion.59
  13.0 2.5 convolution_bitcast_fusion
  15.5 0.0 all-reduce.2.cloned.1.call-update
  15.6 0.0 all-gather.4.cloned.1.call-start
  15.6 0.5 all-gather.4.cloned.1.call-update
  16.2 0.1 reshape.657
  16.2 0.1 copy.57
  16.3 0.7 fusion.61
  17.0 0.1 copy.58
  17.1 0.7 fusion.110
  17.8 0.1 copy.59
  17.9 0.1 select_reduce_fusion.2
  18.0 0.1 add.351
  18.1 0.1 fusion.88
  18.2 0.1 and.266
  18.3 0.3 fusion.111
  18.6 34.1 %all-reduce.2.cloned.1.call-done = f32[128,1280]{1,0:T(8,128)} async-done(((f32[128,1280]{1,0:T(8,128)}), f32[128,1280]{1,0:T(8,128)}) %all-reduce.2.cloned.1.call-update) | async-done | bytes 655376 | tf_op jit(solution)/shard_map/psum | solution.py:120
  52.6 1.2 fusion.58
  53.9 1.3 multiply_reduce_fusion
  55.2 1.3 add_convert_fusion
  56.5 0.2 reshape.660
  56.7 114.2 %all-gather.4.cloned.1.call-done = bf16[5120,1024]{1,0:T(8,128)(2,1)} async-done(((bf16[640,1024]{1,0:T(8,128)(2,1)}), bf16[5120,1024]{1,0:T(8,128)(2,1)}) %all-gather.4.cloned.1.call-update) | async-done | bytes 10485776 | tf_op jit(solution)/shard_map/all_gather | solution.py:125
  171.0 6.1 %convolution_convert_fusion.2 = bf16[32,1024]{1,0:T(8,128)(2,1)S(1)} fusion(bf16[32,5120]{1,0:T(8,128)(2,1)S(1)} %reshape.660, bf16[5120,1024]{1,0:T(8,128)(2,1)} %all-gather.4.cloned.1.call-done, s32[32]{0:T(128)S(1)} %multiply_add_fusion.1, pred[32]{0:T(512)(128)(4,1)S(1)} %get-tuple-element.54), kind=kOutput, calls=%fused_computation.28 | convolution fusion | flops 337709056 | bytes 10879136 | tf_op jit(solution)/shard_map/dot_general | solution.py:143
  177.0 0.7 reshape.661
  177.7 3.4 %all-to-all-start = ((bf16[8,4,1024]{2,1,0:T(4,128)(2,1)}), bf16[8,4,1024]{2,1,0:T(4,128)(2,1)S(1)}, u32[]{:S(2)}, u32[]{:S(2)}) async-start(bf16[8,4,1024]{2,1,0:T(4,128)(2,1)} %reshape.661), calls=%async_computation | async-start | bytes 131072 | tf_op jit(solution)/shard_map/all_to_all | solution.py:144
  181.1 0.0 all-gather.6.cloned.1.call-start
  181.1 6.8 %all-to-all-done = bf16[8,4,1024]{2,1,0:T(4,128)(2,1)S(1)} async-done(((bf16[8,4,1024]{2,1,0:T(4,128)(2,1)}), bf16[8,4,1024]{2,1,0:T(4,128)(2,1)S(1)}, u32[]{:S(2)}, u32[]{:S(2)}) %all-to-all-start) | async-done | bytes 65568 | tf_op jit(solution)/shard_map/all_to_all | solution.py:144
  187.9 1.0 fusion.16
  188.9 0.0 all-gather.6.cloned.1.call-update
  188.9 0.2 all-gather.8.cloned.1.call-start
  189.2 0.1 select_reduce_fusion.3
  189.3 1.0 gather_fusion.1
  190.3 0.5 and_select_fusion.8
  190.8 5.0 %copy.79 = bf16[512,8,4,128]{3,1,2,0:T(8,128)(2,1)} copy(bf16[512,8,4,128]{3,2,1,0:T(4,128)(2,1)} %bitcast.116) | data formatting | bytes 8388608
  195.8 6.4 %copy.63 = bf16[512,4096]{1,0:T(8,128)(2,1)} copy(bf16[512,4096]{0,1:T(8,128)(2,1)} %bitcast.114) | data formatting | bytes 8388608 | tf_op jit(solution)/shard_map/dot_general | solution.py:183
  202.2 0.2 multiply_cosine_fusion
  202.4 0.8 all-gather.6.cloned.1.call-done
  203.2 1.5 fusion.3
  204.8 3.8 %fusion.25 = f32[128,4,128]{0,2,1:T(8,128)S(1)} fusion(bf16[4,128,4096]{2,1,0:T(8,128)(2,1)} %bitcast.117, bf16[128,4096]{1,0:T(8,128)(2,1)} %all-gather.6.cloned.1.call-done, f32[4096]{0:T(1024)S(1)} %copy-done.14, f32[128]{0:T(128)S(1)} %add_rsqrt_fusion), kind=kOutput, calls=%fused_computation.35 | convolution fusion | flops 538968064 | bytes 5521920 | tf_op jit(solution)/shard_map/dot_general | solution.py:183
  208.7 0.7 fusion.54
  209.4 0.0 all-gather.8.cloned.1.call-update
  209.4 0.1 select_reduce_fusion
  209.5 4.5 %gather_fusion = s32[1024]{0:T(1024)S(1)} fusion(s32[1024]{0:T(1024)S(1)} %copy-done.1, s32[1024]{0:T(1024)S(1)} %broadcast_clamp_fusion), kind=kCustom, calls=%fused_computation | custom fusion | bytes 12288 | tf_op jit(solution)/shard_map/jit(_take)/gather | solution.py:203
  214.1 14.4 %reshape.663 = bf16[4096,1024]{1,0:T(8,128)(2,1)} reshape(bf16[4096,4,2,128]{3,2,1,0:T(2,128)(2,1)} %param.32) | data formatting | bytes 16777216 | tf_op jit(solution)/shard_map/reshape | solution.py:180
  228.4 11.4 %copy.64 = bf16[1024,4096]{1,0:T(8,128)(2,1)} copy(bf16[1024,4096]{0,1:T(8,128)(2,1)} %bitcast.113) | data formatting | bytes 16777216 | tf_op jit(solution)/shard_map/dot_general | solution.py:179
  239.8 9.0 %all-gather.8.cloned.1.call-done = bf16[1024,4,128]{0,2,1:T(8,128)(2,1)} async-done(((bf16[128,4,128]{0,2,1:T(8,128)(2,1)}), bf16[1024,4,128]{0,2,1:T(8,128)(2,1)}) %all-gather.8.cloned.1.call-update) | async-done | bytes 1048592 | tf_op jit(solution)/shard_map/all_gather | solution.py:194
  248.8 0.0 collective-permute-start
  248.8 0.9 compare_and_fusion
  249.8 5.9 %fusion.23 = f32[128,4,2,128]{0,3,2,1:T(8,128)S(1)} fusion(bf16[4,2,128,4096]{3,2,1,0:T(8,128)(2,1)} %bitcast.115, bf16[128,4096]{1,0:T(8,128)(2,1)S(1)} %copy-done.3, f32[4096]{0:T(1024)} %param.31, f32[128]{0:T(128)} %copy-done.15), kind=kOutput, calls=%fused_computation.33 | convolution fusion | flops 1075838976 | bytes 9978368 | tf_op jit(solution)/shard_map/dot_general | solution.py:179
  255.7 0.1 subtract_convert_fusion
  255.8 0.0 collective-permute-done
  255.8 1.0 fusion
  256.8 1.0 fusion.1
  257.8 1.3 fusion.36
  259.2 0.9 copy.68
  (55 shorter events, 0.3 us)
Async XLA Ops:
  7.4 3.4 %copy-start = (bf16[1280,3,4,80]{0,3,2,1:T(8,128)(2,1)S(1)}, bf16[1280,3,4,80]{0,3,2,1:T(8,128)(2,1)}, u32[]{:S(2)}) copy-start(bf16[1280,3,4,80]{0,3,2,1:T(8,128)(2,1)} %param.20) | copy-start | bytes 7372804
  7.4 8.8 %copy-start.10 = (s32[256]{0:T(256)S(1)}, s32[256]{0:T(256)}, u32[]{:S(2)}) copy-start(s32[256]{0:T(256)} %param.27) | copy-start | bytes 3076
  7.4 9.0 %copy-start.9 = (s32[8]{0:T(128)S(1)}, s32[8]{0:T(128)}, u32[]{:S(2)}) copy-start(s32[8]{0:T(128)} %param.28) | copy-start | bytes 100
  7.4 45.3 %all-reduce.2.cloned.1.call-start = ((), (), s32[]{:S(2)}) async-start(), calls=%async_computation.1 | async-start | bytes 1310720 | tf_op jit(solution)/shard_map/psum | solution.py:120
  8.6 9.4 %copy-start.12 = (s32[8,2]{0,1:T(2,128)S(1)}, s32[8,2]{0,1:T(2,128)}, u32[]{:S(2)}) copy-start(s32[8,2]{0,1:T(2,128)} %param.25) | copy-start | bytes 196
  8.6 44.0 %copy-start.2 = (bf16[128,1280]{1,0:T(8,128)(2,1)S(1)}, bf16[128,1280]{1,0:T(8,128)(2,1)}, u32[]{:S(2)}) copy-start(bf16[128,1280]{1,0:T(8,128)(2,1)} %param.17) | copy-start | bytes 983044
  12.7 42.5 %copy-start.7 = (f32[1280]{0:T(1024)S(1)}, f32[1280]{0:T(1024)}, u32[]{:S(2)}) copy-start(f32[1280]{0:T(1024)} %param.23) | copy-start | bytes 15364
  12.7 42.5 %copy-start.8 = (f32[1280]{0:T(1024)S(1)}, f32[1280]{0:T(1024)}, u32[]{:S(2)}) copy-start(f32[1280]{0:T(1024)} %param.22) | copy-start | bytes 15364
  15.6 155.4 %all-gather.4.cloned.1.call-start = ((), (), s32[]{:S(2)}) async-start(), calls=%async_computation.2 | async-start | bytes 11796480 | tf_op jit(solution)/shard_map/all_gather | solution.py:125
  171.0 17.0 %copy-start.6 = (bf16[128,1024]{1,0:T(8,128)(2,1)S(1)}, bf16[128,1024]{1,0:T(8,128)(2,1)}, u32[]{:S(2)}) copy-start(bf16[128,1024]{1,0:T(8,128)(2,1)} %param.30) | copy-start | bytes 786436
  171.0 18.3 %copy-start.1 = (s32[1024]{0:T(1024)S(1)}, s32[1024]{0:T(1024)}, u32[]{:S(2)}) copy-start(s32[1024]{0:T(1024)} %param.29) | copy-start | bytes 12292
  177.7 10.2 %all-to-all-start = ((bf16[8,4,1024]{2,1,0:T(4,128)(2,1)}), bf16[8,4,1024]{2,1,0:T(4,128)(2,1)S(1)}, u32[]{:S(2)}, u32[]{:S(2)}) async-start(bf16[8,4,1024]{2,1,0:T(4,128)(2,1)} %reshape.661), calls=%async_computation | async-start | bytes 131072 | tf_op jit(solution)/shard_map/all_to_all | solution.py:144
  181.1 22.2 %all-gather.6.cloned.1.call-start = ((), (), s32[]{:S(2)}) async-start(), calls=%async_computation.3 | async-start | bytes 1310720 | tf_op jit(solution)/shard_map/all_gather | solution.py:166
  188.9 59.9 %all-gather.8.cloned.1.call-start = ((), (), s32[]{:S(2)}) async-start(), calls=%async_computation.4 | async-start | bytes 1179648 | tf_op jit(solution)/shard_map/all_gather | solution.py:194
  190.8 5.0 %copy-start.11 = (s32[128]{0:T(128)}, s32[128]{0:T(128)S(1)}, u32[]{:S(2)}) copy-start(s32[128]{0:T(128)S(1)} %get-tuple-element.30) | copy-start | bytes 1540
  195.8 9.0 %copy-start.14 = (f32[4096]{0:T(1024)S(1)}, f32[4096]{0:T(1024)}, u32[]{:S(2)}) copy-start(f32[4096]{0:T(1024)} %param.31) | copy-start | bytes 49156
  202.4 6.2 %copy-start.4 = (f32[128,64]{0,1:T(8,128)}, f32[128,64]{0,1:T(8,128)S(1)}, u32[]{:S(2)}) copy-start(f32[128,64]{0,1:T(8,128)S(1)} %get-tuple-element.52) | copy-start | bytes 98308
  204.8 4.6 %copy-start.15 = (f32[128]{0:T(128)}, f32[128]{0:T(128)S(1)}, u32[]{:S(2)}) copy-start(f32[128]{0:T(128)S(1)} %add_rsqrt_fusion) | copy-start | bytes 1540
  228.4 21.3 %copy-start.3 = (bf16[128,4096]{1,0:T(8,128)(2,1)S(1)}, bf16[128,4096]{1,0:T(8,128)(2,1)}, u32[]{:S(2)}) copy-start(bf16[128,4096]{1,0:T(8,128)(2,1)} %all-gather.6.cloned.1.call-done) | copy-start | bytes 3145732
  248.8 7.0 %collective-permute-start = (bf16[1024,4,128]{0,2,1:T(8,128)(2,1)}, bf16[1024,4,128]{0,2,1:T(8,128)(2,1)S(1)}, u32[]{:S(2)}, u32[]{:S(2)}) collective-permute-start(bf16[1024,4,128]{0,2,1:T(8,128)(2,1)} %all-gather.8.cloned.1.call-done), channel_id=1, source_target_pairs={{0,1},{1,0},{2,3},{3,2},{4,5},{5,4},{6,7},{7,6},{8,9},{9,8},{10,11... | collective-permute-start | bytes 3145736 | tf_op jit(solution)/shard_map/ppermute | solution.py:23
  249.7 5.9 %copy-start.5 = (f32[128,64]{0,1:T(8,128)S(1)}, f32[128,64]{0,1:T(8,128)}, u32[]{:S(2)}) copy-start(f32[128,64]{0,1:T(8,128)} %copy-done.4) | copy-start | bytes 98308
  249.8 6.0 %copy-start.13 = (bf16[1024,4,128]{0,2,1:T(8,128)(2,1)S(1)}, bf16[1024,4,128]{0,2,1:T(8,128)(2,1)}, u32[]{:S(2)}) copy-start(bf16[1024,4,128]{0,2,1:T(8,128)(2,1)} %all-gather.8.cloned.1.call-done) | copy-start | bytes 3145732
Sparse Core Ops, SparseCore 0:
  15.7 36.9 all-reduce.1
  189.0 14.1 all-gather.5
Sparse Core Ops, SparseCore 1:
  18.2 152.7 all-gather.3
  209.5 39.3 all-gather.7
where the time goes:
time: 269 us; the launch traced here: 267 us
  waiting for transfers between devices  165 us (61%)
  local copies, waits for them, and re-layouts  44.9 us (17%)
  matrix products  24 us (9%)
  between operations  15.2 us (6%)
  other arithmetic  14.2 us (5%)
  starting transfers between devices  3.67 us (1%)
    all_gather x1, waiting for transfers between devices, local(): lax.all_gather(merge_weight, 'ctx', axis=0, tiled=True)  114 us
    psum x1, waiting for transfers between devices, local(): branch_sum = lax.psum(branch_part, ('vis', 'tp'))  34.1 us
    reshape x1, local copies, waits for them, and re-layouts, local(): w_query.reshape(D, kv_heads * groups * HD)  14.4 us
    dot_general x1, local copies, waits for them, and re-layouts, local(): jnp.dot(normed_rows, w_query.reshape(D, kv_heads * groups * HD), preferre...  11.4 us
    all_gather x1, waiting for transfers between devices, local(): gathered = lax.all_gather(own_half, 'ctx', axis=0, tiled=True)  8.99 us
    all_to_all x1, waiting for transfers between devices, local(): lax.all_to_all(outgoing.reshape(shards, send_each, slab_width), 'ctx', sp...  6.78 us
    dot_general x1, local copies, waits for them, and re-layouts, local(): jnp.dot(normed_rows, w_keyval[0].reshape(D, kv_heads * HD), preferred_ele...  6.42 us
    dot_general x1, matrix products, local(): jnp.dot(picker, image_emb, preferred_element_type=jnp.float32)  6.07 us
  transfers between devices with their start and end apart: 6, of which 5 were waited for; matrix products, arithmetic and copies ran while one was open for 21% of the time, Pallas kernels for 0%

commit v1 on v0

--- a/solution.py
+++ b/solution.py
@@ -90,13 +90,11 @@
     shards = lax.axis_size("ctx")
     ctx_index = lax.axis_index("ctx")
     tp_index = lax.axis_index("tp")
-    vit_heads = vit_qkv.shape[2]
-    slab_width = merge_weight.shape[1]
+    block_feats = merge_weight.shape[0]
     normed = layer_norm(patch_rows.astype(jnp.float32), vit_gain, vit_bias).astype(jnp.bfloat16)
-    projected = jnp.dot(
-        normed, vit_qkv.reshape(VD, 3 * vit_heads * VHD), preferred_element_type=jnp.float32
-    )
-    projected = projected.astype(jnp.bfloat16).reshape(PCAP, 3, vit_heads, VHD)
+    projected = jnp.einsum(
+        "pf,fxhd->pxhd", normed, vit_qkv, preferred_element_type=jnp.float32
+    ).astype(jnp.bfloat16)
     scores = jnp.einsum(
         "qhd,khd->hqk", projected[:, 0], projected[:, 1], preferred_element_type=jnp.float32
     ) / math.sqrt(VHD)
@@ -110,21 +108,11 @@
         projected[:, 2],
         preferred_element_type=jnp.float32,
     )
-    blended = (
-        (blended / jnp.transpose(totals)[:, :, None])
-        .astype(jnp.bfloat16)
-        .reshape(PCAP, vit_heads * VHD)
-    )
-    out_flat = vit_out.reshape(vit_heads * VHD, VD)
-    branch_part = jnp.dot(blended, out_flat, preferred_element_type=jnp.float32)
+    blended = (blended / jnp.transpose(totals)[:, :, None]).astype(jnp.bfloat16)
+    branch_part = jnp.einsum("phd,hdf->pf", blended, vit_out, preferred_element_type=jnp.float32)
     branch_sum = lax.psum(branch_part, ("vis", "tp"))
     hidden = patch_rows.astype(jnp.float32) + branch_sum
     merged = layer_norm(hidden, merge_gain, merge_bias).astype(jnp.bfloat16).reshape(ICAP, 4 * VD)
-    image_emb = jnp.dot(
-        merged,
-        lax.all_gather(merge_weight, "ctx", axis=0, tiled=True),
-        preferred_element_type=jnp.float32,
-    ).astype(jnp.bfloat16)
     send_each = ICAP // shards
     slot_ids = jnp.arange(ICAP, dtype=jnp.int32)
     shard_ids = jnp.arange(shards, dtype=jnp.int32)
@@ -137,16 +125,17 @@
     own_hot = (shard_ids == ctx_index)[:, None]
     own_owner = jnp.sum(jnp.where(own_hot, owner_dev, 0), axis=0)
     own_rank = jnp.sum(jnp.where(own_hot, rank_in, 0), axis=0)
-    own_live = jnp.any(own_hot & is_live, axis=0)
     target_slot = own_owner * send_each + own_rank
-    picker = ((target_slot[None, :] == slot_ids[:, None]) & own_live[None, :]).astype(jnp.bfloat16)
-    outgoing = jnp.dot(picker, image_emb, preferred_element_type=jnp.float32).astype(jnp.bfloat16)
-    incoming = lax.all_to_all(
-        outgoing.reshape(shards, send_each, slab_width),
-        "ctx",
-        split_axis=0,
-        concat_axis=0,
-        tiled=True,
+    picker = (target_slot[None, :] == slot_ids[:, None]).astype(jnp.bfloat16)
+    ordered = jnp.dot(picker, merged, preferred_element_type=jnp.float32).astype(jnp.bfloat16)
+    blocks = jnp.transpose(ordered.reshape(ICAP, shards, block_feats), (1, 0, 2))
+    received = lax.all_to_all(blocks, "ctx", split_axis=0, concat_axis=0, tiled=True)
+    by_dest = jnp.transpose(
+        received.reshape(shards, shards, send_each, block_feats), (1, 0, 2, 3)
+    ).reshape(shards * ICAP, block_feats)
+    partial = jnp.dot(by_dest, merge_weight, preferred_element_type=jnp.float32)
+    incoming = lax.psum_scatter(partial, "ctx", scatter_dimension=0, tiled=True).astype(
+        jnp.bfloat16
     )
     mine_live = ((owner_dev == ctx_index) & is_live).reshape(-1)
     column_of = (shard_ids[:, None] * send_each + rank_in).reshape(-1)
@@ -157,11 +146,7 @@
     column_hot = (column_of[:, None] == slot_ids[None, :]).astype(jnp.bfloat16)
     placing = jnp.dot(row_hot, column_hot, preferred_element_type=jnp.float32)
     is_image = jnp.sum(placing, axis=1) > 0.5
-    image_part = jnp.dot(
-        placing.astype(jnp.bfloat16),
-        incoming.reshape(ICAP, slab_width),
-        preferred_element_type=jnp.float32,
-    )
+    image_part = jnp.dot(placing.astype(jnp.bfloat16), incoming, preferred_element_type=jnp.float32)
     embeds = jnp.where(is_image[:, None], image_part.astype(jnp.bfloat16), text_rows)
     full_rows = lax.all_gather(embeds, ("vis", "tp"), axis=1, tiled=True)
     widened = full_rows.astype(jnp.float32)
@@ -176,64 +161,40 @@
     own_doc = jnp.take(doc_ids, own_positions)
     kv_heads = w_query.shape[1]
     groups = w_query.shape[2]
-    queries = jnp.dot(
-        normed_rows, w_query.reshape(D, kv_heads * groups * HD), preferred_element_type=jnp.float32
-    ).reshape(TOK, kv_heads, groups, HD)
+    queries = jnp.einsum(
+        "td,dhgk->thgk", normed_rows, w_query, preferred_element_type=jnp.float32
+    )
     queries = rotate(queries, own_positions).astype(jnp.bfloat16)
-    projected_half = jnp.dot(
-        normed_rows, w_keyval[0].reshape(D, kv_heads * HD), preferred_element_type=jnp.float32
-    ).reshape(TOK, kv_heads, HD)
+    projected_half = jnp.einsum(
+        "td,dhk->thk", normed_rows, w_keyval[0], preferred_element_type=jnp.float32
+    )
     own_half = jnp.where(
         tp_index == 0, rotate(projected_half, own_positions), projected_half
     ).astype(jnp.bfloat16)
-    initial = (
-        jnp.full((kv_heads, groups, TOK), big_negative, jnp.float32),
-        jnp.zeros((kv_heads, groups, TOK), jnp.float32),
-        jnp.zeros((kv_heads, groups, TOK, HD), jnp.float32),
-    )
-    gathered = lax.all_gather(own_half, "ctx", axis=0, tiled=True)
-    partner_all = swapped(gathered, "tp", 0)
-    keys_every = jnp.where(tp_index == 0, gathered, partner_all)
-    values_every = jnp.where(tp_index == 0, partner_all, gathered)
-    carry_state = initial
-    key_count = keys_every.shape[0]
-    block_rows = key_count if key_count <= 1024 else math.gcd(key_count, 1024)
-    block_count = key_count // block_rows
+    both = lax.all_gather(own_half, ("ctx", "tp"), axis=0, tiled=False).reshape(
+        shards, 2, TOK, kv_heads, HD
+    )
+    key_count = shards * TOK
+    keys_every = both[:, 0].reshape(key_count, kv_heads, HD)
+    values_every = both[:, 1].reshape(key_count, kv_heads, HD)
     key_pos = row_positions(jnp.arange(key_count, dtype=jnp.int32), slice_order, TOK)
     key_doc = jnp.take(doc_ids, key_pos)
-    stacked = (
-        keys_every.reshape(block_count, block_rows, kv_heads, HD),
-        values_every.reshape(block_count, block_rows, kv_heads, HD),
-        key_pos.reshape(block_count, block_rows),
-        key_doc.reshape(block_count, block_rows),
-    )
-
-    def key_block(state_now, inputs_now):
-        keys_blk, values_blk, pos_blk, doc_blk = inputs_now
-        best_old, total_old, accum_old = state_now
-        allowed_now = (pos_blk[None, :] <= own_positions[:, None]) & (
-            doc_blk[None, :] == own_doc[:, None]
-        )
-        scores_now = jnp.einsum(
-            "qkgd,nkd->kgqn", queries, keys_blk, preferred_element_type=jnp.float32
-        ) / math.sqrt(HD)
-        scores_now = jnp.where(allowed_now[None, None], scores_now, big_negative)
-        best_new = jnp.maximum(best_old, jnp.max(scores_now, axis=-1))
-        factor = jnp.exp(best_old - best_new)
-        powers_now = jnp.where(
-            allowed_now[None, None], jnp.exp(scores_now - best_new[..., None]), 0.0
-        )
-        total_new = total_old * factor + jnp.sum(powers_now, axis=-1)
-        accum_new = accum_old * factor[..., None] + jnp.einsum(
-            "kgqn,nkd->kgqd",
-            powers_now.astype(jnp.bfloat16),
-            values_blk,
-            preferred_element_type=jnp.float32,
-        )
-        return ((best_new, total_new, accum_new), None)
-
-    carry_state, unused = lax.scan(key_block, carry_state, stacked)
-    best_final, total_final, accum_final = carry_state
+    allowed_now = (key_pos[None, :] <= own_positions[:, None]) & (
+        key_doc[None, :] == own_doc[:, None]
+    )
+    scores_now = jnp.einsum(
+        "qkgd,nkd->kgqn", queries, keys_every, preferred_element_type=jnp.float32
+    ) / math.sqrt(HD)
+    scores_now = jnp.where(allowed_now[None, None], scores_now, big_negative)
+    best = jnp.max(scores_now, axis=-1, keepdims=True)
+    powers_now = jnp.exp(scores_now - best)
+    total_final = jnp.sum(powers_now, axis=-1)
+    accum_final = jnp.einsum(
+        "kgqn,nkd->kgqd",
+        powers_now.astype(jnp.bfloat16),
+        values_every,
+        preferred_element_type=jnp.float32,
+    )
     result = accum_final / total_final[..., None]
     return (
         jnp.transpose(result, (2, 0, 1, 3)).reshape(TOK, kv_heads, groups * HD).astype(jnp.bfloat16)

time: 269 us -> 238 us (0.88)
  waiting for transfers between devices: 165 us -> 110 us
  blocking collectives: 0 us -> 15.4 us
  local copies, waits for them, and re-layouts: 44.9 us -> 59.1 us
  starting transfers between devices: 3.67 us -> 0.34 us
    all_gather x2 -> x1, waiting for transfers between devices: 123 us -> 6.88 us  [local(): lax.all_gather(own_half, ('ctx', 'tp'), axis=0, tiled=False)]
    reduce_scatter x0 -> x1, waiting for transfers between devices: none -> 61.8 us  [local(): lax.psum_scatter(partial, 'ctx', scatter_dimension=0, tiled=True)]
    unnamed x33 -> x36, local copies, waits for them, and re-layouts: 5.02 us -> 26.1 us
    dot_general x2 -> x0, local copies, waits for them, and re-layouts: 17.8 us -> none  [the longest x1 11.4 us: local(): jnp.dot(normed_rows, w_query.reshape(D, kv_heads * groups * HD), preferre...]
    all_to_all x0 -> x1, blocking collectives: none -> 15.4 us  [local(): lax.all_to_all(blocks, 'ctx', split_axis=0, concat_axis=0, tiled=True)]
    slice x0 -> x2, local copies, waits for them, and re-layouts: none -> 12.6 us  [local(): keys_every = both[:, 0].reshape(key_count, kv_heads, HD)]
    dot_general x8 -> x6, matrix products: 23.5 us -> 11.5 us  [the longest x1 2.9 us: local(): partial = jnp.dot(by_dest, merge_weight, preferred_element_type=jnp.float32)]
    unnamed x0 -> x3, matrix products: none -> 11.6 us
  transfers between devices with their start and end apart: 6 -> 4, of which waited for: 5 -> 4; matrix products, arithmetic and copies ran while one was open for 21% -> 20% of each run, Pallas kernels for 0% -> 0%
where the time goes in v1:
time: 238 us; the launch traced here: 237 us
  waiting for transfers between devices  110 us (46%)
  local copies, waits for them, and re-layouts  59.1 us (25%)
  matrix products  23.6 us (10%)
  blocking collectives  15.4 us (6%)
  other arithmetic  14.8 us (6%)
  between operations  13.5 us (6%)
    reduce_scatter x1, waiting for transfers between devices, local(): lax.psum_scatter(partial, 'ctx', scatter_dimension=0, tiled=True)  61.8 us
    psum x1, waiting for transfers between devices, local(): branch_sum = lax.psum(branch_part, ('vis', 'tp'))  35.1 us
    unnamed x36, local copies, waits for them, and re-layouts  26.1 us
    all_to_all x1, blocking collectives, local(): lax.all_to_all(blocks, 'ctx', split_axis=0, concat_axis=0, tiled=True)  15.4 us
    slice x2, local copies, waits for them, and re-layouts, local(): keys_every = both[:, 0].reshape(key_count, kv_heads, HD)  12.6 us
    unnamed x3, matrix products  11.6 us
    squeeze x1, local copies, waits for them, and re-layouts, local(): w_keyval[0]  7.62 us
    all_gather x1, waiting for transfers between devices, local(): lax.all_gather(own_half, ('ctx', 'tp'), axis=0, tiled=False)  6.88 us
  transfers between devices with their start and end apart: 4, of which 4 were waited for; matrix products, arithmetic and copies ran while one was open for 20% of the time, Pallas kernels for 0%

profile of v1, /device:TPU:0, one launch (start us, length us, event | category | flops | bytes accessed | tf_op | source)
XLA Modules:
  0.0 236.7 jit_solution(16527992637986011291)
XLA Ops:
  6.5 0.0 all-reduce.2.cloned.1.call-start
  6.6 1.2 convert_reduce_fusion
  7.9 1.2 fusion.28
  9.1 1.9 fusion.32
  11.0 0.1 broadcast_compare_fusion
  11.1 0.3 fusion.96
  11.4 0.1 fusion.48
  11.5 2.6 %convolution_bitcast_fusion = f32[128,1280]{1,0:T(8,128)} fusion(bf16[4,80,1280]{2,1,0:T(8,128)(2,1)} %param.21, f32[4,128,128]{1,2,0:T(8,128)S(1)} %get-tuple-element.22, f32[4,128]{1,0:T(4,128)S(1)} %get-tuple-element.21, bf16[128,3,4,80]{0,3,2,1:T(8,128)(2,1)S(1)} %convert_element_type.68, f32[128,4]{0,1:T(4,128)S(1)} %bitcast.111), kind=kOutput, calls=%fused_computation.10 | convolution fusion | flops 115556352 | bytes 1822720 | tf_op jit(solution)/shard_map/phd,hdf->pf/dot_general | solution.py:112
  14.0 0.0 all-reduce.2.cloned.1.call-update
  14.0 0.0 reduce-scatter.2.cloned.1.call-start
  14.1 0.1 reshape.664
  14.2 0.1 copy.80
  14.3 0.7 fusion.50
  15.0 0.7 fusion.94
  15.7 0.1 select_reduce_fusion.2
  15.9 35.1 %all-reduce.2.cloned.1.call-done = f32[128,1280]{1,0:T(8,128)} async-done(((f32[128,1280]{1,0:T(8,128)}), f32[128,1280]{1,0:T(8,128)}) %all-reduce.2.cloned.1.call-update) | async-done | bytes 655376 | tf_op jit(solution)/shard_map/psum | solution.py:113
  51.0 1.2 fusion.47
  52.2 1.3 multiply_reduce_fusion
  53.6 1.3 add_convert_fusion
  54.9 0.2 reshape.665
  55.1 0.2 convolution_convert_fusion
  55.4 15.4 %all_to_all.5 = bf16[8,32,640]{2,1,0:T(8,128)(2,1)S(1)} all-to-all(bf16[8,32,640]{2,1,0:T(8,128)(2,1)S(1)} %bitcast.102), channel_id=1, replica_groups=mesh['vis'=2,'ctx'=8,'tp'=2] {'ctx'}, dimensions={0} | all-to-all | bytes 655360 | tf_op jit(solution)/shard_map/all_to_all | solution.py:132
  70.7 0.1 copy.88
  70.8 0.1 copy.89
  71.0 0.1 reshape.668
  71.0 2.9 %fusion.97 = f32[256,1024]{1,0:T(8,128)} fusion(bf16[256,640]{1,0:T(8,128)(2,1)S(1)} %reshape.668, bf16[640,1024]{1,0:T(8,128)(2,1)} %param.24), kind=kOutput, calls=%fused_computation.190 | convolution fusion | flops 335544320 | bytes 2686976 | tf_op jit(solution)/shard_map/dot_general | solution.py:136
  73.9 0.0 reduce-scatter.2.cloned.1.call-update
  74.0 0.0 all-gather.4.cloned.1.call-start
  74.0 0.1 copy.84
  74.1 0.1 copy.85
  74.2 0.1 fusion.80
  74.3 0.1 and.279
  74.4 0.1 broadcast_add_fusion
  74.4 0.1 add.362
  74.5 0.3 fusion.95
  74.8 61.8 %reduce-scatter.2.cloned.1.call-done = f32[32,1024]{1,0:T(8,128)} async-done(((f32[256,1024]{1,0:T(8,128)}), f32[32,1024]{1,0:T(8,128)}) %reduce-scatter.2.cloned.1.call-update) | async-done | bytes 131088 | tf_op jit(solution)/shard_map/reduce_scatter | solution.py:137
  136.6 1.9 fusion.16
  138.5 0.0 all-gather.4.cloned.1.call-update
  138.5 0.2 all-gather.6.cloned.1.call-start
  138.7 0.1 select_reduce_fusion.3
  138.9 1.0 gather_fusion.1
  139.9 0.5 and_select_fusion.8
  140.4 7.6 %copy.90 = bf16[4096,4,128]{0,2,1:T(8,128)(2,1)} copy(bf16[4096,4,128]{2,1,0:T(4,128)(2,1)} %bitcast.97) | data formatting | bytes 8388608 | tf_op jit(solution)/shard_map/squeeze | solution.py:169
  148.0 0.2 multiply_cosine_fusion
  148.2 6.1 %all-gather.4.cloned.1.call-done = bf16[128,4096]{1,0:T(8,128)(2,1)} async-done(((bf16[128,1024]{1,0:T(8,128)(2,1)}), bf16[128,4096]{1,0:T(8,128)(2,1)}) %all-gather.4.cloned.1.call-update) | async-done | bytes 1048592 | tf_op jit(solution)/shard_map/all_gather | solution.py:151
  154.3 1.5 fusion.3
  155.9 3.8 %fusion.40 = f32[128,512]{0,1:S(1)} fusion(bf16[4096,512]{0,1:T(8,128)(2,1)} %bitcast.98, bf16[128,4096]{1,0:T(8,128)(2,1)} %all-gather.4.cloned.1.call-done, f32[4096]{0:T(1024)S(1)} %copy-done.8, f32[128]{0:T(128)S(1)} %add_rsqrt_fusion), kind=kOutput, calls=%fused_computation.50 | convolution fusion | flops 538968064 | bytes 5521920
  159.8 0.7 fusion.42
  160.5 0.0 all-gather.6.cloned.1.call-update
  160.5 21.3 %copy.92 = bf16[4096,4,2,128]{0,3,2,1:T(8,128)(2,1)} copy(bf16[4096,4,2,128]{3,2,1,0:T(2,128)(2,1)} %param.32) | data formatting | bytes 16777216 | tf_op args[15]
  181.8 0.1 select_reduce_fusion
  181.9 4.5 %gather_fusion = s32[1024]{0:T(1024)S(1)} fusion(s32[1024]{0:T(1024)S(1)} %copy-done.1, s32[1024]{0:T(1024)S(1)} %broadcast_clamp_fusion), kind=kCustom, calls=%fused_computation | custom fusion | bytes 12288 | tf_op jit(solution)/shard_map/jit(_take)/gather | solution.py:181
  186.5 1.7 compare_and_fusion
  188.2 5.8 %fusion.38 = f32[128,1024]{0,1:S(1)} fusion(bf16[4096,1024]{0,1:T(8,128)(2,1)} %bitcast.96, bf16[128,4096]{1,0:T(8,128)(2,1)S(1)} %copy-done.3, f32[4096]{0:T(1024)} %param.31, f32[128]{0:T(128)} %copy-done.13), kind=kOutput, calls=%fused_computation.49 | convolution fusion | flops 1075838976 | bytes 9978368
  194.0 0.8 subtract_convert_fusion
  194.8 6.9 %all-gather.6.cloned.1.call-done = bf16[2048,4,128]{0,2,1:T(8,128)(2,1)} async-done(((bf16[128,4,128]{0,2,1:T(8,128)(2,1)}), bf16[2048,4,128]{0,2,1:T(8,128)(2,1)}) %all-gather.6.cloned.1.call-update) | async-done | bytes 2097168 | tf_op jit(solution)/shard_map/all_gather | solution.py:174
  201.7 4.4 %reshape.669 = bf16[8,2,128,4,128]{2,1,0,4,3:T(2,128)(2,1)} reshape(bf16[2048,4,128]{0,2,1:T(8,128)(2,1)} %all-gather.6.cloned.1.call-done) | data formatting | bytes 4194304 | tf_op jit(solution)/shard_map/reshape | solution.py:174
  206.1 6.8 %fusion.93 = (bf16[8,1,128,4,128]{2,1,0,4,3:T(2,128)(2,1)}, bf16[8,1,128,4,128]{2,1,0,4,3:T(2,128)(2,1)}) fusion(bf16[8,2,128,4,128]{2,1,0,4,3:T(2,128)(2,1)} %reshape.669), kind=kLoop, calls=%fused_computation.186 | loop fusion | bytes 4194304 | tf_op jit(solution)/shard_map/slice | solution.py:178
  212.9 5.8 %copy.91 = bf16[8,1,128,4,128]{4,2,0,3,1:T(8,128)(2,1)} copy(bf16[8,1,128,4,128]{2,1,0,4,3:T(2,128)(2,1)} %get-tuple-element.11) | data formatting | bytes 2097152 | tf_op jit(solution)/shard_map/slice | solution.py:178
  218.7 4.7 %copy.105 = bf16[8,1,128,4,128]{4,2,0,3,1:T(8,128)(2,1)S(1)} copy(bf16[8,1,128,4,128]{2,1,0,4,3:T(2,128)(2,1)} %get-tuple-element.12) | data formatting | bytes 2097152
  223.4 2.1 fusion.2
  225.5 0.9 fusion
  226.4 1.9 fusion.23
  228.3 1.8 copy.97
  (59 shorter events, 0.4 us)
Async XLA Ops:
  6.5 2.5 %copy-start = (bf16[1280,3,4,80]{0,3,2,1:T(8,128)(2,1)S(1)}, bf16[1280,3,4,80]{0,3,2,1:T(8,128)(2,1)}, u32[]{:S(2)}) copy-start(bf16[1280,3,4,80]{0,3,2,1:T(8,128)(2,1)} %param.20) | copy-start | bytes 7372804
  6.5 44.5 %copy-start.2 = (bf16[128,1280]{1,0:T(8,128)(2,1)S(1)}, bf16[128,1280]{1,0:T(8,128)(2,1)}, u32[]{:S(2)}) copy-start(bf16[128,1280]{1,0:T(8,128)(2,1)} %param.17) | copy-start | bytes 983044
  6.5 4.5 %copy-start.15 = (s32[128]{0:T(128)S(1)}, s32[128]{0:T(128)}, u32[]{:S(2)}) copy-start(s32[128]{0:T(128)} %param.26) | copy-start | bytes 1540
  6.5 7.6 %copy-start.12 = (s32[256]{0:T(256)S(1)}, s32[256]{0:T(256)}, u32[]{:S(2)}) copy-start(s32[256]{0:T(256)} %param.27) | copy-start | bytes 3076
  6.5 7.7 %copy-start.11 = (s32[8]{0:T(128)S(1)}, s32[8]{0:T(128)}, u32[]{:S(2)}) copy-start(s32[8]{0:T(128)} %param.28) | copy-start | bytes 100
  6.5 44.4 %all-reduce.2.cloned.1.call-start = ((), (), s32[]{:S(2)}) async-start(), calls=%async_computation.2 | async-start | bytes 1310720 | tf_op jit(solution)/shard_map/psum | solution.py:113
  9.1 44.5 %copy-start.9 = (f32[1280]{0:T(1024)S(1)}, f32[1280]{0:T(1024)}, u32[]{:S(2)}) copy-start(f32[1280]{0:T(1024)} %param.23) | copy-start | bytes 15364
  9.1 44.5 %copy-start.10 = (f32[1280]{0:T(1024)S(1)}, f32[1280]{0:T(1024)}, u32[]{:S(2)}) copy-start(f32[1280]{0:T(1024)} %param.22) | copy-start | bytes 15364
  14.0 122.6 %reduce-scatter.2.cloned.1.call-start = ((), (), s32[]{:S(2)}) async-start(), calls=%async_computation.3 | async-start | bytes 1179648 | tf_op jit(solution)/shard_map/reduce_scatter | solution.py:137
  54.8 19.3 %copy-start.16 = (s32[8,2]{0,1:T(2,128)S(1)}, s32[8,2]{0,1:T(2,128)}, u32[]{:S(2)}) copy-start(s32[8,2]{0,1:T(2,128)} %param.25) | copy-start | bytes 196
  54.9 81.8 %copy-start.7 = (bf16[128,1024]{1,0:T(8,128)(2,1)S(1)}, bf16[128,1024]{1,0:T(8,128)(2,1)}, u32[]{:S(2)}) copy-start(bf16[128,1024]{1,0:T(8,128)(2,1)} %param.30) | copy-start | bytes 786436
  55.3 83.6 %copy-start.1 = (s32[1024]{0:T(1024)S(1)}, s32[1024]{0:T(1024)}, u32[]{:S(2)}) copy-start(s32[1024]{0:T(1024)} %param.29) | copy-start | bytes 12292
  74.0 80.3 %all-gather.4.cloned.1.call-start = ((), (), s32[]{:S(2)}) async-start(), calls=%async_computation.4 | async-start | bytes 1310720 | tf_op jit(solution)/shard_map/all_gather | solution.py:151
  138.5 63.2 %all-gather.6.cloned.1.call-start = ((), (), s32[]{:S(2)}) async-start(), calls=%async_computation.5 | async-start | bytes 2228224 | tf_op jit(solution)/shard_map/all_gather | solution.py:174
  140.4 7.6 %copy-start.14 = (s32[128]{0:T(128)}, s32[128]{0:T(128)S(1)}, u32[]{:S(2)}) copy-start(s32[128]{0:T(128)S(1)} %get-tuple-element.10) | copy-start | bytes 1540
  140.4 15.5 %copy-start.8 = (f32[4096]{0:T(1024)S(1)}, f32[4096]{0:T(1024)}, u32[]{:S(2)}) copy-start(f32[4096]{0:T(1024)} %param.31) | copy-start | bytes 49156
  148.2 12.3 %copy-start.5 = (f32[128,64]{0,1:T(8,128)}, f32[128,64]{0,1:T(8,128)S(1)}, u32[]{:S(2)}) copy-start(f32[128,64]{0,1:T(8,128)S(1)} %get-tuple-element.18) | copy-start | bytes 98308
  155.8 26.0 %copy-start.13 = (f32[128]{0:T(128)}, f32[128]{0:T(128)S(1)}, u32[]{:S(2)}) copy-start(f32[128]{0:T(128)S(1)} %add_rsqrt_fusion) | copy-start | bytes 1540
  181.8 6.3 %copy-start.3 = (bf16[128,4096]{1,0:T(8,128)(2,1)S(1)}, bf16[128,4096]{1,0:T(8,128)(2,1)}, u32[]{:S(2)}) copy-start(bf16[128,4096]{1,0:T(8,128)(2,1)} %all-gather.4.cloned.1.call-done) | copy-start | bytes 3145732
  188.2 5.8 %copy-start.6 = (f32[128,64]{0,1:T(8,128)S(1)}, f32[128,64]{0,1:T(8,128)}, u32[]{:S(2)}) copy-start(f32[128,64]{0,1:T(8,128)} %copy-done.5) | copy-start | bytes 98308
  223.4 2.1 copy-start.4
Sparse Core Ops, SparseCore 0:
  14.2 36.7 all-reduce.1
  74.1 62.4 reduce-scatter.1
  138.6 15.6 all-gather.3
  160.6 41.0 all-gather.5

commit v2 on v1

--- a/solution.py
+++ b/solution.py
@@ -66,6 +66,35 @@
     owner_dev = jnp.sum(owner_hot * jnp.arange(shards, dtype=jnp.int32), axis=-1)
     local_row = jnp.where(slice_ids < shards, 0, half_tok) + positions % half_tok
     return (owner_dev, local_row, owner_hot)
+
+
+def halving_scatter(blocks, index, count):
+    remaining = count
+    bit = 0
+    while remaining > 1:
+        lower = blocks.reshape((remaining // 2, 2) + blocks.shape[1:])
+        mine = (index >> bit) & 1
+        keep = jnp.where(mine == 0, lower[:, 0], lower[:, 1])
+        give = jnp.where(mine == 0, lower[:, 1], lower[:, 0])
+        blocks = keep + swapped(give, "ctx", bit)
+        remaining //= 2
+        bit += 1
+    return blocks[0]
+
+
+def rotate_rows(values, positions):
+    half_dim = values.shape[-1] // 2
+    exponent = jnp.arange(half_dim, dtype=jnp.float32) * (-2.0 / values.shape[-1])
+    frequency = jnp.power(jnp.float32(rope_base), exponent)
+    angles = positions.astype(jnp.float32)[:, None] * frequency[None, :]
+    cosine = jnp.cos(angles)
+    sine_part = jnp.sin(angles)
+    lead_half = values[..., :half_dim]
+    tail_half = values[..., half_dim:]
+    return jnp.concatenate(
+        [lead_half * cosine - tail_half * sine_part, tail_half * cosine + lead_half * sine_part],
+        axis=-1,
+    )
 
 
 def local(
@@ -110,7 +139,8 @@
     )
     blended = (blended / jnp.transpose(totals)[:, :, None]).astype(jnp.bfloat16)
     branch_part = jnp.einsum("phd,hdf->pf", blended, vit_out, preferred_element_type=jnp.float32)
-    branch_sum = lax.psum(branch_part, ("vis", "tp"))
+    branch_sum = branch_part + swapped(branch_part, "tp", 0)
+    branch_sum = branch_sum + swapped(branch_sum, "vis", 0)
     hidden = patch_rows.astype(jnp.float32) + branch_sum
     merged = layer_norm(hidden, merge_gain, merge_bias).astype(jnp.bfloat16).reshape(ICAP, 4 * VD)
     send_each = ICAP // shards
@@ -134,7 +164,7 @@
         received.reshape(shards, shards, send_each, block_feats), (1, 0, 2, 3)
     ).reshape(shards * ICAP, block_feats)
     partial = jnp.dot(by_dest, merge_weight, preferred_element_type=jnp.float32)
-    incoming = lax.psum_scatter(partial, "ctx", scatter_dimension=0, tiled=True).astype(
+    incoming = halving_scatter(partial.reshape(shards, ICAP, -1), ctx_index, shards).astype(
         jnp.bfloat16
     )
     mine_live = ((owner_dev == ctx_index) & is_live).reshape(-1)
@@ -162,35 +192,35 @@
     kv_heads = w_query.shape[1]
     groups = w_query.shape[2]
     queries = jnp.einsum(
-        "td,dhgk->thgk", normed_rows, w_query, preferred_element_type=jnp.float32
-    )
-    queries = rotate(queries, own_positions).astype(jnp.bfloat16)
+        "td,dhgk->hgtk", normed_rows, w_query, preferred_element_type=jnp.float32
+    )
+    queries = rotate_rows(queries, own_positions).astype(jnp.bfloat16)
     projected_half = jnp.einsum(
-        "td,dhk->thk", normed_rows, w_keyval[0], preferred_element_type=jnp.float32
+        "td,dhk->htk", normed_rows, w_keyval[0], preferred_element_type=jnp.float32
     )
     own_half = jnp.where(
-        tp_index == 0, rotate(projected_half, own_positions), projected_half
-    ).astype(jnp.bfloat16)
-    both = lax.all_gather(own_half, ("ctx", "tp"), axis=0, tiled=False).reshape(
-        shards, 2, TOK, kv_heads, HD
+        tp_index == 0, rotate_rows(projected_half, own_positions), projected_half
+    ).astype(jnp.bfloat16)
+    both = lax.all_gather(own_half, ("ctx", "tp"), axis=1, tiled=True).reshape(
+        kv_heads, shards, 2, TOK, HD
     )
     key_count = shards * TOK
-    keys_every = both[:, 0].reshape(key_count, kv_heads, HD)
-    values_every = both[:, 1].reshape(key_count, kv_heads, HD)
+    keys_every = both[:, :, 0].reshape(kv_heads, key_count, HD)
+    values_every = both[:, :, 1].reshape(kv_heads, key_count, HD)
     key_pos = row_positions(jnp.arange(key_count, dtype=jnp.int32), slice_order, TOK)
     key_doc = jnp.take(doc_ids, key_pos)
     allowed_now = (key_pos[None, :] <= own_positions[:, None]) & (
         key_doc[None, :] == own_doc[:, None]
     )
     scores_now = jnp.einsum(
-        "qkgd,nkd->kgqn", queries, keys_every, preferred_element_type=jnp.float32
+        "hgtd,hnd->hgtn", queries, keys_every, preferred_element_type=jnp.float32
     ) / math.sqrt(HD)
     scores_now = jnp.where(allowed_now[None, None], scores_now, big_negative)
     best = jnp.max(scores_now, axis=-1, keepdims=True)
     powers_now = jnp.exp(scores_now - best)
     total_final = jnp.sum(powers_now, axis=-1)
     accum_final = jnp.einsum(
-        "kgqn,nkd->kgqd",
+        "hgtn,hnd->hgtd",
         powers_now.astype(jnp.bfloat16),
         values_every,
         preferred_element_type=jnp.float32,

time: 238 us -> 185 us (0.78)
  waiting for transfers between devices: 110 us -> 59.8 us
  blocking collectives: 15.4 us -> 0 us
  starting transfers between devices: 0.34 us -> 14.8 us
  matrix products: 23.6 us -> 20.4 us
    reduce_scatter x1 -> x0, waiting for transfers between devices: 61.8 us -> none  [local(): lax.psum_scatter(partial, 'ctx', scatter_dimension=0, tiled=True)]
    psum x1 -> x0, waiting for transfers between devices: 35.1 us -> none  [local(): branch_sum = lax.psum(branch_part, ('vis', 'tp'))]
    ppermute x0 -> x5, waiting for transfers between devices: none -> 34.7 us  [swapped(): lax.ppermute(value, axis, [(i, i ^ 1 << stride) for i in range(lax.axis_s...]
    all_to_all x1 -> x0, blocking collectives: 15.4 us -> none  [local(): lax.all_to_all(blocks, 'ctx', split_axis=0, concat_axis=0, tiled=True)]
    all_to_all x0 -> x1, waiting for transfers between devices: none -> 9.5 us  [local(): lax.all_to_all(blocks, 'ctx', split_axis=0, concat_axis=0, tiled=True)]
    ppermute x0 -> x5, starting transfers between devices: none -> 8.44 us  [swapped(): lax.ppermute(value, axis, [(i, i ^ 1 << stride) for i in range(lax.axis_s...]
    all_to_all x0 -> x1, starting transfers between devices: none -> 6.08 us  [local(): lax.all_to_all(blocks, 'ctx', split_axis=0, concat_axis=0, tiled=True)]
    unnamed x36 -> x42, local copies, waits for them, and re-layouts: 26.1 us -> 27.9 us
  transfers between devices with their start and end apart: 4 -> 8, of which waited for: 4 -> 8; matrix products, arithmetic and copies ran while one was open for 20% -> 25% of each run, Pallas kernels for 0% -> 0%
where the time goes in v2:
time: 185 us; the launch traced here: 183 us
  waiting for transfers between devices  59.8 us (32%)
  local copies, waits for them, and re-layouts  59.5 us (32%)
  matrix products  20.4 us (11%)
  starting transfers between devices  14.8 us (8%)
  other arithmetic  14.7 us (8%)
  between operations  13.8 us (7%)
    ppermute x5, waiting for transfers between devices, swapped(): lax.ppermute(value, axis, [(i, i ^ 1 << stride) for i in range(lax.axis_s...  34.7 us
    unnamed x42, local copies, waits for them, and re-layouts  27.9 us
    unnamed x3, matrix products  11.6 us
    slice x2, local copies, waits for them, and re-layouts, local(): keys_every = both[:, :, 0].reshape(kv_heads, key_count, HD)  11.5 us
    all_to_all x1, waiting for transfers between devices, local(): lax.all_to_all(blocks, 'ctx', split_axis=0, concat_axis=0, tiled=True)  9.5 us
    ppermute x5, starting transfers between devices, swapped(): lax.ppermute(value, axis, [(i, i ^ 1 << stride) for i in range(lax.axis_s...  8.44 us
    all_gather x1, waiting for transfers between devices, local(): full_rows = lax.all_gather(embeds, ('vis', 'tp'), axis=1, tiled=True)  8.42 us
    squeeze x1, local copies, waits for them, and re-layouts, local(): w_keyval[0]  7.62 us
  transfers between devices with their start and end apart: 8, of which 8 were waited for; matrix products, arithmetic and copies ran while one was open for 25% of the time, Pallas kernels for 0%

profile of v2, /device:TPU:0, one launch (start us, length us, event | category | flops | bytes accessed | tf_op | source)
XLA Modules:
  0.0 183.0 jit_solution(1458814526742477499)
XLA Ops:
  6.5 1.2 convert_reduce_fusion
  7.8 1.2 fusion.30
  9.0 1.9 %fusion.36 = f32[128,960]{0,1:S(1)} fusion(bf16[1280,960]{0,1:T(8,128)(2,1)S(1)} %bitcast.143, bf16[128,1280]{1,0:T(8,128)(2,1)} %param.17, f32[1280]{0:T(1024)} %param.19, f32[1280]{0:T(1024)} %param.18, f32[128]{0:T(128)S(1)} %add_rsqrt_fusion.2, f32[128]{0:T(128)S(1)} %broadcast_multiply_fusion.1), kind=kOutput, calls=%fused_computation.49 | convolution fusion | flops 315555840 | bytes 3288064
  11.1 0.1 broadcast_compare_fusion
  11.1 0.3 fusion.106
  11.5 0.3 copy-done.7
  11.7 0.4 copy-done.6
  12.1 1.8 convolution_bitcast_fusion
  13.9 0.6 collective-permute-start
  14.7 0.7 fusion.56
  15.4 1.0 collective-permute-done
  16.3 1.2 add.378
  17.5 2.9 %collective-permute-start.1 = (f32[128,1280]{1,0:T(8,128)S(1)}, f32[128,1280]{1,0:T(8,128)S(1)}, u32[]{:S(2)}, u32[]{:S(2)}) collective-permute-start(f32[128,1280]{1,0:T(8,128)S(1)} %add.378), channel_id=1, source_target_pairs={{0,16},{16,0},{1,17},{17,1},{2,18},{18,2},{3,19},{19,3},{4,20},{20... | collective-permute-start | bytes 1966088 | tf_op jit(solution)/shard_map/ppermute | solution.py:23
  20.4 0.7 fusion.104
  21.2 0.1 select_reduce_fusion.2
  21.3 14.2 %collective-permute-done.1 = f32[128,1280]{1,0:T(8,128)S(1)} collective-permute-done((f32[128,1280]{1,0:T(8,128)S(1)}, f32[128,1280]{1,0:T(8,128)S(1)}, u32[]{:S(2)}, u32[]{:S(2)}) %collective-permute-start.1) | collective-permute-done | bytes 655392 | tf_op jit(solution)/shard_map/ppermute | solution.py:23
  35.5 0.2 fusion.102
  35.6 0.2 multiply_reduce_fusion
  35.9 0.2 add_convert_fusion
  36.1 0.2 reshape.736
  36.3 0.2 convolution_convert_fusion
  36.5 0.7 copy.134
  37.2 6.1 %all-to-all-start = ((bf16[8,32,640]{2,1,0:T(8,128)(2,1)}), bf16[8,32,640]{2,1,0:T(8,128)(2,1)S(1)}, u32[]{:S(2)}, u32[]{:S(2)}) async-start(bf16[8,32,640]{2,1,0:T(8,128)(2,1)} %bitcast.141), calls=%async_computation | async-start | bytes 655360 | tf_op jit(solution)/shard_map/all_to_all | solution.py:162
  43.5 9.5 %all-to-all-done = bf16[8,32,640]{2,1,0:T(8,128)(2,1)S(1)} async-done(((bf16[8,32,640]{2,1,0:T(8,128)(2,1)}), bf16[8,32,640]{2,1,0:T(8,128)(2,1)S(1)}, u32[]{:S(2)}, u32[]{:S(2)}) %all-to-all-start) | async-done | bytes 327712 | tf_op jit(solution)/shard_map/all_to_all | solution.py:162
  53.1 0.1 reshape.738
  53.1 0.1 copy.135
  53.4 1.9 %fusion.12 = f32[4,2,32,1024]{3,2,1,0:T(8,128)S(1)} fusion(bf16[4,2,32,640]{3,2,1,0:T(8,128)(2,1)S(1)} %dot_general.46, bf16[640,1024]{1,0:T(8,128)(2,1)} %param.24), kind=kOutput, calls=%fused_computation.19 | convolution fusion | flops 335544320 | bytes 2686976 | tf_op jit(solution)/shard_map/dot_general | solution.py:166
  55.4 1.6 collective-permute-start.2
  57.1 9.4 %collective-permute-done.2 = f32[4,32,1024]{2,1,0:T(8,128)S(1)} collective-permute-done((f32[4,32,1024]{2,1,0:T(8,128)S(1)}, f32[4,32,1024]{2,1,0:T(8,128)S(1)}, u32[]{:S(2)}, u32[]{:S(2)}) %collective-permute-start.2) | collective-permute-done | bytes 524320 | tf_op jit(solution)/shard_map/ppermute | solution.py:23
  66.5 0.1 fusion.35
  66.6 0.7 select_bitcast_fusion.1
  67.3 0.7 collective-permute-start.3
  68.0 0.1 and.288
  68.2 0.3 fusion.105
  68.5 5.5 %collective-permute-done.3 = f32[2,32,1024]{2,1,0:T(8,128)} collective-permute-done((f32[2,32,1024]{2,1,0:T(8,128)}, f32[2,32,1024]{2,1,0:T(8,128)}, u32[]{:S(2)}, u32[]{:S(2)}) %collective-permute-start.3) | collective-permute-done | bytes 262176 | tf_op jit(solution)/shard_map/ppermute | solution.py:23
  74.0 1.0 fusion.53
  75.0 2.7 %collective-permute-start.4 = (f32[1,32,1024]{2,1,0:T(8,128)S(1)}, f32[1,32,1024]{2,1,0:T(8,128)S(1)}, u32[]{:S(2)}, u32[]{:S(2)}) collective-permute-start(f32[1,32,1024]{2,1,0:T(8,128)S(1)} %select_bitcast_fusion.2), channel_id=1, source_target_pairs={{0,8},{2,10},{4,12},{6,14},{8,0},{10,2},{12,4},{14,6},{1,9},{3,11}... | collective-permute-start | bytes 393224 | tf_op jit(solution)/shard_map/ppermute | solution.py:23
  77.7 4.6 %collective-permute-done.4 = f32[1,32,1024]{2,1,0:T(8,128)S(1)} collective-permute-done((f32[1,32,1024]{2,1,0:T(8,128)S(1)}, f32[1,32,1024]{2,1,0:T(8,128)S(1)}, u32[]{:S(2)}, u32[]{:S(2)}) %collective-permute-start.4) | collective-permute-done | bytes 131104 | tf_op jit(solution)/shard_map/ppermute | solution.py:23
  82.4 1.0 fusion.18
  83.4 0.2 all-gather.5.cloned.1.call-start
  83.6 0.1 select_reduce_fusion.3
  83.7 1.0 gather_fusion.1
  84.7 0.5 and_select_fusion.8
  85.3 7.6 %copy.115 = bf16[4096,4,128]{0,2,1:T(8,128)(2,1)} copy(bf16[4096,4,128]{2,1,0:T(4,128)(2,1)} %bitcast.148) | data formatting | bytes 8388608 | tf_op jit(solution)/shard_map/squeeze | solution.py:199
  92.9 0.2 multiply_cosine_fusion
  93.1 8.4 %all-gather.3.cloned.1.call-done = bf16[128,4096]{1,0:T(8,128)(2,1)} async-done(((bf16[128,1024]{1,0:T(8,128)(2,1)}), bf16[128,4096]{1,0:T(8,128)(2,1)}) %all-gather.3.cloned.1.call-update) | async-done | bytes 1048592 | tf_op jit(solution)/shard_map/all_gather | solution.py:181
  101.5 1.5 fusion.3
  103.1 3.8 %fusion.42 = f32[128,512]{0,1:S(1)} fusion(bf16[4096,512]{0,1:T(8,128)(2,1)} %bitcast.149, bf16[128,4096]{1,0:T(8,128)(2,1)} %all-gather.3.cloned.1.call-done, f32[4096]{0:T(1024)S(1)} %copy-done.11, f32[128]{0:T(128)S(1)} %add_rsqrt_fusion), kind=kOutput, calls=%fused_computation.56 | convolution fusion | flops 538968064 | bytes 5521920
  107.0 0.7 fusion.50
  107.7 21.3 %copy.114 = bf16[4096,4,2,128]{0,3,2,1:T(8,128)(2,1)} copy(bf16[4096,4,2,128]{3,2,1,0:T(2,128)(2,1)} %param.32) | data formatting | bytes 16777216 | tf_op args[15]
  129.0 0.1 select_reduce_fusion
  129.2 4.5 %gather_fusion = s32[1024]{0:T(1024)S(1)} fusion(s32[1024]{0:T(1024)S(1)} %copy-done.1, s32[1024]{0:T(1024)S(1)} %broadcast_clamp_fusion), kind=kCustom, calls=%fused_computation | custom fusion | bytes 12288 | tf_op jit(solution)/shard_map/jit(_take)/gather | solution.py:211
  133.7 1.5 compare_and_fusion
  135.2 5.8 %fusion.44 = f32[128,1024]{0,1:S(1)} fusion(bf16[4096,1024]{0,1:T(8,128)(2,1)} %bitcast.144, bf16[128,4096]{1,0:T(8,128)(2,1)S(1)} %copy-done.2, f32[4096]{0:T(1024)} %param.31, f32[128]{0:T(128)} %copy-done.16), kind=kOutput, calls=%fused_computation.57 | convolution fusion | flops 1075838976 | bytes 9978368
  141.0 0.8 subtract_convert_fusion
  141.8 7.1 %all-gather.5.cloned.1.call-done = bf16[4,2048,128]{1,2,0:T(8,128)(2,1)} async-done(((bf16[4,128,128]{1,2,0:T(8,128)(2,1)}), bf16[4,2048,128]{1,2,0:T(8,128)(2,1)}) %all-gather.5.cloned.1.call-update) | async-done | bytes 2097168 | tf_op jit(solution)/shard_map/all_gather | solution.py:204
  149.0 4.4 %reshape.741 = bf16[4,8,2,128,128]{3,2,1,4,0:T(2,128)(2,1)} reshape(bf16[4,2048,128]{1,2,0:T(8,128)(2,1)} %all-gather.5.cloned.1.call-done) | data formatting | bytes 4194304 | tf_op jit(solution)/shard_map/reshape | solution.py:204
  153.4 6.8 %fusion.103 = (bf16[4,8,1,128,128]{3,2,1,4,0:T(2,128)(2,1)}, bf16[4,8,1,128,128]{3,2,1,4,0:T(2,128)(2,1)}) fusion(bf16[4,8,2,128,128]{3,2,1,4,0:T(2,128)(2,1)} %reshape.741), kind=kLoop, calls=%fused_computation.202 | loop fusion | bytes 4194304 | tf_op jit(solution)/shard_map/slice | solution.py:208
  160.2 4.7 %copy.116 = bf16[4,8,1,128,128]{4,3,1,0,2:T(8,128)(2,1)S(1)} copy(bf16[4,8,1,128,128]{3,2,1,4,0:T(2,128)(2,1)} %get-tuple-element.13) | data formatting | bytes 2097152 | tf_op jit(solution)/shard_map/slice | solution.py:208
  164.9 5.8 %copy.130 = bf16[4,8,1,128,128]{4,3,1,0,2:T(8,128)(2,1)} copy(bf16[4,8,1,128,128]{3,2,1,4,0:T(2,128)(2,1)} %get-tuple-element.14) | data formatting | bytes 2097152
  170.7 2.1 %fusion = (f32[4,2,128]{2,1,0:T(2,128)S(1)}, f32[4,2,128,1024]{3,2,1,0:T(8,128)S(1)}) fusion(pred[128,1024]{1,0:T(8,128)(4,1)} %compare_and_fusion, bf16[4,1024,128,1]{2,1,3,0:T(8,128)(2,1)S(1)} %bitcast.147, bf16[4,2,128,64]{2,3,1,0:T(8,128)(2,1)} %get-tuple-element.16, bf16[4,2,128,64]{2,3,1,0:T(8,128)(2,1)} %get-tuple-element.15), kind=kOutput, calls=%fused_computation.5 | convolution fusion | flops 272104448 | bytes 5640192 | tf_op jit(solution)/shard_map/hgtd,hnd->hgtn/dot_general | solution.py:215
  172.9 1.1 fusion.1
  174.0 1.2 fusion.25
  175.3 0.9 copy.120
  (76 shorter events, 1.2 us)
Async XLA Ops:
  6.5 2.5 %copy-start = (bf16[1280,3,4,80]{0,3,2,1:T(8,128)(2,1)S(1)}, bf16[1280,3,4,80]{0,3,2,1:T(8,128)(2,1)}, u32[]{:S(2)}) copy-start(bf16[1280,3,4,80]{0,3,2,1:T(8,128)(2,1)} %param.20) | copy-start | bytes 7372804
  6.5 4.5 %copy-start.18 = (s32[128]{0:T(128)S(1)}, s32[128]{0:T(128)}, u32[]{:S(2)}) copy-start(s32[128]{0:T(128)} %param.26) | copy-start | bytes 1540
  6.5 7.9 %copy-start.15 = (s32[256]{0:T(256)S(1)}, s32[256]{0:T(256)}, u32[]{:S(2)}) copy-start(s32[256]{0:T(256)} %param.27) | copy-start | bytes 3076
  6.5 8.1 %copy-start.14 = (s32[8]{0:T(128)S(1)}, s32[8]{0:T(128)}, u32[]{:S(2)}) copy-start(s32[8]{0:T(128)} %param.28) | copy-start | bytes 100
  9.0 26.4 %copy-start.3 = (bf16[128,1280]{1,0:T(8,128)(2,1)S(1)}, bf16[128,1280]{1,0:T(8,128)(2,1)}, u32[]{:S(2)}) copy-start(bf16[128,1280]{1,0:T(8,128)(2,1)} %param.17) | copy-start | bytes 983044
  11.0 24.9 %copy-start.12 = (f32[1280]{0:T(1024)S(1)}, f32[1280]{0:T(1024)}, u32[]{:S(2)}) copy-start(f32[1280]{0:T(1024)} %param.23) | copy-start | bytes 15364
  11.0 24.9 %copy-start.13 = (f32[1280]{0:T(1024)S(1)}, f32[1280]{0:T(1024)}, u32[]{:S(2)}) copy-start(f32[1280]{0:T(1024)} %param.22) | copy-start | bytes 15364
  11.0 0.7 copy-start.7
  11.4 0.7 copy-start.6
  13.9 2.4 %collective-permute-start = (f32[128,1280]{1,0:T(8,128)S(1)}, f32[128,1280]{1,0:T(8,128)}, u32[]{:S(2)}, u32[]{:S(2)}) collective-permute-start(f32[128,1280]{1,0:T(8,128)S(1)} %convolution_bitcast_fusion), channel_id=1, source_target_pairs={{0,1},{1,0},{2,3},{3,2},{4,5},{5,4},{6,7},{7,6},{8,9},{9,8},{10,11... | collective-permute-start | bytes 1966088 | tf_op jit(solution)/shard_map/ppermute | solution.py:23
  15.4 28.1 %copy-start.19 = (s32[8,2]{0,1:T(2,128)S(1)}, s32[8,2]{0,1:T(2,128)}, u32[]{:S(2)}) copy-start(s32[8,2]{0,1:T(2,128)} %param.25) | copy-start | bytes 196
  17.5 17.9 %collective-permute-start.1 = (f32[128,1280]{1,0:T(8,128)S(1)}, f32[128,1280]{1,0:T(8,128)S(1)}, u32[]{:S(2)}, u32[]{:S(2)}) collective-permute-start(f32[128,1280]{1,0:T(8,128)S(1)} %add.378), channel_id=1, source_target_pairs={{0,16},{16,0},{1,17},{17,1},{2,18},{18,2},{3,19},{19,3},{4,20},{20... | collective-permute-start | bytes 1966088 | tf_op jit(solution)/shard_map/ppermute | solution.py:23
  37.2 15.8 %all-to-all-start = ((bf16[8,32,640]{2,1,0:T(8,128)(2,1)}), bf16[8,32,640]{2,1,0:T(8,128)(2,1)S(1)}, u32[]{:S(2)}, u32[]{:S(2)}) async-start(bf16[8,32,640]{2,1,0:T(8,128)(2,1)} %bitcast.141), calls=%async_computation | async-start | bytes 655360 | tf_op jit(solution)/shard_map/all_to_all | solution.py:162
  43.3 58.2 %all-gather.3.cloned.1.call-start = ((), (), s32[]{:S(2)}) async-start(), calls=%async_computation.1 | async-start | bytes 1310720 | tf_op jit(solution)/shard_map/all_gather | solution.py:181
  53.3 29.0 %copy-start.10 = (bf16[128,1024]{1,0:T(8,128)(2,1)S(1)}, bf16[128,1024]{1,0:T(8,128)(2,1)}, u32[]{:S(2)}) copy-start(bf16[128,1024]{1,0:T(8,128)(2,1)} %param.30) | copy-start | bytes 786436
  55.3 28.4 %copy-start.1 = (s32[1024]{0:T(1024)S(1)}, s32[1024]{0:T(1024)}, u32[]{:S(2)}) copy-start(s32[1024]{0:T(1024)} %param.29) | copy-start | bytes 12292
  55.4 11.1 %collective-permute-start.2 = (f32[4,32,1024]{2,1,0:T(8,128)S(1)}, f32[4,32,1024]{2,1,0:T(8,128)S(1)}, u32[]{:S(2)}, u32[]{:S(2)}) collective-permute-start(f32[4,32,1024]{2,1,0:T(8,128)S(1)} %select_bitcast_fusion), channel_id=1, source_target_pairs={{0,2},{2,0},{4,6},{6,4},{8,10},{10,8},{12,14},{14,12},{1,3},{3,1},... | collective-permute-start | bytes 1572872 | tf_op jit(solution)/shard_map/ppermute | solution.py:23
  67.3 6.7 %collective-permute-start.3 = (f32[2,32,1024]{2,1,0:T(8,128)}, f32[2,32,1024]{2,1,0:T(8,128)}, u32[]{:S(2)}, u32[]{:S(2)}) collective-permute-start(f32[2,32,1024]{2,1,0:T(8,128)} %select_bitcast_fusion.1), channel_id=1, source_target_pairs={{0,4},{2,6},{4,0},{6,2},{8,12},{10,14},{12,8},{14,10},{1,5},{3,7},... | collective-permute-start | bytes 786440 | tf_op jit(solution)/shard_map/ppermute | solution.py:23
  75.0 7.3 %collective-permute-start.4 = (f32[1,32,1024]{2,1,0:T(8,128)S(1)}, f32[1,32,1024]{2,1,0:T(8,128)S(1)}, u32[]{:S(2)}, u32[]{:S(2)}) collective-permute-start(f32[1,32,1024]{2,1,0:T(8,128)S(1)} %select_bitcast_fusion.2), channel_id=1, source_target_pairs={{0,8},{2,10},{4,12},{6,14},{8,0},{10,2},{12,4},{14,6},{1,9},{3,11}... | collective-permute-start | bytes 393224 | tf_op jit(solution)/shard_map/ppermute | solution.py:23
  83.4 65.6 %all-gather.5.cloned.1.call-start = ((), (), s32[]{:S(2)}) async-start(), calls=%async_computation.2 | async-start | bytes 2228224 | tf_op jit(solution)/shard_map/all_gather | solution.py:204
  85.2 7.6 %copy-start.17 = (s32[128]{0:T(128)}, s32[128]{0:T(128)S(1)}, u32[]{:S(2)}) copy-start(s32[128]{0:T(128)S(1)} %get-tuple-element.8) | copy-start | bytes 1540
  85.3 17.8 %copy-start.11 = (f32[4096]{0:T(1024)S(1)}, f32[4096]{0:T(1024)}, u32[]{:S(2)}) copy-start(f32[4096]{0:T(1024)} %param.31) | copy-start | bytes 49156
  93.1 14.6 %copy-start.8 = (f32[128,64]{0,1:T(8,128)}, f32[128,64]{0,1:T(8,128)S(1)}, u32[]{:S(2)}) copy-start(f32[128,64]{0,1:T(8,128)S(1)} %get-tuple-element.20) | copy-start | bytes 98308
  103.1 26.0 %copy-start.16 = (f32[128]{0:T(128)}, f32[128]{0:T(128)S(1)}, u32[]{:S(2)}) copy-start(f32[128]{0:T(128)S(1)} %add_rsqrt_fusion) | copy-start | bytes 1540
  129.0 6.2 %copy-start.2 = (bf16[128,4096]{1,0:T(8,128)(2,1)S(1)}, bf16[128,4096]{1,0:T(8,128)(2,1)}, u32[]{:S(2)}) copy-start(bf16[128,4096]{1,0:T(8,128)(2,1)} %all-gather.3.cloned.1.call-done) | copy-start | bytes 3145732
  135.2 5.8 %copy-start.9 = (f32[128,64]{0,1:T(8,128)S(1)}, f32[128,64]{0,1:T(8,128)}, u32[]{:S(2)}) copy-start(f32[128,64]{0,1:T(8,128)} %copy-done.8) | copy-start | bytes 98308
  170.7 2.1 %copy-start.4 = (pred[128,1024]{1,0:T(8,128)(4,1)S(1)}, pred[128,1024]{1,0:T(8,128)(4,1)}, u32[]{:S(2)}) copy-start(pred[128,1024]{1,0:T(8,128)(4,1)} %compare_and_fusion) | copy-start | bytes 393220
  170.7 3.3 %copy-start.5 = (bf16[4,8,1,128,128]{4,3,1,0,2:T(8,128)(2,1)S(1)}, bf16[4,8,1,128,128]{4,3,1,0,2:T(8,128)(2,1)}, u32[]{:S(2)}) copy-start(bf16[4,8,1,128,128]{4,3,1,0,2:T(8,128)(2,1)} %copy.130) | copy-start | bytes 3145732
Sparse Core Ops, SparseCore 0:
  83.5 18.0 all-gather.2
  107.8 41.0 all-gather.4

commit v3 on v2

--- a/solution.py
+++ b/solution.py
@@ -192,35 +192,34 @@
     kv_heads = w_query.shape[1]
     groups = w_query.shape[2]
     queries = jnp.einsum(
-        "td,dhgk->hgtk", normed_rows, w_query, preferred_element_type=jnp.float32
-    )
-    queries = rotate_rows(queries, own_positions).astype(jnp.bfloat16)
+        "td,dhgk->thgk", normed_rows, w_query, preferred_element_type=jnp.float32
+    )
+    queries = rotate(queries, own_positions).astype(jnp.bfloat16)
     projected_half = jnp.einsum(
-        "td,dhk->htk", normed_rows, w_keyval[0], preferred_element_type=jnp.float32
+        "td,dhk->thk", normed_rows, w_keyval[0], preferred_element_type=jnp.float32
     )
     own_half = jnp.where(
-        tp_index == 0, rotate_rows(projected_half, own_positions), projected_half
-    ).astype(jnp.bfloat16)
-    both = lax.all_gather(own_half, ("ctx", "tp"), axis=1, tiled=True).reshape(
-        kv_heads, shards, 2, TOK, HD
-    )
-    key_count = shards * TOK
-    keys_every = both[:, :, 0].reshape(kv_heads, key_count, HD)
-    values_every = both[:, :, 1].reshape(kv_heads, key_count, HD)
+        tp_index == 0, rotate(projected_half, own_positions), projected_half
+    ).astype(jnp.bfloat16)
+    gathered = lax.all_gather(own_half, "ctx", axis=0, tiled=True)
+    partner_all = swapped(gathered, "tp", 0)
+    keys_every = jnp.where(tp_index == 0, gathered, partner_all)
+    values_every = jnp.where(tp_index == 0, partner_all, gathered)
+    key_count = keys_every.shape[0]
     key_pos = row_positions(jnp.arange(key_count, dtype=jnp.int32), slice_order, TOK)
     key_doc = jnp.take(doc_ids, key_pos)
     allowed_now = (key_pos[None, :] <= own_positions[:, None]) & (
         key_doc[None, :] == own_doc[:, None]
     )
     scores_now = jnp.einsum(
-        "hgtd,hnd->hgtn", queries, keys_every, preferred_element_type=jnp.float32
+        "qkgd,nkd->kgqn", queries, keys_every, preferred_element_type=jnp.float32
     ) / math.sqrt(HD)
     scores_now = jnp.where(allowed_now[None, None], scores_now, big_negative)
     best = jnp.max(scores_now, axis=-1, keepdims=True)
     powers_now = jnp.exp(scores_now - best)
     total_final = jnp.sum(powers_now, axis=-1)
     accum_final = jnp.einsum(
-        "hgtn,hnd->hgtd",
+        "kgqn,nkd->kgqd",
         powers_now.astype(jnp.bfloat16),
         values_every,
         preferred_element_type=jnp.float32,

time: 185 us -> 166 us (0.90)
  local copies, waits for them, and re-layouts: 59.5 us -> 42.6 us
    slice x2 -> x0, local copies, waits for them, and re-layouts: 11.5 us -> none  [local(): keys_every = both[:, :, 0].reshape(kv_heads, key_count, HD)]
    unnamed x42 -> x41, local copies, waits for them, and re-layouts: 27.9 us -> 22.6 us
    reshape x1 -> x0, local copies, waits for them, and re-layouts: 4.44 us -> none  [local(): lax.all_gather(own_half, ('ctx', 'tp'), axis=1, tiled=True)]
    gather x1, local copies, waits for them, and re-layouts: 4.53 us -> 8.81 us  [local(): key_doc = jnp.take(doc_ids, key_pos)]
    ppermute x5 -> x6, starting transfers between devices: 8.44 us -> 8.44 us  [swapped(): lax.ppermute(value, axis, [(i, i ^ 1 << stride) for i in range(lax.axis_s...]
    ppermute x5 -> x6, waiting for transfers between devices: 34.7 us -> 34.7 us  [swapped(): lax.ppermute(value, axis, [(i, i ^ 1 << stride) for i in range(lax.axis_s...]
  transfers between devices with their start and end apart: 8 -> 9, of which waited for: 8 -> 8; matrix products, arithmetic and copies ran while one was open for 25% -> 31% of each run, Pallas kernels for 0% -> 0%
where the time goes in v3:
time: 166 us; the launch traced here: 165 us
  waiting for transfers between devices  60.1 us (36%)
  local copies, waits for them, and re-layouts  42.6 us (26%)
  matrix products  19.4 us (12%)
  starting transfers between devices  14.8 us (9%)
  other arithmetic  14.5 us (9%)
  between operations  13.9 us (8%)
    ppermute x6, waiting for transfers between devices, swapped(): lax.ppermute(value, axis, [(i, i ^ 1 << stride) for i in range(lax.axis_s...  34.7 us
    unnamed x41, local copies, waits for them, and re-layouts  22.6 us
    unnamed x3, matrix products  11.6 us
    all_to_all x1, waiting for transfers between devices, local(): lax.all_to_all(blocks, 'ctx', split_axis=0, concat_axis=0, tiled=True)  9.5 us
    gather x1, local copies, waits for them, and re-layouts, local(): key_doc = jnp.take(doc_ids, key_pos)  8.81 us
    ppermute x6, starting transfers between devices, swapped(): lax.ppermute(value, axis, [(i, i ^ 1 << stride) for i in range(lax.axis_s...  8.44 us
    all_gather x1, waiting for transfers between devices, local(): full_rows = lax.all_gather(embeds, ('vis', 'tp'), axis=1, tiled=True)  8.41 us
    squeeze x1, local copies, waits for them, and re-layouts, local(): w_keyval[0]  7.62 us
  transfers between devices with their start and end apart: 9, of which 8 were waited for; matrix products, arithmetic and copies ran while one was open for 31% of the time, Pallas kernels for 0%

profile of v3, /device:TPU:0, one launch (start us, length us, event | category | flops | bytes accessed | tf_op | source)
XLA Modules:
  0.0 165.3 jit_solution(6867229453267922436)
XLA Ops:
  6.5 1.2 convert_reduce_fusion
  7.8 1.2 fusion.41
  9.0 1.9 %fusion.47 = f32[128,960]{0,1:S(1)} fusion(bf16[1280,960]{0,1:T(8,128)(2,1)S(1)} %bitcast.156, bf16[128,1280]{1,0:T(8,128)(2,1)} %param.17, f32[1280]{0:T(1024)} %param.19, f32[1280]{0:T(1024)} %param.18, f32[128]{0:T(128)S(1)} %add_rsqrt_fusion.2, f32[128]{0:T(128)S(1)} %broadcast_multiply_fusion.1), kind=kOutput, calls=%fused_computation.56 | convolution fusion | flops 315555840 | bytes 3288064
  11.1 0.1 broadcast_compare_fusion
  11.1 0.3 fusion.115
  11.5 0.3 copy-done.5
  11.7 0.4 copy-done.4
  12.1 1.8 %convolution_bitcast_fusion = f32[128,1280]{1,0:T(8,128)S(1)} fusion(bf16[4,80,1280]{2,1,0:T(8,128)(2,1)} %param.21, f32[4,128,128]{1,2,0:T(8,128)} %copy-done.4, f32[4,128]{1,0:T(4,128)S(1)} %get-tuple-element.21, bf16[128,3,4,80]{0,3,2,1:T(8,128)(2,1)} %copy-done.5, f32[128,4]{0,1:T(4,128)S(1)} %bitcast.171), kind=kOutput, calls=%fused_computation.10 | convolution fusion | flops 115556352 | bytes 1822720 | tf_op jit(solution)/shard_map/phd,hdf->pf/dot_general | solution.py:141
  13.9 0.6 collective-permute-start
  14.6 0.1 copy.95
  14.7 0.7 fusion.66
  15.4 1.0 collective-permute-done
  16.3 1.2 add.378
  17.5 2.9 %collective-permute-start.1 = (f32[128,1280]{1,0:T(8,128)S(1)}, f32[128,1280]{1,0:T(8,128)S(1)}, u32[]{:S(2)}, u32[]{:S(2)}) collective-permute-start(f32[128,1280]{1,0:T(8,128)S(1)} %add.378), channel_id=1, source_target_pairs={{0,16},{16,0},{1,17},{17,1},{2,18},{18,2},{3,19},{19,3},{4,20},{20... | collective-permute-start | bytes 1966088 | tf_op jit(solution)/shard_map/ppermute | solution.py:23
  20.4 0.7 fusion.113
  21.2 0.1 select_reduce_fusion.2
  21.3 14.2 %collective-permute-done.1 = f32[128,1280]{1,0:T(8,128)S(1)} collective-permute-done((f32[128,1280]{1,0:T(8,128)S(1)}, f32[128,1280]{1,0:T(8,128)S(1)}, u32[]{:S(2)}, u32[]{:S(2)}) %collective-permute-start.1) | collective-permute-done | bytes 655392 | tf_op jit(solution)/shard_map/ppermute | solution.py:23
  35.5 0.2 fusion.112
  35.6 0.2 multiply_reduce_fusion
  35.9 0.2 add_convert_fusion
  36.1 0.2 reshape.721
  36.3 0.2 convolution_convert_fusion
  36.5 0.7 copy.131
  37.2 6.1 %all-to-all-start = ((bf16[8,32,640]{2,1,0:T(8,128)(2,1)}), bf16[8,32,640]{2,1,0:T(8,128)(2,1)S(1)}, u32[]{:S(2)}, u32[]{:S(2)}) async-start(bf16[8,32,640]{2,1,0:T(8,128)(2,1)} %bitcast.154), calls=%async_computation | async-start | bytes 655360 | tf_op jit(solution)/shard_map/all_to_all | solution.py:162
  43.6 9.5 %all-to-all-done = bf16[8,32,640]{2,1,0:T(8,128)(2,1)S(1)} async-done(((bf16[8,32,640]{2,1,0:T(8,128)(2,1)}), bf16[8,32,640]{2,1,0:T(8,128)(2,1)S(1)}, u32[]{:S(2)}, u32[]{:S(2)}) %all-to-all-start) | async-done | bytes 327712 | tf_op jit(solution)/shard_map/all_to_all | solution.py:162
  53.1 0.1 reshape.723
  53.1 0.1 copy.132
  53.3 0.1 dot_general.46
  53.4 1.9 %fusion.12 = f32[4,2,32,1024]{3,2,1,0:T(8,128)S(1)} fusion(bf16[4,2,32,640]{3,2,1,0:T(8,128)(2,1)S(1)} %dot_general.46, bf16[640,1024]{1,0:T(8,128)(2,1)} %param.24), kind=kOutput, calls=%fused_computation.19 | convolution fusion | flops 335544320 | bytes 2686976 | tf_op jit(solution)/shard_map/dot_general | solution.py:166
  55.4 1.6 collective-permute-start.2
  57.1 9.4 %collective-permute-done.2 = f32[4,32,1024]{2,1,0:T(8,128)S(1)} collective-permute-done((f32[4,32,1024]{2,1,0:T(8,128)S(1)}, f32[4,32,1024]{2,1,0:T(8,128)S(1)}, u32[]{:S(2)}, u32[]{:S(2)}) %collective-permute-start.2) | collective-permute-done | bytes 524320 | tf_op jit(solution)/shard_map/ppermute | solution.py:23
  66.5 0.1 fusion.46
  66.6 0.7 select_bitcast_fusion.1
  67.3 0.7 collective-permute-start.3
  68.0 0.1 add.373
  68.1 0.1 and.288
  68.2 0.3 fusion.114
  68.5 5.5 %collective-permute-done.3 = f32[2,32,1024]{2,1,0:T(8,128)} collective-permute-done((f32[2,32,1024]{2,1,0:T(8,128)}, f32[2,32,1024]{2,1,0:T(8,128)}, u32[]{:S(2)}, u32[]{:S(2)}) %collective-permute-start.3) | collective-permute-done | bytes 262176 | tf_op jit(solution)/shard_map/ppermute | solution.py:23
  74.0 1.0 fusion.63
  75.0 2.7 %collective-permute-start.4 = (f32[1,32,1024]{2,1,0:T(8,128)S(1)}, f32[1,32,1024]{2,1,0:T(8,128)S(1)}, u32[]{:S(2)}, u32[]{:S(2)}) collective-permute-start(f32[1,32,1024]{2,1,0:T(8,128)S(1)} %select_bitcast_fusion.2), channel_id=1, source_target_pairs={{0,8},{2,10},{4,12},{6,14},{8,0},{10,2},{12,4},{14,6},{1,9},{3,11}... | collective-permute-start | bytes 393224 | tf_op jit(solution)/shard_map/ppermute | solution.py:23
  77.7 4.6 %collective-permute-done.4 = f32[1,32,1024]{2,1,0:T(8,128)S(1)} collective-permute-done((f32[1,32,1024]{2,1,0:T(8,128)S(1)}, f32[1,32,1024]{2,1,0:T(8,128)S(1)}, u32[]{:S(2)}, u32[]{:S(2)}) %collective-permute-start.4) | collective-permute-done | bytes 131104 | tf_op jit(solution)/shard_map/ppermute | solution.py:23
  82.4 1.0 fusion.18
  83.4 0.2 all-gather.5.cloned.1.call-start
  83.6 0.1 select_reduce_fusion.3
  83.7 1.0 gather_fusion.1
  84.7 0.5 and_select_fusion.8
  85.3 7.6 %copy.112 = bf16[4096,4,128]{0,2,1:T(8,128)(2,1)} copy(bf16[4096,4,128]{2,1,0:T(4,128)(2,1)} %bitcast.160) | data formatting | bytes 8388608 | tf_op jit(solution)/shard_map/squeeze | solution.py:199
  92.9 0.2 multiply_cosine_fusion
  93.1 8.4 %all-gather.3.cloned.1.call-done = bf16[128,4096]{1,0:T(8,128)(2,1)} async-done(((bf16[128,1024]{1,0:T(8,128)(2,1)}), bf16[128,4096]{1,0:T(8,128)(2,1)}) %all-gather.3.cloned.1.call-update) | async-done | bytes 1048592 | tf_op jit(solution)/shard_map/all_gather | solution.py:181
  101.5 1.5 fusion.3
  103.1 3.8 %fusion.55 = f32[128,512]{0,1:S(1)} fusion(bf16[4096,512]{0,1:T(8,128)(2,1)} %bitcast.161, bf16[128,4096]{1,0:T(8,128)(2,1)} %all-gather.3.cloned.1.call-done, f32[4096]{0:T(1024)S(1)} %copy-done.9, f32[128]{0:T(128)S(1)} %add_rsqrt_fusion), kind=kOutput, calls=%fused_computation.64 | convolution fusion | flops 538968064 | bytes 5521920
  107.0 0.7 fusion.57
  107.7 0.1 select_reduce_fusion
  107.9 0.5 copy-done.10
  108.4 8.8 %gather_fusion = s32[1024]{0:T(1024)} fusion(s32[1024]{0:T(1024)S(1)} %copy-done.1, s32[1024]{0:T(1024)S(1)} %broadcast_clamp_fusion), kind=kCustom, calls=%fused_computation | custom fusion | bytes 12288 | tf_op jit(solution)/shard_map/jit(_take)/gather | solution.py:210
  117.2 21.4 %copy.113 = bf16[4096,4,2,128]{0,3,2,1:T(8,128)(2,1)} copy(bf16[4096,4,2,128]{3,2,1,0:T(2,128)(2,1)} %param.32) | data formatting | bytes 16777216 | tf_op args[15]
  138.6 1.3 and_select_fusion.2
  139.9 7.5 %all-gather.5.cloned.1.call-done = bf16[1024,4,128]{0,2,1:T(8,128)(2,1)} async-done(((bf16[128,4,128]{0,2,1:T(8,128)(2,1)}), bf16[1024,4,128]{0,2,1:T(8,128)(2,1)}) %all-gather.5.cloned.1.call-update) | async-done | bytes 1048592 | tf_op jit(solution)/shard_map/all_gather | solution.py:204
  147.3 1.0 compare_and_fusion
  148.4 5.9 %fusion.53 = f32[128,1024]{0,1:S(1)} fusion(bf16[4096,1024]{0,1:T(8,128)(2,1)} %bitcast.157, bf16[128,4096]{1,0:T(8,128)(2,1)S(1)} %copy-done.2, f32[4096]{0:T(1024)S(1)} %copy-done.9, f32[128]{0:T(128)} %copy-done.15), kind=kOutput, calls=%fused_computation.63 | convolution fusion | flops 1075838976 | bytes 9978368
  154.4 1.0 fusion.2
  155.4 0.9 fusion
  156.3 1.3 fusion.34
  157.5 0.9 copy.117
  (74 shorter events, 1.0 us)
Async XLA Ops:
  6.5 2.5 %copy-start = (bf16[1280,3,4,80]{0,3,2,1:T(8,128)(2,1)S(1)}, bf16[1280,3,4,80]{0,3,2,1:T(8,128)(2,1)}, u32[]{:S(2)}) copy-start(bf16[1280,3,4,80]{0,3,2,1:T(8,128)(2,1)} %param.20) | copy-start | bytes 7372804
  6.5 4.5 %copy-start.17 = (s32[128]{0:T(128)S(1)}, s32[128]{0:T(128)}, u32[]{:S(2)}) copy-start(s32[128]{0:T(128)} %param.26) | copy-start | bytes 1540
  6.5 7.9 %copy-start.14 = (s32[256]{0:T(256)S(1)}, s32[256]{0:T(256)}, u32[]{:S(2)}) copy-start(s32[256]{0:T(256)} %param.27) | copy-start | bytes 3076
  6.5 8.1 %copy-start.13 = (s32[8]{0:T(128)S(1)}, s32[8]{0:T(128)}, u32[]{:S(2)}) copy-start(s32[8]{0:T(128)} %param.28) | copy-start | bytes 100
  9.0 26.4 %copy-start.3 = (bf16[128,1280]{1,0:T(8,128)(2,1)S(1)}, bf16[128,1280]{1,0:T(8,128)(2,1)}, u32[]{:S(2)}) copy-start(bf16[128,1280]{1,0:T(8,128)(2,1)} %param.17) | copy-start | bytes 983044
  11.0 24.9 %copy-start.11 = (f32[1280]{0:T(1024)S(1)}, f32[1280]{0:T(1024)}, u32[]{:S(2)}) copy-start(f32[1280]{0:T(1024)} %param.23) | copy-start | bytes 15364
  11.0 24.9 %copy-start.12 = (f32[1280]{0:T(1024)S(1)}, f32[1280]{0:T(1024)}, u32[]{:S(2)}) copy-start(f32[1280]{0:T(1024)} %param.22) | copy-start | bytes 15364
  11.0 0.7 copy-start.5
  11.4 0.7 copy-start.4
  13.9 2.4 %collective-permute-start = (f32[128,1280]{1,0:T(8,128)S(1)}, f32[128,1280]{1,0:T(8,128)}, u32[]{:S(2)}, u32[]{:S(2)}) collective-permute-start(f32[128,1280]{1,0:T(8,128)S(1)} %convolution_bitcast_fusion), channel_id=1, source_target_pairs={{0,1},{1,0},{2,3},{3,2},{4,5},{5,4},{6,7},{7,6},{8,9},{9,8},{10,11... | collective-permute-start | bytes 1966088 | tf_op jit(solution)/shard_map/ppermute | solution.py:23
  15.4 28.1 %copy-start.18 = (s32[8,2]{0,1:T(2,128)S(1)}, s32[8,2]{0,1:T(2,128)}, u32[]{:S(2)}) copy-start(s32[8,2]{0,1:T(2,128)} %param.25) | copy-start | bytes 196
  17.5 17.9 %collective-permute-start.1 = (f32[128,1280]{1,0:T(8,128)S(1)}, f32[128,1280]{1,0:T(8,128)S(1)}, u32[]{:S(2)}, u32[]{:S(2)}) collective-permute-start(f32[128,1280]{1,0:T(8,128)S(1)} %add.378), channel_id=1, source_target_pairs={{0,16},{16,0},{1,17},{17,1},{2,18},{18,2},{3,19},{19,3},{4,20},{20... | collective-permute-start | bytes 1966088 | tf_op jit(solution)/shard_map/ppermute | solution.py:23
  37.2 15.8 %all-to-all-start = ((bf16[8,32,640]{2,1,0:T(8,128)(2,1)}), bf16[8,32,640]{2,1,0:T(8,128)(2,1)S(1)}, u32[]{:S(2)}, u32[]{:S(2)}) async-start(bf16[8,32,640]{2,1,0:T(8,128)(2,1)} %bitcast.154), calls=%async_computation | async-start | bytes 655360 | tf_op jit(solution)/shard_map/all_to_all | solution.py:162
  43.3 58.2 %all-gather.3.cloned.1.call-start = ((), (), s32[]{:S(2)}) async-start(), calls=%async_computation.1 | async-start | bytes 1310720 | tf_op jit(solution)/shard_map/all_gather | solution.py:181
  53.3 29.0 %copy-start.8 = (bf16[128,1024]{1,0:T(8,128)(2,1)S(1)}, bf16[128,1024]{1,0:T(8,128)(2,1)}, u32[]{:S(2)}) copy-start(bf16[128,1024]{1,0:T(8,128)(2,1)} %param.30) | copy-start | bytes 786436
  55.3 28.4 %copy-start.1 = (s32[1024]{0:T(1024)S(1)}, s32[1024]{0:T(1024)}, u32[]{:S(2)}) copy-start(s32[1024]{0:T(1024)} %param.29) | copy-start | bytes 12292
  55.4 11.1 %collective-permute-start.2 = (f32[4,32,1024]{2,1,0:T(8,128)S(1)}, f32[4,32,1024]{2,1,0:T(8,128)S(1)}, u32[]{:S(2)}, u32[]{:S(2)}) collective-permute-start(f32[4,32,1024]{2,1,0:T(8,128)S(1)} %select_bitcast_fusion), channel_id=1, source_target_pairs={{0,2},{2,0},{4,6},{6,4},{8,10},{10,8},{12,14},{14,12},{1,3},{3,1},... | collective-permute-start | bytes 1572872 | tf_op jit(solution)/shard_map/ppermute | solution.py:23
  67.3 6.7 %collective-permute-start.3 = (f32[2,32,1024]{2,1,0:T(8,128)}, f32[2,32,1024]{2,1,0:T(8,128)}, u32[]{:S(2)}, u32[]{:S(2)}) collective-permute-start(f32[2,32,1024]{2,1,0:T(8,128)} %select_bitcast_fusion.1), channel_id=1, source_target_pairs={{0,4},{2,6},{4,0},{6,2},{8,12},{10,14},{12,8},{14,10},{1,5},{3,7},... | collective-permute-start | bytes 786440 | tf_op jit(solution)/shard_map/ppermute | solution.py:23
  75.0 7.3 %collective-permute-start.4 = (f32[1,32,1024]{2,1,0:T(8,128)S(1)}, f32[1,32,1024]{2,1,0:T(8,128)S(1)}, u32[]{:S(2)}, u32[]{:S(2)}) collective-permute-start(f32[1,32,1024]{2,1,0:T(8,128)S(1)} %select_bitcast_fusion.2), channel_id=1, source_target_pairs={{0,8},{2,10},{4,12},{6,14},{8,0},{10,2},{12,4},{14,6},{1,9},{3,11}... | collective-permute-start | bytes 393224 | tf_op jit(solution)/shard_map/ppermute | solution.py:23
  83.4 64.0 %all-gather.5.cloned.1.call-start = ((), (), s32[]{:S(2)}) async-start(), calls=%async_computation.2 | async-start | bytes 1179648 | tf_op jit(solution)/shard_map/all_gather | solution.py:204
  85.3 7.6 %copy-start.16 = (s32[128]{0:T(128)}, s32[128]{0:T(128)S(1)}, u32[]{:S(2)}) copy-start(s32[128]{0:T(128)S(1)} %get-tuple-element.10) | copy-start | bytes 1540
  85.3 17.8 %copy-start.9 = (f32[4096]{0:T(1024)S(1)}, f32[4096]{0:T(1024)}, u32[]{:S(2)}) copy-start(f32[4096]{0:T(1024)} %param.31) | copy-start | bytes 49156
  93.1 14.7 %copy-start.6 = (f32[128,64]{0,1:T(8,128)}, f32[128,64]{0,1:T(8,128)S(1)}, u32[]{:S(2)}) copy-start(f32[128,64]{0,1:T(8,128)S(1)} %get-tuple-element.18) | copy-start | bytes 98308
  103.1 4.8 %copy-start.15 = (f32[128]{0:T(128)}, f32[128]{0:T(128)S(1)}, u32[]{:S(2)}) copy-start(f32[128]{0:T(128)S(1)} %add_rsqrt_fusion) | copy-start | bytes 1540
  107.8 0.6 copy-start.10
  117.2 31.2 %copy-start.2 = (bf16[128,4096]{1,0:T(8,128)(2,1)S(1)}, bf16[128,4096]{1,0:T(8,128)(2,1)}, u32[]{:S(2)}) copy-start(bf16[128,4096]{1,0:T(8,128)(2,1)} %all-gather.3.cloned.1.call-done) | copy-start | bytes 3145732
  147.3 7.0 %collective-permute-start.5 = (bf16[1024,4,128]{0,2,1:T(8,128)(2,1)}, bf16[1024,4,128]{0,2,1:T(8,128)(2,1)S(1)}, u32[]{:S(2)}, u32[]{:S(2)}) collective-permute-start(bf16[1024,4,128]{0,2,1:T(8,128)(2,1)} %all-gather.5.cloned.1.call-done), channel_id=1, source_target_pairs={{0,1},{1,0},{2,3},{3,2},{4,5},{5,4},{6,7},{7,6},{8,9},{9,8},{10,11... | collective-permute-start | bytes 3145736 | tf_op jit(solution)/shard_map/ppermute | solution.py:23
  148.4 5.9 %copy-start.7 = (f32[128,64]{0,1:T(8,128)S(1)}, f32[128,64]{0,1:T(8,128)}, u32[]{:S(2)}) copy-start(f32[128,64]{0,1:T(8,128)} %copy-done.6) | copy-start | bytes 98308
  148.4 6.0 %copy-start.19 = (bf16[1024,4,128]{0,2,1:T(8,128)(2,1)S(1)}, bf16[1024,4,128]{0,2,1:T(8,128)(2,1)}, u32[]{:S(2)}) copy-start(bf16[1024,4,128]{0,2,1:T(8,128)(2,1)} %all-gather.5.cloned.1.call-done) | copy-start | bytes 3145732
Sparse Core Ops, SparseCore 0:
  83.5 18.0 all-gather.2
  107.8 39.4 all-gather.4

commit v4 on v3

--- a/solution.py
+++ b/solution.py
@@ -68,7 +68,7 @@
     return (owner_dev, local_row, owner_hot)
 
 
-def halving_scatter(blocks, index, count):
+def halving_scatter(blocks, index, count, rider):
     remaining = count
     bit = 0
     while remaining > 1:
@@ -76,10 +76,13 @@
         mine = (index >> bit) & 1
         keep = jnp.where(mine == 0, lower[:, 0], lower[:, 1])
         give = jnp.where(mine == 0, lower[:, 1], lower[:, 0])
-        blocks = keep + swapped(give, "ctx", bit)
+        arrived = swapped(give, "ctx", bit)
+        if bit == 0:
+            rider, arrived = lax.optimization_barrier((rider, arrived))
+        blocks = keep + arrived
         remaining //= 2
         bit += 1
-    return blocks[0]
+    return blocks[0], rider
 
 
 def rotate_rows(values, positions):
@@ -139,8 +142,48 @@
     )
     blended = (blended / jnp.transpose(totals)[:, :, None]).astype(jnp.bfloat16)
     branch_part = jnp.einsum("phd,hdf->pf", blended, vit_out, preferred_element_type=jnp.float32)
-    branch_sum = branch_part + swapped(branch_part, "tp", 0)
-    branch_sum = branch_sum + swapped(branch_sum, "vis", 0)
+    own_positions = row_positions(
+        ctx_index * TOK + jnp.arange(TOK, dtype=jnp.int32), slice_order, TOK
+    )
+    kv_heads = w_query.shape[1]
+    groups = w_query.shape[2]
+
+    def normalize(rows):
+        full_rows = lax.all_gather(rows, ("vis", "tp"), axis=1, tiled=True)
+        widened = full_rows.astype(jnp.float32)
+        return (
+            widened
+            * lax.rsqrt(jnp.mean(widened * widened, axis=1, keepdims=True) + norm_eps)
+            * norm_gain
+        ).astype(jnp.bfloat16)
+
+    def query_part(normed_rows, positions, weights):
+        queries = jnp.einsum(
+            "td,dhgk->thgk", normed_rows, weights, preferred_element_type=jnp.float32
+        )
+        return rotate(queries, positions).astype(jnp.bfloat16)
+
+    def keyval_part(normed_rows, positions, weights):
+        projected_half = jnp.einsum(
+            "td,dhk->thk", normed_rows, weights, preferred_element_type=jnp.float32
+        )
+        return jnp.where(
+            tp_index == 0, rotate(projected_half, positions), projected_half
+        ).astype(jnp.bfloat16)
+
+    def after(value, anchor):
+        return lax.optimization_barrier((value, anchor))[0]
+
+    text_normed = normalize(text_rows)
+    from_tp = swapped(branch_part, "tp", 0)
+    query_weights = after(w_query, from_tp)
+    text_queries = query_part(text_normed, own_positions, query_weights)
+    branch_sum = branch_part + from_tp
+    from_vis = swapped(branch_sum, "vis", 0)
+    text_queries, from_vis = lax.optimization_barrier((text_queries, from_vis))
+    branch_sum = branch_sum + from_vis
+    keyval_weights = after(w_keyval[0], from_vis)
+    text_half = keyval_part(text_normed, own_positions, keyval_weights)
     hidden = patch_rows.astype(jnp.float32) + branch_sum
     merged = layer_norm(hidden, merge_gain, merge_bias).astype(jnp.bfloat16).reshape(ICAP, 4 * VD)
     send_each = ICAP // shards
@@ -164,50 +207,51 @@
         received.reshape(shards, shards, send_each, block_feats), (1, 0, 2, 3)
     ).reshape(shards * ICAP, block_feats)
     partial = jnp.dot(by_dest, merge_weight, preferred_element_type=jnp.float32)
-    incoming = halving_scatter(partial.reshape(shards, ICAP, -1), ctx_index, shards).astype(
-        jnp.bfloat16
-    )
-    mine_live = ((owner_dev == ctx_index) & is_live).reshape(-1)
+    incoming, text_half = halving_scatter(
+        partial.reshape(shards, ICAP, -1), ctx_index, shards, text_half
+    )
+    incoming = incoming.astype(jnp.bfloat16)
+    mine_all = (owner_dev == ctx_index).reshape(-1)
+    mine_live = mine_all & is_live.reshape(-1)
     column_of = (shard_ids[:, None] * send_each + rank_in).reshape(-1)
     row_hot = (
         (local_row.reshape(-1)[None, :] == jnp.arange(TOK, dtype=jnp.int32)[:, None])
         & mine_live[None, :]
     ).astype(jnp.bfloat16)
-    column_hot = (column_of[:, None] == slot_ids[None, :]).astype(jnp.bfloat16)
+    column_match = column_of[:, None] == slot_ids[None, :]
+    column_hot = column_match.astype(jnp.bfloat16)
     placing = jnp.dot(row_hot, column_hot, preferred_element_type=jnp.float32)
     is_image = jnp.sum(placing, axis=1) > 0.5
-    image_part = jnp.dot(placing.astype(jnp.bfloat16), incoming, preferred_element_type=jnp.float32)
-    embeds = jnp.where(is_image[:, None], image_part.astype(jnp.bfloat16), text_rows)
-    full_rows = lax.all_gather(embeds, ("vis", "tp"), axis=1, tiled=True)
-    widened = full_rows.astype(jnp.float32)
-    normed_rows = (
-        widened
-        * lax.rsqrt(jnp.mean(widened * widened, axis=1, keepdims=True) + norm_eps)
-        * norm_gain
-    ).astype(jnp.bfloat16)
-    own_positions = row_positions(
-        ctx_index * TOK + jnp.arange(TOK, dtype=jnp.int32), slice_order, TOK
-    )
-    own_doc = jnp.take(doc_ids, own_positions)
-    kv_heads = w_query.shape[1]
-    groups = w_query.shape[2]
-    queries = jnp.einsum(
-        "td,dhgk->thgk", normed_rows, w_query, preferred_element_type=jnp.float32
-    )
-    queries = rotate(queries, own_positions).astype(jnp.bfloat16)
-    projected_half = jnp.einsum(
-        "td,dhk->thk", normed_rows, w_keyval[0], preferred_element_type=jnp.float32
-    )
-    own_half = jnp.where(
-        tp_index == 0, rotate(projected_half, own_positions), projected_half
-    ).astype(jnp.bfloat16)
+    placing = placing.astype(jnp.bfloat16)
+    incoming_pos = jnp.sum(
+        jnp.where(column_match & mine_all[:, None], image_pos[:, None], 0), axis=0
+    )
+    image_normed = normalize(incoming)
+    image_queries = query_part(image_normed, incoming_pos, query_weights)
+    image_half = keyval_part(image_normed, incoming_pos, keyval_weights)
+    placed_queries = jnp.einsum(
+        "tq,qhgk->thgk", placing, image_queries, preferred_element_type=jnp.float32
+    ).astype(jnp.bfloat16)
+    placed_half = jnp.einsum(
+        "tq,qhk->thk", placing, image_half, preferred_element_type=jnp.float32
+    ).astype(jnp.bfloat16)
+    queries = jnp.where(is_image[:, None, None, None], placed_queries, text_queries)
+    own_half = jnp.where(is_image[:, None, None], placed_half, text_half)
+    doc_slices = doc_ids.reshape(2 * shards, TOK // 2)
+    slice_ids = jnp.stack([slice_order, 2 * shards - 1 - slice_order], axis=1)
+    slice_hot = slice_ids[:, :, None] == jnp.arange(2 * shards, dtype=jnp.int32)[None, None, :]
+    key_doc = jnp.sum(
+        jnp.where(slice_hot[..., None], doc_slices[None, None], 0), axis=2
+    ).reshape(shards * TOK)
+    own_doc = jnp.sum(
+        jnp.where((shard_ids == ctx_index)[:, None], key_doc.reshape(shards, TOK), 0), axis=0
+    )
     gathered = lax.all_gather(own_half, "ctx", axis=0, tiled=True)
     partner_all = swapped(gathered, "tp", 0)
     keys_every = jnp.where(tp_index == 0, gathered, partner_all)
     values_every = jnp.where(tp_index == 0, partner_all, gathered)
     key_count = keys_every.shape[0]
     key_pos = row_positions(jnp.arange(key_count, dtype=jnp.int32), slice_order, TOK)
-    key_doc = jnp.take(doc_ids, key_pos)
     allowed_now = (key_pos[None, :] <= own_positions[:, None]) & (
         key_doc[None, :] == own_doc[:, None]
     )

time: 166 us -> 190 us (1.14)
  matrix products: 19.4 us -> 31.8 us
  blocking collectives: 0 us -> 5.96 us
  waiting for transfers between devices: 60.1 us -> 65.5 us
  local copies, waits for them, and re-layouts: 42.6 us -> 38.2 us
  other arithmetic: 14.5 us -> 18.3 us
    all_gather x1, waiting for transfers between devices: 7.46 us -> 40.3 us  [local(): gathered = lax.all_gather(own_half, 'ctx', axis=0, tiled=True)]
    optimization_barrier x0 -> x2, local copies, waits for them, and re-layouts: none -> 28.9 us  [after(): return lax.optimization_barrier((value, anchor))[0]]
    unnamed x41 -> x62, local copies, waits for them, and re-layouts: 22.6 us -> 1.24 us
    ppermute x6, waiting for transfers between devices: 34.7 us -> 24.1 us  [swapped(): lax.ppermute(value, axis, [(i, i ^ 1 << stride) for i in range(lax.axis_s...]
    gather x2 -> x0, local copies, waits for them, and re-layouts: 9.79 us -> none  [the longest x1 8.81 us: local(): key_doc = jnp.take(doc_ids, key_pos)]
    dot_general x1 -> x3, matrix products: 0.96 us -> 9.85 us  [the longest x1 6 us: query_part(): jnp.einsum('td,dhgk->thgk', normed_rows, weights, preferred_element_type=...]
    all_gather x1, waiting for transfers between devices: 8.41 us -> 0.01 us  [normalize(): full_rows = lax.all_gather(rows, ('vis', 'tp'), axis=1, tiled=True)]
    all_to_all x1, waiting for transfers between devices: 9.5 us -> 1.14 us  [local(): lax.all_to_all(blocks, 'ctx', split_axis=0, concat_axis=0, tiled=True)]
  transfers between devices with their start and end apart: 9 -> 9, of which waited for: 8 -> 6; matrix products, arithmetic and copies ran while one was open for 31% -> 28% of each run, Pallas kernels for 0% -> 0%
where the time goes in v4:
time: 190 us; the launch traced here: 189 us
  waiting for transfers between devices  65.5 us (34%)
  local copies, waits for them, and re-layouts  38.2 us (20%)
  matrix products  31.8 us (17%)
  other arithmetic  18.3 us (10%)
  starting transfers between devices  15.4 us (8%)
  between operations  13.9 us (7%)
  blocking collectives  5.96 us (3%)
    all_gather x1, waiting for transfers between devices, local(): gathered = lax.all_gather(own_half, 'ctx', axis=0, tiled=True)  40.3 us
    optimization_barrier x2, local copies, waits for them, and re-layouts, after(): return lax.optimization_barrier((value, anchor))[0]  28.9 us
    ppermute x6, waiting for transfers between devices, swapped(): lax.ppermute(value, axis, [(i, i ^ 1 << stride) for i in range(lax.axis_s...  24.1 us
    unnamed x3, matrix products  9.36 us
    ppermute x6, starting transfers between devices, swapped(): lax.ppermute(value, axis, [(i, i ^ 1 << stride) for i in range(lax.axis_s...  9.22 us
    all_to_all x1, starting transfers between devices, local(): lax.all_to_all(blocks, 'ctx', split_axis=0, concat_axis=0, tiled=True)  6.1 us
    dot_general x1, matrix products, query_part(): jnp.einsum('td,dhgk->thgk', normed_rows, weights, preferred_element_type=...  6 us
    all_gather x1, blocking collectives, normalize(): full_rows = lax.all_gather(rows, ('vis', 'tp'), axis=1, tiled=True)  5.96 us
  transfers between devices with their start and end apart: 9, of which 6 were waited for; matrix products, arithmetic and copies ran while one was open for 28% of the time, Pallas kernels for 0%

profile of v4, /device:TPU:0, one launch (start us, length us, event | category | flops | bytes accessed | tf_op | source)
XLA Modules:
  0.0 189.0 jit_solution(17635692143233096816)
XLA Ops:
  6.6 1.2 convert_reduce_fusion
  7.9 1.2 fusion.40
  9.1 1.9 fusion.49
  11.1 0.3 fusion.125
  11.4 0.3 copy-done.5
  11.7 1.7 convolution_bitcast_fusion
  13.5 0.6 collective-permute-start
  14.3 0.7 fusion.126
  15.0 0.7 fusion.69
  16.0 0.1 eq.214
  16.2 0.1 select_reduce_fusion.4
  16.4 0.6 fusion.123
  16.9 0.2 multiply_cosine_fusion
  17.2 21.4 %copy.115 = bf16[4096,4,2,128]{0,3,2,1:T(8,128)(2,1)} copy(bf16[4096,4,2,128]{3,2,1,0:T(2,128)(2,1)} %param.32) | data formatting | bytes 16777216 | tf_op jit(solution)/shard_map/optimization_barrier | solution.py:175
  38.5 2.0 %add.232 = f32[128,1280]{1,0:T(8,128)} add(f32[128,1280]{1,0:T(8,128)S(1)} %convolution_bitcast_fusion, f32[128,1280]{1,0:T(8,128)} %collective-permute-done) | non-fusion elementwise | flops 163840 | bytes 1966080 | tf_op jit(solution)/shard_map/add | solution.py:181
  40.6 2.5 %collective-permute-start.1 = (f32[128,1280]{1,0:T(8,128)}, f32[128,1280]{1,0:T(8,128)S(1)}, u32[]{:S(2)}, u32[]{:S(2)}) collective-permute-start(f32[128,1280]{1,0:T(8,128)} %add.232), channel_id=1, source_target_pairs={{0,16},{16,0},{1,17},{17,1},{2,18},{18,2},{3,19},{19,3},{4,20},{20... | collective-permute-start | bytes 1966088 | tf_op jit(solution)/shard_map/ppermute | solution.py:23
  43.1 1.5 fusion.3
  44.6 0.6 copy-done.21
  45.2 6.1 %fusion.57 = f32[128,1024]{0,1:S(1)} fusion(bf16[4096,1024]{0,1:T(8,128)(2,1)} %bitcast.172, bf16[128,4096]{1,0:T(8,128)(2,1)} %all-gather.4.cloned.1.call-done, f32[4096]{0:T(1024)S(1)} %copy-done.6, f32[128]{0:T(128)S(1)} %add_rsqrt_fusion.2), kind=kOutput, calls=%fused_computation.67 | convolution fusion | flops 1075838976 | bytes 9978368
  51.5 0.7 pad_maximum_fusion
  52.2 6.4 %collective-permute-done.1 = f32[128,1280]{1,0:T(8,128)S(1)} collective-permute-done((f32[128,1280]{1,0:T(8,128)}, f32[128,1280]{1,0:T(8,128)S(1)}, u32[]{:S(2)}, u32[]{:S(2)}) %collective-permute-start.1) | collective-permute-done | bytes 655392 | tf_op jit(solution)/shard_map/ppermute | solution.py:23
  58.6 1.3 fusion.122
  59.9 0.2 multiply_reduce_fusion
  60.2 0.2 add_convert_fusion
  60.4 0.2 reshape.667
  60.6 0.2 convolution_convert_fusion
  60.8 0.8 copy.152
  61.6 6.1 %all-to-all-start = ((bf16[8,32,640]{2,1,0:T(8,128)(2,1)}), bf16[8,32,640]{2,1,0:T(8,128)(2,1)}, u32[]{:S(2)}, u32[]{:S(2)}) async-start(bf16[8,32,640]{2,1,0:T(8,128)(2,1)} %bitcast.169), calls=%async_computation | async-start | bytes 655360 | tf_op jit(solution)/shard_map/all_to_all | solution.py:205
  67.8 0.1 lt.86
  67.9 1.3 fusion.127
  69.2 7.5 %copy.120 = bf16[4096,4,128]{0,2,1:T(8,128)(2,1)} copy(bf16[4096,4,128]{2,1,0:T(4,128)(2,1)} %bitcast.176) | data formatting | bytes 8388608 | tf_op jit(solution)/shard_map/optimization_barrier | solution.py:175
  76.8 1.1 all-to-all-done
  77.9 1.8 reshape.669
  79.7 1.8 copy.153
  81.5 1.8 dot_general.56
  83.3 2.1 %fusion.12 = f32[4,2,32,1024]{3,2,1,0:T(8,128)S(1)} fusion(bf16[4,2,32,640]{3,2,1,0:T(8,128)(2,1)} %dot_general.56, bf16[640,1024]{1,0:T(8,128)(2,1)} %param.24), kind=kOutput, calls=%fused_computation.17 | convolution fusion | flops 335544320 | bytes 2686976 | tf_op jit(solution)/shard_map/dot_general | solution.py:209
  85.5 1.5 collective-permute-start.2
  87.0 1.3 fusion.55
  88.4 9.2 %collective-permute-done.2 = f32[4,32,1024]{2,1,0:T(8,128)S(1)} collective-permute-done((f32[4,32,1024]{2,1,0:T(8,128)S(1)}, f32[4,32,1024]{2,1,0:T(8,128)S(1)}, u32[]{:S(2)}, u32[]{:S(2)}) %collective-permute-start.2) | collective-permute-done | bytes 524320 | tf_op jit(solution)/shard_map/ppermute | solution.py:23
  97.7 0.1 fusion.48
  97.8 0.7 select_bitcast_fusion.1
  98.6 1.8 collective-permute-start.3
  100.3 0.1 select_reduce_fusion.1
  100.5 0.7 multiply_cosine_fusion.1
  101.2 4.0 %collective-permute-done.3 = f32[2,32,1024]{2,1,0:T(8,128)S(1)} collective-permute-done((f32[2,32,1024]{2,1,0:T(8,128)}, f32[2,32,1024]{2,1,0:T(8,128)S(1)}, u32[]{:S(2)}, u32[]{:S(2)}) %collective-permute-start.3) | collective-permute-done | bytes 262176 | tf_op jit(solution)/shard_map/ppermute | solution.py:23
  105.3 2.9 %collective-permute-start.4 = (f32[1,32,1024]{2,1,0:T(8,128)S(1)}, f32[1,32,1024]{2,1,0:T(8,128)S(1)}, u32[]{:S(2)}, u32[]{:S(2)}) collective-permute-start(f32[1,32,1024]{2,1,0:T(8,128)S(1)} %select_bitcast_fusion.2), channel_id=1, source_target_pairs={{0,8},{2,10},{4,12},{6,14},{8,0},{10,2},{12,4},{14,6},{1,9},{3,11}... | collective-permute-start | bytes 393224 | tf_op jit(solution)/shard_map/ppermute | solution.py:23
  108.2 4.4 %collective-permute-done.4 = f32[1,32,1024]{2,1,0:T(8,128)S(1)} collective-permute-done((f32[1,32,1024]{2,1,0:T(8,128)S(1)}, f32[1,32,1024]{2,1,0:T(8,128)S(1)}, u32[]{:S(2)}, u32[]{:S(2)}) %collective-permute-start.4) | collective-permute-done | bytes 131104 | tf_op jit(solution)/shard_map/ppermute | solution.py:23
  112.6 6.0 %all-gather = bf16[1,32,4096]{2,1,0:T(8,128)(2,1)S(1)} all-gather(bf16[1,32,1024]{2,1,0:T(8,128)(2,1)S(1)} %fusion.72), channel_id=2, replica_groups=mesh['vis'=2,'ctx'=8,'tp'=2] {'vis','tp'}, dimensions={2}, use_global_device_ids=true | all-gather | bytes 327680 | tf_op jit(solution)/shard_map/all_gather | solution.py:152
  118.6 0.2 fusion.44
  118.8 3.5 %fusion.62 = f32[32,4,128]{2,0,1:T(8,128)S(1)} fusion(bf16[4096,4,128]{0,2,1:T(8,128)(2,1)} %copy.120, bf16[1,32,4096]{2,1,0:T(8,128)(2,1)S(1)} %all-gather, f32[4096]{0:T(1024)S(1)} %copy-done.6, f32[32]{0:T(128)S(1)} %add_rsqrt_fusion), kind=kOutput, calls=%fused_computation.75 | convolution fusion | flops 134742016 | bytes 4538496 | tf_op jit(solution)/shard_map/td,dhk->thk/dot_general | solution.py:167
  122.3 0.1 multiply_subtract_fusion.1
  122.4 0.3 convolution_convert_fusion.2
  122.8 0.7 broadcast_select_fusion
  123.6 0.1 copy.106
  123.8 0.1 select_reduce_fusion
  123.9 40.3 %all-gather.6.cloned.1.call-done = bf16[1024,4,128]{0,2,1:T(8,128)(2,1)} async-done(((bf16[128,4,128]{0,2,1:T(8,128)(2,1)}), bf16[1024,4,128]{0,2,1:T(8,128)(2,1)}) %all-gather.6.cloned.1.call-update) | async-done | bytes 1048592 | tf_op jit(solution)/shard_map/all_gather | solution.py:249
  164.5 0.3 compare_and_fusion
  164.8 6.0 %fusion.60 = f32[32,4,2,128]{3,0,2,1:T(8,128)S(1)} fusion(bf16[4096,4,2,128]{0,3,2,1:T(8,128)(2,1)} %copy.115, bf16[1,32,4096]{2,1,0:T(8,128)(2,1)S(1)} %all-gather, f32[4096]{0:T(1024)S(1)} %copy-done.6, f32[32]{0:T(128)S(1)} %add_rsqrt_fusion), kind=kOutput, calls=%fused_computation.73 | convolution fusion | flops 268959744 | bytes 8798336 | tf_op jit(solution)/shard_map/td,dhgk->thgk/dot_general | solution.py:161
  170.8 0.1 subtract_convert_fusion.1
  171.0 4.4 %fusion.2 = (f32[4,2,128]{2,1,0:T(2,128)S(1)}, f32[4,1024,128,2]{2,1,3,0:T(8,128)}) fusion(pred[128,1024]{0,1:T(8,128)(4,1)S(1)} %compare_and_fusion, bf16[128,4,2,128]{0,3,2,1:T(8,128)(2,1)S(1)} %copy-done.9, pred[128]{0:T(512)(128)(4,1)S(1)} %broadcast_compare_fusion.2, bf16[32,4,2,64]{3,0,2,1:T(8,128)(2,1)S(1)} %get-tuple-element.28, ...), kind=kOutput, calls=%fused_computation.5 | convolution fusion | flops 280886272 | bytes 6762625 | tf_op jit(solution)/shard_map/qkgd,nkd->kgqn/dot_general | solution.py:258
  175.4 3.2 %fusion = f32[4,2,128]{2,1,0:T(2,128)S(1)} fusion(f32[4,1024,128,2]{2,1,3,0:T(8,128)} %get-tuple-element.40, f32[4,2,128]{2,1,0:T(2,128)S(1)} %get-tuple-element.39, pred[128,1024]{0,1:T(8,128)(4,1)S(1)} %compare_and_fusion), kind=kLoop, calls=%fused_computation.3 | loop fusion | flops 4193280 | bytes 4333568 | tf_op jit(solution)/shard_map/reduce_sum | solution.py:264
  178.6 0.2 copy-done.4
  178.8 2.5 %fusion.33 = bf16[128,4,2,128]{0,3,2,1:T(8,128)(2,1)S(1)} fusion(f32[4,1024,128,2]{2,1,3,0:T(8,128)S(1)} %copy-done.4, f32[4,2,128]{2,1,0:T(2,128)S(1)} %get-tuple-element.39, pred[128,1024]{0,1:T(8,128)(4,1)S(1)} %compare_and_fusion, bf16[1024,4,128]{0,2,1:T(8,128)(2,1)} %collective-permute-done.5, bf16[1024,4,128]{0,2,1:T(8,128)(2,1)} %all-gather.6.cloned.1.call-done, ...), kind=kOutput, calls=%fused_computation.37 | convolution fusion | flops 273416192 | bytes 6692865 | tf_op jit(solution)/shard_map/kgqn,nkd->kgqd/dot_general | solution.py:265
  181.3 0.9 copy.132
  (114 shorter events, 2.0 us)
Async XLA Ops:
  6.5 2.5 %copy-start = (bf16[1280,3,4,80]{0,3,2,1:T(8,128)(2,1)S(1)}, bf16[1280,3,4,80]{0,3,2,1:T(8,128)(2,1)}, u32[]{:S(2)}) copy-start(bf16[1280,3,4,80]{0,3,2,1:T(8,128)(2,1)} %param.20) | copy-start | bytes 7372804
  6.5 4.5 %copy-start.26 = (s32[128]{0:T(128)S(1)}, s32[128]{0:T(128)}, u32[]{:S(2)}) copy-start(s32[128]{0:T(128)} %param.26) | copy-start | bytes 1540
  6.5 7.5 %copy-start.12 = (s32[256]{0:T(256)S(1)}, s32[256]{0:T(256)}, u32[]{:S(2)}) copy-start(s32[256]{0:T(256)} %param.27) | copy-start | bytes 3076
  6.5 7.7 %copy-start.10 = (s32[8]{0:T(128)S(1)}, s32[8]{0:T(128)}, u32[]{:S(2)}) copy-start(s32[8]{0:T(128)} %param.28) | copy-start | bytes 100
  6.5 9.5 %copy-start.27 = (s32[8,2]{0,1:T(2,128)S(1)}, s32[8,2]{0,1:T(2,128)}, u32[]{:S(2)}) copy-start(s32[8,2]{0,1:T(2,128)} %param.25) | copy-start | bytes 196
  6.5 36.5 %all-gather.4.cloned.1.call-start = ((), (), s32[]{:S(2)}) async-start(), calls=%async_computation.1 | async-start | bytes 1310720 | tf_op jit(solution)/shard_map/all_gather | solution.py:152
  11.0 0.7 copy-start.5
  13.5 3.7 %collective-permute-start = (f32[128,1280]{1,0:T(8,128)S(1)}, f32[128,1280]{1,0:T(8,128)}, u32[]{:S(2)}, u32[]{:S(2)}) collective-permute-start(f32[128,1280]{1,0:T(8,128)S(1)} %convolution_bitcast_fusion), channel_id=1, source_target_pairs={{0,1},{1,0},{2,3},{3,2},{4,5},{5,4},{6,7},{7,6},{8,9},{9,8},{10,11... | collective-permute-start | bytes 1966088 | tf_op jit(solution)/shard_map/ppermute | solution.py:23
  16.0 51.9 %copy-start.18 = (s32[256]{0:T(256)}, s32[256]{0:T(256)S(1)}, u32[]{:S(2)}) copy-start(s32[256]{0:T(256)S(1)} %add.227) | copy-start | bytes 3076
  16.1 51.8 %copy-start.28 = (pred[256]{0:T(512)(128)(4,1)}, pred[256]{0:T(512)(128)(4,1)S(1)}, u32[]{:S(2)}) copy-start(pred[256]{0:T(512)(128)(4,1)S(1)} %eq.214) | copy-start | bytes 772
  16.1 22.4 %copy-start.23 = (pred[8]{0:T(512)(128)(4,1)}, pred[8]{0:T(512)(128)(4,1)S(1)}, u32[]{:S(2)}) copy-start(pred[8]{0:T(512)(128)(4,1)S(1)} %iota_compare_fusion.9) | copy-start | bytes 28
  16.1 22.4 %copy-start.20 = (f32[64]{0:T(128)}, f32[64]{0:T(128)S(1)}, u32[]{:S(2)}) copy-start(f32[64]{0:T(128)S(1)} %multiply_power_fusion) | copy-start | bytes 772
  17.1 34.3 %copy-start.7 = (f32[128,64]{0,1:T(8,128)}, f32[128,64]{0,1:T(8,128)S(1)}, u32[]{:S(2)}) copy-start(f32[128,64]{0,1:T(8,128)S(1)} %get-tuple-element.34) | copy-start | bytes 98308
  17.1 28.1 %copy-start.6 = (f32[4096]{0:T(1024)S(1)}, f32[4096]{0:T(1024)}, u32[]{:S(2)}) copy-start(f32[4096]{0:T(1024)} %param.31) | copy-start | bytes 49156
  40.6 18.1 %collective-permute-start.1 = (f32[128,1280]{1,0:T(8,128)}, f32[128,1280]{1,0:T(8,128)S(1)}, u32[]{:S(2)}, u32[]{:S(2)}) collective-permute-start(f32[128,1280]{1,0:T(8,128)} %add.232), channel_id=1, source_target_pairs={{0,16},{16,0},{1,17},{17,1},{2,18},{18,2},{3,19},{19,3},{4,20},{20... | collective-permute-start | bytes 1966088 | tf_op jit(solution)/shard_map/ppermute | solution.py:23
  44.6 0.6 copy-start.21
  45.2 13.4 %copy-start.3 = (bf16[128,1280]{1,0:T(8,128)(2,1)S(1)}, bf16[128,1280]{1,0:T(8,128)(2,1)}, u32[]{:S(2)}) copy-start(bf16[128,1280]{1,0:T(8,128)(2,1)} %param.17) | copy-start | bytes 983044
  51.4 8.8 %copy-start.14 = (f32[1280]{0:T(1024)S(1)}, f32[1280]{0:T(1024)}, u32[]{:S(2)}) copy-start(f32[1280]{0:T(1024)} %param.23) | copy-start | bytes 15364
  51.4 8.8 %copy-start.15 = (f32[1280]{0:T(1024)S(1)}, f32[1280]{0:T(1024)}, u32[]{:S(2)}) copy-start(f32[1280]{0:T(1024)} %param.22) | copy-start | bytes 15364
  61.6 16.3 %all-to-all-start = ((bf16[8,32,640]{2,1,0:T(8,128)(2,1)}), bf16[8,32,640]{2,1,0:T(8,128)(2,1)}, u32[]{:S(2)}, u32[]{:S(2)}) async-start(bf16[8,32,640]{2,1,0:T(8,128)(2,1)} %bitcast.169), calls=%async_computation | async-start | bytes 655360 | tf_op jit(solution)/shard_map/all_to_all | solution.py:205
  67.7 96.5 %all-gather.6.cloned.1.call-start = ((), (), s32[]{:S(2)}) async-start(), calls=%async_computation.2 | async-start | bytes 1179648 | tf_op jit(solution)/shard_map/all_gather | solution.py:249
  76.8 10.2 %copy-start.2 = (bf16[128,4096]{1,0:T(8,128)(2,1)S(1)}, bf16[128,4096]{1,0:T(8,128)(2,1)}, u32[]{:S(2)}) copy-start(bf16[128,4096]{1,0:T(8,128)(2,1)} %all-gather.4.cloned.1.call-done) | copy-start | bytes 3145732
  83.3 3.7 %copy-start.1 = (bf16[4096,4,128]{0,2,1:T(8,128)(2,1)S(1)}, bf16[4096,4,128]{0,2,1:T(8,128)(2,1)}, u32[]{:S(2)}) copy-start(bf16[4096,4,128]{0,2,1:T(8,128)(2,1)} %copy.120) | copy-start | bytes 12582916
  83.3 3.7 %copy-start.22 = (f32[128]{0:T(128)S(1)}, f32[128]{0:T(128)}, u32[]{:S(2)}) copy-start(f32[128]{0:T(128)} %copy-done.21) | copy-start | bytes 1540
  85.4 2.9 %copy-start.8 = (f32[128,64]{0,1:T(8,128)S(1)}, f32[128,64]{0,1:T(8,128)}, u32[]{:S(2)}) copy-start(f32[128,64]{0,1:T(8,128)} %copy-done.7) | copy-start | bytes 98308
  85.5 12.2 %collective-permute-start.2 = (f32[4,32,1024]{2,1,0:T(8,128)S(1)}, f32[4,32,1024]{2,1,0:T(8,128)S(1)}, u32[]{:S(2)}, u32[]{:S(2)}) collective-permute-start(f32[4,32,1024]{2,1,0:T(8,128)S(1)} %select_bitcast_fusion), channel_id=1, source_target_pairs={{0,2},{2,0},{4,6},{6,4},{8,10},{10,8},{12,14},{14,12},{1,3},{3,1},... | collective-permute-start | bytes 1572872 | tf_op jit(solution)/shard_map/ppermute | solution.py:23
  87.0 13.3 %copy-start.13 = (s32[256]{0:T(256)S(1)}, s32[256]{0:T(256)}, u32[]{:S(2)}) copy-start(s32[256]{0:T(256)} %param.27) | copy-start | bytes 3076
  87.0 13.3 %copy-start.19 = (s32[256]{0:T(256)S(1)}, s32[256]{0:T(256)}, u32[]{:S(2)}) copy-start(s32[256]{0:T(256)} %copy-done.18) | copy-start | bytes 3076
  87.0 13.3 %copy-start.29 = (pred[256]{0:T(512)(128)(4,1)S(1)}, pred[256]{0:T(512)(128)(4,1)}, u32[]{:S(2)}) copy-start(pred[256]{0:T(512)(128)(4,1)} %copy-done.28) | copy-start | bytes 772
  88.3 19.9 %copy-start.30 = (f32[128]{0:T(128)S(1)}, f32[128]{0:T(128)}, u32[]{:S(2)}) copy-start(f32[128]{0:T(128)} %get-tuple-element.37) | copy-start | bytes 1540
  97.8 24.6 %copy-start.16 = (bf16[128,32]{0,1:T(8,128)(2,1)S(1)}, bf16[128,32]{0,1:T(8,128)(2,1)}, u32[]{:S(2)}) copy-start(bf16[128,32]{0,1:T(8,128)(2,1)} %get-tuple-element.38) | copy-start | bytes 24580
  98.5 24.9 %copy-start.17 = (s32[1024]{0:T(1024)S(1)}, s32[1024]{0:T(1024)}, u32[]{:S(2)}) copy-start(s32[1024]{0:T(1024)} %param.29) | copy-start | bytes 12292
  98.5 25.0 %copy-start.11 = (s32[8]{0:T(128)S(1)}, s32[8]{0:T(128)}, u32[]{:S(2)}) copy-start(s32[8]{0:T(128)} %param.28) | copy-start | bytes 100
  98.6 65.7 %copy-start.24 = (pred[8]{0:T(512)(128)(4,1)S(1)}, pred[8]{0:T(512)(128)(4,1)}, u32[]{:S(2)}) copy-start(pred[8]{0:T(512)(128)(4,1)} %copy-done.23) | copy-start | bytes 28
  98.6 65.9 %copy-start.25 = (s32[128]{0:T(128)S(1)}, s32[128]{0:T(128)}, u32[]{:S(2)}) copy-start(s32[128]{0:T(128)} %get-tuple-element.22) | copy-start | bytes 1540
  98.6 6.6 %collective-permute-start.3 = (f32[2,32,1024]{2,1,0:T(8,128)}, f32[2,32,1024]{2,1,0:T(8,128)S(1)}, u32[]{:S(2)}, u32[]{:S(2)}) collective-permute-start(f32[2,32,1024]{2,1,0:T(8,128)} %select_bitcast_fusion.1), channel_id=1, source_target_pairs={{0,4},{2,6},{4,0},{6,2},{8,12},{10,14},{12,8},{14,10},{1,5},{3,7},... | collective-permute-start | bytes 786440 | tf_op jit(solution)/shard_map/ppermute | solution.py:23
  105.3 7.3 %collective-permute-start.4 = (f32[1,32,1024]{2,1,0:T(8,128)S(1)}, f32[1,32,1024]{2,1,0:T(8,128)S(1)}, u32[]{:S(2)}, u32[]{:S(2)}) collective-permute-start(f32[1,32,1024]{2,1,0:T(8,128)S(1)} %select_bitcast_fusion.2), channel_id=1, source_target_pairs={{0,8},{2,10},{4,12},{6,14},{8,0},{10,2},{12,4},{14,6},{1,9},{3,11}... | collective-permute-start | bytes 393224 | tf_op jit(solution)/shard_map/ppermute | solution.py:23
  164.2 6.8 %collective-permute-start.5 = (bf16[1024,4,128]{0,2,1:T(8,128)(2,1)}, bf16[1024,4,128]{0,2,1:T(8,128)(2,1)}, u32[]{:S(2)}, u32[]{:S(2)}) collective-permute-start(bf16[1024,4,128]{0,2,1:T(8,128)(2,1)} %all-gather.6.cloned.1.call-done), channel_id=1, source_target_pairs={{0,1},{1,0},{2,3},{3,2},{4,5},{5,4},{6,7},{7,6},{8,9},{9,8},{10,11... | collective-permute-start | bytes 3145736 | tf_op jit(solution)/shard_map/ppermute | solution.py:23
  164.8 6.2 %copy-start.9 = (bf16[128,4,2,128]{0,3,2,1:T(8,128)(2,1)S(1)}, bf16[128,4,2,128]{0,3,2,1:T(8,128)(2,1)}, u32[]{:S(2)}) copy-start(bf16[128,4,2,128]{0,3,2,1:T(8,128)(2,1)} %pad_maximum_fusion) | copy-start | bytes 786436
  175.4 3.4 %copy-start.4 = (f32[4,1024,128,2]{2,1,3,0:T(8,128)S(1)}, f32[4,1024,128,2]{2,1,3,0:T(8,128)}, u32[]{:S(2)}) copy-start(f32[4,1024,128,2]{2,1,3,0:T(8,128)} %get-tuple-element.40) | copy-start | bytes 12582916
Sparse Core Ops, SparseCore 0:
  14.2 19.0 all-gather.3
  123.6 40.5 all-gather.5

commit v5 on v4

--- a/solution.py
+++ b/solution.py
@@ -83,6 +83,24 @@
         remaining //= 2
         bit += 1
     return blocks[0], rider
+
+
+def doubling_gather(block, axis, index, count, bits):
+    have = block[None]
+    for bit in bits:
+        arrived = swapped(have, axis, bit)
+        mine = (index >> bit) & 1
+        have = jnp.where(
+            mine == 0,
+            jnp.concatenate([have, arrived], axis=0),
+            jnp.concatenate([arrived, have], axis=0),
+        )
+    order = list(bits)
+    have = have.reshape((2,) * len(order) + block.shape)
+    by_bit = {bit: len(order) - 1 - place for place, bit in enumerate(order)}
+    wanted = [by_bit[bit] for bit in sorted(order, reverse=True)]
+    have = jnp.transpose(have, wanted + list(range(len(order), have.ndim)))
+    return have.reshape((count,) + block.shape)
 
 
 def rotate_rows(values, positions):
@@ -148,8 +166,23 @@
     kv_heads = w_query.shape[1]
     groups = w_query.shape[2]
 
-    def normalize(rows):
-        full_rows = lax.all_gather(rows, ("vis", "tp"), axis=1, tiled=True)
+    def normalize(rows, by_swaps=False):
+        if by_swaps:
+            tp_size = lax.axis_size("tp")
+            vis_size = lax.axis_size("vis")
+            stacked = doubling_gather(
+                rows, "tp", tp_index, tp_size, list(range(tp_size.bit_length() - 1))
+            )
+            stacked = doubling_gather(
+                stacked,
+                "vis",
+                lax.axis_index("vis"),
+                vis_size,
+                list(range(vis_size.bit_length() - 1)),
+            )
+            full_rows = jnp.transpose(stacked, (2, 0, 1, 3)).reshape(rows.shape[0], -1)
+        else:
+            full_rows = lax.all_gather(rows, ("vis", "tp"), axis=1, tiled=True)
         widened = full_rows.astype(jnp.float32)
         return (
             widened
@@ -226,7 +259,7 @@
     incoming_pos = jnp.sum(
         jnp.where(column_match & mine_all[:, None], image_pos[:, None], 0), axis=0
     )
-    image_normed = normalize(incoming)
+    image_normed = normalize(incoming, by_swaps=True)
     image_queries = query_part(image_normed, incoming_pos, query_weights)
     image_half = keyval_part(image_normed, incoming_pos, keyval_weights)
     placed_queries = jnp.einsum(
@@ -246,7 +279,10 @@
     own_doc = jnp.sum(
         jnp.where((shard_ids == ctx_index)[:, None], key_doc.reshape(shards, TOK), 0), axis=0
     )
-    gathered = lax.all_gather(own_half, "ctx", axis=0, tiled=True)
+    ctx_bits = list(range(shards.bit_length() - 1))[::-1]
+    gathered = doubling_gather(own_half, "ctx", ctx_index, shards, ctx_bits).reshape(
+        (shards * TOK,) + own_half.shape[1:]
+    )
     partner_all = swapped(gathered, "tp", 0)
     keys_every = jnp.where(tp_index == 0, gathered, partner_all)
     values_every = jnp.where(tp_index == 0, partner_all, gathered)

time: 190 us -> 190 us (level)
  waiting for transfers between devices: 65.5 us -> 45.6 us
  local copies, waits for them, and re-layouts: 38.2 us -> 49.6 us
  other arithmetic: 18.3 us -> 25.8 us
  blocking collectives: 5.96 us -> 0 us
  starting transfers between devices: 15.4 us -> 20.5 us
    all_gather x1 -> x0, waiting for transfers between devices: 40.3 us -> none  [local(): gathered = lax.all_gather(own_half, 'ctx', axis=0, tiled=True)]
    ppermute x6 -> x11, waiting for transfers between devices: 24.1 us -> 44.3 us  [swapped(): lax.ppermute(value, axis, [(i, i ^ 1 << stride) for i in range(lax.axis_s...]
    all_gather x1 -> x0, blocking collectives: 5.96 us -> none  [normalize(): full_rows = lax.all_gather(rows, ('vis', 'tp'), axis=1, tiled=True)]
    ppermute x6 -> x11, starting transfers between devices: 9.22 us -> 14.4 us  [swapped(): lax.ppermute(value, axis, [(i, i ^ 1 << stride) for i in range(lax.axis_s...]
    another operation x0 -> x1, local copies, waits for them, and re-layouts: none -> 2.57 us  [local(): doubling_gather(own_half, 'ctx', ctx_index, shards, ctx_bits)]
    transpose x0 -> x1, local copies, waits for them, and re-layouts: none -> 2.15 us  [doubling_gather(): have = jnp.transpose(have, wanted + list(range(len(order), have.ndim)))]
  transfers between devices with their start and end apart: 9 -> 13, of which waited for: 6 -> 9; matrix products, arithmetic and copies ran while one was open for 28% -> 35% of each run, Pallas kernels for 0% -> 0%
where the time goes in v5:
time: 190 us; the launch traced here: 188 us
  local copies, waits for them, and re-layouts  49.6 us (26%)
  waiting for transfers between devices  45.6 us (24%)
  matrix products  32.7 us (17%)
  other arithmetic  25.8 us (14%)
  starting transfers between devices  20.5 us (11%)
  between operations  14 us (7%)
    ppermute x11, waiting for transfers between devices, swapped(): lax.ppermute(value, axis, [(i, i ^ 1 << stride) for i in range(lax.axis_s...  44.3 us
    optimization_barrier x2, local copies, waits for them, and re-layouts, after(): return lax.optimization_barrier((value, anchor))[0]  28.8 us
    ppermute x11, starting transfers between devices, swapped(): lax.ppermute(value, axis, [(i, i ^ 1 << stride) for i in range(lax.axis_s...  14.4 us
    unnamed x3, matrix products  9.36 us
    all_to_all x1, starting transfers between devices, local(): lax.all_to_all(blocks, 'ctx', split_axis=0, concat_axis=0, tiled=True)  6.06 us
    dot_general x1, matrix products, query_part(): jnp.einsum('td,dhgk->thgk', normed_rows, weights, preferred_element_type=...  5.96 us
    dot_general x1, matrix products, local(): jnp.einsum('qkgd,nkd->kgqn', queries, keys_every, preferred_element_type=...  4.6 us
  transfers between devices with their start and end apart: 13, of which 9 were waited for; matrix products, arithmetic and copies ran while one was open for 35% of the time, Pallas kernels for 0%

profile of v5, /device:TPU:0, one launch (start us, length us, event | category | flops | bytes accessed | tf_op | source)
XLA Modules:
  0.0 188.2 jit_solution(9584122708089383325)
XLA Ops:
  6.6 1.2 convert_reduce_fusion
  7.8 1.2 fusion.40
  9.1 1.9 %fusion.47 = f32[128,960]{0,1:S(1)} fusion(bf16[1280,960]{0,1:T(8,128)(2,1)S(1)} %bitcast.176, bf16[128,1280]{1,0:T(8,128)(2,1)} %param.17, f32[1280]{0:T(1024)} %param.19, f32[1280]{0:T(1024)} %param.18, f32[128]{0:T(128)S(1)} %add_rsqrt_fusion.3, f32[128]{0:T(128)S(1)} %broadcast_multiply_fusion.1), kind=kOutput, calls=%fused_computation.60 | convolution fusion | flops 315555840 | bytes 3288064
  11.7 1.7 convolution_bitcast_fusion
  14.3 0.7 fusion.124
  15.1 0.7 add.227
  15.8 0.7 fusion.69
  16.8 0.6 fusion.121
  17.6 21.3 %copy.131 = bf16[4096,4,2,128]{0,3,2,1:T(8,128)(2,1)} copy(bf16[4096,4,2,128]{3,2,1,0:T(2,128)(2,1)} %param.32) | data formatting | bytes 16777216 | tf_op jit(solution)/shard_map/optimization_barrier | solution.py:208
  38.9 2.0 %add.232 = f32[128,1280]{1,0:T(8,128)} add(f32[128,1280]{1,0:T(8,128)S(1)} %convolution_bitcast_fusion, f32[128,1280]{1,0:T(8,128)} %collective-permute-done) | non-fusion elementwise | flops 163840 | bytes 1966080 | tf_op jit(solution)/shard_map/add | solution.py:214
  41.0 2.5 %collective-permute-start.1 = (f32[128,1280]{1,0:T(8,128)}, f32[128,1280]{1,0:T(8,128)S(1)}, u32[]{:S(2)}, u32[]{:S(2)}) collective-permute-start(f32[128,1280]{1,0:T(8,128)} %add.232), channel_id=1, source_target_pairs={{0,16},{16,0},{1,17},{17,1},{2,18},{18,2},{3,19},{19,3},{4,20},{20... | collective-permute-start | bytes 1966088 | tf_op jit(solution)/shard_map/ppermute | solution.py:23
  43.5 1.5 fusion.3
  45.0 0.6 copy-done.25
  45.6 6.2 %fusion.55 = f32[128,1024]{0,1:S(1)} fusion(bf16[4096,1024]{0,1:T(8,128)(2,1)} %bitcast.177, bf16[128,4096]{1,0:T(8,128)(2,1)} %all-gather.2.cloned.1.call-done, f32[4096]{0:T(1024)S(1)} %copy-done.11, f32[128]{0:T(128)S(1)} %add_rsqrt_fusion.2), kind=kOutput, calls=%fused_computation.68 | convolution fusion | flops 1075838976 | bytes 9978368
  51.9 0.7 pad_maximum_fusion
  52.6 6.5 %collective-permute-done.1 = f32[128,1280]{1,0:T(8,128)S(1)} collective-permute-done((f32[128,1280]{1,0:T(8,128)}, f32[128,1280]{1,0:T(8,128)S(1)}, u32[]{:S(2)}, u32[]{:S(2)}) %collective-permute-start.1) | collective-permute-done | bytes 655392 | tf_op jit(solution)/shard_map/ppermute | solution.py:23
  59.1 1.3 fusion.120
  61.3 0.8 copy.171
  62.0 6.1 %all-to-all-start = ((bf16[8,32,640]{2,1,0:T(8,128)(2,1)}), bf16[8,32,640]{2,1,0:T(8,128)(2,1)}, u32[]{:S(2)}, u32[]{:S(2)}) async-start(bf16[8,32,640]{2,1,0:T(8,128)(2,1)} %bitcast.174), calls=%async_computation | async-start | bytes 655360 | tf_op jit(solution)/shard_map/all_to_all | solution.py:238
  68.1 0.6 eq.226
  68.7 0.7 iota_compare_fusion.7
  69.4 7.5 %copy.136 = bf16[4096,4,128]{0,2,1:T(8,128)(2,1)} copy(bf16[4096,4,128]{2,1,0:T(4,128)(2,1)} %bitcast.182) | data formatting | bytes 8388608 | tf_op jit(solution)/shard_map/optimization_barrier | solution.py:208
  76.9 1.3 all-to-all-done
  78.3 1.8 reshape.731
  80.0 1.8 copy.172
  81.8 1.8 dot_general.56
  83.6 2.1 %fusion.12 = f32[4,2,32,1024]{3,2,1,0:T(8,128)S(1)} fusion(bf16[4,2,32,640]{3,2,1,0:T(8,128)(2,1)} %dot_general.56, bf16[640,1024]{1,0:T(8,128)(2,1)} %param.24), kind=kOutput, calls=%fused_computation.17 | convolution fusion | flops 335544320 | bytes 2686976 | tf_op jit(solution)/shard_map/dot_general | solution.py:242
  85.8 1.5 collective-permute-start.2
  87.4 1.3 fusion.53
  88.8 0.7 fusion.57
  89.4 8.4 %collective-permute-done.2 = f32[4,32,1024]{2,1,0:T(8,128)S(1)} collective-permute-done((f32[4,32,1024]{2,1,0:T(8,128)S(1)}, f32[4,32,1024]{2,1,0:T(8,128)S(1)}, u32[]{:S(2)}, u32[]{:S(2)}) %collective-permute-start.2) | collective-permute-done | bytes 524320 | tf_op jit(solution)/shard_map/ppermute | solution.py:23
  97.9 1.8 collective-permute-start.3
  99.9 0.8 lt.86
  100.6 1.1 and.189
  101.8 0.7 multiply_cosine_fusion.1
  102.5 1.9 collective-permute-done.3
  104.5 3.2 %collective-permute-start.4 = (f32[1,32,1024]{2,1,0:T(8,128)S(1)}, f32[1,32,1024]{2,1,0:T(8,128)S(1)}, u32[]{:S(2)}, u32[]{:S(2)}) collective-permute-start(f32[1,32,1024]{2,1,0:T(8,128)S(1)} %select_bitcast_fusion.3), channel_id=1, source_target_pairs={{0,8},{2,10},{4,12},{6,14},{8,0},{10,2},{12,4},{14,6},{1,9},{3,11}... | collective-permute-start | bytes 393224 | tf_op jit(solution)/shard_map/ppermute | solution.py:23
  107.6 0.7 fusion.112
  108.3 3.7 %collective-permute-done.4 = f32[1,32,1024]{2,1,0:T(8,128)S(1)} collective-permute-done((f32[1,32,1024]{2,1,0:T(8,128)S(1)}, f32[1,32,1024]{2,1,0:T(8,128)S(1)}, u32[]{:S(2)}, u32[]{:S(2)}) %collective-permute-start.4) | collective-permute-done | bytes 131104 | tf_op jit(solution)/shard_map/ppermute | solution.py:23
  112.1 1.4 fusion.125
  113.6 1.4 collective-permute-start.6
  115.5 4.1 %collective-permute-done.6 = bf16[1,2,32,1024]{3,2,1,0:T(8,128)(2,1)S(1)} collective-permute-done((bf16[1,2,32,1024]{3,2,1,0:T(8,128)(2,1)S(1)}, bf16[1,2,32,1024]{3,2,1,0:T(8,128)(2,1)S(1)}, u32[]{:S(2)}, u32[]{:S(2)}) %collective-permute-start.6) | collective-permute-done | bytes 131104 | tf_op jit(solution)/shard_map/ppermute | solution.py:23
  119.5 0.6 copy-done.9
  121.1 1.3 fusion.44
  122.5 3.5 %fusion.63 = f32[32,4,128]{2,0,1:T(8,128)S(1)} fusion(bf16[4096,4,128]{0,2,1:T(8,128)(2,1)} %copy.136, f32[32,4096]{1,0:T(8,128)S(1)} %reshape.734, f32[4096]{0:T(1024)S(1)} %copy-done.11, f32[32]{0:T(128)S(1)} %add_rsqrt_fusion), kind=kOutput, calls=%fused_computation.80 | convolution fusion | flops 134610944 | bytes 4800640 | tf_op jit(solution)/shard_map/td,dhk->thk/dot_general | solution.py:200
  126.5 1.7 collective-permute-start.7
  128.2 7.1 %collective-permute-done.7 = bf16[1,128,4,128]{1,3,2,0:T(8,128)(2,1)S(1)} collective-permute-done((bf16[1,128,4,128]{1,3,2,0:T(8,128)(2,1)S(1)}, bf16[1,128,4,128]{1,3,2,0:T(8,128)(2,1)S(1)}, u32[]{:S(2)}, u32[]{:S(2)}) %collective-permute-start.7) | collective-permute-done | bytes 131104 | tf_op jit(solution)/shard_map/ppermute | solution.py:23
  136.0 1.3 broadcast_in_dim.131
  137.3 1.3 copy.122
  138.6 0.7 select_reduce_fusion.2
  139.4 3.6 %collective-permute-done.8 = bf16[2,128,4,128]{1,3,2,0:T(8,128)(2,1)S(1)} collective-permute-done((bf16[2,128,4,128]{1,3,2,0:T(8,128)(2,1)S(1)}, bf16[2,128,4,128]{1,3,2,0:T(8,128)(2,1)S(1)}, u32[]{:S(2)}, u32[]{:S(2)}) %collective-permute-start.8) | collective-permute-done | bytes 262176 | tf_op jit(solution)/shard_map/ppermute | solution.py:23
  143.1 1.7 collective-permute-start.9
  144.7 0.8 iota_compare_fusion.6
  145.5 0.8 select_reduce_fusion
  146.3 9.1 %collective-permute-done.9 = bf16[4,128,4,128]{1,3,2,0:T(8,128)(2,1)S(1)} collective-permute-done((bf16[4,128,4,128]{1,3,2,0:T(8,128)(2,1)S(1)}, bf16[4,128,4,128]{1,3,2,0:T(8,128)(2,1)S(1)}, u32[]{:S(2)}, u32[]{:S(2)}) %collective-permute-start.9) | collective-permute-done | bytes 524320 | tf_op jit(solution)/shard_map/ppermute | solution.py:23
  155.6 2.1 %copy.146 = bf16[2,2,2,128,4,128]{3,2,1,0,5,4:T(2,128)(2,1)} copy(bf16[2,2,2,128,4,128]{3,5,4,0,1,2:T(8,128)(2,1)S(1)} %bitcast.181) | data formatting | bytes 2097152 | tf_op jit(solution)/shard_map/transpose | solution.py:102
  157.8 2.6 %reshape_reshape.2 = bf16[1024,4,128]{0,2,1:T(8,128)(2,1)} reshape(bf16[2,2,2,128,4,128]{3,2,1,0,5,4:T(2,128)(2,1)} %copy.146) | data formatting | bytes 2097152 | tf_op jit(solution)/shard_map/reshape;reshape | solution.py:283
  160.6 1.0 compare_and_fusion
  161.6 6.0 %fusion.61 = f32[32,4,2,128]{3,0,2,1:T(8,128)S(1)} fusion(bf16[4096,4,2,128]{0,3,2,1:T(8,128)(2,1)} %copy.131, f32[32,4096]{1,0:T(8,128)S(1)} %reshape.734, f32[4096]{0:T(1024)S(1)} %copy-done.11, f32[32]{0:T(128)S(1)} %copy-done.24), kind=kOutput, calls=%fused_computation.78 | convolution fusion | flops 268828672 | bytes 9060480 | tf_op jit(solution)/shard_map/td,dhgk->thgk/dot_general | solution.py:194
  167.5 0.8 subtract_convert_fusion.1
  168.3 4.6 %fusion.2 = (f32[4,2,128]{2,1,0:T(2,128)S(1)}, f32[4,1024,128,2]{2,1,3,0:T(8,128)}) fusion(pred[128,1024]{0,1:T(8,128)(4,1)} %compare_and_fusion, bf16[128,4,2,128]{0,3,2,1:T(8,128)(2,1)} %pad_maximum_fusion, pred[128]{0:T(512)(128)(4,1)} %broadcast_compare_fusion.2, bf16[32,4,2,64]{3,0,2,1:T(8,128)(2,1)} %get-tuple-element.28, ...), kind=kOutput, calls=%fused_computation.5 | convolution fusion | flops 280886272 | bytes 6762625 | tf_op jit(solution)/shard_map/qkgd,nkd->kgqn/dot_general | solution.py:294
  172.9 3.2 %fusion = f32[4,2,128]{2,1,0:T(2,128)S(1)} fusion(f32[4,1024,128,2]{2,1,3,0:T(8,128)} %get-tuple-element.40, f32[4,2,128]{2,1,0:T(2,128)S(1)} %get-tuple-element.39, pred[128,1024]{0,1:T(8,128)(4,1)} %compare_and_fusion), kind=kLoop, calls=%fused_computation.3 | loop fusion | flops 4193280 | bytes 4333568 | tf_op jit(solution)/shard_map/reduce_sum | solution.py:300
  176.4 3.2 %fusion.33 = bf16[128,4,2,128]{0,3,2,1:T(8,128)(2,1)} fusion(f32[4,1024,128,2]{2,1,3,0:T(8,128)S(1)} %copy-done.4, f32[4,2,128]{2,1,0:T(2,128)S(1)} %get-tuple-element.39, pred[128,1024]{0,1:T(8,128)(4,1)S(1)} %copy-done.8, bf16[1024,4,128]{0,2,1:T(8,128)(2,1)} %collective-permute-done.10, bf16[1024,4,128]{0,2,1:T(8,128)(2,1)S(1)} %copy-done.6, ...), kind=kOutput, calls=%fused_computation.38 | convolution fusion | flops 273416192 | bytes 6692865 | tf_op jit(solution)/shard_map/kgqn,nkd->kgqd/dot_general | solution.py:301
  179.6 1.8 copy.152
  (135 shorter events, 7.0 us)
Async XLA Ops:
  6.5 2.5 %copy-start = (bf16[1280,3,4,80]{0,3,2,1:T(8,128)(2,1)S(1)}, bf16[1280,3,4,80]{0,3,2,1:T(8,128)(2,1)}, u32[]{:S(2)}) copy-start(bf16[1280,3,4,80]{0,3,2,1:T(8,128)(2,1)} %param.20) | copy-start | bytes 7372804
  6.5 4.5 %copy-start.30 = (s32[128]{0:T(128)S(1)}, s32[128]{0:T(128)}, u32[]{:S(2)}) copy-start(s32[128]{0:T(128)} %param.26) | copy-start | bytes 1540
  6.5 7.5 %copy-start.16 = (s32[256]{0:T(256)S(1)}, s32[256]{0:T(256)}, u32[]{:S(2)}) copy-start(s32[256]{0:T(256)} %param.27) | copy-start | bytes 3076
  6.5 7.7 %copy-start.14 = (s32[8]{0:T(128)S(1)}, s32[8]{0:T(128)}, u32[]{:S(2)}) copy-start(s32[8]{0:T(128)} %param.28) | copy-start | bytes 100
  6.5 36.9 %all-gather.2.cloned.1.call-start = ((), (), s32[]{:S(2)}) async-start(), calls=%async_computation.1 | async-start | bytes 1310720 | tf_op jit(solution)/shard_map/all_gather | solution.py:185
  11.0 0.7 copy-start.10
  13.4 4.1 %collective-permute-start = (f32[128,1280]{1,0:T(8,128)S(1)}, f32[128,1280]{1,0:T(8,128)}, u32[]{:S(2)}, u32[]{:S(2)}) collective-permute-start(f32[128,1280]{1,0:T(8,128)S(1)} %convolution_bitcast_fusion), channel_id=1, source_target_pairs={{0,1},{1,0},{2,3},{3,2},{4,5},{5,4},{6,7},{7,6},{8,9},{9,8},{10,11... | collective-permute-start | bytes 1966088 | tf_op jit(solution)/shard_map/ppermute | solution.py:23
  16.6 0.8 copy-start.27
  16.6 22.4 %copy-start.22 = (f32[64]{0:T(128)}, f32[64]{0:T(128)S(1)}, u32[]{:S(2)}) copy-start(f32[64]{0:T(128)S(1)} %multiply_power_fusion) | copy-start | bytes 772
  17.6 34.2 %copy-start.12 = (f32[128,64]{0,1:T(8,128)}, f32[128,64]{0,1:T(8,128)S(1)}, u32[]{:S(2)}) copy-start(f32[128,64]{0,1:T(8,128)S(1)} %get-tuple-element.34) | copy-start | bytes 98308
  17.6 28.0 %copy-start.11 = (f32[4096]{0:T(1024)S(1)}, f32[4096]{0:T(1024)}, u32[]{:S(2)}) copy-start(f32[4096]{0:T(1024)} %param.31) | copy-start | bytes 49156
  41.0 18.1 %collective-permute-start.1 = (f32[128,1280]{1,0:T(8,128)}, f32[128,1280]{1,0:T(8,128)S(1)}, u32[]{:S(2)}, u32[]{:S(2)}) collective-permute-start(f32[128,1280]{1,0:T(8,128)} %add.232), channel_id=1, source_target_pairs={{0,16},{16,0},{1,17},{17,1},{2,18},{18,2},{3,19},{19,3},{4,20},{20... | collective-permute-start | bytes 1966088 | tf_op jit(solution)/shard_map/ppermute | solution.py:23
  45.0 0.6 copy-start.25
  45.6 13.5 %copy-start.3 = (bf16[128,1280]{1,0:T(8,128)(2,1)S(1)}, bf16[128,1280]{1,0:T(8,128)(2,1)}, u32[]{:S(2)}) copy-start(bf16[128,1280]{1,0:T(8,128)(2,1)} %param.17) | copy-start | bytes 983044
  51.7 8.9 %copy-start.18 = (f32[1280]{0:T(1024)S(1)}, f32[1280]{0:T(1024)}, u32[]{:S(2)}) copy-start(f32[1280]{0:T(1024)} %param.23) | copy-start | bytes 15364
  51.8 8.9 %copy-start.19 = (f32[1280]{0:T(1024)S(1)}, f32[1280]{0:T(1024)}, u32[]{:S(2)}) copy-start(f32[1280]{0:T(1024)} %param.22) | copy-start | bytes 15364
  51.8 16.9 %copy-start.31 = (s32[8,2]{0,1:T(2,128)S(1)}, s32[8,2]{0,1:T(2,128)}, u32[]{:S(2)}) copy-start(s32[8,2]{0,1:T(2,128)} %param.25) | copy-start | bytes 196
  62.0 16.2 %all-to-all-start = ((bf16[8,32,640]{2,1,0:T(8,128)(2,1)}), bf16[8,32,640]{2,1,0:T(8,128)(2,1)}, u32[]{:S(2)}, u32[]{:S(2)}) async-start(bf16[8,32,640]{2,1,0:T(8,128)(2,1)} %bitcast.174), calls=%async_computation | async-start | bytes 655360 | tf_op jit(solution)/shard_map/all_to_all | solution.py:238
  76.9 10.4 %copy-start.2 = (bf16[128,4096]{1,0:T(8,128)(2,1)S(1)}, bf16[128,4096]{1,0:T(8,128)(2,1)}, u32[]{:S(2)}) copy-start(bf16[128,4096]{1,0:T(8,128)(2,1)} %all-gather.2.cloned.1.call-done) | copy-start | bytes 3145732
  83.6 3.7 %copy-start.1 = (bf16[4096,4,128]{0,2,1:T(8,128)(2,1)S(1)}, bf16[4096,4,128]{0,2,1:T(8,128)(2,1)}, u32[]{:S(2)}) copy-start(bf16[4096,4,128]{0,2,1:T(8,128)(2,1)} %copy.136) | copy-start | bytes 12582916
  83.6 3.7 %copy-start.26 = (f32[128]{0:T(128)S(1)}, f32[128]{0:T(128)}, u32[]{:S(2)}) copy-start(f32[128]{0:T(128)} %copy-done.25) | copy-start | bytes 1540
  85.8 2.9 %copy-start.13 = (f32[128,64]{0,1:T(8,128)S(1)}, f32[128,64]{0,1:T(8,128)}, u32[]{:S(2)}) copy-start(f32[128,64]{0,1:T(8,128)} %copy-done.12) | copy-start | bytes 98308
  85.8 12.0 %collective-permute-start.2 = (f32[4,32,1024]{2,1,0:T(8,128)S(1)}, f32[4,32,1024]{2,1,0:T(8,128)S(1)}, u32[]{:S(2)}, u32[]{:S(2)}) collective-permute-start(f32[4,32,1024]{2,1,0:T(8,128)S(1)} %select_bitcast_fusion), channel_id=1, source_target_pairs={{0,2},{2,0},{4,6},{6,4},{8,10},{10,8},{12,14},{14,12},{1,3},{3,1},... | collective-permute-start | bytes 1572872 | tf_op jit(solution)/shard_map/ppermute | solution.py:23
  87.3 12.4 %copy-start.17 = (s32[256]{0:T(256)S(1)}, s32[256]{0:T(256)}, u32[]{:S(2)}) copy-start(s32[256]{0:T(256)} %param.27) | copy-start | bytes 3076
  87.3 12.4 %copy-start.21 = (s32[256]{0:T(256)S(1)}, s32[256]{0:T(256)}, u32[]{:S(2)}) copy-start(s32[256]{0:T(256)} %add.227) | copy-start | bytes 3076
  87.4 12.4 %copy-start.33 = (pred[256]{0:T(512)(128)(4,1)S(1)}, pred[256]{0:T(512)(128)(4,1)}, u32[]{:S(2)}) copy-start(pred[256]{0:T(512)(128)(4,1)} %eq.226) | copy-start | bytes 772
  97.9 6.4 %collective-permute-start.3 = (f32[2,32,1024]{2,1,0:T(8,128)S(1)}, f32[2,32,1024]{2,1,0:T(8,128)S(1)}, u32[]{:S(2)}, u32[]{:S(2)}) collective-permute-start(f32[2,32,1024]{2,1,0:T(8,128)S(1)} %select_bitcast_fusion.1), channel_id=1, source_target_pairs={{0,4},{2,6},{4,0},{6,2},{8,12},{10,14},{12,8},{14,10},{1,5},{3,7},... | collective-permute-start | bytes 786440 | tf_op jit(solution)/shard_map/ppermute | solution.py:23
  104.5 7.5 %collective-permute-start.4 = (f32[1,32,1024]{2,1,0:T(8,128)S(1)}, f32[1,32,1024]{2,1,0:T(8,128)S(1)}, u32[]{:S(2)}, u32[]{:S(2)}) collective-permute-start(f32[1,32,1024]{2,1,0:T(8,128)S(1)} %select_bitcast_fusion.3), channel_id=1, source_target_pairs={{0,8},{2,10},{4,12},{6,14},{8,0},{10,2},{12,4},{14,6},{1,9},{3,11}... | collective-permute-start | bytes 393224 | tf_op jit(solution)/shard_map/ppermute | solution.py:23
  112.0 1.5 collective-permute-start.5
  113.6 6.0 %copy-start.5 = (bf16[1,2,32,1024]{3,2,1,0:T(8,128)(2,1)}, bf16[1,2,32,1024]{3,2,1,0:T(8,128)(2,1)S(1)}, u32[]{:S(2)}) copy-start(bf16[1,2,32,1024]{3,2,1,0:T(8,128)(2,1)S(1)} %maximum_select_fusion.5) | copy-start | bytes 393220
  113.6 6.0 %collective-permute-start.6 = (bf16[1,2,32,1024]{3,2,1,0:T(8,128)(2,1)S(1)}, bf16[1,2,32,1024]{3,2,1,0:T(8,128)(2,1)S(1)}, u32[]{:S(2)}, u32[]{:S(2)}) collective-permute-start(bf16[1,2,32,1024]{3,2,1,0:T(8,128)(2,1)S(1)} %maximum_select_fusion.5), channel_id=1, source_target_pairs={{0,16},{16,0},{1,17},{17,1},{2,18},{18,2},{3,19},{19,3},{4,20},{20... | collective-permute-start | bytes 393224 | tf_op jit(solution)/shard_map/ppermute | solution.py:23
  119.5 0.6 copy-start.9
  121.1 5.1 %copy-start.20 = (bf16[128,32]{0,1:T(8,128)(2,1)S(1)}, bf16[128,32]{0,1:T(8,128)(2,1)}, u32[]{:S(2)}) copy-start(bf16[128,32]{0,1:T(8,128)(2,1)} %get-tuple-element.38) | copy-start | bytes 24580
  121.1 5.4 %copy-start.7 = (bf16[128,4,128]{0,2,1:T(8,128)(2,1)S(1)}, bf16[128,4,128]{0,2,1:T(8,128)(2,1)}, u32[]{:S(2)}) copy-start(bf16[128,4,128]{0,2,1:T(8,128)(2,1)} %fusion.57) | copy-start | bytes 393220
  121.1 5.4 %copy-start.32 = (pred[128]{0:T(512)(128)(4,1)S(1)}, pred[128]{0:T(512)(128)(4,1)}, u32[]{:S(2)}) copy-start(pred[128]{0:T(512)(128)(4,1)} %broadcast_compare_fusion.2) | copy-start | bytes 388
  121.1 7.1 %copy-start.15 = (s32[8]{0:T(128)S(1)}, s32[8]{0:T(128)}, u32[]{:S(2)}) copy-start(s32[8]{0:T(128)} %param.28) | copy-start | bytes 100
  122.5 3.5 %copy-start.23 = (f32[32]{0:T(128)}, f32[32]{0:T(128)S(1)}, u32[]{:S(2)}) copy-start(f32[32]{0:T(128)S(1)} %add_rsqrt_fusion) | copy-start | bytes 388
  126.5 8.8 %collective-permute-start.7 = (bf16[1,128,4,128]{1,3,2,0:T(8,128)(2,1)S(1)}, bf16[1,128,4,128]{1,3,2,0:T(8,128)(2,1)S(1)}, u32[]{:S(2)}, u32[]{:S(2)}) collective-permute-start(bf16[1,128,4,128]{1,3,2,0:T(8,128)(2,1)S(1)} %select_bitcast_fusion.2), channel_id=1, source_target_pairs={{0,8},{2,10},{4,12},{6,14},{8,0},{10,2},{12,4},{14,6},{1,9},{3,11}... | collective-permute-start | bytes 393224 | tf_op jit(solution)/shard_map/ppermute | solution.py:23
  135.4 7.6 %collective-permute-start.8 = (bf16[2,128,4,128]{1,3,2,0:T(8,128)(2,1)S(1)}, bf16[2,128,4,128]{1,3,2,0:T(8,128)(2,1)S(1)}, u32[]{:S(2)}, u32[]{:S(2)}) collective-permute-start(bf16[2,128,4,128]{1,3,2,0:T(8,128)(2,1)S(1)} %maximum_select_fusion.4), channel_id=1, source_target_pairs={{0,4},{2,6},{4,0},{6,2},{8,12},{10,14},{12,8},{14,10},{1,5},{3,7},... | collective-permute-start | bytes 786440 | tf_op jit(solution)/shard_map/ppermute | solution.py:23
  143.0 17.3 %copy-start.28 = (pred[8]{0:T(512)(128)(4,1)S(1)}, pred[8]{0:T(512)(128)(4,1)}, u32[]{:S(2)}) copy-start(pred[8]{0:T(512)(128)(4,1)} %copy-done.27) | copy-start | bytes 28
  143.1 17.5 %copy-start.29 = (s32[128]{0:T(128)S(1)}, s32[128]{0:T(128)}, u32[]{:S(2)}) copy-start(s32[128]{0:T(128)} %get-tuple-element.22) | copy-start | bytes 1540
  143.1 18.5 %copy-start.24 = (f32[32]{0:T(128)S(1)}, f32[32]{0:T(128)}, u32[]{:S(2)}) copy-start(f32[32]{0:T(128)} %copy-done.23) | copy-start | bytes 388
  143.1 12.4 %collective-permute-start.9 = (bf16[4,128,4,128]{1,3,2,0:T(8,128)(2,1)S(1)}, bf16[4,128,4,128]{1,3,2,0:T(8,128)(2,1)S(1)}, u32[]{:S(2)}, u32[]{:S(2)}) collective-permute-start(bf16[4,128,4,128]{1,3,2,0:T(8,128)(2,1)S(1)} %maximum_select_fusion.1), channel_id=1, source_target_pairs={{0,2},{2,0},{4,6},{6,4},{8,10},{10,8},{12,14},{14,12},{1,3},{3,1},... | collective-permute-start | bytes 1572872 | tf_op jit(solution)/shard_map/ppermute | solution.py:23
  160.3 8.0 %collective-permute-start.10 = (bf16[1024,4,128]{0,2,1:T(8,128)(2,1)}, bf16[1024,4,128]{0,2,1:T(8,128)(2,1)}, u32[]{:S(2)}, u32[]{:S(2)}) collective-permute-start(bf16[1024,4,128]{0,2,1:T(8,128)(2,1)} %reshape_reshape.2), channel_id=1, source_target_pairs={{0,1},{1,0},{2,3},{3,2},{4,5},{5,4},{6,7},{7,6},{8,9},{9,8},{10,11... | collective-permute-start | bytes 3145736 | tf_op jit(solution)/shard_map/ppermute | solution.py:23
  168.3 7.8 %copy-start.6 = (bf16[1024,4,128]{0,2,1:T(8,128)(2,1)S(1)}, bf16[1024,4,128]{0,2,1:T(8,128)(2,1)}, u32[]{:S(2)}) copy-start(bf16[1024,4,128]{0,2,1:T(8,128)(2,1)} %reshape_reshape.2) | copy-start | bytes 3145732
  172.9 3.5 %copy-start.4 = (f32[4,1024,128,2]{2,1,3,0:T(8,128)S(1)}, f32[4,1024,128,2]{2,1,3,0:T(8,128)}, u32[]{:S(2)}) copy-start(f32[4,1024,128,2]{2,1,3,0:T(8,128)} %get-tuple-element.40) | copy-start | bytes 12582916
  172.9 3.5 %copy-start.8 = (pred[128,1024]{0,1:T(8,128)(4,1)S(1)}, pred[128,1024]{0,1:T(8,128)(4,1)}, u32[]{:S(2)}) copy-start(pred[128,1024]{0,1:T(8,128)(4,1)} %compare_and_fusion) | copy-start | bytes 393220
Sparse Core Ops, SparseCore 0:
  14.2 19.0 all-gather.1

commit v6 on v3

--- a/solution.py
+++ b/solution.py
@@ -80,6 +80,24 @@
         remaining //= 2
         bit += 1
     return blocks[0]
+
+
+def doubling_gather(block, axis, index, count, bits):
+    have = block[None]
+    for bit in bits:
+        arrived = swapped(have, axis, bit)
+        mine = (index >> bit) & 1
+        have = jnp.where(
+            mine == 0,
+            jnp.concatenate([have, arrived], axis=0),
+            jnp.concatenate([arrived, have], axis=0),
+        )
+    order = list(bits)
+    have = have.reshape((2,) * len(order) + block.shape)
+    by_bit = {bit: len(order) - 1 - place for place, bit in enumerate(order)}
+    wanted = [by_bit[bit] for bit in sorted(order, reverse=True)]
+    have = jnp.transpose(have, wanted + list(range(len(order), have.ndim)))
+    return have.reshape((count,) + block.shape)
 
 
 def rotate_rows(values, positions):
@@ -188,7 +206,6 @@
     own_positions = row_positions(
         ctx_index * TOK + jnp.arange(TOK, dtype=jnp.int32), slice_order, TOK
     )
-    own_doc = jnp.take(doc_ids, own_positions)
     kv_heads = w_query.shape[1]
     groups = w_query.shape[2]
     queries = jnp.einsum(
@@ -201,13 +218,24 @@
     own_half = jnp.where(
         tp_index == 0, rotate(projected_half, own_positions), projected_half
     ).astype(jnp.bfloat16)
-    gathered = lax.all_gather(own_half, "ctx", axis=0, tiled=True)
+    ctx_bits = list(range(shards.bit_length() - 1))[::-1]
+    gathered = doubling_gather(own_half, "ctx", ctx_index, shards, ctx_bits).reshape(
+        (shards * TOK,) + own_half.shape[1:]
+    )
     partner_all = swapped(gathered, "tp", 0)
     keys_every = jnp.where(tp_index == 0, gathered, partner_all)
     values_every = jnp.where(tp_index == 0, partner_all, gathered)
     key_count = keys_every.shape[0]
     key_pos = row_positions(jnp.arange(key_count, dtype=jnp.int32), slice_order, TOK)
-    key_doc = jnp.take(doc_ids, key_pos)
+    doc_slices = doc_ids.reshape(2 * shards, TOK // 2)
+    slice_ids = jnp.stack([slice_order, 2 * shards - 1 - slice_order], axis=1)
+    slice_hot = slice_ids[:, :, None] == jnp.arange(2 * shards, dtype=jnp.int32)[None, None, :]
+    key_doc = jnp.sum(
+        jnp.where(slice_hot[..., None], doc_slices[None, None], 0), axis=2
+    ).reshape(shards * TOK)
+    own_doc = jnp.sum(
+        jnp.where((shard_ids == ctx_index)[:, None], key_doc.reshape(shards, TOK), 0), axis=0
+    )
     allowed_now = (key_pos[None, :] <= own_positions[:, None]) & (
         key_doc[None, :] == own_doc[:, None]
     )

time: 166 us -> 175 us (1.054)
  waiting for transfers between devices: 60.1 us -> 66.7 us
  starting transfers between devices: 14.8 us -> 19.3 us
  local copies, waits for them, and re-layouts: 42.6 us -> 38.2 us
  other arithmetic: 14.5 us -> 16.8 us
    ppermute x6 -> x9, waiting for transfers between devices: 34.7 us -> 47.7 us  [swapped(): lax.ppermute(value, axis, [(i, i ^ 1 << stride) for i in range(lax.axis_s...]
    gather x2 -> x0, local copies, waits for them, and re-layouts: 9.79 us -> none  [the longest x1 8.81 us: local(): key_doc = jnp.take(doc_ids, key_pos)]
    all_gather x1 -> x0, waiting for transfers between devices: 7.46 us -> none  [local(): gathered = lax.all_gather(own_half, 'ctx', axis=0, tiled=True)]
    ppermute x6 -> x9, starting transfers between devices: 8.44 us -> 13 us  [swapped(): lax.ppermute(value, axis, [(i, i ^ 1 << stride) for i in range(lax.axis_s...]
    another operation x0 -> x2, local copies, waits for them, and re-layouts: none -> 2.65 us  [the longest x1 2.57 us: local(): doubling_gather(own_half, 'ctx', ctx_index, shards, ctx_bits)]
    transpose x0 -> x1, local copies, waits for them, and re-layouts: none -> 2.06 us  [doubling_gather(): have = jnp.transpose(have, wanted + list(range(len(order), have.ndim)))]
    unnamed x41 -> x37, local copies, waits for them, and re-layouts: 22.6 us -> 22 us
  transfers between devices with their start and end apart: 9 -> 11, of which waited for: 8 -> 9; matrix products, arithmetic and copies ran while one was open for 31% -> 24% of each run, Pallas kernels for 0% -> 0%
where the time goes in v6:
time: 175 us; the launch traced here: 174 us
  waiting for transfers between devices  66.7 us (38%)
  local copies, waits for them, and re-layouts  38.2 us (22%)
  matrix products  19.3 us (11%)
  starting transfers between devices  19.3 us (11%)
  other arithmetic  16.8 us (10%)
  between operations  13.8 us (8%)
    ppermute x9, waiting for transfers between devices, swapped(): lax.ppermute(value, axis, [(i, i ^ 1 << stride) for i in range(lax.axis_s...  47.7 us
    unnamed x37, local copies, waits for them, and re-layouts  22 us
    ppermute x9, starting transfers between devices, swapped(): lax.ppermute(value, axis, [(i, i ^ 1 << stride) for i in range(lax.axis_s...  13 us
    unnamed x3, matrix products  11.6 us
    all_gather x1, waiting for transfers between devices, local(): full_rows = lax.all_gather(embeds, ('vis', 'tp'), axis=1, tiled=True)  9.7 us
    all_to_all x1, waiting for transfers between devices, local(): lax.all_to_all(blocks, 'ctx', split_axis=0, concat_axis=0, tiled=True)  9.31 us
    squeeze x1, local copies, waits for them, and re-layouts, local(): w_keyval[0]  7.59 us
    all_to_all x1, starting transfers between devices, local(): lax.all_to_all(blocks, 'ctx', split_axis=0, concat_axis=0, tiled=True)  6.08 us
  transfers between devices with their start and end apart: 11, of which 9 were waited for; matrix products, arithmetic and copies ran while one was open for 24% of the time, Pallas kernels for 0%

profile of v6, /device:TPU:0, one launch (start us, length us, event | category | flops | bytes accessed | tf_op | source)
XLA Modules:
  0.0 174.0 jit_solution(5768139941257901455)
XLA Ops:
  6.5 1.2 convert_reduce_fusion
  7.8 1.2 fusion.41
  9.0 1.9 %fusion.47 = f32[128,960]{0,1:S(1)} fusion(bf16[1280,960]{0,1:T(8,128)(2,1)S(1)} %bitcast.158, bf16[128,1280]{1,0:T(8,128)(2,1)} %param.17, f32[1280]{0:T(1024)} %param.19, f32[1280]{0:T(1024)} %param.18, f32[128]{0:T(128)S(1)} %add_rsqrt_fusion.2, f32[128]{0:T(128)S(1)} %broadcast_multiply_fusion.1), kind=kOutput, calls=%fused_computation.56 | convolution fusion | flops 315555840 | bytes 3288064
  11.1 0.3 fusion.110
  11.5 0.3 copy-done.5
  11.7 0.4 copy-done.3
  12.1 1.8 %convolution_bitcast_fusion = f32[128,1280]{1,0:T(8,128)S(1)} fusion(bf16[4,80,1280]{2,1,0:T(8,128)(2,1)} %param.21, f32[4,128,128]{1,2,0:T(8,128)} %copy-done.3, f32[4,128]{1,0:T(4,128)S(1)} %get-tuple-element.19, bf16[128,3,4,80]{0,3,2,1:T(8,128)(2,1)} %copy-done.5, f32[128,4]{0,1:T(4,128)S(1)} %bitcast.173), kind=kOutput, calls=%fused_computation.8 | convolution fusion | flops 115556352 | bytes 1822720 | tf_op jit(solution)/shard_map/phd,hdf->pf/dot_general | solution.py:159
  13.9 0.6 collective-permute-start
  14.7 0.7 fusion.66
  15.4 1.0 collective-permute-done
  16.3 1.2 add.215
  17.5 2.9 %collective-permute-start.1 = (f32[128,1280]{1,0:T(8,128)S(1)}, f32[128,1280]{1,0:T(8,128)S(1)}, u32[]{:S(2)}, u32[]{:S(2)}) collective-permute-start(f32[128,1280]{1,0:T(8,128)S(1)} %add.215), channel_id=1, source_target_pairs={{0,16},{16,0},{1,17},{17,1},{2,18},{18,2},{3,19},{19,3},{4,20},{20... | collective-permute-start | bytes 1966088 | tf_op jit(solution)/shard_map/ppermute | solution.py:23
  20.4 0.7 fusion.108
  21.2 0.1 select_reduce_fusion.3
  21.3 14.2 %collective-permute-done.1 = f32[128,1280]{1,0:T(8,128)S(1)} collective-permute-done((f32[128,1280]{1,0:T(8,128)S(1)}, f32[128,1280]{1,0:T(8,128)S(1)}, u32[]{:S(2)}, u32[]{:S(2)}) %collective-permute-start.1) | collective-permute-done | bytes 655392 | tf_op jit(solution)/shard_map/ppermute | solution.py:23
  35.5 0.2 fusion.107
  35.6 0.2 multiply_reduce_fusion
  35.9 0.2 add_convert_fusion
  36.1 0.2 reshape.554
  36.3 0.2 convolution_convert_fusion
  36.5 0.7 copy.144
  37.2 6.1 %all-to-all-start = ((bf16[8,32,640]{2,1,0:T(8,128)(2,1)}), bf16[8,32,640]{2,1,0:T(8,128)(2,1)S(1)}, u32[]{:S(2)}, u32[]{:S(2)}) async-start(bf16[8,32,640]{2,1,0:T(8,128)(2,1)} %bitcast.156), calls=%async_computation | async-start | bytes 655360 | tf_op jit(solution)/shard_map/all_to_all | solution.py:180
  43.3 0.2 all-gather.2.cloned.1.call-start
  43.7 9.3 %all-to-all-done = bf16[8,32,640]{2,1,0:T(8,128)(2,1)S(1)} async-done(((bf16[8,32,640]{2,1,0:T(8,128)(2,1)}), bf16[8,32,640]{2,1,0:T(8,128)(2,1)S(1)}, u32[]{:S(2)}, u32[]{:S(2)}) %all-to-all-start) | async-done | bytes 327712 | tf_op jit(solution)/shard_map/all_to_all | solution.py:180
  53.1 0.1 copy.145
  53.4 1.9 %fusion.12 = f32[4,2,32,1024]{3,2,1,0:T(8,128)S(1)} fusion(bf16[4,2,32,640]{3,2,1,0:T(8,128)(2,1)S(1)} %dot_general.46, bf16[640,1024]{1,0:T(8,128)(2,1)} %param.24), kind=kOutput, calls=%fused_computation.17 | convolution fusion | flops 335544320 | bytes 2686976 | tf_op jit(solution)/shard_map/dot_general | solution.py:184
  55.4 1.6 collective-permute-start.2
  57.1 9.4 %collective-permute-done.2 = f32[4,32,1024]{2,1,0:T(8,128)S(1)} collective-permute-done((f32[4,32,1024]{2,1,0:T(8,128)S(1)}, f32[4,32,1024]{2,1,0:T(8,128)S(1)}, u32[]{:S(2)}, u32[]{:S(2)}) %collective-permute-start.2) | collective-permute-done | bytes 524320 | tf_op jit(solution)/shard_map/ppermute | solution.py:23
  66.5 0.1 fusion.46
  66.6 0.7 select_bitcast_fusion.1
  67.3 0.7 collective-permute-start.3
  68.2 0.3 fusion.109
  68.5 5.5 %collective-permute-done.3 = f32[2,32,1024]{2,1,0:T(8,128)} collective-permute-done((f32[2,32,1024]{2,1,0:T(8,128)}, f32[2,32,1024]{2,1,0:T(8,128)}, u32[]{:S(2)}, u32[]{:S(2)}) %collective-permute-start.3) | collective-permute-done | bytes 262176 | tf_op jit(solution)/shard_map/ppermute | solution.py:23
  74.0 1.0 fusion.63
  75.0 2.7 %collective-permute-start.4 = (f32[1,32,1024]{2,1,0:T(8,128)S(1)}, f32[1,32,1024]{2,1,0:T(8,128)S(1)}, u32[]{:S(2)}, u32[]{:S(2)}) collective-permute-start(f32[1,32,1024]{2,1,0:T(8,128)S(1)} %select_bitcast_fusion.2), channel_id=1, source_target_pairs={{0,8},{2,10},{4,12},{6,14},{8,0},{10,2},{12,4},{14,6},{1,9},{3,11}... | collective-permute-start | bytes 393224 | tf_op jit(solution)/shard_map/ppermute | solution.py:23
  77.7 4.6 %collective-permute-done.4 = f32[1,32,1024]{2,1,0:T(8,128)S(1)} collective-permute-done((f32[1,32,1024]{2,1,0:T(8,128)S(1)}, f32[1,32,1024]{2,1,0:T(8,128)S(1)}, u32[]{:S(2)}, u32[]{:S(2)}) %collective-permute-start.4) | collective-permute-done | bytes 131104 | tf_op jit(solution)/shard_map/ppermute | solution.py:23
  82.3 1.0 fusion.18
  83.3 7.6 %copy.123 = bf16[4096,4,128]{0,2,1:T(8,128)(2,1)} copy(bf16[4096,4,128]{2,1,0:T(4,128)(2,1)} %bitcast.163) | data formatting | bytes 8388608 | tf_op jit(solution)/shard_map/squeeze | solution.py:216
  91.1 0.5 fusion.105
  91.6 0.2 multiply_cosine_fusion
  91.8 9.7 %all-gather.2.cloned.1.call-done = bf16[128,4096]{1,0:T(8,128)(2,1)} async-done(((bf16[128,1024]{1,0:T(8,128)(2,1)}), bf16[128,4096]{1,0:T(8,128)(2,1)}) %all-gather.2.cloned.1.call-update) | async-done | bytes 1048592 | tf_op jit(solution)/shard_map/all_gather | solution.py:199
  101.5 1.5 fusion.3
  103.1 3.8 %fusion.55 = f32[128,512]{0,1:S(1)} fusion(bf16[4096,512]{0,1:T(8,128)(2,1)} %bitcast.164, bf16[128,4096]{1,0:T(8,128)(2,1)} %all-gather.2.cloned.1.call-done, f32[4096]{0:T(1024)S(1)} %copy-done.9, f32[128]{0:T(128)S(1)} %add_rsqrt_fusion), kind=kOutput, calls=%fused_computation.64 | convolution fusion | flops 538968064 | bytes 5521920
  107.0 2.5 %collective-permute-start.5 = (bf16[1,128,4,128]{1,3,2,0:T(8,128)(2,1)S(1)}, bf16[1,128,4,128]{1,3,2,0:T(8,128)(2,1)S(1)}, u32[]{:S(2)}, u32[]{:S(2)}) collective-permute-start(bf16[1,128,4,128]{1,3,2,0:T(8,128)(2,1)S(1)} %fusion.69), channel_id=1, source_target_pairs={{0,8},{2,10},{4,12},{6,14},{8,0},{10,2},{12,4},{14,6},{1,9},{3,11}... | collective-permute-start | bytes 393224 | tf_op jit(solution)/shard_map/ppermute | solution.py:23
  109.6 6.8 %collective-permute-done.5 = bf16[1,128,4,128]{1,3,2,0:T(8,128)(2,1)S(1)} collective-permute-done((bf16[1,128,4,128]{1,3,2,0:T(8,128)(2,1)S(1)}, bf16[1,128,4,128]{1,3,2,0:T(8,128)(2,1)S(1)}, u32[]{:S(2)}, u32[]{:S(2)}) %collective-permute-start.5) | collective-permute-done | bytes 131104 | tf_op jit(solution)/shard_map/ppermute | solution.py:23
  116.4 0.6 collective-permute-start.6
  117.0 0.1 select_reduce_fusion
  117.2 0.7 eq.193
  117.9 6.2 %collective-permute-done.6 = bf16[2,128,4,128]{1,3,2,0:T(8,128)(2,1)S(1)} collective-permute-done((bf16[2,128,4,128]{1,3,2,0:T(8,128)(2,1)S(1)}, bf16[2,128,4,128]{1,3,2,0:T(8,128)(2,1)S(1)}, u32[]{:S(2)}, u32[]{:S(2)}) %collective-permute-start.6) | collective-permute-done | bytes 262176 | tf_op jit(solution)/shard_map/ppermute | solution.py:23
  124.1 0.9 maximum_select_fusion.1
  124.9 1.5 collective-permute-start.7
  126.5 0.6 eq.197
  127.1 21.3 %copy.125 = bf16[4096,4,2,128]{0,3,2,1:T(8,128)(2,1)} copy(bf16[4096,4,2,128]{3,2,1,0:T(2,128)(2,1)} %param.32) | data formatting | bytes 16777216 | tf_op args[15]
  148.4 0.8 select_reduce_fusion.1
  149.2 0.6 fusion.91
  149.8 1.7 maximum_select_fusion
  151.5 2.1 %copy.124 = bf16[2,2,2,128,4,128]{3,2,1,0,5,4:T(2,128)(2,1)} copy(bf16[2,2,2,128,4,128]{3,5,4,0,1,2:T(8,128)(2,1)S(1)} %bitcast.162) | data formatting | bytes 2097152 | tf_op jit(solution)/shard_map/transpose | solution.py:99
  153.5 2.6 %reshape_reshape.2 = bf16[1024,4,128]{0,2,1:T(8,128)(2,1)} reshape(bf16[2,2,2,128,4,128]{3,2,1,0,5,4:T(2,128)(2,1)} %copy.124) | data formatting | bytes 2097152 | tf_op jit(solution)/shard_map/reshape;reshape | solution.py:222
  156.1 1.0 compare_and_fusion
  157.2 5.9 %fusion.53 = f32[128,1024]{0,1:S(1)} fusion(bf16[4096,1024]{0,1:T(8,128)(2,1)} %bitcast.159, bf16[128,4096]{1,0:T(8,128)(2,1)S(1)} %copy-done.1, f32[4096]{0:T(1024)S(1)} %copy-done.9, f32[128]{0:T(128)} %copy-done.15), kind=kOutput, calls=%fused_computation.63 | convolution fusion | flops 1075838976 | bytes 9978368
  163.2 1.0 fusion.2
  164.2 0.9 fusion
  165.1 1.2 fusion.34
  166.3 0.9 copy.129
  (80 shorter events, 1.8 us)
Async XLA Ops:
  6.5 2.5 %copy-start = (bf16[1280,3,4,80]{0,3,2,1:T(8,128)(2,1)S(1)}, bf16[1280,3,4,80]{0,3,2,1:T(8,128)(2,1)}, u32[]{:S(2)}) copy-start(bf16[1280,3,4,80]{0,3,2,1:T(8,128)(2,1)} %param.20) | copy-start | bytes 7372804
  6.5 4.5 %copy-start.16 = (s32[128]{0:T(128)S(1)}, s32[128]{0:T(128)}, u32[]{:S(2)}) copy-start(s32[128]{0:T(128)} %param.26) | copy-start | bytes 1540
  6.5 7.9 %copy-start.14 = (s32[256]{0:T(256)S(1)}, s32[256]{0:T(256)}, u32[]{:S(2)}) copy-start(s32[256]{0:T(256)} %param.27) | copy-start | bytes 3076
  6.5 8.1 %copy-start.10 = (s32[8]{0:T(128)S(1)}, s32[8]{0:T(128)}, u32[]{:S(2)}) copy-start(s32[8]{0:T(128)} %param.28) | copy-start | bytes 100
  9.0 26.4 %copy-start.2 = (bf16[128,1280]{1,0:T(8,128)(2,1)S(1)}, bf16[128,1280]{1,0:T(8,128)(2,1)}, u32[]{:S(2)}) copy-start(bf16[128,1280]{1,0:T(8,128)(2,1)} %param.17) | copy-start | bytes 983044
  11.0 24.9 %copy-start.11 = (f32[1280]{0:T(1024)S(1)}, f32[1280]{0:T(1024)}, u32[]{:S(2)}) copy-start(f32[1280]{0:T(1024)} %param.23) | copy-start | bytes 15364
  11.0 24.9 %copy-start.12 = (f32[1280]{0:T(1024)S(1)}, f32[1280]{0:T(1024)}, u32[]{:S(2)}) copy-start(f32[1280]{0:T(1024)} %param.22) | copy-start | bytes 15364
  11.0 0.7 copy-start.5
  11.4 0.7 copy-start.3
  13.9 2.4 %collective-permute-start = (f32[128,1280]{1,0:T(8,128)S(1)}, f32[128,1280]{1,0:T(8,128)}, u32[]{:S(2)}, u32[]{:S(2)}) collective-permute-start(f32[128,1280]{1,0:T(8,128)S(1)} %convolution_bitcast_fusion), channel_id=1, source_target_pairs={{0,1},{1,0},{2,3},{3,2},{4,5},{5,4},{6,7},{7,6},{8,9},{9,8},{10,11... | collective-permute-start | bytes 1966088 | tf_op jit(solution)/shard_map/ppermute | solution.py:23
  15.4 28.3 %copy-start.17 = (s32[8,2]{0,1:T(2,128)S(1)}, s32[8,2]{0,1:T(2,128)}, u32[]{:S(2)}) copy-start(s32[8,2]{0,1:T(2,128)} %param.25) | copy-start | bytes 196
  17.5 17.9 %collective-permute-start.1 = (f32[128,1280]{1,0:T(8,128)S(1)}, f32[128,1280]{1,0:T(8,128)S(1)}, u32[]{:S(2)}, u32[]{:S(2)}) collective-permute-start(f32[128,1280]{1,0:T(8,128)S(1)} %add.215), channel_id=1, source_target_pairs={{0,16},{16,0},{1,17},{17,1},{2,18},{18,2},{3,19},{19,3},{4,20},{20... | collective-permute-start | bytes 1966088 | tf_op jit(solution)/shard_map/ppermute | solution.py:23
  37.2 15.8 %all-to-all-start = ((bf16[8,32,640]{2,1,0:T(8,128)(2,1)}), bf16[8,32,640]{2,1,0:T(8,128)(2,1)S(1)}, u32[]{:S(2)}, u32[]{:S(2)}) async-start(bf16[8,32,640]{2,1,0:T(8,128)(2,1)} %bitcast.156), calls=%async_computation | async-start | bytes 655360 | tf_op jit(solution)/shard_map/all_to_all | solution.py:180
  43.3 58.2 %all-gather.2.cloned.1.call-start = ((), (), s32[]{:S(2)}) async-start(), calls=%async_computation.1 | async-start | bytes 1310720 | tf_op jit(solution)/shard_map/all_gather | solution.py:199
  53.3 29.0 %copy-start.8 = (bf16[128,1024]{1,0:T(8,128)(2,1)S(1)}, bf16[128,1024]{1,0:T(8,128)(2,1)}, u32[]{:S(2)}) copy-start(bf16[128,1024]{1,0:T(8,128)(2,1)} %param.30) | copy-start | bytes 786436
  55.4 11.1 %collective-permute-start.2 = (f32[4,32,1024]{2,1,0:T(8,128)S(1)}, f32[4,32,1024]{2,1,0:T(8,128)S(1)}, u32[]{:S(2)}, u32[]{:S(2)}) collective-permute-start(f32[4,32,1024]{2,1,0:T(8,128)S(1)} %select_bitcast_fusion), channel_id=1, source_target_pairs={{0,2},{2,0},{4,6},{6,4},{8,10},{10,8},{12,14},{14,12},{1,3},{3,1},... | collective-permute-start | bytes 1572872 | tf_op jit(solution)/shard_map/ppermute | solution.py:23
  67.3 6.7 %collective-permute-start.3 = (f32[2,32,1024]{2,1,0:T(8,128)}, f32[2,32,1024]{2,1,0:T(8,128)}, u32[]{:S(2)}, u32[]{:S(2)}) collective-permute-start(f32[2,32,1024]{2,1,0:T(8,128)} %select_bitcast_fusion.1), channel_id=1, source_target_pairs={{0,4},{2,6},{4,0},{6,2},{8,12},{10,14},{12,8},{14,10},{1,5},{3,7},... | collective-permute-start | bytes 786440 | tf_op jit(solution)/shard_map/ppermute | solution.py:23
  75.0 7.3 %collective-permute-start.4 = (f32[1,32,1024]{2,1,0:T(8,128)S(1)}, f32[1,32,1024]{2,1,0:T(8,128)S(1)}, u32[]{:S(2)}, u32[]{:S(2)}) collective-permute-start(f32[1,32,1024]{2,1,0:T(8,128)S(1)} %select_bitcast_fusion.2), channel_id=1, source_target_pairs={{0,8},{2,10},{4,12},{6,14},{8,0},{10,2},{12,4},{14,6},{1,9},{3,11}... | collective-permute-start | bytes 393224 | tf_op jit(solution)/shard_map/ppermute | solution.py:23
  83.3 19.7 %copy-start.9 = (f32[4096]{0:T(1024)S(1)}, f32[4096]{0:T(1024)}, u32[]{:S(2)}) copy-start(f32[4096]{0:T(1024)} %param.31) | copy-start | bytes 49156
  90.9 18.5 %copy-start.13 = (s32[1024]{0:T(1024)S(1)}, s32[1024]{0:T(1024)}, u32[]{:S(2)}) copy-start(s32[1024]{0:T(1024)} %param.29) | copy-start | bytes 12292
  91.8 17.8 %copy-start.6 = (f32[128,64]{0,1:T(8,128)}, f32[128,64]{0,1:T(8,128)S(1)}, u32[]{:S(2)}) copy-start(f32[128,64]{0,1:T(8,128)S(1)} %get-tuple-element.16) | copy-start | bytes 98308
  103.0 24.0 %copy-start.15 = (f32[128]{0:T(128)}, f32[128]{0:T(128)S(1)}, u32[]{:S(2)}) copy-start(f32[128]{0:T(128)S(1)} %add_rsqrt_fusion) | copy-start | bytes 1540
  107.0 9.4 %collective-permute-start.5 = (bf16[1,128,4,128]{1,3,2,0:T(8,128)(2,1)S(1)}, bf16[1,128,4,128]{1,3,2,0:T(8,128)(2,1)S(1)}, u32[]{:S(2)}, u32[]{:S(2)}) collective-permute-start(bf16[1,128,4,128]{1,3,2,0:T(8,128)(2,1)S(1)} %fusion.69), channel_id=1, source_target_pairs={{0,8},{2,10},{4,12},{6,14},{8,0},{10,2},{12,4},{14,6},{1,9},{3,11}... | collective-permute-start | bytes 393224 | tf_op jit(solution)/shard_map/ppermute | solution.py:23
  116.4 7.6 %collective-permute-start.6 = (bf16[2,128,4,128]{1,3,2,0:T(8,128)(2,1)S(1)}, bf16[2,128,4,128]{1,3,2,0:T(8,128)(2,1)S(1)}, u32[]{:S(2)}, u32[]{:S(2)}) collective-permute-start(bf16[2,128,4,128]{1,3,2,0:T(8,128)(2,1)S(1)} %maximum_select_fusion.3), channel_id=1, source_target_pairs={{0,4},{2,6},{4,0},{6,2},{8,12},{10,14},{12,8},{14,10},{1,5},{3,7},... | collective-permute-start | bytes 786440 | tf_op jit(solution)/shard_map/ppermute | solution.py:23
  124.9 24.9 %collective-permute-start.7 = (bf16[4,128,4,128]{1,3,2,0:T(8,128)(2,1)}, bf16[4,128,4,128]{1,3,2,0:T(8,128)(2,1)}, u32[]{:S(2)}, u32[]{:S(2)}) collective-permute-start(bf16[4,128,4,128]{1,3,2,0:T(8,128)(2,1)} %maximum_select_fusion.1), channel_id=1, source_target_pairs={{0,2},{2,0},{4,6},{6,4},{8,10},{10,8},{12,14},{14,12},{1,3},{3,1},... | collective-permute-start | bytes 1572872 | tf_op jit(solution)/shard_map/ppermute | solution.py:23
  148.4 8.8 %copy-start.1 = (bf16[128,4096]{1,0:T(8,128)(2,1)S(1)}, bf16[128,4096]{1,0:T(8,128)(2,1)}, u32[]{:S(2)}) copy-start(bf16[128,4096]{1,0:T(8,128)(2,1)} %all-gather.2.cloned.1.call-done) | copy-start | bytes 3145732
  156.1 7.0 %collective-permute-start.8 = (bf16[1024,4,128]{0,2,1:T(8,128)(2,1)}, bf16[1024,4,128]{0,2,1:T(8,128)(2,1)S(1)}, u32[]{:S(2)}, u32[]{:S(2)}) collective-permute-start(bf16[1024,4,128]{0,2,1:T(8,128)(2,1)} %reshape_reshape.2), channel_id=1, source_target_pairs={{0,1},{1,0},{2,3},{3,2},{4,5},{5,4},{6,7},{7,6},{8,9},{9,8},{10,11... | collective-permute-start | bytes 3145736 | tf_op jit(solution)/shard_map/ppermute | solution.py:23
  157.2 5.9 %copy-start.7 = (f32[128,64]{0,1:T(8,128)S(1)}, f32[128,64]{0,1:T(8,128)}, u32[]{:S(2)}) copy-start(f32[128,64]{0,1:T(8,128)} %copy-done.6) | copy-start | bytes 98308
  157.2 6.0 %copy-start.4 = (bf16[1024,4,128]{0,2,1:T(8,128)(2,1)S(1)}, bf16[1024,4,128]{0,2,1:T(8,128)(2,1)}, u32[]{:S(2)}) copy-start(bf16[1024,4,128]{0,2,1:T(8,128)(2,1)} %reshape_reshape.2) | copy-start | bytes 3145732
Sparse Core Ops, SparseCore 0:
  83.5 18.0 all-gather.1

commit v7 on v6

--- a/solution.py
+++ b/solution.py
@@ -157,6 +157,25 @@
     )
     blended = (blended / jnp.transpose(totals)[:, :, None]).astype(jnp.bfloat16)
     branch_part = jnp.einsum("phd,hdf->pf", blended, vit_out, preferred_element_type=jnp.float32)
+    own_positions = row_positions(
+        ctx_index * TOK + jnp.arange(TOK, dtype=jnp.int32), slice_order, TOK
+    )
+
+    def keyval_part(normed_part, positions):
+        projected_half = jnp.einsum(
+            "td,dhk->thk", normed_part, w_keyval[0], preferred_element_type=jnp.float32
+        )
+        return jnp.where(
+            tp_index == 0, rotate(projected_half, positions), projected_half
+        ).astype(jnp.bfloat16)
+
+    text_wide = lax.all_gather(text_rows, ("vis", "tp"), axis=1, tiled=True).astype(jnp.float32)
+    text_normed = (
+        text_wide
+        * lax.rsqrt(jnp.mean(text_wide * text_wide, axis=1, keepdims=True) + norm_eps)
+        * norm_gain
+    ).astype(jnp.bfloat16)
+    text_half = keyval_part(text_normed, own_positions)
     branch_sum = branch_part + swapped(branch_part, "tp", 0)
     branch_sum = branch_sum + swapped(branch_sum, "vis", 0)
     hidden = patch_rows.astype(jnp.float32) + branch_sum
@@ -178,6 +197,8 @@
     ordered = jnp.dot(picker, merged, preferred_element_type=jnp.float32).astype(jnp.bfloat16)
     blocks = jnp.transpose(ordered.reshape(ICAP, shards, block_feats), (1, 0, 2))
     received = lax.all_to_all(blocks, "ctx", split_axis=0, concat_axis=0, tiled=True)
+    text_half, received = lax.optimization_barrier((text_half, received))
+    text_all = lax.all_gather(text_half, "ctx", axis=0, tiled=True)
     by_dest = jnp.transpose(
         received.reshape(shards, shards, send_each, block_feats), (1, 0, 2, 3)
     ).reshape(shards * ICAP, block_feats)
@@ -185,6 +206,7 @@
     incoming = halving_scatter(partial.reshape(shards, ICAP, -1), ctx_index, shards).astype(
         jnp.bfloat16
     )
+    text_all, incoming = lax.optimization_barrier((text_all, incoming))
     mine_live = ((owner_dev == ctx_index) & is_live).reshape(-1)
     column_of = (shard_ids[:, None] * send_each + rank_in).reshape(-1)
     row_hot = (
@@ -194,7 +216,8 @@
     column_hot = (column_of[:, None] == slot_ids[None, :]).astype(jnp.bfloat16)
     placing = jnp.dot(row_hot, column_hot, preferred_element_type=jnp.float32)
     is_image = jnp.sum(placing, axis=1) > 0.5
-    image_part = jnp.dot(placing.astype(jnp.bfloat16), incoming, preferred_element_type=jnp.float32)
+    placing = placing.astype(jnp.bfloat16)
+    image_part = jnp.dot(placing, incoming, preferred_element_type=jnp.float32)
     embeds = jnp.where(is_image[:, None], image_part.astype(jnp.bfloat16), text_rows)
     full_rows = lax.all_gather(embeds, ("vis", "tp"), axis=1, tiled=True)
     widened = full_rows.astype(jnp.float32)
@@ -203,24 +226,40 @@
         * lax.rsqrt(jnp.mean(widened * widened, axis=1, keepdims=True) + norm_eps)
         * norm_gain
     ).astype(jnp.bfloat16)
-    own_positions = row_positions(
-        ctx_index * TOK + jnp.arange(TOK, dtype=jnp.int32), slice_order, TOK
-    )
     kv_heads = w_query.shape[1]
     groups = w_query.shape[2]
     queries = jnp.einsum(
         "td,dhgk->thgk", normed_rows, w_query, preferred_element_type=jnp.float32
     )
     queries = rotate(queries, own_positions).astype(jnp.bfloat16)
-    projected_half = jnp.einsum(
-        "td,dhk->thk", normed_rows, w_keyval[0], preferred_element_type=jnp.float32
-    )
-    own_half = jnp.where(
-        tp_index == 0, rotate(projected_half, own_positions), projected_half
-    ).astype(jnp.bfloat16)
+    image_normed = jnp.einsum(
+        "tq,td->qd", placing, normed_rows, preferred_element_type=jnp.float32
+    ).astype(jnp.bfloat16)
+    mine_all = (owner_dev == ctx_index).reshape(-1)
+    incoming_pos = jnp.sum(
+        jnp.where((column_of[:, None] == slot_ids[None, :]) & mine_all[:, None], image_pos[:, None], 0),
+        axis=0,
+    )
+    image_half = keyval_part(image_normed, incoming_pos)
     ctx_bits = list(range(shards.bit_length() - 1))[::-1]
-    gathered = doubling_gather(own_half, "ctx", ctx_index, shards, ctx_bits).reshape(
-        (shards * TOK,) + own_half.shape[1:]
+    image_all = doubling_gather(image_half, "ctx", ctx_index, shards, ctx_bits).reshape(
+        shards * ICAP, -1
+    )
+    slot_row = (owner_dev * TOK + local_row).reshape(-1)
+    slot_col = (owner_dev * ICAP + column_of.reshape(shards, ICAP)).reshape(-1)
+    key_rows = jnp.arange(shards * TOK, dtype=jnp.int32)
+    all_cols = jnp.arange(shards * ICAP, dtype=jnp.int32)
+    global_rows = (
+        (slot_row[None, :] == key_rows[:, None]) & is_live.reshape(-1)[None, :]
+    ).astype(jnp.bfloat16)
+    global_cols = (slot_col[:, None] == all_cols[None, :]).astype(jnp.bfloat16)
+    global_place = jnp.dot(global_rows, global_cols, preferred_element_type=jnp.float32)
+    is_image_key = jnp.sum(global_place, axis=1) > 0.5
+    placed_all = jnp.dot(
+        global_place.astype(jnp.bfloat16), image_all, preferred_element_type=jnp.float32
+    ).astype(jnp.bfloat16)
+    gathered = jnp.where(
+        is_image_key[:, None, None], placed_all.reshape(text_all.shape), text_all
     )
     partner_all = swapped(gathered, "tp", 0)
     keys_every = jnp.where(tp_index == 0, gathered, partner_all)

time: 175 us -> 195 us (1.11)
  other arithmetic: 16.8 us -> 31.6 us
  matrix products: 19.3 us -> 29 us
  waiting for transfers between devices: 66.7 us -> 58.6 us
    dot_general x1 -> x4, matrix products: 0.96 us -> 10.2 us  [the longest x1 4.26 us: keyval_part(): jnp.einsum('td,dhk->thk', normed_part, w_keyval[0], preferred_element_typ...]
    all_gather x0 -> x2, waiting for transfers between devices: none -> 8 us  [the longest x1 7.98 us: local(): text_all = lax.all_gather(text_half, 'ctx', axis=0, tiled=True)]
    ppermute x9, waiting for transfers between devices: 47.7 us -> 41.2 us  [swapped(): lax.ppermute(value, axis, [(i, i ^ 1 << stride) for i in range(lax.axis_s...]
    all_to_all x1, waiting for transfers between devices: 9.31 us -> 4.2 us  [local(): lax.all_to_all(blocks, 'ctx', split_axis=0, concat_axis=0, tiled=True)]
    all_gather x1, waiting for transfers between devices: 9.7 us -> 5.17 us  [local(): full_rows = lax.all_gather(embeds, ('vis', 'tp'), axis=1, tiled=True)]
    another operation x1 -> x0, local copies, waits for them, and re-layouts: 2.57 us -> none  [local(): doubling_gather(own_half, 'ctx', ctx_index, shards, ctx_bits)]
    reduce_sum x0 -> x2, other arithmetic: none -> 2.32 us  [the longest x1 1.52 us: local(): jnp.mean(text_wide * text_wide, axis=1, keepdims=True) + norm_eps]
    unnamed x37 -> x47, local copies, waits for them, and re-layouts: 22 us -> 22.5 us
  transfers between devices with their start and end apart: 11 -> 13, of which waited for: 9 -> 9; matrix products, arithmetic and copies ran while one was open for 24% -> 37% of each run, Pallas kernels for 0% -> 0%
where the time goes in v7:
time: 195 us; the launch traced here: 193 us
  waiting for transfers between devices  58.6 us (30%)
  local copies, waits for them, and re-layouts  39.9 us (20%)
  other arithmetic  31.6 us (16%)
  matrix products  29 us (15%)
  starting transfers between devices  20 us (10%)
  between operations  13.6 us (7%)
    ppermute x9, waiting for transfers between devices, swapped(): lax.ppermute(value, axis, [(i, i ^ 1 << stride) for i in range(lax.axis_s...  41.2 us
    unnamed x47, local copies, waits for them, and re-layouts  22.5 us
    ppermute x9, starting transfers between devices, swapped(): lax.ppermute(value, axis, [(i, i ^ 1 << stride) for i in range(lax.axis_s...  14.2 us
    unnamed x3, matrix products  11.5 us
    all_gather x1, waiting for transfers between devices, local(): text_all = lax.all_gather(text_half, 'ctx', axis=0, tiled=True)  7.98 us
    squeeze x1, local copies, waits for them, and re-layouts, keyval_part(): w_keyval[0]  7.66 us
    all_to_all x1, starting transfers between devices, local(): lax.all_to_all(blocks, 'ctx', split_axis=0, concat_axis=0, tiled=True)  5.52 us
    all_gather x1, waiting for transfers between devices, local(): full_rows = lax.all_gather(embeds, ('vis', 'tp'), axis=1, tiled=True)  5.17 us
  transfers between devices with their start and end apart: 13, of which 9 were waited for; matrix products, arithmetic and copies ran while one was open for 37% of the time, Pallas kernels for 0%

profile of v7, /device:TPU:0, one launch (start us, length us, event | category | flops | bytes accessed | tf_op | source)
XLA Modules:
  0.0 192.7 jit_solution(3794265094503153445)
XLA Ops:
  6.6 1.2 convert_reduce_fusion
  7.8 1.2 fusion.52
  9.1 1.9 fusion.62
  11.7 1.7 convolution_bitcast_fusion
  14.2 0.7 fusion.129
  15.0 0.7 fusion.83
  16.6 7.7 %copy.121 = bf16[4096,4,128]{0,2,1:T(8,128)(2,1)} copy(bf16[4096,4,128]{2,1,0:T(4,128)(2,1)} %bitcast.171) | data formatting | bytes 8388608 | tf_op jit(solution)/shard_map/squeeze | solution.py:166
  25.6 1.2 add.248
  26.8 2.6 %collective-permute-start.1 = (f32[128,1280]{1,0:T(8,128)S(1)}, f32[128,1280]{1,0:T(8,128)S(1)}, u32[]{:S(2)}, u32[]{:S(2)}) collective-permute-start(f32[128,1280]{1,0:T(8,128)S(1)} %add.248), channel_id=1, source_target_pairs={{0,16},{16,0},{1,17},{17,1},{2,18},{18,2},{3,19},{19,3},{4,20},{20... | collective-permute-start | bytes 1966088 | tf_op jit(solution)/shard_map/ppermute | solution.py:23
  30.7 15.1 %collective-permute-done.1 = f32[128,1280]{1,0:T(8,128)S(1)} collective-permute-done((f32[128,1280]{1,0:T(8,128)S(1)}, f32[128,1280]{1,0:T(8,128)S(1)}, u32[]{:S(2)}, u32[]{:S(2)}) %collective-permute-start.1) | collective-permute-done | bytes 655392 | tf_op jit(solution)/shard_map/ppermute | solution.py:23
  46.9 0.8 copy.158
  47.6 5.5 %all-to-all-start = ((bf16[8,32,640]{2,1,0:T(8,128)(2,1)}), bf16[8,32,640]{2,1,0:T(8,128)(2,1)S(1)}, u32[]{:S(2)}, u32[]{:S(2)}) async-start(bf16[8,32,640]{2,1,0:T(8,128)(2,1)} %bitcast.164), calls=%async_computation | async-start | bytes 655360 | tf_op jit(solution)/shard_map/all_to_all | solution.py:199
  53.2 1.5 fusion.4
  54.8 3.8 %fusion.26 = f32[128,512]{0,1:S(1)} fusion(bf16[4096,512]{0,1:T(8,128)(2,1)} %bitcast.167, bf16[128,4096]{1,0:T(8,128)(2,1)} %all-gather.4.cloned.1.call-done, f32[4096]{0:T(1024)S(1)} %copy-done.7, f32[128]{0:T(128)S(1)} %add_rsqrt_fusion.3), kind=kOutput, calls=%fused_computation.37 | convolution fusion | flops 538968064 | bytes 5521920
  58.7 0.7 fusion.74
  59.4 4.2 %all-to-all-done = bf16[8,32,640]{2,1,0:T(8,128)(2,1)S(1)} async-done(((bf16[8,32,640]{2,1,0:T(8,128)(2,1)}), bf16[8,32,640]{2,1,0:T(8,128)(2,1)S(1)}, u32[]{:S(2)}, u32[]{:S(2)}) %all-to-all-start) | async-done | bytes 327712 | tf_op jit(solution)/shard_map/all_to_all | solution.py:199
  63.8 0.8 dot_general.60
  64.6 2.0 %fusion.16 = f32[4,2,32,1024]{3,2,1,0:T(8,128)S(1)} fusion(bf16[4,2,32,640]{3,2,1,0:T(8,128)(2,1)} %dot_general.60, bf16[640,1024]{1,0:T(8,128)(2,1)} %param.24), kind=kOutput, calls=%fused_computation.25 | convolution fusion | flops 335544320 | bytes 2686976 | tf_op jit(solution)/shard_map/dot_general | solution.py:205
  66.6 0.9 select_bitcast_fusion
  67.4 1.5 collective-permute-start.2
  68.9 1.2 broadcast_compare_fusion.1
  70.1 1.3 broadcast_add_fusion
  71.7 8.5 %collective-permute-done.2 = f32[4,32,1024]{2,1,0:T(8,128)} collective-permute-done((f32[4,32,1024]{2,1,0:T(8,128)}, f32[4,32,1024]{2,1,0:T(8,128)}, u32[]{:S(2)}, u32[]{:S(2)}) %collective-permute-start.2) | collective-permute-done | bytes 524320 | tf_op jit(solution)/shard_map/ppermute | solution.py:23
  80.2 1.1 fusion.58
  81.3 0.8 copy-done.3
  82.2 0.7 iota_compare_fusion.10
  82.9 0.7 eq.260
  83.7 0.8 add.240
  84.5 0.8 fusion.131
  85.3 4.1 %collective-permute-done.3 = f32[2,32,1024]{2,1,0:T(8,128)S(1)} collective-permute-done((f32[2,32,1024]{2,1,0:T(8,128)S(1)}, f32[2,32,1024]{2,1,0:T(8,128)S(1)}, u32[]{:S(2)}, u32[]{:S(2)}) %collective-permute-start.3) | collective-permute-done | bytes 262176 | tf_op jit(solution)/shard_map/ppermute | solution.py:23
  89.4 1.1 fusion.80
  90.5 4.0 %collective-permute-start.4 = (f32[1,32,1024]{2,1,0:T(8,128)S(1)}, f32[1,32,1024]{2,1,0:T(8,128)S(1)}, u32[]{:S(2)}, u32[]{:S(2)}) collective-permute-start(f32[1,32,1024]{2,1,0:T(8,128)S(1)} %select_bitcast_fusion.2), channel_id=1, source_target_pairs={{0,8},{2,10},{4,12},{6,14},{8,0},{10,2},{12,4},{14,6},{1,9},{3,11}... | collective-permute-start | bytes 393224 | tf_op jit(solution)/shard_map/ppermute | solution.py:23
  94.5 10.2 %collective-permute-done.4 = f32[1,32,1024]{2,1,0:T(8,128)S(1)} collective-permute-done((f32[1,32,1024]{2,1,0:T(8,128)S(1)}, f32[1,32,1024]{2,1,0:T(8,128)S(1)}, u32[]{:S(2)}, u32[]{:S(2)}) %collective-permute-start.4) | collective-permute-done | bytes 131104 | tf_op jit(solution)/shard_map/ppermute | solution.py:23
  104.7 8.0 %all-gather.6.cloned.1.call-done = bf16[1024,4,128]{0,2,1:T(8,128)(2,1)} async-done(((bf16[128,4,128]{0,2,1:T(8,128)(2,1)}), bf16[1024,4,128]{0,2,1:T(8,128)(2,1)}) %all-gather.6.cloned.1.call-update) | async-done | bytes 1048592 | tf_op jit(solution)/shard_map/all_gather | solution.py:201
  112.7 1.9 fusion.22
  114.6 0.8 select_reduce_fusion.1
  115.4 0.7 mul.306
  117.6 0.8 broadcast_in_dim.131
  118.3 0.7 select_reduce_fusion.2
  119.7 0.8 multiply_cosine_fusion.1
  120.5 2.5 %fusion.132 = (f32[1024]{0:T(1024)}, bf16[1024,256]{0,1:T(8,128)(2,1)}) fusion(s32[256]{0:T(256)S(1)} %add.241, s32[256]{0:T(256)} %get-tuple-element.19, pred[256]{0:T(512)(128)(4,1)S(1)} %lt.89), kind=kOutput, calls=%fused_computation.227 | convolution fusion | flops 135330816 | bytes 530688 | tf_op jit(solution)/shard_map/dot_general | solution.py:256
  123.0 5.2 %all-gather.8.cloned.1.call-done = bf16[128,4096]{1,0:T(8,128)(2,1)} async-done(((bf16[128,1024]{1,0:T(8,128)(2,1)}), bf16[128,4096]{1,0:T(8,128)(2,1)}) %all-gather.8.cloned.1.call-update) | async-done | bytes 1048592 | tf_op jit(solution)/shard_map/all_gather | solution.py:222
  128.2 1.5 fusion.7
  129.7 4.3 %fusion.56 = f32[32,4,128]{2,0,1:T(8,128)S(1)} fusion(bf16[4096,4,128]{0,2,1:T(8,128)(2,1)} %copy.121, bf16[128,4096]{1,0:T(8,128)(2,1)} %all-gather.8.cloned.1.call-done, f32[128]{0:T(128)S(1)} %add_rsqrt_fusion, f32[4096]{0:T(1024)S(1)} %copy-done.7, bf16[128,32]{0,1:T(8,128)(2,1)S(1)} %get-tuple-element.36), kind=kOutput, calls=%fused_computation.64 | convolution fusion | flops 170000384 | bytes 5333504 | tf_op jit(solution)/shard_map/td,dhk->thk/dot_general | solution.py:165
  134.1 0.7 fusion.100
  134.8 2.4 %collective-permute-start.5 = (bf16[1,32,4,128]{3,1,2,0:T(8,128)(2,1)}, bf16[1,32,4,128]{3,1,2,0:T(8,128)(2,1)}, u32[]{:S(2)}, u32[]{:S(2)}) collective-permute-start(bf16[1,32,4,128]{3,1,2,0:T(8,128)(2,1)} %fusion.100), channel_id=1, source_target_pairs={{0,8},{2,10},{4,12},{6,14},{8,0},{10,2},{12,4},{14,6},{1,9},{3,11}... | collective-permute-start | bytes 98312 | tf_op jit(solution)/shard_map/ppermute | solution.py:23
  137.2 0.7 select_reduce_fusion
  137.9 21.3 %copy.135 = bf16[4096,4,2,128]{0,3,2,1:T(8,128)(2,1)} copy(bf16[4096,4,2,128]{3,2,1,0:T(2,128)(2,1)} %param.32) | data formatting | bytes 16777216 | tf_op args[15]
  159.2 1.4 eq.235
  160.6 1.5 maximum_select_fusion.4
  162.1 1.5 collective-permute-start.6
  163.6 1.3 select_reduce_fusion.5
  164.9 1.2 eq.239
  166.7 1.0 maximum_select_fusion.2
  167.7 1.5 collective-permute-start.7
  169.2 0.7 broadcast_compare_fusion.2
  169.9 2.8 %collective-permute-done.7 = bf16[4,32,4,128]{3,1,2,0:T(8,128)(2,1)S(1)} collective-permute-done((bf16[4,32,4,128]{3,1,2,0:T(8,128)(2,1)S(1)}, bf16[4,32,4,128]{3,1,2,0:T(8,128)(2,1)S(1)}, u32[]{:S(2)}, u32[]{:S(2)}) %collective-permute-start.7) | collective-permute-done | bytes 131104 | tf_op jit(solution)/shard_map/ppermute | solution.py:23
  172.9 1.5 convolution_convert_fusion.2
  174.4 1.4 broadcast_select_fusion
  176.3 5.8 %fusion.68 = f32[128,1024]{0,1:S(1)} fusion(bf16[4096,1024]{0,1:T(8,128)(2,1)} %bitcast.166, bf16[128,4096]{1,0:T(8,128)(2,1)S(1)} %copy-done.1, f32[128]{0:T(128)S(1)} %copy-done.16, f32[4096]{0:T(1024)S(1)} %copy-done.7), kind=kOutput, calls=%fused_computation.79 | convolution fusion | flops 1075838976 | bytes 9978368
  182.1 1.0 fusion.3
  183.2 0.9 fusion.1
  184.0 1.2 fusion.45
  185.3 0.9 copy.139
  (115 shorter events, 10.4 us)
Async XLA Ops:
  6.5 2.5 %copy-start = (bf16[1280,3,4,80]{0,3,2,1:T(8,128)(2,1)S(1)}, bf16[1280,3,4,80]{0,3,2,1:T(8,128)(2,1)}, u32[]{:S(2)}) copy-start(bf16[1280,3,4,80]{0,3,2,1:T(8,128)(2,1)} %param.20) | copy-start | bytes 7372804
  6.5 4.5 %copy-start.20 = (s32[128]{0:T(128)S(1)}, s32[128]{0:T(128)}, u32[]{:S(2)}) copy-start(s32[128]{0:T(128)} %param.26) | copy-start | bytes 1540
  6.5 7.5 %copy-start.12 = (s32[256]{0:T(256)S(1)}, s32[256]{0:T(256)}, u32[]{:S(2)}) copy-start(s32[256]{0:T(256)} %param.27) | copy-start | bytes 3076
  6.5 7.7 %copy-start.11 = (s32[8]{0:T(128)S(1)}, s32[8]{0:T(128)}, u32[]{:S(2)}) copy-start(s32[8]{0:T(128)} %param.28) | copy-start | bytes 100
  6.5 46.7 %all-gather.4.cloned.1.call-start = ((), (), s32[]{:S(2)}) async-start(), calls=%async_computation.1 | async-start | bytes 1310720 | tf_op jit(solution)/shard_map/all_gather | solution.py:172
  11.0 0.7 copy-start.4
  13.4 12.2 %collective-permute-start = (f32[128,1280]{1,0:T(8,128)S(1)}, f32[128,1280]{1,0:T(8,128)}, u32[]{:S(2)}, u32[]{:S(2)}) collective-permute-start(f32[128,1280]{1,0:T(8,128)S(1)} %convolution_bitcast_fusion), channel_id=1, source_target_pairs={{0,1},{1,0},{2,3},{3,2},{4,5},{5,4},{6,7},{7,6},{8,9},{9,8},{10,11... | collective-permute-start | bytes 1966088 | tf_op jit(solution)/shard_map/ppermute | solution.py:23
  15.7 14.8 %copy-start.17 = (f32[64]{0:T(128)}, f32[64]{0:T(128)S(1)}, u32[]{:S(2)}) copy-start(f32[64]{0:T(128)S(1)} %multiply_power_fusion) | copy-start | bytes 772
  15.7 8.5 %copy-start.18 = (pred[8]{0:T(512)(128)(4,1)}, pred[8]{0:T(512)(128)(4,1)S(1)}, u32[]{:S(2)}) copy-start(pred[8]{0:T(512)(128)(4,1)S(1)} %iota_compare_fusion.12) | copy-start | bytes 28
  15.8 8.5 %copy-start.8 = (s32[8,32]{1,0:T(8,128)}, s32[8,32]{1,0:T(8,128)S(1)}, u32[]{:S(2)}) copy-start(s32[8,32]{1,0:T(8,128)S(1)} %copy.117) | copy-start | bytes 3076
  16.6 7.7 %copy-start.21 = (s32[8,2]{0,1:T(2,128)S(1)}, s32[8,2]{0,1:T(2,128)}, u32[]{:S(2)}) copy-start(s32[8,2]{0,1:T(2,128)} %param.25) | copy-start | bytes 196
  16.6 29.3 %copy-start.2 = (bf16[128,1280]{1,0:T(8,128)(2,1)S(1)}, bf16[128,1280]{1,0:T(8,128)(2,1)}, u32[]{:S(2)}) copy-start(bf16[128,1280]{1,0:T(8,128)(2,1)} %param.17) | copy-start | bytes 983044
  24.2 22.0 %copy-start.13 = (f32[1280]{0:T(1024)S(1)}, f32[1280]{0:T(1024)}, u32[]{:S(2)}) copy-start(f32[1280]{0:T(1024)} %param.23) | copy-start | bytes 15364
  24.2 22.0 %copy-start.14 = (f32[1280]{0:T(1024)S(1)}, f32[1280]{0:T(1024)}, u32[]{:S(2)}) copy-start(f32[1280]{0:T(1024)} %param.22) | copy-start | bytes 15364
  26.8 28.0 %copy-start.7 = (f32[4096]{0:T(1024)S(1)}, f32[4096]{0:T(1024)}, u32[]{:S(2)}) copy-start(f32[4096]{0:T(1024)} %param.31) | copy-start | bytes 49156
  26.8 19.0 %collective-permute-start.1 = (f32[128,1280]{1,0:T(8,128)S(1)}, f32[128,1280]{1,0:T(8,128)S(1)}, u32[]{:S(2)}, u32[]{:S(2)}) collective-permute-start(f32[128,1280]{1,0:T(8,128)S(1)} %add.248), channel_id=1, source_target_pairs={{0,16},{16,0},{1,17},{17,1},{2,18},{18,2},{3,19},{19,3},{4,20},{20... | collective-permute-start | bytes 1966088 | tf_op jit(solution)/shard_map/ppermute | solution.py:23
  30.7 27.9 %copy-start.5 = (f32[128,64]{0,1:T(8,128)}, f32[128,64]{0,1:T(8,128)S(1)}, u32[]{:S(2)}) copy-start(f32[128,64]{0,1:T(8,128)S(1)} %get-tuple-element.32) | copy-start | bytes 98308
  47.6 15.9 %all-to-all-start = ((bf16[8,32,640]{2,1,0:T(8,128)(2,1)}), bf16[8,32,640]{2,1,0:T(8,128)(2,1)S(1)}, u32[]{:S(2)}, u32[]{:S(2)}) async-start(bf16[8,32,640]{2,1,0:T(8,128)(2,1)} %bitcast.164), calls=%async_computation | async-start | bytes 655360 | tf_op jit(solution)/shard_map/all_to_all | solution.py:199
  53.2 59.5 %all-gather.6.cloned.1.call-start = ((), (), s32[]{:S(2)}) async-start(), calls=%async_computation.2 | async-start | bytes 1179648 | tf_op jit(solution)/shard_map/all_gather | solution.py:201
  67.4 12.8 %collective-permute-start.2 = (f32[4,32,1024]{2,1,0:T(8,128)}, f32[4,32,1024]{2,1,0:T(8,128)}, u32[]{:S(2)}, u32[]{:S(2)}) collective-permute-start(f32[4,32,1024]{2,1,0:T(8,128)} %select_bitcast_fusion), channel_id=1, source_target_pairs={{0,2},{2,0},{4,6},{6,4},{8,10},{10,8},{12,14},{14,12},{1,3},{3,1},... | collective-permute-start | bytes 1572872 | tf_op jit(solution)/shard_map/ppermute | solution.py:23
  71.5 56.7 %all-gather.8.cloned.1.call-start = ((), (), s32[]{:S(2)}) async-start(), calls=%async_computation.3 | async-start | bytes 1310720 | tf_op jit(solution)/shard_map/all_gather | solution.py:222
  81.3 0.8 copy-start.3
  82.1 7.2 %collective-permute-start.3 = (f32[2,32,1024]{2,1,0:T(8,128)S(1)}, f32[2,32,1024]{2,1,0:T(8,128)S(1)}, u32[]{:S(2)}, u32[]{:S(2)}) collective-permute-start(f32[2,32,1024]{2,1,0:T(8,128)S(1)} %select_bitcast_fusion.1), channel_id=1, source_target_pairs={{0,4},{2,6},{4,0},{6,2},{8,12},{10,14},{12,8},{14,10},{1,5},{3,7},... | collective-permute-start | bytes 786440 | tf_op jit(solution)/shard_map/ppermute | solution.py:23
  90.5 14.2 %collective-permute-start.4 = (f32[1,32,1024]{2,1,0:T(8,128)S(1)}, f32[1,32,1024]{2,1,0:T(8,128)S(1)}, u32[]{:S(2)}, u32[]{:S(2)}) collective-permute-start(f32[1,32,1024]{2,1,0:T(8,128)S(1)} %select_bitcast_fusion.2), channel_id=1, source_target_pairs={{0,8},{2,10},{4,12},{6,14},{8,0},{10,2},{12,4},{14,6},{1,9},{3,11}... | collective-permute-start | bytes 393224 | tf_op jit(solution)/shard_map/ppermute | solution.py:23
  129.7 4.3 %copy-start.15 = (f32[128]{0:T(128)}, f32[128]{0:T(128)S(1)}, u32[]{:S(2)}) copy-start(f32[128]{0:T(128)S(1)} %add_rsqrt_fusion) | copy-start | bytes 1540
  134.8 25.9 %collective-permute-start.5 = (bf16[1,32,4,128]{3,1,2,0:T(8,128)(2,1)}, bf16[1,32,4,128]{3,1,2,0:T(8,128)(2,1)}, u32[]{:S(2)}, u32[]{:S(2)}) collective-permute-start(bf16[1,32,4,128]{3,1,2,0:T(8,128)(2,1)} %fusion.100), channel_id=1, source_target_pairs={{0,8},{2,10},{4,12},{6,14},{8,0},{10,2},{12,4},{14,6},{1,9},{3,11}... | collective-permute-start | bytes 98312 | tf_op jit(solution)/shard_map/ppermute | solution.py:23
  159.2 17.0 %copy-start.1 = (bf16[128,4096]{1,0:T(8,128)(2,1)S(1)}, bf16[128,4096]{1,0:T(8,128)(2,1)}, u32[]{:S(2)}) copy-start(bf16[128,4096]{1,0:T(8,128)(2,1)} %all-gather.8.cloned.1.call-done) | copy-start | bytes 3145732
  162.1 4.6 %collective-permute-start.6 = (bf16[2,32,4,128]{3,1,2,0:T(8,128)(2,1)}, bf16[2,32,4,128]{3,1,2,0:T(8,128)(2,1)}, u32[]{:S(2)}, u32[]{:S(2)}) collective-permute-start(bf16[2,32,4,128]{3,1,2,0:T(8,128)(2,1)} %maximum_select_fusion.4), channel_id=1, source_target_pairs={{0,4},{2,6},{4,0},{6,2},{8,12},{10,14},{12,8},{14,10},{1,5},{3,7},... | collective-permute-start | bytes 196616 | tf_op jit(solution)/shard_map/ppermute | solution.py:23
  166.1 9.7 %copy-start.9 = (s32[1024]{0:T(1024)S(1)}, s32[1024]{0:T(1024)}, u32[]{:S(2)}) copy-start(s32[1024]{0:T(1024)} %eq.235) | copy-start | bytes 12292
  166.1 9.7 %copy-start.10 = (s32[1024]{0:T(1024)S(1)}, s32[1024]{0:T(1024)}, u32[]{:S(2)}) copy-start(s32[1024]{0:T(1024)} %fusion.108) | copy-start | bytes 12292
  166.1 9.7 %copy-start.19 = (s32[128]{0:T(128)S(1)}, s32[128]{0:T(128)}, u32[]{:S(2)}) copy-start(s32[128]{0:T(128)} %get-tuple-element.18) | copy-start | bytes 1540
  166.1 9.7 %copy-start.22 = (s32[128]{0:T(128)S(1)}, s32[128]{0:T(128)}, u32[]{:S(2)}) copy-start(s32[128]{0:T(128)} %eq.239) | copy-start | bytes 1540
  166.1 10.1 %copy-start.16 = (f32[128]{0:T(128)S(1)}, f32[128]{0:T(128)}, u32[]{:S(2)}) copy-start(f32[128]{0:T(128)} %copy-done.15) | copy-start | bytes 1540
  167.7 5.0 %collective-permute-start.7 = (bf16[4,32,4,128]{3,1,2,0:T(8,128)(2,1)S(1)}, bf16[4,32,4,128]{3,1,2,0:T(8,128)(2,1)S(1)}, u32[]{:S(2)}, u32[]{:S(2)}) collective-permute-start(bf16[4,32,4,128]{3,1,2,0:T(8,128)(2,1)S(1)} %maximum_select_fusion.2), channel_id=1, source_target_pairs={{0,2},{2,0},{4,6},{6,4},{8,10},{10,8},{12,14},{14,12},{1,3},{3,1},... | collective-permute-start | bytes 393224 | tf_op jit(solution)/shard_map/ppermute | solution.py:23
  175.8 6.4 %collective-permute-start.8 = (bf16[1024,4,128]{0,2,1:T(8,128)(2,1)S(1)}, bf16[1024,4,128]{0,2,1:T(8,128)(2,1)S(1)}, u32[]{:S(2)}, u32[]{:S(2)}) collective-permute-start(bf16[1024,4,128]{0,2,1:T(8,128)(2,1)S(1)} %broadcast_select_fusion), channel_id=1, source_target_pairs={{0,1},{1,0},{2,3},{3,2},{4,5},{5,4},{6,7},{7,6},{8,9},{9,8},{10,11... | collective-permute-start | bytes 3145736 | tf_op jit(solution)/shard_map/ppermute | solution.py:23
  176.2 5.8 %copy-start.6 = (f32[128,64]{0,1:T(8,128)S(1)}, f32[128,64]{0,1:T(8,128)}, u32[]{:S(2)}) copy-start(f32[128,64]{0,1:T(8,128)} %copy-done.5) | copy-start | bytes 98308
Sparse Core Ops, SparseCore 0:
  14.2 20.3 all-gather.3
  71.6 41.0 all-gather.5
  114.7 13.4 all-gather.7

commit v8 on v6

--- a/solution.py
+++ b/solution.py
@@ -68,7 +68,7 @@
     return (owner_dev, local_row, owner_hot)
 
 
-def halving_scatter(blocks, index, count):
+def halving_scatter(blocks, index, count, axis="ctx"):
     remaining = count
     bit = 0
     while remaining > 1:
@@ -76,7 +76,7 @@
         mine = (index >> bit) & 1
         keep = jnp.where(mine == 0, lower[:, 0], lower[:, 1])
         give = jnp.where(mine == 0, lower[:, 1], lower[:, 0])
-        blocks = keep + swapped(give, "ctx", bit)
+        blocks = keep + swapped(give, axis, bit)
         remaining //= 2
         bit += 1
     return blocks[0]
@@ -157,10 +157,28 @@
     )
     blended = (blended / jnp.transpose(totals)[:, :, None]).astype(jnp.bfloat16)
     branch_part = jnp.einsum("phd,hdf->pf", blended, vit_out, preferred_element_type=jnp.float32)
-    branch_sum = branch_part + swapped(branch_part, "tp", 0)
-    branch_sum = branch_sum + swapped(branch_sum, "vis", 0)
-    hidden = patch_rows.astype(jnp.float32) + branch_sum
-    merged = layer_norm(hidden, merge_gain, merge_bias).astype(jnp.bfloat16).reshape(ICAP, 4 * VD)
+    tp_size = lax.axis_size("tp")
+    vis_size = lax.axis_size("vis")
+    vis_index = lax.axis_index("vis")
+    tp_rows = PCAP // tp_size
+    part_rows = tp_rows // vis_size
+    branch_sum = halving_scatter(
+        branch_part.reshape(tp_size, tp_rows, VD), tp_index, tp_size, "tp"
+    )
+    branch_sum = halving_scatter(
+        branch_sum.reshape(vis_size, part_rows, VD), vis_index, vis_size, "vis"
+    )
+    first_row = tp_index * tp_rows + vis_index * part_rows
+    hidden = lax.dynamic_slice_in_dim(patch_rows, first_row, part_rows, 0).astype(
+        jnp.float32
+    ) + branch_sum
+    merged_part = layer_norm(hidden, merge_gain, merge_bias).astype(jnp.bfloat16).reshape(
+        part_rows // 4, 4 * VD
+    )
+    merged_part = doubling_gather(
+        merged_part, "vis", vis_index, vis_size, list(range(vis_size.bit_length() - 1))
+    )
+    merged = doubling_gather(merged_part, "tp", tp_index, tp_size, [0]).reshape(ICAP, 4 * VD)
     send_each = ICAP // shards
     slot_ids = jnp.arange(ICAP, dtype=jnp.int32)
     shard_ids = jnp.arange(shards, dtype=jnp.int32)
@@ -206,6 +224,7 @@
     own_positions = row_positions(
         ctx_index * TOK + jnp.arange(TOK, dtype=jnp.int32), slice_order, TOK
     )
+    own_doc = jnp.take(doc_ids, own_positions)
     kv_heads = w_query.shape[1]
     groups = w_query.shape[2]
     queries = jnp.einsum(
@@ -218,24 +237,13 @@
     own_half = jnp.where(
         tp_index == 0, rotate(projected_half, own_positions), projected_half
     ).astype(jnp.bfloat16)
-    ctx_bits = list(range(shards.bit_length() - 1))[::-1]
-    gathered = doubling_gather(own_half, "ctx", ctx_index, shards, ctx_bits).reshape(
-        (shards * TOK,) + own_half.shape[1:]
-    )
+    gathered = lax.all_gather(own_half, "ctx", axis=0, tiled=True)
     partner_all = swapped(gathered, "tp", 0)
     keys_every = jnp.where(tp_index == 0, gathered, partner_all)
     values_every = jnp.where(tp_index == 0, partner_all, gathered)
     key_count = keys_every.shape[0]
     key_pos = row_positions(jnp.arange(key_count, dtype=jnp.int32), slice_order, TOK)
-    doc_slices = doc_ids.reshape(2 * shards, TOK // 2)
-    slice_ids = jnp.stack([slice_order, 2 * shards - 1 - slice_order], axis=1)
-    slice_hot = slice_ids[:, :, None] == jnp.arange(2 * shards, dtype=jnp.int32)[None, None, :]
-    key_doc = jnp.sum(
-        jnp.where(slice_hot[..., None], doc_slices[None, None], 0), axis=2
-    ).reshape(shards * TOK)
-    own_doc = jnp.sum(
-        jnp.where((shard_ids == ctx_index)[:, None], key_doc.reshape(shards, TOK), 0), axis=0
-    )
+    key_doc = jnp.take(doc_ids, key_pos)
     allowed_now = (key_pos[None, :] <= own_positions[:, None]) & (
         key_doc[None, :] == own_doc[:, None]
     )

time: 175 us -> 164 us (0.937)
  waiting for transfers between devices: 66.7 us -> 54.9 us
  local copies, waits for them, and re-layouts: 38.2 us -> 42.1 us
  starting transfers between devices: 19.3 us -> 17 us
    ppermute x9 -> x8, waiting for transfers between devices: 47.7 us -> 28.4 us  [swapped(): lax.ppermute(value, axis, [(i, i ^ 1 << stride) for i in range(lax.axis_s...]
    gather x0 -> x2, local copies, waits for them, and re-layouts: none -> 9.79 us  [the longest x1 8.81 us: local(): key_doc = jnp.take(doc_ids, key_pos)]
    all_gather x0 -> x1, waiting for transfers between devices: none -> 7.36 us  [local(): gathered = lax.all_gather(own_half, 'ctx', axis=0, tiled=True)]
    another operation x2 -> x1, local copies, waits for them, and re-layouts: 2.65 us -> 0.07 us  [doubling_gather(): have = block[None]]
    select_n x3 -> x2, other arithmetic: 2.58 us -> 0.05 us  [doubling_gather(): jnp.where(mine == 0, jnp.concatenate([have, arrived], axis=0), jnp.concat...]
    ppermute x9 -> x8, starting transfers between devices: 13 us -> 10.6 us  [swapped(): lax.ppermute(value, axis, [(i, i ^ 1 << stride) for i in range(lax.axis_s...]
    transpose x1 -> x0, local copies, waits for them, and re-layouts: 2.06 us -> none  [doubling_gather(): have = jnp.transpose(have, wanted + list(range(len(order), have.ndim)))]
    select_n x0 -> x4, other arithmetic: none -> 1.86 us  [the longest x2 1.29 us: local(): key_doc = jnp.take(doc_ids, key_pos)]
  transfers between devices with their start and end apart: 11 -> 11, of which waited for: 9 -> 10; matrix products, arithmetic and copies ran while one was open for 24% -> 31% of each run, Pallas kernels for 0% -> 0%
where the time goes in v8:
time: 164 us; the launch traced here: 162 us
  waiting for transfers between devices  54.9 us (33%)
  local copies, waits for them, and re-layouts  42.1 us (26%)
  matrix products  19.3 us (12%)
  starting transfers between devices  17 us (10%)
  other arithmetic  15.3 us (9%)
  between operations  13.9 us (8%)
    ppermute x8, waiting for transfers between devices, swapped(): lax.ppermute(value, axis, [(i, i ^ 1 << stride) for i in range(lax.axis_s...  28.4 us
    unnamed x37, local copies, waits for them, and re-layouts  22.3 us
    unnamed x3, matrix products  11.6 us
    ppermute x8, starting transfers between devices, swapped(): lax.ppermute(value, axis, [(i, i ^ 1 << stride) for i in range(lax.axis_s...  10.6 us
    all_to_all x1, waiting for transfers between devices, local(): lax.all_to_all(blocks, 'ctx', split_axis=0, concat_axis=0, tiled=True)  10.4 us
    gather x1, local copies, waits for them, and re-layouts, local(): key_doc = jnp.take(doc_ids, key_pos)  8.81 us
    all_gather x1, waiting for transfers between devices, local(): full_rows = lax.all_gather(embeds, ('vis', 'tp'), axis=1, tiled=True)  8.69 us
    squeeze x1, local copies, waits for them, and re-layouts, local(): w_keyval[0]  7.62 us
  transfers between devices with their start and end apart: 11, of which 10 were waited for; matrix products, arithmetic and copies ran while one was open for 31% of the time, Pallas kernels for 0%

profile of v8, /device:TPU:0, one launch (start us, length us, event | category | flops | bytes accessed | tf_op | source)
XLA Modules:
  0.0 162.4 jit_solution(9325889656057551280)
XLA Ops:
  6.5 1.2 convert_reduce_fusion
  7.8 1.2 fusion.42
  9.0 1.9 %fusion.48 = f32[128,960]{0,1:S(1)} fusion(bf16[1280,960]{0,1:T(8,128)(2,1)S(1)} %bitcast.174, bf16[128,1280]{1,0:T(8,128)(2,1)} %param.17, f32[1280]{0:T(1024)} %param.19, f32[1280]{0:T(1024)} %param.18, f32[128]{0:T(128)S(1)} %add_rsqrt_fusion.2, f32[128]{0:T(128)S(1)} %broadcast_multiply_fusion.1), kind=kOutput, calls=%fused_computation.53 | convolution fusion | flops 315555840 | bytes 3288064
  11.0 0.1 broadcast_compare_fusion
  11.1 0.3 fusion.116
  11.4 0.3 copy-done.3
  11.7 1.7 %fusion.22 = f32[128,1280,1]{1,0,2:T(8,128)S(1)} fusion(bf16[4,80,1280]{2,1,0:T(8,128)(2,1)} %param.21, f32[4,128,128]{1,2,0:T(8,128)S(1)} %get-tuple-element.22, f32[4,128]{1,0:T(4,128)S(1)} %get-tuple-element.21, bf16[128,3,4,80]{0,3,2,1:T(8,128)(2,1)} %copy-done.3, f32[128,4]{0,1:T(4,128)S(1)} %bitcast.195), kind=kOutput, calls=%fused_computation.30 | convolution fusion | flops 115556352 | bytes 1822720 | tf_op jit(solution)/shard_map/phd,hdf->pf/dot_general | solution.py:159
  13.5 0.6 collective-permute-start
  14.1 0.1 copy.95
  14.2 0.7 fusion.114
  15.0 0.4 collective-permute-done
  15.4 1.0 bitcast_add_fusion
  16.5 2.9 %collective-permute-start.1 = (f32[1,32,1280]{2,1,0:T(8,128)S(1)}, f32[1,32,1280]{2,1,0:T(8,128)S(1)}, u32[]{:S(2)}, u32[]{:S(2)}) collective-permute-start(f32[1,32,1280]{2,1,0:T(8,128)S(1)} %select_bitcast_fusion.3), channel_id=1, source_target_pairs={{0,16},{16,0},{1,17},{17,1},{2,18},{18,2},{3,19},{19,3},{4,20},{20... | collective-permute-start | bytes 491528 | tf_op jit(solution)/shard_map/ppermute | solution.py:23
  19.4 0.7 fusion.67
  20.1 3.8 %collective-permute-done.1 = f32[1,32,1280]{2,1,0:T(8,128)S(1)} collective-permute-done((f32[1,32,1280]{2,1,0:T(8,128)S(1)}, f32[1,32,1280]{2,1,0:T(8,128)S(1)}, u32[]{:S(2)}, u32[]{:S(2)}) %collective-permute-start.1) | collective-permute-done | bytes 163872 | tf_op jit(solution)/shard_map/ppermute | solution.py:23
  23.9 1.0 fusion.113
  24.9 0.2 multiply_reduce_fusion
  25.2 0.1 add_convert_fusion.1
  25.3 1.8 %collective-permute-start.2 = (bf16[1,8,5120]{2,1,0:T(8,128)(2,1)S(1)}, bf16[1,8,5120]{2,1,0:T(8,128)(2,1)S(1)}, u32[]{:S(2)}, u32[]{:S(2)}) collective-permute-start(bf16[1,8,5120]{2,1,0:T(8,128)(2,1)S(1)} %broadcast_in_dim_reshape.2), channel_id=1, source_target_pairs={{0,16},{16,0},{1,17},{17,1},{2,18},{18,2},{3,19},{19,3},{4,20},{20... | collective-permute-start | bytes 245768 | tf_op jit(solution)/shard_map/ppermute | solution.py:23
  27.1 0.1 select_reduce_fusion.2
  27.3 2.5 %collective-permute-done.2 = bf16[1,8,5120]{2,1,0:T(8,128)(2,1)S(1)} collective-permute-done((bf16[1,8,5120]{2,1,0:T(8,128)(2,1)S(1)}, bf16[1,8,5120]{2,1,0:T(8,128)(2,1)S(1)}, u32[]{:S(2)}, u32[]{:S(2)}) %collective-permute-start.2) | collective-permute-done | bytes 81952 | tf_op jit(solution)/shard_map/ppermute | solution.py:23
  30.0 1.4 collective-permute-done.3
  31.4 0.2 convolution_convert_fusion
  31.6 0.7 copy.131
  32.3 6.1 %all-to-all-start = ((bf16[8,32,640]{2,1,0:T(8,128)(2,1)}), bf16[8,32,640]{2,1,0:T(8,128)(2,1)S(1)}, u32[]{:S(2)}, u32[]{:S(2)}) async-start(bf16[8,32,640]{2,1,0:T(8,128)(2,1)} %bitcast.172), calls=%async_computation | async-start | bytes 655360 | tf_op jit(solution)/shard_map/all_to_all | solution.py:198
  38.6 10.4 %all-to-all-done = bf16[8,32,640]{2,1,0:T(8,128)(2,1)S(1)} async-done(((bf16[8,32,640]{2,1,0:T(8,128)(2,1)}), bf16[8,32,640]{2,1,0:T(8,128)(2,1)S(1)}, u32[]{:S(2)}, u32[]{:S(2)}) %all-to-all-start) | async-done | bytes 327712 | tf_op jit(solution)/shard_map/all_to_all | solution.py:198
  49.0 0.1 reshape.869
  49.1 0.1 copy.132
  49.2 0.1 dot_general.46
  49.3 1.9 %fusion.12 = f32[4,2,32,1024]{3,2,1,0:T(8,128)S(1)} fusion(bf16[4,2,32,640]{3,2,1,0:T(8,128)(2,1)S(1)} %dot_general.46, bf16[640,1024]{1,0:T(8,128)(2,1)} %param.24), kind=kOutput, calls=%fused_computation.18 | convolution fusion | flops 335544320 | bytes 2686976 | tf_op jit(solution)/shard_map/dot_general | solution.py:202
  51.3 1.5 collective-permute-start.4
  53.0 10.2 %collective-permute-done.4 = f32[4,32,1024]{2,1,0:T(8,128)S(1)} collective-permute-done((f32[4,32,1024]{2,1,0:T(8,128)S(1)}, f32[4,32,1024]{2,1,0:T(8,128)S(1)}, u32[]{:S(2)}, u32[]{:S(2)}) %collective-permute-start.4) | collective-permute-done | bytes 524320 | tf_op jit(solution)/shard_map/ppermute | solution.py:23
  63.2 0.1 fusion.47
  63.3 0.7 select_bitcast_fusion.2
  64.0 0.5 collective-permute-start.5
  64.6 0.1 and.297
  64.7 0.3 fusion.115
  65.0 5.7 %collective-permute-done.5 = f32[2,32,1024]{2,1,0:T(8,128)} collective-permute-done((f32[2,32,1024]{2,1,0:T(8,128)}, f32[2,32,1024]{2,1,0:T(8,128)}, u32[]{:S(2)}, u32[]{:S(2)}) %collective-permute-start.5) | collective-permute-done | bytes 262176 | tf_op jit(solution)/shard_map/ppermute | solution.py:23
  70.7 1.0 fusion.64
  71.7 3.2 %collective-permute-start.6 = (f32[1,32,1024]{2,1,0:T(8,128)S(1)}, f32[1,32,1024]{2,1,0:T(8,128)S(1)}, u32[]{:S(2)}, u32[]{:S(2)}) collective-permute-start(f32[1,32,1024]{2,1,0:T(8,128)S(1)} %select_bitcast_fusion.4), channel_id=1, source_target_pairs={{0,8},{2,10},{4,12},{6,14},{8,0},{10,2},{12,4},{14,6},{1,9},{3,11}... | collective-permute-start | bytes 393224 | tf_op jit(solution)/shard_map/ppermute | solution.py:23
  74.9 4.4 %collective-permute-done.6 = f32[1,32,1024]{2,1,0:T(8,128)S(1)} collective-permute-done((f32[1,32,1024]{2,1,0:T(8,128)S(1)}, f32[1,32,1024]{2,1,0:T(8,128)S(1)}, u32[]{:S(2)}, u32[]{:S(2)}) %collective-permute-start.6) | collective-permute-done | bytes 131104 | tf_op jit(solution)/shard_map/ppermute | solution.py:23
  79.3 1.0 fusion.18
  80.3 0.2 all-gather.5.cloned.1.call-start
  80.6 0.1 select_reduce_fusion.3
  80.7 1.0 gather_fusion.1
  81.7 0.5 and_select_fusion.8
  82.2 7.6 %copy.112 = bf16[4096,4,128]{0,2,1:T(8,128)(2,1)} copy(bf16[4096,4,128]{2,1,0:T(4,128)(2,1)} %bitcast.180) | data formatting | bytes 8388608 | tf_op jit(solution)/shard_map/squeeze | solution.py:235
  89.9 0.2 multiply_cosine_fusion
  90.1 8.7 %all-gather.3.cloned.1.call-done = bf16[128,4096]{1,0:T(8,128)(2,1)} async-done(((bf16[128,1024]{1,0:T(8,128)(2,1)}), bf16[128,4096]{1,0:T(8,128)(2,1)}) %all-gather.3.cloned.1.call-update) | async-done | bytes 1048592 | tf_op jit(solution)/shard_map/all_gather | solution.py:217
  98.8 1.5 fusion.3
  100.3 3.8 %fusion.56 = f32[128,512]{0,1:S(1)} fusion(bf16[4096,512]{0,1:T(8,128)(2,1)} %bitcast.181, bf16[128,4096]{1,0:T(8,128)(2,1)} %all-gather.3.cloned.1.call-done, f32[4096]{0:T(1024)S(1)} %copy-done.7, f32[128]{0:T(128)S(1)} %add_rsqrt_fusion), kind=kOutput, calls=%fused_computation.64 | convolution fusion | flops 538968064 | bytes 5521920
  104.2 0.7 fusion.58
  104.9 0.1 select_reduce_fusion
  105.1 0.5 copy-done.8
  105.6 8.8 %gather_fusion = s32[1024]{0:T(1024)} fusion(s32[1024]{0:T(1024)S(1)} %copy-done.1, s32[1024]{0:T(1024)S(1)} %broadcast_clamp_fusion), kind=kCustom, calls=%fused_computation | custom fusion | bytes 12288 | tf_op jit(solution)/shard_map/jit(_take)/gather | solution.py:246
  114.4 21.4 %copy.113 = bf16[4096,4,2,128]{0,3,2,1:T(8,128)(2,1)} copy(bf16[4096,4,2,128]{3,2,1,0:T(2,128)(2,1)} %param.32) | data formatting | bytes 16777216 | tf_op args[15]
  135.8 1.3 and_select_fusion.2
  137.1 7.4 %all-gather.5.cloned.1.call-done = bf16[1024,4,128]{0,2,1:T(8,128)(2,1)} async-done(((bf16[128,4,128]{0,2,1:T(8,128)(2,1)}), bf16[1024,4,128]{0,2,1:T(8,128)(2,1)}) %all-gather.5.cloned.1.call-update) | async-done | bytes 1048592 | tf_op jit(solution)/shard_map/all_gather | solution.py:240
  144.5 1.0 compare_and_fusion
  145.5 5.9 %fusion.54 = f32[128,1024]{0,1:S(1)} fusion(bf16[4096,1024]{0,1:T(8,128)(2,1)} %bitcast.175, bf16[128,4096]{1,0:T(8,128)(2,1)S(1)} %copy-done.2, f32[4096]{0:T(1024)S(1)} %copy-done.7, f32[128]{0:T(128)} %copy-done.13), kind=kOutput, calls=%fused_computation.63 | convolution fusion | flops 1075838976 | bytes 9978368
  151.5 1.0 fusion.2
  152.5 0.9 fusion
  153.4 1.3 fusion.35
  154.7 0.9 copy.117
  (79 shorter events, 1.4 us)
Async XLA Ops:
  6.5 2.5 %copy-start = (bf16[1280,3,4,80]{0,3,2,1:T(8,128)(2,1)S(1)}, bf16[1280,3,4,80]{0,3,2,1:T(8,128)(2,1)}, u32[]{:S(2)}) copy-start(bf16[1280,3,4,80]{0,3,2,1:T(8,128)(2,1)} %param.20) | copy-start | bytes 7372804
  6.5 4.4 %copy-start.15 = (s32[128]{0:T(128)S(1)}, s32[128]{0:T(128)}, u32[]{:S(2)}) copy-start(s32[128]{0:T(128)} %param.26) | copy-start | bytes 1540
  6.5 7.5 %copy-start.12 = (s32[256]{0:T(256)S(1)}, s32[256]{0:T(256)}, u32[]{:S(2)}) copy-start(s32[256]{0:T(256)} %param.27) | copy-start | bytes 3076
  6.5 7.7 %copy-start.9 = (s32[8]{0:T(128)S(1)}, s32[8]{0:T(128)}, u32[]{:S(2)}) copy-start(s32[8]{0:T(128)} %param.28) | copy-start | bytes 100
  10.9 14.2 %copy-start.10 = (f32[1280]{0:T(1024)S(1)}, f32[1280]{0:T(1024)}, u32[]{:S(2)}) copy-start(f32[1280]{0:T(1024)} %param.23) | copy-start | bytes 15364
  10.9 14.2 %copy-start.11 = (f32[1280]{0:T(1024)S(1)}, f32[1280]{0:T(1024)}, u32[]{:S(2)}) copy-start(f32[1280]{0:T(1024)} %param.22) | copy-start | bytes 15364
  11.0 0.7 copy-start.3
  13.4 25.2 %copy-start.16 = (s32[8,2]{0,1:T(2,128)S(1)}, s32[8,2]{0,1:T(2,128)}, u32[]{:S(2)}) copy-start(s32[8,2]{0,1:T(2,128)} %param.25) | copy-start | bytes 196
  13.5 1.9 %collective-permute-start = (f32[1,64,1280]{2,1,0:T(8,128)S(1)}, f32[1,64,1280]{2,1,0:T(8,128)}, u32[]{:S(2)}, u32[]{:S(2)}) collective-permute-start(f32[1,64,1280]{2,1,0:T(8,128)S(1)} %select_bitcast_fusion.1), channel_id=1, source_target_pairs={{0,1},{1,0},{2,3},{3,2},{4,5},{5,4},{6,7},{7,6},{8,9},{9,8},{10,11... | collective-permute-start | bytes 983048 | tf_op jit(solution)/shard_map/ppermute | solution.py:23
  16.5 7.4 %collective-permute-start.1 = (f32[1,32,1280]{2,1,0:T(8,128)S(1)}, f32[1,32,1280]{2,1,0:T(8,128)S(1)}, u32[]{:S(2)}, u32[]{:S(2)}) collective-permute-start(f32[1,32,1280]{2,1,0:T(8,128)S(1)} %select_bitcast_fusion.3), channel_id=1, source_target_pairs={{0,16},{16,0},{1,17},{17,1},{2,18},{18,2},{3,19},{19,3},{4,20},{20... | collective-permute-start | bytes 491528 | tf_op jit(solution)/shard_map/ppermute | solution.py:23
  25.3 4.5 %collective-permute-start.2 = (bf16[1,8,5120]{2,1,0:T(8,128)(2,1)S(1)}, bf16[1,8,5120]{2,1,0:T(8,128)(2,1)S(1)}, u32[]{:S(2)}, u32[]{:S(2)}) collective-permute-start(bf16[1,8,5120]{2,1,0:T(8,128)(2,1)S(1)} %broadcast_in_dim_reshape.2), channel_id=1, source_target_pairs={{0,16},{16,0},{1,17},{17,1},{2,18},{18,2},{3,19},{19,3},{4,20},{20... | collective-permute-start | bytes 245768 | tf_op jit(solution)/shard_map/ppermute | solution.py:23
  29.9 1.5 collective-permute-start.3
  32.3 16.7 %all-to-all-start = ((bf16[8,32,640]{2,1,0:T(8,128)(2,1)}), bf16[8,32,640]{2,1,0:T(8,128)(2,1)S(1)}, u32[]{:S(2)}, u32[]{:S(2)}) async-start(bf16[8,32,640]{2,1,0:T(8,128)(2,1)} %bitcast.172), calls=%async_computation | async-start | bytes 655360 | tf_op jit(solution)/shard_map/all_to_all | solution.py:198
  38.4 60.3 %all-gather.3.cloned.1.call-start = ((), (), s32[]{:S(2)}) async-start(), calls=%async_computation.1 | async-start | bytes 1310720 | tf_op jit(solution)/shard_map/all_gather | solution.py:217
  49.3 30.0 %copy-start.6 = (bf16[128,1024]{1,0:T(8,128)(2,1)S(1)}, bf16[128,1024]{1,0:T(8,128)(2,1)}, u32[]{:S(2)}) copy-start(bf16[128,1024]{1,0:T(8,128)(2,1)} %param.30) | copy-start | bytes 786436
  51.2 29.5 %copy-start.1 = (s32[1024]{0:T(1024)S(1)}, s32[1024]{0:T(1024)}, u32[]{:S(2)}) copy-start(s32[1024]{0:T(1024)} %param.29) | copy-start | bytes 12292
  51.3 11.9 %collective-permute-start.4 = (f32[4,32,1024]{2,1,0:T(8,128)S(1)}, f32[4,32,1024]{2,1,0:T(8,128)S(1)}, u32[]{:S(2)}, u32[]{:S(2)}) collective-permute-start(f32[4,32,1024]{2,1,0:T(8,128)S(1)} %select_bitcast_fusion), channel_id=1, source_target_pairs={{0,2},{2,0},{4,6},{6,4},{8,10},{10,8},{12,14},{14,12},{1,3},{3,1},... | collective-permute-start | bytes 1572872 | tf_op jit(solution)/shard_map/ppermute | solution.py:23
  64.0 6.7 %collective-permute-start.5 = (f32[2,32,1024]{2,1,0:T(8,128)}, f32[2,32,1024]{2,1,0:T(8,128)}, u32[]{:S(2)}, u32[]{:S(2)}) collective-permute-start(f32[2,32,1024]{2,1,0:T(8,128)} %select_bitcast_fusion.2), channel_id=1, source_target_pairs={{0,4},{2,6},{4,0},{6,2},{8,12},{10,14},{12,8},{14,10},{1,5},{3,7},... | collective-permute-start | bytes 786440 | tf_op jit(solution)/shard_map/ppermute | solution.py:23
  71.7 7.6 %collective-permute-start.6 = (f32[1,32,1024]{2,1,0:T(8,128)S(1)}, f32[1,32,1024]{2,1,0:T(8,128)S(1)}, u32[]{:S(2)}, u32[]{:S(2)}) collective-permute-start(f32[1,32,1024]{2,1,0:T(8,128)S(1)} %select_bitcast_fusion.4), channel_id=1, source_target_pairs={{0,8},{2,10},{4,12},{6,14},{8,0},{10,2},{12,4},{14,6},{1,9},{3,11}... | collective-permute-start | bytes 393224 | tf_op jit(solution)/shard_map/ppermute | solution.py:23
  80.3 64.1 %all-gather.5.cloned.1.call-start = ((), (), s32[]{:S(2)}) async-start(), calls=%async_computation.2 | async-start | bytes 1179648 | tf_op jit(solution)/shard_map/all_gather | solution.py:240
  82.2 7.6 %copy-start.14 = (s32[128]{0:T(128)}, s32[128]{0:T(128)S(1)}, u32[]{:S(2)}) copy-start(s32[128]{0:T(128)S(1)} %get-tuple-element.10) | copy-start | bytes 1540
  82.2 18.1 %copy-start.7 = (f32[4096]{0:T(1024)S(1)}, f32[4096]{0:T(1024)}, u32[]{:S(2)}) copy-start(f32[4096]{0:T(1024)} %param.31) | copy-start | bytes 49156
  90.1 15.0 %copy-start.4 = (f32[128,64]{0,1:T(8,128)}, f32[128,64]{0,1:T(8,128)S(1)}, u32[]{:S(2)}) copy-start(f32[128,64]{0,1:T(8,128)S(1)} %get-tuple-element.18) | copy-start | bytes 98308
  100.3 4.8 %copy-start.13 = (f32[128]{0:T(128)}, f32[128]{0:T(128)S(1)}, u32[]{:S(2)}) copy-start(f32[128]{0:T(128)S(1)} %add_rsqrt_fusion) | copy-start | bytes 1540
  105.0 0.6 copy-start.8
  114.4 31.1 %copy-start.2 = (bf16[128,4096]{1,0:T(8,128)(2,1)S(1)}, bf16[128,4096]{1,0:T(8,128)(2,1)}, u32[]{:S(2)}) copy-start(bf16[128,4096]{1,0:T(8,128)(2,1)} %all-gather.3.cloned.1.call-done) | copy-start | bytes 3145732
  144.5 7.0 %collective-permute-start.7 = (bf16[1024,4,128]{0,2,1:T(8,128)(2,1)}, bf16[1024,4,128]{0,2,1:T(8,128)(2,1)S(1)}, u32[]{:S(2)}, u32[]{:S(2)}) collective-permute-start(bf16[1024,4,128]{0,2,1:T(8,128)(2,1)} %all-gather.5.cloned.1.call-done), channel_id=1, source_target_pairs={{0,1},{1,0},{2,3},{3,2},{4,5},{5,4},{6,7},{7,6},{8,9},{9,8},{10,11... | collective-permute-start | bytes 3145736 | tf_op jit(solution)/shard_map/ppermute | solution.py:23
  145.5 5.9 %copy-start.5 = (f32[128,64]{0,1:T(8,128)S(1)}, f32[128,64]{0,1:T(8,128)}, u32[]{:S(2)}) copy-start(f32[128,64]{0,1:T(8,128)} %copy-done.4) | copy-start | bytes 98308
  145.5 6.0 %copy-start.17 = (bf16[1024,4,128]{0,2,1:T(8,128)(2,1)S(1)}, bf16[1024,4,128]{0,2,1:T(8,128)(2,1)}, u32[]{:S(2)}) copy-start(bf16[1024,4,128]{0,2,1:T(8,128)(2,1)} %all-gather.5.cloned.1.call-done) | copy-start | bytes 3145732
Sparse Core Ops, SparseCore 0:
  80.4 18.2 all-gather.2
  105.0 39.3 all-gather.4

commit v9 on v8

--- a/solution.py
+++ b/solution.py
@@ -224,7 +224,6 @@
     own_positions = row_positions(
         ctx_index * TOK + jnp.arange(TOK, dtype=jnp.int32), slice_order, TOK
     )
-    own_doc = jnp.take(doc_ids, own_positions)
     kv_heads = w_query.shape[1]
     groups = w_query.shape[2]
     queries = jnp.einsum(
@@ -243,7 +242,15 @@
     values_every = jnp.where(tp_index == 0, partner_all, gathered)
     key_count = keys_every.shape[0]
     key_pos = row_positions(jnp.arange(key_count, dtype=jnp.int32), slice_order, TOK)
-    key_doc = jnp.take(doc_ids, key_pos)
+    doc_slices = doc_ids.reshape(2 * shards, TOK // 2)
+    slice_ids = jnp.stack([slice_order, 2 * shards - 1 - slice_order], axis=1)
+    slice_hot = slice_ids[:, :, None] == jnp.arange(2 * shards, dtype=jnp.int32)[None, None, :]
+    key_doc = jnp.sum(
+        jnp.where(slice_hot[..., None], doc_slices[None, None], 0), axis=2
+    ).reshape(shards * TOK)
+    own_doc = jnp.sum(
+        jnp.where((shard_ids == ctx_index)[:, None], key_doc.reshape(shards, TOK), 0), axis=0
+    )
     allowed_now = (key_pos[None, :] <= own_positions[:, None]) & (
         key_doc[None, :] == own_doc[:, None]
     )

time: 164 us -> 164 us (level)
  local copies, waits for them, and re-layouts: 42.1 us -> 33.2 us
  waiting for transfers between devices: 54.9 us -> 63.6 us
    gather x2 -> x0, local copies, waits for them, and re-layouts: 9.79 us -> none  [the longest x1 8.81 us: local(): key_doc = jnp.take(doc_ids, key_pos)]
    all_gather x1, waiting for transfers between devices: 7.36 us -> 15 us  [local(): gathered = lax.all_gather(own_half, 'ctx', axis=0, tiled=True)]
    select_n x4 -> x0, other arithmetic: 1.86 us -> none  [the longest x2 1.29 us: local(): key_doc = jnp.take(doc_ids, key_pos)]
    unnamed x37 -> x33, local copies, waits for them, and re-layouts: 22.3 us -> 21.8 us
  transfers between devices with their start and end apart: 11 -> 11, of which waited for: 10 -> 10; matrix products, arithmetic and copies ran while one was open for 31% -> 26% of each run, Pallas kernels for 0% -> 0%
where the time goes in v9:
time: 164 us; the launch traced here: 162 us
  waiting for transfers between devices  63.6 us (39%)
  local copies, waits for them, and re-layouts  33.2 us (20%)
  matrix products  19.3 us (12%)
  starting transfers between devices  16.9 us (10%)
  other arithmetic  15.4 us (9%)
  between operations  13.9 us (8%)
    ppermute x8, waiting for transfers between devices, swapped(): lax.ppermute(value, axis, [(i, i ^ 1 << stride) for i in range(lax.axis_s...  28.4 us
    unnamed x33, local copies, waits for them, and re-layouts  21.8 us
    all_gather x1, waiting for transfers between devices, local(): gathered = lax.all_gather(own_half, 'ctx', axis=0, tiled=True)  15 us
    unnamed x3, matrix products  11.6 us
    ppermute x8, starting transfers between devices, swapped(): lax.ppermute(value, axis, [(i, i ^ 1 << stride) for i in range(lax.axis_s...  10.6 us
    all_to_all x1, waiting for transfers between devices, local(): lax.all_to_all(blocks, 'ctx', split_axis=0, concat_axis=0, tiled=True)  10.4 us
    all_gather x1, waiting for transfers between devices, local(): full_rows = lax.all_gather(embeds, ('vis', 'tp'), axis=1, tiled=True)  9.74 us
    squeeze x1, local copies, waits for them, and re-layouts, local(): w_keyval[0]  7.59 us
  transfers between devices with their start and end apart: 11, of which 10 were waited for; matrix products, arithmetic and copies ran while one was open for 26% of the time, Pallas kernels for 0%

profile of v9, /device:TPU:0, one launch (start us, length us, event | category | flops | bytes accessed | tf_op | source)
XLA Modules:
  0.0 162.4 jit_solution(7742216306771705617)
XLA Ops:
  6.5 1.2 convert_reduce_fusion
  7.8 1.2 fusion.42
  9.0 1.9 %fusion.48 = f32[128,960]{0,1:S(1)} fusion(bf16[1280,960]{0,1:T(8,128)(2,1)S(1)} %bitcast.169, bf16[128,1280]{1,0:T(8,128)(2,1)} %param.17, f32[1280]{0:T(1024)} %param.19, f32[1280]{0:T(1024)} %param.18, f32[128]{0:T(128)S(1)} %add_rsqrt_fusion.2, f32[128]{0:T(128)S(1)} %broadcast_multiply_fusion.1), kind=kOutput, calls=%fused_computation.51 | convolution fusion | flops 315555840 | bytes 3288064
  11.0 0.1 broadcast_compare_fusion
  11.1 0.3 fusion.110
  11.4 0.3 copy-done.2
  11.7 1.7 %fusion.22 = f32[128,1280,1]{1,0,2:T(8,128)S(1)} fusion(bf16[4,80,1280]{2,1,0:T(8,128)(2,1)} %param.21, f32[4,128,128]{1,2,0:T(8,128)S(1)} %get-tuple-element.20, f32[4,128]{1,0:T(4,128)S(1)} %get-tuple-element.19, bf16[128,3,4,80]{0,3,2,1:T(8,128)(2,1)} %copy-done.2, f32[128,4]{0,1:T(4,128)S(1)} %bitcast.189), kind=kOutput, calls=%fused_computation.28 | convolution fusion | flops 115556352 | bytes 1822720 | tf_op jit(solution)/shard_map/phd,hdf->pf/dot_general | solution.py:159
  13.5 0.6 collective-permute-start
  14.2 0.7 fusion.108
  15.0 0.4 collective-permute-done
  15.4 1.0 bitcast_add_fusion
  16.5 2.9 %collective-permute-start.1 = (f32[1,32,1280]{2,1,0:T(8,128)S(1)}, f32[1,32,1280]{2,1,0:T(8,128)S(1)}, u32[]{:S(2)}, u32[]{:S(2)}) collective-permute-start(f32[1,32,1280]{2,1,0:T(8,128)S(1)} %select_bitcast_fusion.3), channel_id=1, source_target_pairs={{0,16},{16,0},{1,17},{17,1},{2,18},{18,2},{3,19},{19,3},{4,20},{20... | collective-permute-start | bytes 491528 | tf_op jit(solution)/shard_map/ppermute | solution.py:23
  19.4 0.7 fusion.67
  20.1 3.8 %collective-permute-done.1 = f32[1,32,1280]{2,1,0:T(8,128)S(1)} collective-permute-done((f32[1,32,1280]{2,1,0:T(8,128)S(1)}, f32[1,32,1280]{2,1,0:T(8,128)S(1)}, u32[]{:S(2)}, u32[]{:S(2)}) %collective-permute-start.1) | collective-permute-done | bytes 163872 | tf_op jit(solution)/shard_map/ppermute | solution.py:23
  23.9 1.0 fusion.107
  24.9 0.2 multiply_reduce_fusion
  25.2 0.1 add_convert_fusion.1
  25.3 1.8 %collective-permute-start.2 = (bf16[1,8,5120]{2,1,0:T(8,128)(2,1)S(1)}, bf16[1,8,5120]{2,1,0:T(8,128)(2,1)S(1)}, u32[]{:S(2)}, u32[]{:S(2)}) collective-permute-start(bf16[1,8,5120]{2,1,0:T(8,128)(2,1)S(1)} %broadcast_in_dim_reshape.2), channel_id=1, source_target_pairs={{0,16},{16,0},{1,17},{17,1},{2,18},{18,2},{3,19},{19,3},{4,20},{20... | collective-permute-start | bytes 245768 | tf_op jit(solution)/shard_map/ppermute | solution.py:23
  27.1 0.1 select_reduce_fusion.3
  27.3 2.5 %collective-permute-done.2 = bf16[1,8,5120]{2,1,0:T(8,128)(2,1)S(1)} collective-permute-done((bf16[1,8,5120]{2,1,0:T(8,128)(2,1)S(1)}, bf16[1,8,5120]{2,1,0:T(8,128)(2,1)S(1)}, u32[]{:S(2)}, u32[]{:S(2)}) %collective-permute-start.2) | collective-permute-done | bytes 81952 | tf_op jit(solution)/shard_map/ppermute | solution.py:23
  30.0 1.4 collective-permute-done.3
  31.4 0.2 convolution_convert_fusion
  31.6 0.7 copy.139
  32.3 6.1 %all-to-all-start = ((bf16[8,32,640]{2,1,0:T(8,128)(2,1)}), bf16[8,32,640]{2,1,0:T(8,128)(2,1)S(1)}, u32[]{:S(2)}, u32[]{:S(2)}) async-start(bf16[8,32,640]{2,1,0:T(8,128)(2,1)} %bitcast.167), calls=%async_computation | async-start | bytes 655360 | tf_op jit(solution)/shard_map/all_to_all | solution.py:198
  38.6 10.4 %all-to-all-done = bf16[8,32,640]{2,1,0:T(8,128)(2,1)S(1)} async-done(((bf16[8,32,640]{2,1,0:T(8,128)(2,1)}), bf16[8,32,640]{2,1,0:T(8,128)(2,1)S(1)}, u32[]{:S(2)}, u32[]{:S(2)}) %all-to-all-start) | async-done | bytes 327712 | tf_op jit(solution)/shard_map/all_to_all | solution.py:198
  49.0 0.1 reshape.697
  49.1 0.1 copy.140
  49.3 1.9 %fusion.12 = f32[4,2,32,1024]{3,2,1,0:T(8,128)S(1)} fusion(bf16[4,2,32,640]{3,2,1,0:T(8,128)(2,1)S(1)} %dot_general.46, bf16[640,1024]{1,0:T(8,128)(2,1)} %param.24), kind=kOutput, calls=%fused_computation.16 | convolution fusion | flops 335544320 | bytes 2686976 | tf_op jit(solution)/shard_map/dot_general | solution.py:202
  51.3 1.5 collective-permute-start.4
  53.0 10.2 %collective-permute-done.4 = f32[4,32,1024]{2,1,0:T(8,128)S(1)} collective-permute-done((f32[4,32,1024]{2,1,0:T(8,128)S(1)}, f32[4,32,1024]{2,1,0:T(8,128)S(1)}, u32[]{:S(2)}, u32[]{:S(2)}) %collective-permute-start.4) | collective-permute-done | bytes 524320 | tf_op jit(solution)/shard_map/ppermute | solution.py:23
  63.2 0.1 fusion.47
  63.2 0.7 select_bitcast_fusion.2
  64.0 0.5 collective-permute-start.5
  64.6 0.1 and.181
  64.7 0.3 fusion.109
  65.0 5.7 %collective-permute-done.5 = f32[2,32,1024]{2,1,0:T(8,128)} collective-permute-done((f32[2,32,1024]{2,1,0:T(8,128)}, f32[2,32,1024]{2,1,0:T(8,128)}, u32[]{:S(2)}, u32[]{:S(2)}) %collective-permute-start.5) | collective-permute-done | bytes 262176 | tf_op jit(solution)/shard_map/ppermute | solution.py:23
  70.7 1.0 fusion.64
  71.7 3.2 %collective-permute-start.6 = (f32[1,32,1024]{2,1,0:T(8,128)S(1)}, f32[1,32,1024]{2,1,0:T(8,128)S(1)}, u32[]{:S(2)}, u32[]{:S(2)}) collective-permute-start(f32[1,32,1024]{2,1,0:T(8,128)S(1)} %select_bitcast_fusion.4), channel_id=1, source_target_pairs={{0,8},{2,10},{4,12},{6,14},{8,0},{10,2},{12,4},{14,6},{1,9},{3,11}... | collective-permute-start | bytes 393224 | tf_op jit(solution)/shard_map/ppermute | solution.py:23
  74.9 4.4 %collective-permute-done.6 = f32[1,32,1024]{2,1,0:T(8,128)S(1)} collective-permute-done((f32[1,32,1024]{2,1,0:T(8,128)S(1)}, f32[1,32,1024]{2,1,0:T(8,128)S(1)}, u32[]{:S(2)}, u32[]{:S(2)}) %collective-permute-start.6) | collective-permute-done | bytes 131104 | tf_op jit(solution)/shard_map/ppermute | solution.py:23
  79.3 1.0 fusion.18
  80.3 0.2 all-gather.5.cloned.1.call-start
  80.5 7.6 %copy.119 = bf16[4096,4,128]{0,2,1:T(8,128)(2,1)} copy(bf16[4096,4,128]{2,1,0:T(4,128)(2,1)} %bitcast.175) | data formatting | bytes 8388608 | tf_op jit(solution)/shard_map/squeeze | solution.py:234
  88.2 0.1 select_reduce_fusion.5
  88.3 0.5 fusion.105
  88.8 0.2 multiply_cosine_fusion
  89.0 9.7 %all-gather.3.cloned.1.call-done = bf16[128,4096]{1,0:T(8,128)(2,1)} async-done(((bf16[128,1024]{1,0:T(8,128)(2,1)}), bf16[128,4096]{1,0:T(8,128)(2,1)}) %all-gather.3.cloned.1.call-update) | async-done | bytes 1048592 | tf_op jit(solution)/shard_map/all_gather | solution.py:217
  98.7 1.5 fusion.3
  100.3 3.8 %fusion.56 = f32[128,512]{0,1:S(1)} fusion(bf16[4096,512]{0,1:T(8,128)(2,1)} %bitcast.176, bf16[128,4096]{1,0:T(8,128)(2,1)} %all-gather.3.cloned.1.call-done, f32[4096]{0:T(1024)S(1)} %copy-done.6, f32[128]{0:T(128)S(1)} %add_rsqrt_fusion), kind=kOutput, calls=%fused_computation.62 | convolution fusion | flops 538968064 | bytes 5521920
  104.2 0.7 fusion.58
  105.0 0.1 copy.100
  105.1 0.1 select_reduce_fusion
  105.3 0.7 eq.200
  105.9 0.1 select_reduce_fusion.4
  106.0 0.6 eq.204
  106.6 21.4 %copy.120 = bf16[4096,4,2,128]{0,3,2,1:T(8,128)(2,1)} copy(bf16[4096,4,2,128]{3,2,1,0:T(2,128)(2,1)} %param.32) | data formatting | bytes 16777216 | tf_op args[15]
  128.1 0.7 select_reduce_fusion.1
  128.8 0.6 fusion.91
  129.4 15.0 %all-gather.5.cloned.1.call-done = bf16[1024,4,128]{0,2,1:T(8,128)(2,1)} async-done(((bf16[128,4,128]{0,2,1:T(8,128)(2,1)}), bf16[1024,4,128]{0,2,1:T(8,128)(2,1)}) %all-gather.5.cloned.1.call-update) | async-done | bytes 1048592 | tf_op jit(solution)/shard_map/all_gather | solution.py:239
  144.4 1.0 compare_and_fusion
  145.5 5.9 %fusion.54 = f32[128,1024]{0,1:S(1)} fusion(bf16[4096,1024]{0,1:T(8,128)(2,1)} %bitcast.170, bf16[128,4096]{1,0:T(8,128)(2,1)S(1)} %copy-done.1, f32[4096]{0:T(1024)S(1)} %copy-done.6, f32[128]{0:T(128)} %copy-done.12), kind=kOutput, calls=%fused_computation.61 | convolution fusion | flops 1075838976 | bytes 9978368
  151.5 1.0 fusion.2
  152.5 0.9 fusion
  153.4 1.3 fusion.35
  154.7 0.9 copy.124
  (77 shorter events, 1.6 us)
Async XLA Ops:
  6.5 2.5 %copy-start = (bf16[1280,3,4,80]{0,3,2,1:T(8,128)(2,1)S(1)}, bf16[1280,3,4,80]{0,3,2,1:T(8,128)(2,1)}, u32[]{:S(2)}) copy-start(bf16[1280,3,4,80]{0,3,2,1:T(8,128)(2,1)} %param.20) | copy-start | bytes 7372804
  6.5 4.4 %copy-start.13 = (s32[128]{0:T(128)S(1)}, s32[128]{0:T(128)}, u32[]{:S(2)}) copy-start(s32[128]{0:T(128)} %param.26) | copy-start | bytes 1540
  6.5 7.5 %copy-start.11 = (s32[256]{0:T(256)S(1)}, s32[256]{0:T(256)}, u32[]{:S(2)}) copy-start(s32[256]{0:T(256)} %param.27) | copy-start | bytes 3076
  6.5 7.7 %copy-start.7 = (s32[8]{0:T(128)S(1)}, s32[8]{0:T(128)}, u32[]{:S(2)}) copy-start(s32[8]{0:T(128)} %param.28) | copy-start | bytes 100
  10.9 14.2 %copy-start.8 = (f32[1280]{0:T(1024)S(1)}, f32[1280]{0:T(1024)}, u32[]{:S(2)}) copy-start(f32[1280]{0:T(1024)} %param.23) | copy-start | bytes 15364
  10.9 14.2 %copy-start.9 = (f32[1280]{0:T(1024)S(1)}, f32[1280]{0:T(1024)}, u32[]{:S(2)}) copy-start(f32[1280]{0:T(1024)} %param.22) | copy-start | bytes 15364
  11.0 0.7 copy-start.2
  13.4 25.2 %copy-start.14 = (s32[8,2]{0,1:T(2,128)S(1)}, s32[8,2]{0,1:T(2,128)}, u32[]{:S(2)}) copy-start(s32[8,2]{0,1:T(2,128)} %param.25) | copy-start | bytes 196
  13.5 1.9 %collective-permute-start = (f32[1,64,1280]{2,1,0:T(8,128)S(1)}, f32[1,64,1280]{2,1,0:T(8,128)}, u32[]{:S(2)}, u32[]{:S(2)}) collective-permute-start(f32[1,64,1280]{2,1,0:T(8,128)S(1)} %select_bitcast_fusion.1), channel_id=1, source_target_pairs={{0,1},{1,0},{2,3},{3,2},{4,5},{5,4},{6,7},{7,6},{8,9},{9,8},{10,11... | collective-permute-start | bytes 983048 | tf_op jit(solution)/shard_map/ppermute | solution.py:23
  16.5 7.4 %collective-permute-start.1 = (f32[1,32,1280]{2,1,0:T(8,128)S(1)}, f32[1,32,1280]{2,1,0:T(8,128)S(1)}, u32[]{:S(2)}, u32[]{:S(2)}) collective-permute-start(f32[1,32,1280]{2,1,0:T(8,128)S(1)} %select_bitcast_fusion.3), channel_id=1, source_target_pairs={{0,16},{16,0},{1,17},{17,1},{2,18},{18,2},{3,19},{19,3},{4,20},{20... | collective-permute-start | bytes 491528 | tf_op jit(solution)/shard_map/ppermute | solution.py:23
  25.3 4.5 %collective-permute-start.2 = (bf16[1,8,5120]{2,1,0:T(8,128)(2,1)S(1)}, bf16[1,8,5120]{2,1,0:T(8,128)(2,1)S(1)}, u32[]{:S(2)}, u32[]{:S(2)}) collective-permute-start(bf16[1,8,5120]{2,1,0:T(8,128)(2,1)S(1)} %broadcast_in_dim_reshape.2), channel_id=1, source_target_pairs={{0,16},{16,0},{1,17},{17,1},{2,18},{18,2},{3,19},{19,3},{4,20},{20... | collective-permute-start | bytes 245768 | tf_op jit(solution)/shard_map/ppermute | solution.py:23
  29.9 1.5 collective-permute-start.3
  32.3 16.7 %all-to-all-start = ((bf16[8,32,640]{2,1,0:T(8,128)(2,1)}), bf16[8,32,640]{2,1,0:T(8,128)(2,1)S(1)}, u32[]{:S(2)}, u32[]{:S(2)}) async-start(bf16[8,32,640]{2,1,0:T(8,128)(2,1)} %bitcast.167), calls=%async_computation | async-start | bytes 655360 | tf_op jit(solution)/shard_map/all_to_all | solution.py:198
  38.4 60.3 %all-gather.3.cloned.1.call-start = ((), (), s32[]{:S(2)}) async-start(), calls=%async_computation.1 | async-start | bytes 1310720 | tf_op jit(solution)/shard_map/all_gather | solution.py:217
  49.3 30.0 %copy-start.5 = (bf16[128,1024]{1,0:T(8,128)(2,1)S(1)}, bf16[128,1024]{1,0:T(8,128)(2,1)}, u32[]{:S(2)}) copy-start(bf16[128,1024]{1,0:T(8,128)(2,1)} %param.30) | copy-start | bytes 786436
  51.3 11.9 %collective-permute-start.4 = (f32[4,32,1024]{2,1,0:T(8,128)S(1)}, f32[4,32,1024]{2,1,0:T(8,128)S(1)}, u32[]{:S(2)}, u32[]{:S(2)}) collective-permute-start(f32[4,32,1024]{2,1,0:T(8,128)S(1)} %select_bitcast_fusion), channel_id=1, source_target_pairs={{0,2},{2,0},{4,6},{6,4},{8,10},{10,8},{12,14},{14,12},{1,3},{3,1},... | collective-permute-start | bytes 1572872 | tf_op jit(solution)/shard_map/ppermute | solution.py:23
  64.0 6.7 %collective-permute-start.5 = (f32[2,32,1024]{2,1,0:T(8,128)}, f32[2,32,1024]{2,1,0:T(8,128)}, u32[]{:S(2)}, u32[]{:S(2)}) collective-permute-start(f32[2,32,1024]{2,1,0:T(8,128)} %select_bitcast_fusion.2), channel_id=1, source_target_pairs={{0,4},{2,6},{4,0},{6,2},{8,12},{10,14},{12,8},{14,10},{1,5},{3,7},... | collective-permute-start | bytes 786440 | tf_op jit(solution)/shard_map/ppermute | solution.py:23
  71.7 7.6 %collective-permute-start.6 = (f32[1,32,1024]{2,1,0:T(8,128)S(1)}, f32[1,32,1024]{2,1,0:T(8,128)S(1)}, u32[]{:S(2)}, u32[]{:S(2)}) collective-permute-start(f32[1,32,1024]{2,1,0:T(8,128)S(1)} %select_bitcast_fusion.4), channel_id=1, source_target_pairs={{0,8},{2,10},{4,12},{6,14},{8,0},{10,2},{12,4},{14,6},{1,9},{3,11}... | collective-permute-start | bytes 393224 | tf_op jit(solution)/shard_map/ppermute | solution.py:23
  80.3 64.1 %all-gather.5.cloned.1.call-start = ((), (), s32[]{:S(2)}) async-start(), calls=%async_computation.2 | async-start | bytes 1179648 | tf_op jit(solution)/shard_map/all_gather | solution.py:239
  80.5 19.7 %copy-start.6 = (f32[4096]{0:T(1024)S(1)}, f32[4096]{0:T(1024)}, u32[]{:S(2)}) copy-start(f32[4096]{0:T(1024)} %param.31) | copy-start | bytes 49156
  88.1 16.7 %copy-start.10 = (s32[1024]{0:T(1024)S(1)}, s32[1024]{0:T(1024)}, u32[]{:S(2)}) copy-start(s32[1024]{0:T(1024)} %param.29) | copy-start | bytes 12292
  89.0 17.0 %copy-start.3 = (f32[128,64]{0,1:T(8,128)}, f32[128,64]{0,1:T(8,128)S(1)}, u32[]{:S(2)}) copy-start(f32[128,64]{0,1:T(8,128)S(1)} %get-tuple-element.16) | copy-start | bytes 98308
  100.2 5.8 %copy-start.12 = (f32[128]{0:T(128)}, f32[128]{0:T(128)S(1)}, u32[]{:S(2)}) copy-start(f32[128]{0:T(128)S(1)} %add_rsqrt_fusion) | copy-start | bytes 1540
  106.6 38.8 %copy-start.1 = (bf16[128,4096]{1,0:T(8,128)(2,1)S(1)}, bf16[128,4096]{1,0:T(8,128)(2,1)}, u32[]{:S(2)}) copy-start(bf16[128,4096]{1,0:T(8,128)(2,1)} %all-gather.3.cloned.1.call-done) | copy-start | bytes 3145732
  144.4 7.0 %collective-permute-start.7 = (bf16[1024,4,128]{0,2,1:T(8,128)(2,1)}, bf16[1024,4,128]{0,2,1:T(8,128)(2,1)S(1)}, u32[]{:S(2)}, u32[]{:S(2)}) collective-permute-start(bf16[1024,4,128]{0,2,1:T(8,128)(2,1)} %all-gather.5.cloned.1.call-done), channel_id=1, source_target_pairs={{0,1},{1,0},{2,3},{3,2},{4,5},{5,4},{6,7},{7,6},{8,9},{9,8},{10,11... | collective-permute-start | bytes 3145736 | tf_op jit(solution)/shard_map/ppermute | solution.py:23
  145.5 5.9 %copy-start.4 = (f32[128,64]{0,1:T(8,128)S(1)}, f32[128,64]{0,1:T(8,128)}, u32[]{:S(2)}) copy-start(f32[128,64]{0,1:T(8,128)} %copy-done.3) | copy-start | bytes 98308
  145.5 6.0 %copy-start.15 = (bf16[1024,4,128]{0,2,1:T(8,128)(2,1)S(1)}, bf16[1024,4,128]{0,2,1:T(8,128)(2,1)}, u32[]{:S(2)}) copy-start(bf16[1024,4,128]{0,2,1:T(8,128)(2,1)} %all-gather.5.cloned.1.call-done) | copy-start | bytes 3145732
Sparse Core Ops, SparseCore 0:
  80.4 18.2 all-gather.2
  105.0 39.3 all-gather.4

commit v10 on v9

--- a/solution.py
+++ b/solution.py
@@ -226,22 +226,19 @@
     )
     kv_heads = w_query.shape[1]
     groups = w_query.shape[2]
-    queries = jnp.einsum(
-        "td,dhgk->thgk", normed_rows, w_query, preferred_element_type=jnp.float32
-    )
-    queries = rotate(queries, own_positions).astype(jnp.bfloat16)
     projected_half = jnp.einsum(
         "td,dhk->thk", normed_rows, w_keyval[0], preferred_element_type=jnp.float32
     )
     own_half = jnp.where(
         tp_index == 0, rotate(projected_half, own_positions), projected_half
     ).astype(jnp.bfloat16)
+    query_weights, own_half = lax.optimization_barrier((w_query, own_half))
     gathered = lax.all_gather(own_half, "ctx", axis=0, tiled=True)
-    partner_all = swapped(gathered, "tp", 0)
-    keys_every = jnp.where(tp_index == 0, gathered, partner_all)
-    values_every = jnp.where(tp_index == 0, partner_all, gathered)
-    key_count = keys_every.shape[0]
-    key_pos = row_positions(jnp.arange(key_count, dtype=jnp.int32), slice_order, TOK)
+    queries = jnp.einsum(
+        "td,dhgk->thgk", normed_rows, query_weights, preferred_element_type=jnp.float32
+    )
+    queries = rotate(queries, own_positions).astype(jnp.bfloat16)
+    key_pos = row_positions(jnp.arange(shards * TOK, dtype=jnp.int32), slice_order, TOK)
     doc_slices = doc_ids.reshape(2 * shards, TOK // 2)
     slice_ids = jnp.stack([slice_order, 2 * shards - 1 - slice_order], axis=1)
     slice_hot = slice_ids[:, :, None] == jnp.arange(2 * shards, dtype=jnp.int32)[None, None, :]
@@ -254,6 +251,11 @@
     allowed_now = (key_pos[None, :] <= own_positions[:, None]) & (
         key_doc[None, :] == own_doc[:, None]
     )
+    queries, allowed_now, gathered = lax.optimization_barrier((queries, allowed_now, gathered))
+    partner_all = swapped(gathered, "tp", 0)
+    keys_every = jnp.where(tp_index == 0, gathered, partner_all)
+    values_every = jnp.where(tp_index == 0, partner_all, gathered)
+    key_count = keys_every.shape[0]
     scores_now = jnp.einsum(
         "qkgd,nkd->kgqn", queries, keys_every, preferred_element_type=jnp.float32
     ) / math.sqrt(HD)

time: 164 us -> 161 us (0.982)
  other arithmetic: 15.4 us -> 13.7 us
    unnamed x33 -> x34, local copies, waits for them, and re-layouts: 21.8 us -> 0.35 us
    optimization_barrier x0 -> x1, local copies, waits for them, and re-layouts: none -> 21.4 us  [local(): query_weights, own_half = lax.optimization_barrier((w_query, own_half))]
    all_gather x1, waiting for transfers between devices: 15 us -> 10.6 us  [local(): gathered = lax.all_gather(own_half, 'ctx', axis=0, tiled=True)]
    ppermute x8, waiting for transfers between devices: 28.4 us -> 31.3 us  [swapped(): lax.ppermute(value, axis, [(i, i ^ 1 << stride) for i in range(lax.axis_s...]
  transfers between devices with their start and end apart: 11 -> 11, of which waited for: 10 -> 11; matrix products, arithmetic and copies ran while one was open for 26% -> 25% of each run, Pallas kernels for 0% -> 0%
where the time goes in v10:
time: 161 us; the launch traced here: 159 us
  waiting for transfers between devices  62.3 us (39%)
  local copies, waits for them, and re-layouts  32.1 us (20%)
  matrix products  20.5 us (13%)
  starting transfers between devices  16.9 us (10%)
  between operations  13.9 us (9%)
  other arithmetic  13.7 us (9%)
    ppermute x8, waiting for transfers between devices, swapped(): lax.ppermute(value, axis, [(i, i ^ 1 << stride) for i in range(lax.axis_s...  31.3 us
    optimization_barrier x1, local copies, waits for them, and re-layouts, local(): query_weights, own_half = lax.optimization_barrier((w_query, own_half))  21.4 us
    unnamed x3, matrix products  11.6 us
    ppermute x8, starting transfers between devices, swapped(): lax.ppermute(value, axis, [(i, i ^ 1 << stride) for i in range(lax.axis_s...  10.6 us
    all_gather x1, waiting for transfers between devices, local(): gathered = lax.all_gather(own_half, 'ctx', axis=0, tiled=True)  10.6 us
    all_to_all x1, waiting for transfers between devices, local(): lax.all_to_all(blocks, 'ctx', split_axis=0, concat_axis=0, tiled=True)  10.4 us
    all_gather x1, waiting for transfers between devices, local(): full_rows = lax.all_gather(embeds, ('vis', 'tp'), axis=1, tiled=True)  9.98 us
    squeeze x1, local copies, waits for them, and re-layouts, local(): w_keyval[0]  7.6 us
  transfers between devices with their start and end apart: 11, of which 11 were waited for; matrix products, arithmetic and copies ran while one was open for 25% of the time, Pallas kernels for 0%

profile of v10, /device:TPU:0, one launch (start us, length us, event | category | flops | bytes accessed | tf_op | source)
XLA Modules:
  0.0 159.4 jit_solution(6405909331193901018)
XLA Ops:
  6.5 1.2 convert_reduce_fusion
  7.8 1.2 fusion.42
  9.0 1.9 %fusion.48 = f32[128,960]{0,1:S(1)} fusion(bf16[1280,960]{0,1:T(8,128)(2,1)S(1)} %bitcast.170, bf16[128,1280]{1,0:T(8,128)(2,1)} %param.17, f32[1280]{0:T(1024)} %param.19, f32[1280]{0:T(1024)} %param.18, f32[128]{0:T(128)S(1)} %add_rsqrt_fusion.2, f32[128]{0:T(128)S(1)} %broadcast_multiply_fusion.1), kind=kOutput, calls=%fused_computation.51 | convolution fusion | flops 315555840 | bytes 3288064
  11.0 0.1 broadcast_compare_fusion
  11.1 0.3 fusion.106
  11.4 0.3 copy-done.3
  11.7 1.7 %fusion.22 = f32[128,1280,1]{1,0,2:T(8,128)S(1)} fusion(bf16[4,80,1280]{2,1,0:T(8,128)(2,1)} %param.21, f32[4,128,128]{1,2,0:T(8,128)S(1)} %get-tuple-element.30, f32[4,128]{1,0:T(4,128)S(1)} %get-tuple-element.29, bf16[128,3,4,80]{0,3,2,1:T(8,128)(2,1)} %copy-done.3, f32[128,4]{0,1:T(4,128)S(1)} %bitcast.190), kind=kOutput, calls=%fused_computation.28 | convolution fusion | flops 115556352 | bytes 1822720 | tf_op jit(solution)/shard_map/phd,hdf->pf/dot_general | solution.py:159
  13.5 0.6 collective-permute-start
  14.2 0.7 fusion.104
  15.0 0.4 collective-permute-done
  15.4 1.0 bitcast_add_fusion
  16.5 2.9 %collective-permute-start.1 = (f32[1,32,1280]{2,1,0:T(8,128)S(1)}, f32[1,32,1280]{2,1,0:T(8,128)S(1)}, u32[]{:S(2)}, u32[]{:S(2)}) collective-permute-start(f32[1,32,1280]{2,1,0:T(8,128)S(1)} %select_bitcast_fusion.3), channel_id=1, source_target_pairs={{0,16},{16,0},{1,17},{17,1},{2,18},{18,2},{3,19},{19,3},{4,20},{20... | collective-permute-start | bytes 491528 | tf_op jit(solution)/shard_map/ppermute | solution.py:23
  19.4 0.7 fusion.64
  20.1 3.8 %collective-permute-done.1 = f32[1,32,1280]{2,1,0:T(8,128)S(1)} collective-permute-done((f32[1,32,1280]{2,1,0:T(8,128)S(1)}, f32[1,32,1280]{2,1,0:T(8,128)S(1)}, u32[]{:S(2)}, u32[]{:S(2)}) %collective-permute-start.1) | collective-permute-done | bytes 163872 | tf_op jit(solution)/shard_map/ppermute | solution.py:23
  23.9 1.0 fusion.103
  24.9 0.2 multiply_reduce_fusion
  25.2 0.1 add_convert_fusion.1
  25.3 1.8 %collective-permute-start.2 = (bf16[1,8,5120]{2,1,0:T(8,128)(2,1)S(1)}, bf16[1,8,5120]{2,1,0:T(8,128)(2,1)S(1)}, u32[]{:S(2)}, u32[]{:S(2)}) collective-permute-start(bf16[1,8,5120]{2,1,0:T(8,128)(2,1)S(1)} %broadcast_in_dim_reshape.2), channel_id=1, source_target_pairs={{0,16},{16,0},{1,17},{17,1},{2,18},{18,2},{3,19},{19,3},{4,20},{20... | collective-permute-start | bytes 245768 | tf_op jit(solution)/shard_map/ppermute | solution.py:23
  27.1 0.1 select_reduce_fusion.3
  27.3 2.5 %collective-permute-done.2 = bf16[1,8,5120]{2,1,0:T(8,128)(2,1)S(1)} collective-permute-done((bf16[1,8,5120]{2,1,0:T(8,128)(2,1)S(1)}, bf16[1,8,5120]{2,1,0:T(8,128)(2,1)S(1)}, u32[]{:S(2)}, u32[]{:S(2)}) %collective-permute-start.2) | collective-permute-done | bytes 81952 | tf_op jit(solution)/shard_map/ppermute | solution.py:23
  30.0 1.4 collective-permute-done.3
  31.4 0.2 convolution_convert_fusion
  31.6 0.7 copy.139
  32.3 6.1 %all-to-all-start = ((bf16[8,32,640]{2,1,0:T(8,128)(2,1)}), bf16[8,32,640]{2,1,0:T(8,128)(2,1)S(1)}, u32[]{:S(2)}, u32[]{:S(2)}) async-start(bf16[8,32,640]{2,1,0:T(8,128)(2,1)} %bitcast.168), calls=%async_computation | async-start | bytes 655360 | tf_op jit(solution)/shard_map/all_to_all | solution.py:198
  38.6 10.4 %all-to-all-done = bf16[8,32,640]{2,1,0:T(8,128)(2,1)S(1)} async-done(((bf16[8,32,640]{2,1,0:T(8,128)(2,1)}), bf16[8,32,640]{2,1,0:T(8,128)(2,1)S(1)}, u32[]{:S(2)}, u32[]{:S(2)}) %all-to-all-start) | async-done | bytes 327712 | tf_op jit(solution)/shard_map/all_to_all | solution.py:198
  49.0 0.1 reshape.639
  49.1 0.1 copy.140
  49.2 0.1 dot_general.46
  49.3 1.9 %fusion.12 = f32[4,2,32,1024]{3,2,1,0:T(8,128)S(1)} fusion(bf16[4,2,32,640]{3,2,1,0:T(8,128)(2,1)S(1)} %dot_general.46, bf16[640,1024]{1,0:T(8,128)(2,1)} %param.24), kind=kOutput, calls=%fused_computation.16 | convolution fusion | flops 335544320 | bytes 2686976 | tf_op jit(solution)/shard_map/dot_general | solution.py:202
  51.3 1.5 collective-permute-start.4
  53.0 10.2 %collective-permute-done.4 = f32[4,32,1024]{2,1,0:T(8,128)S(1)} collective-permute-done((f32[4,32,1024]{2,1,0:T(8,128)S(1)}, f32[4,32,1024]{2,1,0:T(8,128)S(1)}, u32[]{:S(2)}, u32[]{:S(2)}) %collective-permute-start.4) | collective-permute-done | bytes 524320 | tf_op jit(solution)/shard_map/ppermute | solution.py:23
  63.2 0.1 fusion.47
  63.2 0.7 select_bitcast_fusion.2
  64.0 0.5 collective-permute-start.5
  64.5 0.1 and.170
  64.7 0.3 fusion.105
  65.0 5.7 %collective-permute-done.5 = f32[2,32,1024]{2,1,0:T(8,128)} collective-permute-done((f32[2,32,1024]{2,1,0:T(8,128)}, f32[2,32,1024]{2,1,0:T(8,128)}, u32[]{:S(2)}, u32[]{:S(2)}) %collective-permute-start.5) | collective-permute-done | bytes 262176 | tf_op jit(solution)/shard_map/ppermute | solution.py:23
  70.7 1.0 fusion.61
  71.7 3.2 %collective-permute-start.6 = (f32[1,32,1024]{2,1,0:T(8,128)S(1)}, f32[1,32,1024]{2,1,0:T(8,128)S(1)}, u32[]{:S(2)}, u32[]{:S(2)}) collective-permute-start(f32[1,32,1024]{2,1,0:T(8,128)S(1)} %select_bitcast_fusion.4), channel_id=1, source_target_pairs={{0,8},{2,10},{4,12},{6,14},{8,0},{10,2},{12,4},{14,6},{1,9},{3,11}... | collective-permute-start | bytes 393224 | tf_op jit(solution)/shard_map/ppermute | solution.py:23
  74.9 4.4 %collective-permute-done.6 = f32[1,32,1024]{2,1,0:T(8,128)S(1)} collective-permute-done((f32[1,32,1024]{2,1,0:T(8,128)S(1)}, f32[1,32,1024]{2,1,0:T(8,128)S(1)}, u32[]{:S(2)}, u32[]{:S(2)}) %collective-permute-start.6) | collective-permute-done | bytes 131104 | tf_op jit(solution)/shard_map/ppermute | solution.py:23
  79.3 1.0 fusion.18
  80.3 0.2 all-gather.5.cloned.1.call-start
  80.6 7.6 %copy.117 = bf16[4096,4,128]{0,2,1:T(8,128)(2,1)} copy(bf16[4096,4,128]{2,1,0:T(4,128)(2,1)} %bitcast.176) | data formatting | bytes 8388608 | tf_op jit(solution)/shard_map/squeeze | solution.py:230
  88.2 0.1 copy.119
  88.4 0.1 select_reduce_fusion.5
  88.5 0.2 multiply_cosine_fusion
  88.7 10.0 %all-gather.3.cloned.1.call-done = bf16[128,4096]{1,0:T(8,128)(2,1)} async-done(((bf16[128,1024]{1,0:T(8,128)(2,1)}), bf16[128,4096]{1,0:T(8,128)(2,1)}) %all-gather.3.cloned.1.call-update) | async-done | bytes 1048592 | tf_op jit(solution)/shard_map/all_gather | solution.py:217
  98.7 1.5 fusion.3
  100.3 3.8 %fusion.56 = f32[128,512]{0,1:S(1)} fusion(bf16[4096,512]{0,1:T(8,128)(2,1)} %bitcast.177, bf16[128,4096]{1,0:T(8,128)(2,1)} %all-gather.3.cloned.1.call-done, f32[4096]{0:T(1024)S(1)} %copy-done.7, f32[128]{0:T(128)S(1)} %add_rsqrt_fusion), kind=kOutput, calls=%fused_computation.62 | convolution fusion | flops 538968064 | bytes 5521920
  104.2 0.7 fusion.58
  104.9 0.1 select_reduce_fusion
  105.1 0.1 select_reduce_fusion.4
  105.2 0.1 eq.223
  105.2 0.1 select_reduce_fusion.1
  105.4 1.0 compare_and_fusion
  106.4 21.4 %copy.118 = bf16[4096,4,2,128]{0,3,2,1:T(8,128)(2,1)} copy(bf16[4096,4,2,128]{3,2,1,0:T(2,128)(2,1)} %param.32) | data formatting | bytes 16777216 | tf_op jit(solution)/shard_map/optimization_barrier | solution.py:235
  127.8 5.9 %fusion.54 = f32[128,1024]{0,1:S(1)} fusion(bf16[4096,1024]{0,1:T(8,128)(2,1)} %bitcast.171, bf16[128,4096]{1,0:T(8,128)(2,1)S(1)} %copy-done.1, f32[4096]{0:T(1024)S(1)} %copy-done.7, f32[128]{0:T(128)} %copy-done.13), kind=kOutput, calls=%fused_computation.61 | convolution fusion | flops 1075838976 | bytes 9978368
  133.7 0.1 subtract_convert_fusion
  133.8 10.6 %all-gather.5.cloned.1.call-done = bf16[1024,4,128]{0,2,1:T(8,128)(2,1)} async-done(((bf16[128,4,128]{0,2,1:T(8,128)(2,1)}), bf16[1024,4,128]{0,2,1:T(8,128)(2,1)}) %all-gather.5.cloned.1.call-update) | async-done | bytes 1048592 | tf_op jit(solution)/shard_map/all_gather | solution.py:236
  144.4 2.9 %collective-permute-done.7 = bf16[1024,4,128]{0,2,1:T(8,128)(2,1)S(1)} collective-permute-done((bf16[1024,4,128]{0,2,1:T(8,128)(2,1)}, bf16[1024,4,128]{0,2,1:T(8,128)(2,1)S(1)}, u32[]{:S(2)}, u32[]{:S(2)}) %collective-permute-start.7) | collective-permute-done | bytes 1048608 | tf_op jit(solution)/shard_map/ppermute | solution.py:23
  147.3 2.2 %fusion.2 = (f32[4,2,128]{2,1,0:T(2,128)S(1)}, f32[4,1024,128,2]{2,1,3,0:T(8,128)S(1)}) fusion(pred[128,1024]{0,1:T(8,128)(4,1)} %compare_and_fusion, bf16[128,4,2,128]{0,3,2,1:T(8,128)(2,1)S(1)} %pad_maximum_fusion, bf16[1024,4,128]{0,2,1:T(8,128)(2,1)} %all-gather.5.cloned.1.call-done, bf16[1024,4,128]{0,2,1:T(8,128)(2,1)S(1)} %collective-permute-done.7, ...), kind=kOutput, calls=%fused_computation.5 | convolution fusion | flops 272104448 | bytes 6688769 | tf_op jit(solution)/shard_map/qkgd,nkd->kgqn/dot_general | solution.py:259
  149.6 0.9 fusion
  150.4 1.3 fusion.35
  151.7 0.9 copy.124
  (80 shorter events, 1.6 us)
Async XLA Ops:
  6.5 2.5 %copy-start = (bf16[1280,3,4,80]{0,3,2,1:T(8,128)(2,1)S(1)}, bf16[1280,3,4,80]{0,3,2,1:T(8,128)(2,1)}, u32[]{:S(2)}) copy-start(bf16[1280,3,4,80]{0,3,2,1:T(8,128)(2,1)} %param.20) | copy-start | bytes 7372804
  6.5 4.4 %copy-start.14 = (s32[128]{0:T(128)S(1)}, s32[128]{0:T(128)}, u32[]{:S(2)}) copy-start(s32[128]{0:T(128)} %param.26) | copy-start | bytes 1540
  6.5 7.5 %copy-start.12 = (s32[256]{0:T(256)S(1)}, s32[256]{0:T(256)}, u32[]{:S(2)}) copy-start(s32[256]{0:T(256)} %param.27) | copy-start | bytes 3076
  6.5 7.7 %copy-start.8 = (s32[8]{0:T(128)S(1)}, s32[8]{0:T(128)}, u32[]{:S(2)}) copy-start(s32[8]{0:T(128)} %param.28) | copy-start | bytes 100
  10.9 14.2 %copy-start.9 = (f32[1280]{0:T(1024)S(1)}, f32[1280]{0:T(1024)}, u32[]{:S(2)}) copy-start(f32[1280]{0:T(1024)} %param.23) | copy-start | bytes 15364
  10.9 14.2 %copy-start.10 = (f32[1280]{0:T(1024)S(1)}, f32[1280]{0:T(1024)}, u32[]{:S(2)}) copy-start(f32[1280]{0:T(1024)} %param.22) | copy-start | bytes 15364
  11.0 0.7 copy-start.3
  13.4 25.2 %copy-start.15 = (s32[8,2]{0,1:T(2,128)S(1)}, s32[8,2]{0,1:T(2,128)}, u32[]{:S(2)}) copy-start(s32[8,2]{0,1:T(2,128)} %param.25) | copy-start | bytes 196
  13.5 1.9 %collective-permute-start = (f32[1,64,1280]{2,1,0:T(8,128)S(1)}, f32[1,64,1280]{2,1,0:T(8,128)}, u32[]{:S(2)}, u32[]{:S(2)}) collective-permute-start(f32[1,64,1280]{2,1,0:T(8,128)S(1)} %select_bitcast_fusion.1), channel_id=1, source_target_pairs={{0,1},{1,0},{2,3},{3,2},{4,5},{5,4},{6,7},{7,6},{8,9},{9,8},{10,11... | collective-permute-start | bytes 983048 | tf_op jit(solution)/shard_map/ppermute | solution.py:23
  16.5 7.4 %collective-permute-start.1 = (f32[1,32,1280]{2,1,0:T(8,128)S(1)}, f32[1,32,1280]{2,1,0:T(8,128)S(1)}, u32[]{:S(2)}, u32[]{:S(2)}) collective-permute-start(f32[1,32,1280]{2,1,0:T(8,128)S(1)} %select_bitcast_fusion.3), channel_id=1, source_target_pairs={{0,16},{16,0},{1,17},{17,1},{2,18},{18,2},{3,19},{19,3},{4,20},{20... | collective-permute-start | bytes 491528 | tf_op jit(solution)/shard_map/ppermute | solution.py:23
  25.3 4.5 %collective-permute-start.2 = (bf16[1,8,5120]{2,1,0:T(8,128)(2,1)S(1)}, bf16[1,8,5120]{2,1,0:T(8,128)(2,1)S(1)}, u32[]{:S(2)}, u32[]{:S(2)}) collective-permute-start(bf16[1,8,5120]{2,1,0:T(8,128)(2,1)S(1)} %broadcast_in_dim_reshape.2), channel_id=1, source_target_pairs={{0,16},{16,0},{1,17},{17,1},{2,18},{18,2},{3,19},{19,3},{4,20},{20... | collective-permute-start | bytes 245768 | tf_op jit(solution)/shard_map/ppermute | solution.py:23
  29.9 1.5 collective-permute-start.3
  32.3 16.7 %all-to-all-start = ((bf16[8,32,640]{2,1,0:T(8,128)(2,1)}), bf16[8,32,640]{2,1,0:T(8,128)(2,1)S(1)}, u32[]{:S(2)}, u32[]{:S(2)}) async-start(bf16[8,32,640]{2,1,0:T(8,128)(2,1)} %bitcast.168), calls=%async_computation | async-start | bytes 655360 | tf_op jit(solution)/shard_map/all_to_all | solution.py:198
  38.4 60.3 %all-gather.3.cloned.1.call-start = ((), (), s32[]{:S(2)}) async-start(), calls=%async_computation.1 | async-start | bytes 1310720 | tf_op jit(solution)/shard_map/all_gather | solution.py:217
  49.3 30.0 %copy-start.6 = (bf16[128,1024]{1,0:T(8,128)(2,1)S(1)}, bf16[128,1024]{1,0:T(8,128)(2,1)}, u32[]{:S(2)}) copy-start(bf16[128,1024]{1,0:T(8,128)(2,1)} %param.30) | copy-start | bytes 786436
  51.3 11.9 %collective-permute-start.4 = (f32[4,32,1024]{2,1,0:T(8,128)S(1)}, f32[4,32,1024]{2,1,0:T(8,128)S(1)}, u32[]{:S(2)}, u32[]{:S(2)}) collective-permute-start(f32[4,32,1024]{2,1,0:T(8,128)S(1)} %select_bitcast_fusion), channel_id=1, source_target_pairs={{0,2},{2,0},{4,6},{6,4},{8,10},{10,8},{12,14},{14,12},{1,3},{3,1},... | collective-permute-start | bytes 1572872 | tf_op jit(solution)/shard_map/ppermute | solution.py:23
  64.0 6.7 %collective-permute-start.5 = (f32[2,32,1024]{2,1,0:T(8,128)}, f32[2,32,1024]{2,1,0:T(8,128)}, u32[]{:S(2)}, u32[]{:S(2)}) collective-permute-start(f32[2,32,1024]{2,1,0:T(8,128)} %select_bitcast_fusion.2), channel_id=1, source_target_pairs={{0,4},{2,6},{4,0},{6,2},{8,12},{10,14},{12,8},{14,10},{1,5},{3,7},... | collective-permute-start | bytes 786440 | tf_op jit(solution)/shard_map/ppermute | solution.py:23
  71.7 7.6 %collective-permute-start.6 = (f32[1,32,1024]{2,1,0:T(8,128)S(1)}, f32[1,32,1024]{2,1,0:T(8,128)S(1)}, u32[]{:S(2)}, u32[]{:S(2)}) collective-permute-start(f32[1,32,1024]{2,1,0:T(8,128)S(1)} %select_bitcast_fusion.4), channel_id=1, source_target_pairs={{0,8},{2,10},{4,12},{6,14},{8,0},{10,2},{12,4},{14,6},{1,9},{3,11}... | collective-permute-start | bytes 393224 | tf_op jit(solution)/shard_map/ppermute | solution.py:23
  80.3 64.1 %all-gather.5.cloned.1.call-start = ((), (), s32[]{:S(2)}) async-start(), calls=%async_computation.2 | async-start | bytes 1179648 | tf_op jit(solution)/shard_map/all_gather | solution.py:236
  80.5 7.7 %copy-start.11 = (s32[1024]{0:T(1024)S(1)}, s32[1024]{0:T(1024)}, u32[]{:S(2)}) copy-start(s32[1024]{0:T(1024)} %param.29) | copy-start | bytes 12292
  80.5 19.7 %copy-start.7 = (f32[4096]{0:T(1024)S(1)}, f32[4096]{0:T(1024)}, u32[]{:S(2)}) copy-start(f32[4096]{0:T(1024)} %param.31) | copy-start | bytes 49156
  88.7 16.6 %copy-start.4 = (f32[128,64]{0,1:T(8,128)}, f32[128,64]{0,1:T(8,128)S(1)}, u32[]{:S(2)}) copy-start(f32[128,64]{0,1:T(8,128)S(1)} %get-tuple-element.26) | copy-start | bytes 98308
  100.2 5.1 %copy-start.13 = (f32[128]{0:T(128)}, f32[128]{0:T(128)S(1)}, u32[]{:S(2)}) copy-start(f32[128]{0:T(128)S(1)} %add_rsqrt_fusion) | copy-start | bytes 1540
  106.4 21.4 %copy-start.1 = (bf16[128,4096]{1,0:T(8,128)(2,1)S(1)}, bf16[128,4096]{1,0:T(8,128)(2,1)}, u32[]{:S(2)}) copy-start(bf16[128,4096]{1,0:T(8,128)(2,1)} %all-gather.3.cloned.1.call-done) | copy-start | bytes 3145732
  127.8 5.9 %copy-start.5 = (f32[128,64]{0,1:T(8,128)S(1)}, f32[128,64]{0,1:T(8,128)}, u32[]{:S(2)}) copy-start(f32[128,64]{0,1:T(8,128)} %copy-done.4) | copy-start | bytes 98308
  133.7 15.9 %copy-start.2 = (pred[128,1024]{0,1:T(8,128)(4,1)S(1)}, pred[128,1024]{0,1:T(8,128)(4,1)}, u32[]{:S(2)}) copy-start(pred[128,1024]{0,1:T(8,128)(4,1)} %compare_and_fusion) | copy-start | bytes 393220
  144.4 6.0 %copy-start.16 = (bf16[1024,4,128]{0,2,1:T(8,128)(2,1)S(1)}, bf16[1024,4,128]{0,2,1:T(8,128)(2,1)}, u32[]{:S(2)}) copy-start(bf16[1024,4,128]{0,2,1:T(8,128)(2,1)} %all-gather.5.cloned.1.call-done) | copy-start | bytes 3145732
  144.4 2.9 %collective-permute-start.7 = (bf16[1024,4,128]{0,2,1:T(8,128)(2,1)}, bf16[1024,4,128]{0,2,1:T(8,128)(2,1)S(1)}, u32[]{:S(2)}, u32[]{:S(2)}) collective-permute-start(bf16[1024,4,128]{0,2,1:T(8,128)(2,1)} %all-gather.5.cloned.1.call-done), channel_id=1, source_target_pairs={{0,1},{1,0},{2,3},{3,2},{4,5},{5,4},{6,7},{7,6},{8,9},{9,8},{10,11... | collective-permute-start | bytes 3145736 | tf_op jit(solution)/shard_map/ppermute | solution.py:23
Sparse Core Ops, SparseCore 0:
  80.4 18.2 all-gather.2
  105.0 39.3 all-gather.4

commit v11 on v10

--- a/solution.py
+++ b/solution.py
@@ -3,6 +3,7 @@
 import jax
 import jax.numpy as jnp
 from jax import lax
+from jax.experimental.layout import Layout, with_layout_constraint
 from jax.sharding import PartitionSpec as P
 
 D = 4096
@@ -233,7 +234,10 @@
         tp_index == 0, rotate(projected_half, own_positions), projected_half
     ).astype(jnp.bfloat16)
     query_weights, own_half = lax.optimization_barrier((w_query, own_half))
-    gathered = lax.all_gather(own_half, "ctx", axis=0, tiled=True)
+    flat_half = with_layout_constraint(own_half.reshape(TOK, -1), Layout(major_to_minor=(0, 1)))
+    gathered = lax.all_gather(flat_half, "ctx", axis=0, tiled=True)
+    gathered = with_layout_constraint(gathered, Layout(major_to_minor=(0, 1)))
+    gathered = gathered.reshape((shards * TOK,) + own_half.shape[1:])
     queries = jnp.einsum(
         "td,dhgk->thgk", normed_rows, query_weights, preferred_element_type=jnp.float32
     )

time: 161 us -> 165 us (1.025)
  local copies, waits for them, and re-layouts: 32.1 us -> 35.7 us
    reshape x0 -> x2, local copies, waits for them, and re-layouts: none -> 2.11 us  [the longest x1 1.34 us: local(): gathered = gathered.reshape((shards * TOK,) + own_half.shape[1:])]
where the time goes in v11:
time: 165 us; the launch traced here: 163 us
  waiting for transfers between devices  62.5 us (38%)
  local copies, waits for them, and re-layouts  35.7 us (22%)
  matrix products  20.6 us (12%)
  starting transfers between devices  17 us (10%)
  between operations  13.9 us (8%)
  other arithmetic  13.7 us (8%)
    ppermute x8, waiting for transfers between devices, swapped(): lax.ppermute(value, axis, [(i, i ^ 1 << stride) for i in range(lax.axis_s...  31.3 us
    optimization_barrier x1, local copies, waits for them, and re-layouts, local(): query_weights, own_half = lax.optimization_barrier((w_query, own_half))  21.4 us
    unnamed x3, matrix products  11.7 us
    all_gather x1, waiting for transfers between devices, local(): gathered = lax.all_gather(flat_half, 'ctx', axis=0, tiled=True)  10.8 us
    ppermute x8, starting transfers between devices, swapped(): lax.ppermute(value, axis, [(i, i ^ 1 << stride) for i in range(lax.axis_s...  10.6 us
    all_to_all x1, waiting for transfers between devices, local(): lax.all_to_all(blocks, 'ctx', split_axis=0, concat_axis=0, tiled=True)  10.4 us
    all_gather x1, waiting for transfers between devices, local(): full_rows = lax.all_gather(embeds, ('vis', 'tp'), axis=1, tiled=True)  9.98 us
    squeeze x1, local copies, waits for them, and re-layouts, local(): w_keyval[0]  7.6 us
  transfers between devices with their start and end apart: 11, of which 11 were waited for; matrix products, arithmetic and copies ran while one was open for 25% of the time, Pallas kernels for 0%

profile of v11, /device:TPU:0, one launch (start us, length us, event | category | flops | bytes accessed | tf_op | source)
XLA Modules:
  0.0 163.4 jit_solution(10769096041855719291)
XLA Ops:
  6.5 1.2 convert_reduce_fusion
  7.8 1.2 fusion.42
  9.0 1.9 %fusion.48 = f32[128,960]{0,1:S(1)} fusion(bf16[1280,960]{0,1:T(8,128)(2,1)S(1)} %bitcast.171, bf16[128,1280]{1,0:T(8,128)(2,1)} %param.17, f32[1280]{0:T(1024)} %param.19, f32[1280]{0:T(1024)} %param.18, f32[128]{0:T(128)S(1)} %add_rsqrt_fusion.2, f32[128]{0:T(128)S(1)} %broadcast_multiply_fusion.1), kind=kOutput, calls=%fused_computation.51 | convolution fusion | flops 315555840 | bytes 3288064
  11.0 0.1 broadcast_compare_fusion
  11.1 0.3 fusion.106
  11.4 0.3 copy-done.4
  11.7 1.7 %fusion.22 = f32[128,1280,1]{1,0,2:T(8,128)S(1)} fusion(bf16[4,80,1280]{2,1,0:T(8,128)(2,1)} %param.21, f32[4,128,128]{1,2,0:T(8,128)S(1)} %get-tuple-element.30, f32[4,128]{1,0:T(4,128)S(1)} %get-tuple-element.29, bf16[128,3,4,80]{0,3,2,1:T(8,128)(2,1)} %copy-done.4, f32[128,4]{0,1:T(4,128)S(1)} %bitcast.192), kind=kOutput, calls=%fused_computation.28 | convolution fusion | flops 115556352 | bytes 1822720 | tf_op jit(solution)/shard_map/phd,hdf->pf/dot_general | solution.py:160
  13.5 0.6 collective-permute-start
  14.2 0.7 fusion.104
  15.0 0.4 collective-permute-done
  15.4 1.0 bitcast_add_fusion
  16.5 2.9 %collective-permute-start.1 = (f32[1,32,1280]{2,1,0:T(8,128)S(1)}, f32[1,32,1280]{2,1,0:T(8,128)S(1)}, u32[]{:S(2)}, u32[]{:S(2)}) collective-permute-start(f32[1,32,1280]{2,1,0:T(8,128)S(1)} %select_bitcast_fusion.3), channel_id=1, source_target_pairs={{0,16},{16,0},{1,17},{17,1},{2,18},{18,2},{3,19},{19,3},{4,20},{20... | collective-permute-start | bytes 491528 | tf_op jit(solution)/shard_map/ppermute | solution.py:24
  19.4 0.7 fusion.64
  20.1 3.8 %collective-permute-done.1 = f32[1,32,1280]{2,1,0:T(8,128)S(1)} collective-permute-done((f32[1,32,1280]{2,1,0:T(8,128)S(1)}, f32[1,32,1280]{2,1,0:T(8,128)S(1)}, u32[]{:S(2)}, u32[]{:S(2)}) %collective-permute-start.1) | collective-permute-done | bytes 163872 | tf_op jit(solution)/shard_map/ppermute | solution.py:24
  23.9 1.0 fusion.103
  24.9 0.2 multiply_reduce_fusion
  25.2 0.1 add_convert_fusion.1
  25.3 1.8 %collective-permute-start.2 = (bf16[1,8,5120]{2,1,0:T(8,128)(2,1)S(1)}, bf16[1,8,5120]{2,1,0:T(8,128)(2,1)S(1)}, u32[]{:S(2)}, u32[]{:S(2)}) collective-permute-start(bf16[1,8,5120]{2,1,0:T(8,128)(2,1)S(1)} %broadcast_in_dim_reshape.2), channel_id=1, source_target_pairs={{0,16},{16,0},{1,17},{17,1},{2,18},{18,2},{3,19},{19,3},{4,20},{20... | collective-permute-start | bytes 245768 | tf_op jit(solution)/shard_map/ppermute | solution.py:24
  27.1 0.1 select_reduce_fusion.3
  27.3 2.5 %collective-permute-done.2 = bf16[1,8,5120]{2,1,0:T(8,128)(2,1)S(1)} collective-permute-done((bf16[1,8,5120]{2,1,0:T(8,128)(2,1)S(1)}, bf16[1,8,5120]{2,1,0:T(8,128)(2,1)S(1)}, u32[]{:S(2)}, u32[]{:S(2)}) %collective-permute-start.2) | collective-permute-done | bytes 81952 | tf_op jit(solution)/shard_map/ppermute | solution.py:24
  30.0 1.4 collective-permute-done.3
  31.4 0.2 convolution_convert_fusion
  31.6 0.7 copy.160
  32.3 6.1 %all-to-all-start = ((bf16[8,32,640]{2,1,0:T(8,128)(2,1)}), bf16[8,32,640]{2,1,0:T(8,128)(2,1)S(1)}, u32[]{:S(2)}, u32[]{:S(2)}) async-start(bf16[8,32,640]{2,1,0:T(8,128)(2,1)} %bitcast.169), calls=%async_computation | async-start | bytes 655360 | tf_op jit(solution)/shard_map/all_to_all | solution.py:199
  38.6 10.4 %all-to-all-done = bf16[8,32,640]{2,1,0:T(8,128)(2,1)S(1)} async-done(((bf16[8,32,640]{2,1,0:T(8,128)(2,1)}), bf16[8,32,640]{2,1,0:T(8,128)(2,1)S(1)}, u32[]{:S(2)}, u32[]{:S(2)}) %all-to-all-start) | async-done | bytes 327712 | tf_op jit(solution)/shard_map/all_to_all | solution.py:199
  49.1 0.1 copy.161
  49.3 1.9 %fusion.12 = f32[4,2,32,1024]{3,2,1,0:T(8,128)S(1)} fusion(bf16[4,2,32,640]{3,2,1,0:T(8,128)(2,1)S(1)} %dot_general.46, bf16[640,1024]{1,0:T(8,128)(2,1)} %param.24), kind=kOutput, calls=%fused_computation.16 | convolution fusion | flops 335544320 | bytes 2686976 | tf_op jit(solution)/shard_map/dot_general | solution.py:203
  51.3 1.5 collective-permute-start.4
  53.0 10.2 %collective-permute-done.4 = f32[4,32,1024]{2,1,0:T(8,128)S(1)} collective-permute-done((f32[4,32,1024]{2,1,0:T(8,128)S(1)}, f32[4,32,1024]{2,1,0:T(8,128)S(1)}, u32[]{:S(2)}, u32[]{:S(2)}) %collective-permute-start.4) | collective-permute-done | bytes 524320 | tf_op jit(solution)/shard_map/ppermute | solution.py:24
  63.2 0.1 fusion.47
  63.2 0.7 select_bitcast_fusion.2
  64.0 0.5 collective-permute-start.5
  64.5 0.1 and.170
  64.7 0.3 fusion.105
  65.0 5.7 %collective-permute-done.5 = f32[2,32,1024]{2,1,0:T(8,128)} collective-permute-done((f32[2,32,1024]{2,1,0:T(8,128)}, f32[2,32,1024]{2,1,0:T(8,128)}, u32[]{:S(2)}, u32[]{:S(2)}) %collective-permute-start.5) | collective-permute-done | bytes 262176 | tf_op jit(solution)/shard_map/ppermute | solution.py:24
  70.7 1.0 fusion.61
  71.7 3.2 %collective-permute-start.6 = (f32[1,32,1024]{2,1,0:T(8,128)S(1)}, f32[1,32,1024]{2,1,0:T(8,128)S(1)}, u32[]{:S(2)}, u32[]{:S(2)}) collective-permute-start(f32[1,32,1024]{2,1,0:T(8,128)S(1)} %select_bitcast_fusion.4), channel_id=1, source_target_pairs={{0,8},{2,10},{4,12},{6,14},{8,0},{10,2},{12,4},{14,6},{1,9},{3,11}... | collective-permute-start | bytes 393224 | tf_op jit(solution)/shard_map/ppermute | solution.py:24
  74.9 4.4 %collective-permute-done.6 = f32[1,32,1024]{2,1,0:T(8,128)S(1)} collective-permute-done((f32[1,32,1024]{2,1,0:T(8,128)S(1)}, f32[1,32,1024]{2,1,0:T(8,128)S(1)}, u32[]{:S(2)}, u32[]{:S(2)}) %collective-permute-start.6) | collective-permute-done | bytes 131104 | tf_op jit(solution)/shard_map/ppermute | solution.py:24
  79.3 1.0 fusion.18
  80.3 0.2 all-gather.5.cloned.1.call-start
  80.6 7.6 %copy.133 = bf16[4096,4,128]{0,2,1:T(8,128)(2,1)} copy(bf16[4096,4,128]{2,1,0:T(4,128)(2,1)} %bitcast.177) | data formatting | bytes 8388608 | tf_op jit(solution)/shard_map/squeeze | solution.py:231
  88.2 0.1 copy.135
  88.4 0.1 select_reduce_fusion.5
  88.5 0.2 multiply_cosine_fusion
  88.7 10.0 %all-gather.3.cloned.1.call-done = bf16[128,4096]{1,0:T(8,128)(2,1)} async-done(((bf16[128,1024]{1,0:T(8,128)(2,1)}), bf16[128,4096]{1,0:T(8,128)(2,1)}) %all-gather.3.cloned.1.call-update) | async-done | bytes 1048592 | tf_op jit(solution)/shard_map/all_gather | solution.py:218
  98.7 1.5 fusion.3
  100.3 3.8 %fusion.56 = f32[128,512]{0,1:S(1)} fusion(bf16[4096,512]{0,1:T(8,128)(2,1)} %bitcast.178, bf16[128,4096]{1,0:T(8,128)(2,1)} %all-gather.3.cloned.1.call-done, f32[4096]{0:T(1024)S(1)} %copy-done.8, f32[128]{0:T(128)S(1)} %add_rsqrt_fusion), kind=kOutput, calls=%fused_computation.62 | convolution fusion | flops 538968064 | bytes 5521920
  104.2 0.8 copy.151
  105.0 0.1 select_reduce_fusion
  105.2 0.1 select_reduce_fusion.4
  105.3 0.1 eq.223
  105.4 0.1 select_reduce_fusion.1
  105.5 1.0 compare_and_fusion
  106.5 21.4 %copy.134 = bf16[4096,4,2,128]{0,3,2,1:T(8,128)(2,1)} copy(bf16[4096,4,2,128]{3,2,1,0:T(2,128)(2,1)} %param.32) | data formatting | bytes 16777216 | tf_op jit(solution)/shard_map/optimization_barrier | solution.py:236
  127.9 5.9 %fusion.54 = f32[128,1024]{0,1:S(1)} fusion(bf16[4096,1024]{0,1:T(8,128)(2,1)} %bitcast.172, bf16[128,4096]{1,0:T(8,128)(2,1)S(1)} %copy-done.1, f32[4096]{0:T(1024)S(1)} %copy-done.8, f32[128]{0:T(128)} %copy-done.14), kind=kOutput, calls=%fused_computation.61 | convolution fusion | flops 1075838976 | bytes 9978368
  133.9 0.7 pad_maximum_fusion
  134.6 10.8 %all-gather.5.cloned.1.call-done = bf16[1024,512]{1,0:T(8,128)(2,1)} async-done(((bf16[128,512]{1,0:T(8,128)(2,1)}), bf16[1024,512]{1,0:T(8,128)(2,1)}) %all-gather.5.cloned.1.call-update) | async-done | bytes 1048592 | tf_op jit(solution)/shard_map/all_gather | solution.py:238
  145.4 1.3 reshape.649
  146.8 1.5 copy.139
  148.3 2.9 %collective-permute-done.7 = bf16[1024,4,128]{0,2,1:T(8,128)(2,1)S(1)} collective-permute-done((bf16[1024,4,128]{0,2,1:T(8,128)(2,1)}, bf16[1024,4,128]{0,2,1:T(8,128)(2,1)S(1)}, u32[]{:S(2)}, u32[]{:S(2)}) %collective-permute-start.7) | collective-permute-done | bytes 1048608 | tf_op jit(solution)/shard_map/ppermute | solution.py:24
  151.2 2.3 %fusion.2 = (f32[4,2,128]{2,1,0:T(2,128)S(1)}, f32[4,1024,128,2]{2,1,3,0:T(8,128)S(1)}) fusion(pred[128,1024]{0,1:T(8,128)(4,1)} %compare_and_fusion, bf16[128,4,2,128]{0,3,2,1:T(8,128)(2,1)} %pad_maximum_fusion, bf16[1024,4,128]{0,2,1:T(8,128)(2,1)} %copy.139, bf16[1024,4,128]{0,2,1:T(8,128)(2,1)S(1)} %collective-permute-done.7, pred[]{:T(512)S(6)} %eq.211), kind=kOutput, calls=%fused_computation.5 | convolution fusion | flops 272104448 | bytes 6688769 | tf_op jit(solution)/shard_map/qkgd,nkd->kgqn/dot_general | solution.py:263
  153.5 0.9 fusion
  154.4 1.2 fusion.35
  155.6 0.9 copy.144
  (83 shorter events, 1.9 us)
Async XLA Ops:
  6.5 2.5 %copy-start = (bf16[1280,3,4,80]{0,3,2,1:T(8,128)(2,1)S(1)}, bf16[1280,3,4,80]{0,3,2,1:T(8,128)(2,1)}, u32[]{:S(2)}) copy-start(bf16[1280,3,4,80]{0,3,2,1:T(8,128)(2,1)} %param.20) | copy-start | bytes 7372804
  6.5 4.4 %copy-start.15 = (s32[128]{0:T(128)S(1)}, s32[128]{0:T(128)}, u32[]{:S(2)}) copy-start(s32[128]{0:T(128)} %param.26) | copy-start | bytes 1540
  6.5 7.5 %copy-start.13 = (s32[256]{0:T(256)S(1)}, s32[256]{0:T(256)}, u32[]{:S(2)}) copy-start(s32[256]{0:T(256)} %param.27) | copy-start | bytes 3076
  6.5 7.7 %copy-start.9 = (s32[8]{0:T(128)S(1)}, s32[8]{0:T(128)}, u32[]{:S(2)}) copy-start(s32[8]{0:T(128)} %param.28) | copy-start | bytes 100
  10.9 14.2 %copy-start.10 = (f32[1280]{0:T(1024)S(1)}, f32[1280]{0:T(1024)}, u32[]{:S(2)}) copy-start(f32[1280]{0:T(1024)} %param.23) | copy-start | bytes 15364
  10.9 14.2 %copy-start.11 = (f32[1280]{0:T(1024)S(1)}, f32[1280]{0:T(1024)}, u32[]{:S(2)}) copy-start(f32[1280]{0:T(1024)} %param.22) | copy-start | bytes 15364
  11.0 0.7 copy-start.4
  13.4 25.2 %copy-start.16 = (s32[8,2]{0,1:T(2,128)S(1)}, s32[8,2]{0,1:T(2,128)}, u32[]{:S(2)}) copy-start(s32[8,2]{0,1:T(2,128)} %param.25) | copy-start | bytes 196
  13.5 1.9 %collective-permute-start = (f32[1,64,1280]{2,1,0:T(8,128)S(1)}, f32[1,64,1280]{2,1,0:T(8,128)}, u32[]{:S(2)}, u32[]{:S(2)}) collective-permute-start(f32[1,64,1280]{2,1,0:T(8,128)S(1)} %select_bitcast_fusion.1), channel_id=1, source_target_pairs={{0,1},{1,0},{2,3},{3,2},{4,5},{5,4},{6,7},{7,6},{8,9},{9,8},{10,11... | collective-permute-start | bytes 983048 | tf_op jit(solution)/shard_map/ppermute | solution.py:24
  16.5 7.4 %collective-permute-start.1 = (f32[1,32,1280]{2,1,0:T(8,128)S(1)}, f32[1,32,1280]{2,1,0:T(8,128)S(1)}, u32[]{:S(2)}, u32[]{:S(2)}) collective-permute-start(f32[1,32,1280]{2,1,0:T(8,128)S(1)} %select_bitcast_fusion.3), channel_id=1, source_target_pairs={{0,16},{16,0},{1,17},{17,1},{2,18},{18,2},{3,19},{19,3},{4,20},{20... | collective-permute-start | bytes 491528 | tf_op jit(solution)/shard_map/ppermute | solution.py:24
  25.3 4.5 %collective-permute-start.2 = (bf16[1,8,5120]{2,1,0:T(8,128)(2,1)S(1)}, bf16[1,8,5120]{2,1,0:T(8,128)(2,1)S(1)}, u32[]{:S(2)}, u32[]{:S(2)}) collective-permute-start(bf16[1,8,5120]{2,1,0:T(8,128)(2,1)S(1)} %broadcast_in_dim_reshape.2), channel_id=1, source_target_pairs={{0,16},{16,0},{1,17},{17,1},{2,18},{18,2},{3,19},{19,3},{4,20},{20... | collective-permute-start | bytes 245768 | tf_op jit(solution)/shard_map/ppermute | solution.py:24
  29.9 1.5 collective-permute-start.3
  32.3 16.7 %all-to-all-start = ((bf16[8,32,640]{2,1,0:T(8,128)(2,1)}), bf16[8,32,640]{2,1,0:T(8,128)(2,1)S(1)}, u32[]{:S(2)}, u32[]{:S(2)}) async-start(bf16[8,32,640]{2,1,0:T(8,128)(2,1)} %bitcast.169), calls=%async_computation | async-start | bytes 655360 | tf_op jit(solution)/shard_map/all_to_all | solution.py:199
  38.4 60.3 %all-gather.3.cloned.1.call-start = ((), (), s32[]{:S(2)}) async-start(), calls=%async_computation.1 | async-start | bytes 1310720 | tf_op jit(solution)/shard_map/all_gather | solution.py:218
  49.3 30.0 %copy-start.7 = (bf16[128,1024]{1,0:T(8,128)(2,1)S(1)}, bf16[128,1024]{1,0:T(8,128)(2,1)}, u32[]{:S(2)}) copy-start(bf16[128,1024]{1,0:T(8,128)(2,1)} %param.30) | copy-start | bytes 786436
  51.3 11.9 %collective-permute-start.4 = (f32[4,32,1024]{2,1,0:T(8,128)S(1)}, f32[4,32,1024]{2,1,0:T(8,128)S(1)}, u32[]{:S(2)}, u32[]{:S(2)}) collective-permute-start(f32[4,32,1024]{2,1,0:T(8,128)S(1)} %select_bitcast_fusion), channel_id=1, source_target_pairs={{0,2},{2,0},{4,6},{6,4},{8,10},{10,8},{12,14},{14,12},{1,3},{3,1},... | collective-permute-start | bytes 1572872 | tf_op jit(solution)/shard_map/ppermute | solution.py:24
  64.0 6.7 %collective-permute-start.5 = (f32[2,32,1024]{2,1,0:T(8,128)}, f32[2,32,1024]{2,1,0:T(8,128)}, u32[]{:S(2)}, u32[]{:S(2)}) collective-permute-start(f32[2,32,1024]{2,1,0:T(8,128)} %select_bitcast_fusion.2), channel_id=1, source_target_pairs={{0,4},{2,6},{4,0},{6,2},{8,12},{10,14},{12,8},{14,10},{1,5},{3,7},... | collective-permute-start | bytes 786440 | tf_op jit(solution)/shard_map/ppermute | solution.py:24
  71.7 7.6 %collective-permute-start.6 = (f32[1,32,1024]{2,1,0:T(8,128)S(1)}, f32[1,32,1024]{2,1,0:T(8,128)S(1)}, u32[]{:S(2)}, u32[]{:S(2)}) collective-permute-start(f32[1,32,1024]{2,1,0:T(8,128)S(1)} %select_bitcast_fusion.4), channel_id=1, source_target_pairs={{0,8},{2,10},{4,12},{6,14},{8,0},{10,2},{12,4},{14,6},{1,9},{3,11}... | collective-permute-start | bytes 393224 | tf_op jit(solution)/shard_map/ppermute | solution.py:24
  80.3 65.1 %all-gather.5.cloned.1.call-start = ((), (), s32[]{:S(2)}) async-start(), calls=%async_computation.2 | async-start | bytes 1179648 | tf_op jit(solution)/shard_map/all_gather | solution.py:238
  80.5 7.7 %copy-start.12 = (s32[1024]{0:T(1024)S(1)}, s32[1024]{0:T(1024)}, u32[]{:S(2)}) copy-start(s32[1024]{0:T(1024)} %param.29) | copy-start | bytes 12292
  80.5 19.7 %copy-start.8 = (f32[4096]{0:T(1024)S(1)}, f32[4096]{0:T(1024)}, u32[]{:S(2)}) copy-start(f32[4096]{0:T(1024)} %param.31) | copy-start | bytes 49156
  88.7 15.4 %copy-start.5 = (f32[128,64]{0,1:T(8,128)}, f32[128,64]{0,1:T(8,128)S(1)}, u32[]{:S(2)}) copy-start(f32[128,64]{0,1:T(8,128)S(1)} %get-tuple-element.26) | copy-start | bytes 98308
  100.2 5.2 %copy-start.14 = (f32[128]{0:T(128)}, f32[128]{0:T(128)S(1)}, u32[]{:S(2)}) copy-start(f32[128]{0:T(128)S(1)} %add_rsqrt_fusion) | copy-start | bytes 1540
  106.5 21.4 %copy-start.1 = (bf16[128,4096]{1,0:T(8,128)(2,1)S(1)}, bf16[128,4096]{1,0:T(8,128)(2,1)}, u32[]{:S(2)}) copy-start(bf16[128,4096]{1,0:T(8,128)(2,1)} %all-gather.3.cloned.1.call-done) | copy-start | bytes 3145732
  127.9 5.9 %copy-start.6 = (f32[128,64]{0,1:T(8,128)S(1)}, f32[128,64]{0,1:T(8,128)}, u32[]{:S(2)}) copy-start(f32[128,64]{0,1:T(8,128)} %copy-done.5) | copy-start | bytes 98308
  148.3 5.2 %copy-start.3 = (pred[128,1024]{0,1:T(8,128)(4,1)S(1)}, pred[128,1024]{0,1:T(8,128)(4,1)}, u32[]{:S(2)}) copy-start(pred[128,1024]{0,1:T(8,128)(4,1)} %compare_and_fusion) | copy-start | bytes 393220
  148.3 6.1 %copy-start.2 = (bf16[1024,4,128]{0,2,1:T(8,128)(2,1)S(1)}, bf16[1024,4,128]{0,2,1:T(8,128)(2,1)}, u32[]{:S(2)}) copy-start(bf16[1024,4,128]{0,2,1:T(8,128)(2,1)} %copy.139) | copy-start | bytes 3145732
  148.3 2.9 %collective-permute-start.7 = (bf16[1024,4,128]{0,2,1:T(8,128)(2,1)}, bf16[1024,4,128]{0,2,1:T(8,128)(2,1)S(1)}, u32[]{:S(2)}, u32[]{:S(2)}) collective-permute-start(bf16[1024,4,128]{0,2,1:T(8,128)(2,1)} %copy.139), channel_id=1, source_target_pairs={{0,1},{1,0},{2,3},{3,2},{4,5},{5,4},{6,7},{7,6},{8,9},{9,8},{10,11... | collective-permute-start | bytes 3145736 | tf_op jit(solution)/shard_map/ppermute | solution.py:24
Sparse Core Ops, SparseCore 0:
  80.4 18.2 all-gather.2
  105.1 40.2 all-gather.4

commit v12 on v10

--- a/solution.py
+++ b/solution.py
@@ -232,8 +232,14 @@
     own_half = jnp.where(
         tp_index == 0, rotate(projected_half, own_positions), projected_half
     ).astype(jnp.bfloat16)
-    query_weights, own_half = lax.optimization_barrier((w_query, own_half))
-    gathered = lax.all_gather(own_half, "ctx", axis=0, tiled=True)
+    partner_half = swapped(own_half, "tp", 0)
+    both_halves = jnp.where(
+        tp_index == 0,
+        jnp.stack([own_half, partner_half], axis=1),
+        jnp.stack([partner_half, own_half], axis=1),
+    )
+    query_weights, both_halves = lax.optimization_barrier((w_query, both_halves))
+    gathered = lax.all_gather(both_halves, "ctx", axis=0, tiled=True)
     queries = jnp.einsum(
         "td,dhgk->thgk", normed_rows, query_weights, preferred_element_type=jnp.float32
     )
@@ -252,9 +258,8 @@
         key_doc[None, :] == own_doc[:, None]
     )
     queries, allowed_now, gathered = lax.optimization_barrier((queries, allowed_now, gathered))
-    partner_all = swapped(gathered, "tp", 0)
-    keys_every = jnp.where(tp_index == 0, gathered, partner_all)
-    values_every = jnp.where(tp_index == 0, partner_all, gathered)
+    keys_every = gathered[:, 0]
+    values_every = gathered[:, 1]
     key_count = keys_every.shape[0]
     scores_now = jnp.einsum(
         "qkgd,nkd->kgqn", queries, keys_every, preferred_element_type=jnp.float32

time: 161 us -> 170 us (1.056)
  waiting for transfers between devices: 62.3 us -> 71.6 us
    all_gather x1, waiting for transfers between devices: 10.6 us -> 21.4 us  [local(): gathered = lax.all_gather(both_halves, 'ctx', axis=0, tiled=True)]
    ppermute x8, waiting for transfers between devices: 31.3 us -> 29.5 us  [swapped(): lax.ppermute(value, axis, [(i, i ^ 1 << stride) for i in range(lax.axis_s...]
  transfers between devices with their start and end apart: 11 -> 11, of which waited for: 11 -> 11; matrix products, arithmetic and copies ran while one was open for 25% -> 23% of each run, Pallas kernels for 0% -> 0%
where the time goes in v12:
time: 170 us; the launch traced here: 169 us
  waiting for transfers between devices  71.6 us (42%)
  local copies, waits for them, and re-layouts  32.1 us (19%)
  matrix products  20.3 us (12%)
  starting transfers between devices  17.2 us (10%)
  between operations  13.9 us (8%)
  other arithmetic  13.8 us (8%)
    ppermute x8, waiting for transfers between devices, swapped(): lax.ppermute(value, axis, [(i, i ^ 1 << stride) for i in range(lax.axis_s...  29.5 us
    optimization_barrier x1, local copies, waits for them, and re-layouts, local(): lax.optimization_barrier((w_query, both_halves))  21.4 us
    all_gather x1, waiting for transfers between devices, local(): gathered = lax.all_gather(both_halves, 'ctx', axis=0, tiled=True)  21.4 us
    unnamed x3, matrix products  11.5 us
    ppermute x8, starting transfers between devices, swapped(): lax.ppermute(value, axis, [(i, i ^ 1 << stride) for i in range(lax.axis_s...  10.9 us
    all_to_all x1, waiting for transfers between devices, local(): lax.all_to_all(blocks, 'ctx', split_axis=0, concat_axis=0, tiled=True)  10.4 us
    all_gather x1, waiting for transfers between devices, local(): full_rows = lax.all_gather(embeds, ('vis', 'tp'), axis=1, tiled=True)  10.2 us
    squeeze x1, local copies, waits for them, and re-layouts, local(): w_keyval[0]  7.59 us
  transfers between devices with their start and end apart: 11, of which 11 were waited for; matrix products, arithmetic and copies ran while one was open for 23% of the time, Pallas kernels for 0%

profile of v12, /device:TPU:0, one launch (start us, length us, event | category | flops | bytes accessed | tf_op | source)
XLA Modules:
  0.0 168.9 jit_solution(8267173332878162844)
XLA Ops:
  6.5 1.2 convert_reduce_fusion
  7.8 1.2 fusion.40
  9.0 1.9 %fusion.46 = f32[128,960]{0,1:S(1)} fusion(bf16[1280,960]{0,1:T(8,128)(2,1)S(1)} %bitcast.175, bf16[128,1280]{1,0:T(8,128)(2,1)} %param.17, f32[1280]{0:T(1024)} %param.19, f32[1280]{0:T(1024)} %param.18, f32[128]{0:T(128)S(1)} %add_rsqrt_fusion.2, f32[128]{0:T(128)S(1)} %broadcast_multiply_fusion.1), kind=kOutput, calls=%fused_computation.49 | convolution fusion | flops 315555840 | bytes 3288064
  11.0 0.1 broadcast_compare_fusion
  11.1 0.3 fusion.104
  11.4 0.3 copy-done.3
  11.7 1.7 %fusion.22 = f32[128,1280,1]{1,0,2:T(8,128)S(1)} fusion(bf16[4,80,1280]{2,1,0:T(8,128)(2,1)} %param.21, f32[4,128,128]{1,2,0:T(8,128)S(1)} %get-tuple-element.30, f32[4,128]{1,0:T(4,128)S(1)} %get-tuple-element.29, bf16[128,3,4,80]{0,3,2,1:T(8,128)(2,1)} %copy-done.3, f32[128,4]{0,1:T(4,128)S(1)} %bitcast.197), kind=kOutput, calls=%fused_computation.28 | convolution fusion | flops 115556352 | bytes 1822720 | tf_op jit(solution)/shard_map/phd,hdf->pf/dot_general | solution.py:159
  13.5 0.6 collective-permute-start
  14.2 0.7 fusion.102
  15.0 0.4 collective-permute-done
  15.4 1.0 bitcast_add_fusion
  16.5 2.9 %collective-permute-start.1 = (f32[1,32,1280]{2,1,0:T(8,128)S(1)}, f32[1,32,1280]{2,1,0:T(8,128)S(1)}, u32[]{:S(2)}, u32[]{:S(2)}) collective-permute-start(f32[1,32,1280]{2,1,0:T(8,128)S(1)} %select_bitcast_fusion.3), channel_id=1, source_target_pairs={{0,16},{16,0},{1,17},{17,1},{2,18},{18,2},{3,19},{19,3},{4,20},{20... | collective-permute-start | bytes 491528 | tf_op jit(solution)/shard_map/ppermute | solution.py:23
  19.4 0.7 fusion.62
  20.1 3.8 %collective-permute-done.1 = f32[1,32,1280]{2,1,0:T(8,128)S(1)} collective-permute-done((f32[1,32,1280]{2,1,0:T(8,128)S(1)}, f32[1,32,1280]{2,1,0:T(8,128)S(1)}, u32[]{:S(2)}, u32[]{:S(2)}) %collective-permute-start.1) | collective-permute-done | bytes 163872 | tf_op jit(solution)/shard_map/ppermute | solution.py:23
  23.9 1.0 fusion.101
  24.9 0.2 multiply_reduce_fusion
  25.2 0.1 add_convert_fusion.1
  25.3 1.8 %collective-permute-start.2 = (bf16[1,8,5120]{2,1,0:T(8,128)(2,1)S(1)}, bf16[1,8,5120]{2,1,0:T(8,128)(2,1)S(1)}, u32[]{:S(2)}, u32[]{:S(2)}) collective-permute-start(bf16[1,8,5120]{2,1,0:T(8,128)(2,1)S(1)} %broadcast_in_dim_reshape.2), channel_id=1, source_target_pairs={{0,16},{16,0},{1,17},{17,1},{2,18},{18,2},{3,19},{19,3},{4,20},{20... | collective-permute-start | bytes 245768 | tf_op jit(solution)/shard_map/ppermute | solution.py:23
  27.1 0.1 select_reduce_fusion.3
  27.3 2.5 %collective-permute-done.2 = bf16[1,8,5120]{2,1,0:T(8,128)(2,1)S(1)} collective-permute-done((bf16[1,8,5120]{2,1,0:T(8,128)(2,1)S(1)}, bf16[1,8,5120]{2,1,0:T(8,128)(2,1)S(1)}, u32[]{:S(2)}, u32[]{:S(2)}) %collective-permute-start.2) | collective-permute-done | bytes 81952 | tf_op jit(solution)/shard_map/ppermute | solution.py:23
  30.0 1.4 collective-permute-done.3
  31.4 0.2 convolution_convert_fusion
  31.6 0.7 copy.139
  32.3 6.1 %all-to-all-start = ((bf16[8,32,640]{2,1,0:T(8,128)(2,1)}), bf16[8,32,640]{2,1,0:T(8,128)(2,1)S(1)}, u32[]{:S(2)}, u32[]{:S(2)}) async-start(bf16[8,32,640]{2,1,0:T(8,128)(2,1)} %bitcast.173), calls=%async_computation | async-start | bytes 655360 | tf_op jit(solution)/shard_map/all_to_all | solution.py:198
  38.6 10.4 %all-to-all-done = bf16[8,32,640]{2,1,0:T(8,128)(2,1)S(1)} async-done(((bf16[8,32,640]{2,1,0:T(8,128)(2,1)}), bf16[8,32,640]{2,1,0:T(8,128)(2,1)S(1)}, u32[]{:S(2)}, u32[]{:S(2)}) %all-to-all-start) | async-done | bytes 327712 | tf_op jit(solution)/shard_map/all_to_all | solution.py:198
  49.0 0.1 reshape.639
  49.1 0.1 copy.140
  49.3 1.9 %fusion.12 = f32[4,2,32,1024]{3,2,1,0:T(8,128)S(1)} fusion(bf16[4,2,32,640]{3,2,1,0:T(8,128)(2,1)S(1)} %dot_general.46, bf16[640,1024]{1,0:T(8,128)(2,1)} %param.24), kind=kOutput, calls=%fused_computation.16 | convolution fusion | flops 335544320 | bytes 2686976 | tf_op jit(solution)/shard_map/dot_general | solution.py:202
  51.3 1.5 collective-permute-start.4
  53.0 10.2 %collective-permute-done.4 = f32[4,32,1024]{2,1,0:T(8,128)S(1)} collective-permute-done((f32[4,32,1024]{2,1,0:T(8,128)S(1)}, f32[4,32,1024]{2,1,0:T(8,128)S(1)}, u32[]{:S(2)}, u32[]{:S(2)}) %collective-permute-start.4) | collective-permute-done | bytes 524320 | tf_op jit(solution)/shard_map/ppermute | solution.py:23
  63.2 0.1 fusion.45
  63.2 0.7 select_bitcast_fusion.2
  64.0 0.5 collective-permute-start.5
  64.5 0.1 and.170
  64.7 0.3 fusion.103
  65.0 5.7 %collective-permute-done.5 = f32[2,32,1024]{2,1,0:T(8,128)} collective-permute-done((f32[2,32,1024]{2,1,0:T(8,128)}, f32[2,32,1024]{2,1,0:T(8,128)}, u32[]{:S(2)}, u32[]{:S(2)}) %collective-permute-start.5) | collective-permute-done | bytes 262176 | tf_op jit(solution)/shard_map/ppermute | solution.py:23
  70.7 1.0 fusion.59
  71.7 3.2 %collective-permute-start.6 = (f32[1,32,1024]{2,1,0:T(8,128)S(1)}, f32[1,32,1024]{2,1,0:T(8,128)S(1)}, u32[]{:S(2)}, u32[]{:S(2)}) collective-permute-start(f32[1,32,1024]{2,1,0:T(8,128)S(1)} %select_bitcast_fusion.4), channel_id=1, source_target_pairs={{0,8},{2,10},{4,12},{6,14},{8,0},{10,2},{12,4},{14,6},{1,9},{3,11}... | collective-permute-start | bytes 393224 | tf_op jit(solution)/shard_map/ppermute | solution.py:23
  74.9 4.4 %collective-permute-done.6 = f32[1,32,1024]{2,1,0:T(8,128)S(1)} collective-permute-done((f32[1,32,1024]{2,1,0:T(8,128)S(1)}, f32[1,32,1024]{2,1,0:T(8,128)S(1)}, u32[]{:S(2)}, u32[]{:S(2)}) %collective-permute-start.6) | collective-permute-done | bytes 131104 | tf_op jit(solution)/shard_map/ppermute | solution.py:23
  79.3 1.0 fusion.18
  80.3 0.2 all-gather.5.cloned.1.call-start
  80.5 7.6 %copy.117 = bf16[4096,4,128]{0,2,1:T(8,128)(2,1)} copy(bf16[4096,4,128]{2,1,0:T(4,128)(2,1)} %bitcast.181) | data formatting | bytes 8388608 | tf_op jit(solution)/shard_map/squeeze | solution.py:230
  88.2 0.1 select_reduce_fusion.5
  88.3 0.2 multiply_cosine_fusion
  88.5 10.2 %all-gather.3.cloned.1.call-done = bf16[128,4096]{1,0:T(8,128)(2,1)} async-done(((bf16[128,1024]{1,0:T(8,128)(2,1)}), bf16[128,4096]{1,0:T(8,128)(2,1)}) %all-gather.3.cloned.1.call-update) | async-done | bytes 1048592 | tf_op jit(solution)/shard_map/all_gather | solution.py:217
  98.7 1.5 fusion.3
  100.3 3.8 %fusion.54 = f32[128,512]{0,1:S(1)} fusion(bf16[4096,512]{0,1:T(8,128)(2,1)} %bitcast.182, bf16[128,4096]{1,0:T(8,128)(2,1)} %all-gather.3.cloned.1.call-done, f32[4096]{0:T(1024)S(1)} %copy-done.7, f32[128]{0:T(128)S(1)} %add_rsqrt_fusion), kind=kOutput, calls=%fused_computation.60 | convolution fusion | flops 538968064 | bytes 5521920
  104.2 0.3 collective-permute-start.7
  104.5 1.1 collective-permute-done.7
  105.6 0.7 maximum_select_fusion.2
  106.4 0.1 copy.119
  106.6 0.1 select_reduce_fusion
  106.9 0.1 select_reduce_fusion.4
  106.9 0.1 eq.222
  107.0 0.1 select_reduce_fusion.1
  107.1 1.0 compare_and_fusion
  108.1 21.4 %copy.118 = bf16[4096,4,2,128]{0,3,2,1:T(8,128)(2,1)} copy(bf16[4096,4,2,128]{3,2,1,0:T(2,128)(2,1)} %param.32) | data formatting | bytes 16777216 | tf_op jit(solution)/shard_map/optimization_barrier | solution.py:241
  129.5 5.8 %fusion.52 = f32[128,1024]{0,1:S(1)} fusion(bf16[4096,1024]{0,1:T(8,128)(2,1)} %bitcast.176, bf16[128,4096]{1,0:T(8,128)(2,1)S(1)} %copy-done.1, f32[4096]{0:T(1024)S(1)} %copy-done.7, f32[128]{0:T(128)} %copy-done.13), kind=kOutput, calls=%fused_computation.59 | convolution fusion | flops 1075838976 | bytes 9978368
  135.4 0.1 subtract_convert_fusion
  135.5 21.4 %all-gather.5.cloned.1.call-done = bf16[1024,2,4,128]{0,3,2,1:T(8,128)(2,1)} async-done(((bf16[128,2,4,128]{0,3,2,1:T(8,128)(2,1)}), bf16[1024,2,4,128]{0,3,2,1:T(8,128)(2,1)}) %all-gather.5.cloned.1.call-update) | async-done | bytes 2097168 | tf_op jit(solution)/shard_map/all_gather | solution.py:242
  156.9 2.3 %fusion.2 = (f32[4,2,128]{2,1,0:T(2,128)S(1)}, f32[4,1024,128,2]{2,1,3,0:T(8,128)S(1)}) fusion(pred[128,1024]{0,1:T(8,128)(4,1)} %compare_and_fusion, bf16[128,4,2,128]{0,3,2,1:T(8,128)(2,1)S(1)} %pad_maximum_fusion, bf16[1024,2,4,128]{0,3,2,1:T(8,128)(2,1)} %all-gather.5.cloned.1.call-done), kind=kOutput, calls=%fused_computation.5 | convolution fusion | flops 271580160 | bytes 5640192 | tf_op jit(solution)/shard_map/qkgd,nkd->kgqn/dot_general | solution.py:264
  159.1 0.9 fusion
  160.0 1.2 fusion.33
  161.2 0.9 copy.124
  (81 shorter events, 1.7 us)
Async XLA Ops:
  6.5 2.5 %copy-start = (bf16[1280,3,4,80]{0,3,2,1:T(8,128)(2,1)S(1)}, bf16[1280,3,4,80]{0,3,2,1:T(8,128)(2,1)}, u32[]{:S(2)}) copy-start(bf16[1280,3,4,80]{0,3,2,1:T(8,128)(2,1)} %param.20) | copy-start | bytes 7372804
  6.5 4.4 %copy-start.14 = (s32[128]{0:T(128)S(1)}, s32[128]{0:T(128)}, u32[]{:S(2)}) copy-start(s32[128]{0:T(128)} %param.26) | copy-start | bytes 1540
  6.5 7.5 %copy-start.12 = (s32[256]{0:T(256)S(1)}, s32[256]{0:T(256)}, u32[]{:S(2)}) copy-start(s32[256]{0:T(256)} %param.27) | copy-start | bytes 3076
  6.5 7.7 %copy-start.8 = (s32[8]{0:T(128)S(1)}, s32[8]{0:T(128)}, u32[]{:S(2)}) copy-start(s32[8]{0:T(128)} %param.28) | copy-start | bytes 100
  10.9 14.2 %copy-start.9 = (f32[1280]{0:T(1024)S(1)}, f32[1280]{0:T(1024)}, u32[]{:S(2)}) copy-start(f32[1280]{0:T(1024)} %param.23) | copy-start | bytes 15364
  10.9 14.2 %copy-start.10 = (f32[1280]{0:T(1024)S(1)}, f32[1280]{0:T(1024)}, u32[]{:S(2)}) copy-start(f32[1280]{0:T(1024)} %param.22) | copy-start | bytes 15364
  11.0 0.7 copy-start.3
  13.4 25.2 %copy-start.15 = (s32[8,2]{0,1:T(2,128)S(1)}, s32[8,2]{0,1:T(2,128)}, u32[]{:S(2)}) copy-start(s32[8,2]{0,1:T(2,128)} %param.25) | copy-start | bytes 196
  13.5 1.9 %collective-permute-start = (f32[1,64,1280]{2,1,0:T(8,128)S(1)}, f32[1,64,1280]{2,1,0:T(8,128)}, u32[]{:S(2)}, u32[]{:S(2)}) collective-permute-start(f32[1,64,1280]{2,1,0:T(8,128)S(1)} %select_bitcast_fusion.1), channel_id=1, source_target_pairs={{0,1},{1,0},{2,3},{3,2},{4,5},{5,4},{6,7},{7,6},{8,9},{9,8},{10,11... | collective-permute-start | bytes 983048 | tf_op jit(solution)/shard_map/ppermute | solution.py:23
  16.5 7.4 %collective-permute-start.1 = (f32[1,32,1280]{2,1,0:T(8,128)S(1)}, f32[1,32,1280]{2,1,0:T(8,128)S(1)}, u32[]{:S(2)}, u32[]{:S(2)}) collective-permute-start(f32[1,32,1280]{2,1,0:T(8,128)S(1)} %select_bitcast_fusion.3), channel_id=1, source_target_pairs={{0,16},{16,0},{1,17},{17,1},{2,18},{18,2},{3,19},{19,3},{4,20},{20... | collective-permute-start | bytes 491528 | tf_op jit(solution)/shard_map/ppermute | solution.py:23
  25.3 4.5 %collective-permute-start.2 = (bf16[1,8,5120]{2,1,0:T(8,128)(2,1)S(1)}, bf16[1,8,5120]{2,1,0:T(8,128)(2,1)S(1)}, u32[]{:S(2)}, u32[]{:S(2)}) collective-permute-start(bf16[1,8,5120]{2,1,0:T(8,128)(2,1)S(1)} %broadcast_in_dim_reshape.2), channel_id=1, source_target_pairs={{0,16},{16,0},{1,17},{17,1},{2,18},{18,2},{3,19},{19,3},{4,20},{20... | collective-permute-start | bytes 245768 | tf_op jit(solution)/shard_map/ppermute | solution.py:23
  29.9 1.5 collective-permute-start.3
  32.3 16.7 %all-to-all-start = ((bf16[8,32,640]{2,1,0:T(8,128)(2,1)}), bf16[8,32,640]{2,1,0:T(8,128)(2,1)S(1)}, u32[]{:S(2)}, u32[]{:S(2)}) async-start(bf16[8,32,640]{2,1,0:T(8,128)(2,1)} %bitcast.173), calls=%async_computation | async-start | bytes 655360 | tf_op jit(solution)/shard_map/all_to_all | solution.py:198
  38.4 60.3 %all-gather.3.cloned.1.call-start = ((), (), s32[]{:S(2)}) async-start(), calls=%async_computation.1 | async-start | bytes 1310720 | tf_op jit(solution)/shard_map/all_gather | solution.py:217
  49.3 30.0 %copy-start.6 = (bf16[128,1024]{1,0:T(8,128)(2,1)S(1)}, bf16[128,1024]{1,0:T(8,128)(2,1)}, u32[]{:S(2)}) copy-start(bf16[128,1024]{1,0:T(8,128)(2,1)} %param.30) | copy-start | bytes 786436
  51.3 11.9 %collective-permute-start.4 = (f32[4,32,1024]{2,1,0:T(8,128)S(1)}, f32[4,32,1024]{2,1,0:T(8,128)S(1)}, u32[]{:S(2)}, u32[]{:S(2)}) collective-permute-start(f32[4,32,1024]{2,1,0:T(8,128)S(1)} %select_bitcast_fusion), channel_id=1, source_target_pairs={{0,2},{2,0},{4,6},{6,4},{8,10},{10,8},{12,14},{14,12},{1,3},{3,1},... | collective-permute-start | bytes 1572872 | tf_op jit(solution)/shard_map/ppermute | solution.py:23
  64.0 6.7 %collective-permute-start.5 = (f32[2,32,1024]{2,1,0:T(8,128)}, f32[2,32,1024]{2,1,0:T(8,128)}, u32[]{:S(2)}, u32[]{:S(2)}) collective-permute-start(f32[2,32,1024]{2,1,0:T(8,128)} %select_bitcast_fusion.2), channel_id=1, source_target_pairs={{0,4},{2,6},{4,0},{6,2},{8,12},{10,14},{12,8},{14,10},{1,5},{3,7},... | collective-permute-start | bytes 786440 | tf_op jit(solution)/shard_map/ppermute | solution.py:23
  71.7 7.6 %collective-permute-start.6 = (f32[1,32,1024]{2,1,0:T(8,128)S(1)}, f32[1,32,1024]{2,1,0:T(8,128)S(1)}, u32[]{:S(2)}, u32[]{:S(2)}) collective-permute-start(f32[1,32,1024]{2,1,0:T(8,128)S(1)} %select_bitcast_fusion.4), channel_id=1, source_target_pairs={{0,8},{2,10},{4,12},{6,14},{8,0},{10,2},{12,4},{14,6},{1,9},{3,11}... | collective-permute-start | bytes 393224 | tf_op jit(solution)/shard_map/ppermute | solution.py:23
  80.3 76.6 %all-gather.5.cloned.1.call-start = ((), (), s32[]{:S(2)}) async-start(), calls=%async_computation.2 | async-start | bytes 2359296 | tf_op jit(solution)/shard_map/all_gather | solution.py:242
  80.5 19.7 %copy-start.7 = (f32[4096]{0:T(1024)S(1)}, f32[4096]{0:T(1024)}, u32[]{:S(2)}) copy-start(f32[4096]{0:T(1024)} %param.31) | copy-start | bytes 49156
  88.5 17.9 %copy-start.4 = (f32[128,64]{0,1:T(8,128)}, f32[128,64]{0,1:T(8,128)S(1)}, u32[]{:S(2)}) copy-start(f32[128,64]{0,1:T(8,128)S(1)} %get-tuple-element.26) | copy-start | bytes 98308
  88.5 18.0 %copy-start.11 = (s32[1024]{0:T(1024)S(1)}, s32[1024]{0:T(1024)}, u32[]{:S(2)}) copy-start(s32[1024]{0:T(1024)} %param.29) | copy-start | bytes 12292
  100.2 6.1 %copy-start.13 = (f32[128]{0:T(128)}, f32[128]{0:T(128)S(1)}, u32[]{:S(2)}) copy-start(f32[128]{0:T(128)S(1)} %add_rsqrt_fusion) | copy-start | bytes 1540
  104.2 1.4 collective-permute-start.7
  108.1 21.4 %copy-start.1 = (bf16[128,4096]{1,0:T(8,128)(2,1)S(1)}, bf16[128,4096]{1,0:T(8,128)(2,1)}, u32[]{:S(2)}) copy-start(bf16[128,4096]{1,0:T(8,128)(2,1)} %all-gather.3.cloned.1.call-done) | copy-start | bytes 3145732
  129.5 5.8 %copy-start.5 = (f32[128,64]{0,1:T(8,128)S(1)}, f32[128,64]{0,1:T(8,128)}, u32[]{:S(2)}) copy-start(f32[128,64]{0,1:T(8,128)} %copy-done.4) | copy-start | bytes 98308
  135.3 23.8 %copy-start.2 = (pred[128,1024]{0,1:T(8,128)(4,1)S(1)}, pred[128,1024]{0,1:T(8,128)(4,1)}, u32[]{:S(2)}) copy-start(pred[128,1024]{0,1:T(8,128)(4,1)} %compare_and_fusion) | copy-start | bytes 393220
  156.9 3.2 %copy-start.16 = (bf16[1024,2,4,128]{0,3,2,1:T(8,128)(2,1)S(1)}, bf16[1024,2,4,128]{0,3,2,1:T(8,128)(2,1)}, u32[]{:S(2)}) copy-start(bf16[1024,2,4,128]{0,3,2,1:T(8,128)(2,1)} %all-gather.5.cloned.1.call-done) | copy-start | bytes 6291460
Sparse Core Ops, SparseCore 0:
  80.4 18.2 all-gather.2
  106.5 50.3 all-gather.4

commit v13 on v10

--- a/solution.py
+++ b/solution.py
@@ -195,7 +195,19 @@
     picker = (target_slot[None, :] == slot_ids[:, None]).astype(jnp.bfloat16)
     ordered = jnp.dot(picker, merged, preferred_element_type=jnp.float32).astype(jnp.bfloat16)
     blocks = jnp.transpose(ordered.reshape(ICAP, shards, block_feats), (1, 0, 2))
-    received = lax.all_to_all(blocks, "ctx", split_axis=0, concat_axis=0, tiled=True)
+    by_shift = [lax.dynamic_index_in_dim(blocks, ctx_index, 0, keepdims=False)]
+    for shift in range(1, shards):
+        outgoing = lax.dynamic_index_in_dim(blocks, (ctx_index + shift) % shards, 0, keepdims=False)
+        by_shift.append(
+            lax.ppermute(outgoing, "ctx", [(i, (i + shift) % shards) for i in range(shards)])
+        )
+    by_shift = jnp.stack(by_shift, axis=0)
+    source_hot = (
+        shard_ids[None, :] == (ctx_index - shard_ids[:, None]) % shards
+    ).astype(jnp.bfloat16)
+    received = jnp.einsum(
+        "sk,kqf->sqf", source_hot, by_shift, preferred_element_type=jnp.float32
+    ).astype(jnp.bfloat16)
     by_dest = jnp.transpose(
         received.reshape(shards, shards, send_each, block_feats), (1, 0, 2, 3)
     ).reshape(shards * ICAP, block_feats)

time: 161 us -> 160 us (level)
  waiting for transfers between devices: 62.3 us -> 52.4 us
  starting transfers between devices: 16.9 us -> 23 us
  local copies, waits for them, and re-layouts: 32.1 us -> 34.7 us
    ppermute x0 -> x7, starting transfers between devices: none -> 12.8 us  [local(): lax.ppermute(outgoing, 'ctx', [(i, (i + shift) % shards) for i in range(s...]
    all_to_all x1 -> x0, waiting for transfers between devices: 10.4 us -> none  [local(): lax.all_to_all(blocks, 'ctx', split_axis=0, concat_axis=0, tiled=True)]
    all_to_all x1 -> x0, starting transfers between devices: 6.08 us -> none  [local(): lax.all_to_all(blocks, 'ctx', split_axis=0, concat_axis=0, tiled=True)]
    another operation x0 -> x9, local copies, waits for them, and re-layouts: none -> 3.28 us  [the longest x8 2.59 us: local(): by_shift = jnp.stack(by_shift, axis=0)]
    ppermute x0 -> x7, waiting for transfers between devices: none -> 2 us  [local(): lax.ppermute(outgoing, 'ctx', [(i, (i + shift) % shards) for i in range(s...]
  transfers between devices with their start and end apart: 11 -> 17, of which waited for: 11 -> 12; matrix products, arithmetic and copies ran while one was open for 25% -> 25% of each run, Pallas kernels for 0% -> 0%
where the time goes in v13:
time: 160 us; the launch traced here: 159 us
  waiting for transfers between devices  52.4 us (33%)
  local copies, waits for them, and re-layouts  34.7 us (22%)
  starting transfers between devices  23 us (14%)
  matrix products  20.8 us (13%)
  between operations  14.1 us (9%)
  other arithmetic  13.7 us (9%)
    ppermute x8, waiting for transfers between devices, swapped(): lax.ppermute(value, axis, [(i, i ^ 1 << stride) for i in range(lax.axis_s...  31.1 us
    optimization_barrier x1, local copies, waits for them, and re-layouts, local(): query_weights, own_half = lax.optimization_barrier((w_query, own_half))  21.4 us
    ppermute x7, starting transfers between devices, local(): lax.ppermute(outgoing, 'ctx', [(i, (i + shift) % shards) for i in range(s...  12.8 us
    unnamed x3, matrix products  11.6 us
    all_gather x1, waiting for transfers between devices, local(): gathered = lax.all_gather(own_half, 'ctx', axis=0, tiled=True)  10.6 us
    ppermute x8, starting transfers between devices, swapped(): lax.ppermute(value, axis, [(i, i ^ 1 << stride) for i in range(lax.axis_s...  9.86 us
    all_gather x1, waiting for transfers between devices, local(): full_rows = lax.all_gather(embeds, ('vis', 'tp'), axis=1, tiled=True)  8.63 us
    squeeze x1, local copies, waits for them, and re-layouts, local(): w_keyval[0]  7.62 us
  transfers between devices with their start and end apart: 17, of which 12 were waited for; matrix products, arithmetic and copies ran while one was open for 25% of the time, Pallas kernels for 0%

profile of v13, /device:TPU:0, one launch (start us, length us, event | category | flops | bytes accessed | tf_op | source)
XLA Modules:
  0.0 158.7 jit_solution(16570307759665006982)
XLA Ops:
  6.6 1.2 convert_reduce_fusion
  7.8 1.2 fusion.42
  9.1 1.9 %fusion.48 = f32[128,960]{0,1:S(1)} fusion(bf16[1280,960]{0,1:T(8,128)(2,1)S(1)} %bitcast.199, bf16[128,1280]{1,0:T(8,128)(2,1)} %param.17, f32[1280]{0:T(1024)} %param.19, f32[1280]{0:T(1024)} %param.18, f32[128]{0:T(128)S(1)} %add_rsqrt_fusion.2, f32[128]{0:T(128)S(1)} %broadcast_multiply_fusion.1), kind=kOutput, calls=%fused_computation.52 | convolution fusion | flops 315555840 | bytes 3288064
  11.2 0.3 fusion.110
  11.5 0.3 copy-done.3
  11.7 1.7 %fusion.22 = f32[128,1280,1]{1,0,2:T(8,128)S(1)} fusion(bf16[4,80,1280]{2,1,0:T(8,128)(2,1)} %param.21, f32[4,128,128]{1,2,0:T(8,128)S(1)} %get-tuple-element.38, f32[4,128]{1,0:T(4,128)S(1)} %get-tuple-element.37, bf16[128,3,4,80]{0,3,2,1:T(8,128)(2,1)} %copy-done.3, f32[128,4]{0,1:T(4,128)S(1)} %bitcast.234), kind=kOutput, calls=%fused_computation.29 | convolution fusion | flops 115556352 | bytes 1822720 | tf_op jit(solution)/shard_map/phd,hdf->pf/dot_general | solution.py:159
  13.5 0.6 collective-permute-start
  14.3 0.7 fusion.108
  15.0 0.4 collective-permute-done
  15.5 1.0 bitcast_add_fusion
  16.5 2.9 %collective-permute-start.1 = (f32[1,32,1280]{2,1,0:T(8,128)S(1)}, f32[1,32,1280]{2,1,0:T(8,128)S(1)}, u32[]{:S(2)}, u32[]{:S(2)}) collective-permute-start(f32[1,32,1280]{2,1,0:T(8,128)S(1)} %select_bitcast_fusion.3), channel_id=1, source_target_pairs={{0,16},{16,0},{1,17},{17,1},{2,18},{18,2},{3,19},{19,3},{4,20},{20... | collective-permute-start | bytes 491528 | tf_op jit(solution)/shard_map/ppermute | solution.py:23
  19.5 0.7 fusion.64
  20.2 3.7 %collective-permute-done.1 = f32[1,32,1280]{2,1,0:T(8,128)S(1)} collective-permute-done((f32[1,32,1280]{2,1,0:T(8,128)S(1)}, f32[1,32,1280]{2,1,0:T(8,128)S(1)}, u32[]{:S(2)}, u32[]{:S(2)}) %collective-permute-start.1) | collective-permute-done | bytes 163872 | tf_op jit(solution)/shard_map/ppermute | solution.py:23
  23.9 1.0 fusion.107
  25.0 0.2 multiply_reduce_fusion
  25.2 0.1 add_convert_fusion.1
  25.4 1.8 %collective-permute-start.2 = (bf16[1,8,5120]{2,1,0:T(8,128)(2,1)S(1)}, bf16[1,8,5120]{2,1,0:T(8,128)(2,1)S(1)}, u32[]{:S(2)}, u32[]{:S(2)}) collective-permute-start(bf16[1,8,5120]{2,1,0:T(8,128)(2,1)S(1)} %broadcast_in_dim_reshape.2), channel_id=1, source_target_pairs={{0,16},{16,0},{1,17},{17,1},{2,18},{18,2},{3,19},{19,3},{4,20},{20... | collective-permute-start | bytes 245768 | tf_op jit(solution)/shard_map/ppermute | solution.py:23
  27.2 0.1 select_reduce_fusion.3
  27.4 2.5 %collective-permute-done.2 = bf16[1,8,5120]{2,1,0:T(8,128)(2,1)S(1)} collective-permute-done((bf16[1,8,5120]{2,1,0:T(8,128)(2,1)S(1)}, bf16[1,8,5120]{2,1,0:T(8,128)(2,1)S(1)}, u32[]{:S(2)}, u32[]{:S(2)}) %collective-permute-start.2) | collective-permute-done | bytes 81952 | tf_op jit(solution)/shard_map/ppermute | solution.py:23
  30.0 1.4 collective-permute-done.3
  31.4 0.2 convolution_convert_fusion
  31.7 0.7 constant_dynamic-slice_fusion
  32.4 1.8 %collective-permute-start.4 = (bf16[32,640]{1,0:T(8,128)(2,1)S(1)}, bf16[32,640]{1,0:T(8,128)(2,1)S(1)}, u32[]{:S(2)}, u32[]{:S(2)}) collective-permute-start(bf16[32,640]{1,0:T(8,128)(2,1)S(1)} %bitcast.232), channel_id=1, source_target_pairs={{0,2},{2,4},{4,6},{6,8},{8,10},{10,12},{12,14},{14,0},{1,3},{3,5},... | collective-permute-start | bytes 122888 | tf_op jit(solution)/shard_map/ppermute | solution.py:202
  34.2 1.6 %collective-permute-start.5 = (bf16[32,640]{1,0:T(8,128)(2,1)S(1)}, bf16[32,640]{1,0:T(8,128)(2,1)S(1)}, u32[]{:S(2)}, u32[]{:S(2)}) collective-permute-start(bf16[32,640]{1,0:T(8,128)(2,1)S(1)} %bitcast.231), channel_id=1, source_target_pairs={{0,4},{2,6},{4,8},{6,10},{8,12},{10,14},{12,0},{14,2},{1,5},{3,7},... | collective-permute-start | bytes 122888 | tf_op jit(solution)/shard_map/ppermute | solution.py:202
  35.9 2.6 %collective-permute-start.6 = (bf16[32,640]{1,0:T(8,128)(2,1)S(1)}, bf16[32,640]{1,0:T(8,128)(2,1)S(1)}, u32[]{:S(2)}, u32[]{:S(2)}) collective-permute-start(bf16[32,640]{1,0:T(8,128)(2,1)S(1)} %bitcast.222), channel_id=1, source_target_pairs={{0,6},{2,8},{4,10},{6,12},{8,14},{10,0},{12,2},{14,4},{1,7},{3,9},... | collective-permute-start | bytes 122888 | tf_op jit(solution)/shard_map/ppermute | solution.py:202
  38.5 1.3 collective-permute-start.7
  39.8 2.7 %collective-permute-start.8 = (bf16[32,640]{1,0:T(8,128)(2,1)S(1)}, bf16[32,640]{1,0:T(8,128)(2,1)S(1)}, u32[]{:S(2)}, u32[]{:S(2)}) collective-permute-start(bf16[32,640]{1,0:T(8,128)(2,1)S(1)} %bitcast.226), channel_id=1, source_target_pairs={{0,10},{2,12},{4,14},{6,0},{8,2},{10,4},{12,6},{14,8},{1,11},{3,13... | collective-permute-start | bytes 122888 | tf_op jit(solution)/shard_map/ppermute | solution.py:202
  42.5 1.4 collective-permute-start.9
  43.9 1.4 collective-permute-start.10
  45.9 0.7 collective-permute-done.9
  46.7 1.3 collective-permute-done.10
  48.0 2.1 %stack.41 = bf16[8,32,640]{2,0,1:T(8,128)(2,1)S(1)} concatenate(bf16[1,32,640]{2,0,1:T(2,128)(2,1)S(1)} %get-tuple-element.32, bf16[1,32,640]{2,0,1:T(2,128)(2,1)S(1)} %copy.154, bf16[1,32,640]{2,0,1:T(2,128)(2,1)S(1)} %copy.155, bf16[1,32,640]{2,0,1:T(2,128)(2,1)S(1)} %copy.156, bf16[1,32,640]{2,0,1:T(2,128)(2,1)S(1)} %copy.157, bf16[1,32,640]{2,0,1:T(2,128)(2,1)S(1)} %copy.158, ...), dimensions={0} | concatenate | bytes 655360 | tf_op jit(solution)/shard_map/stack | solution.py:204
  50.2 0.3 convolution_convert_fusion.1
  50.5 0.1 copy.161
  50.7 1.9 %fusion.12 = f32[4,2,32,1024]{3,2,1,0:T(8,128)S(1)} fusion(bf16[4,2,32,640]{3,2,1,0:T(8,128)(2,1)S(1)} %dot_general.50, bf16[640,1024]{1,0:T(8,128)(2,1)} %param.24), kind=kOutput, calls=%fused_computation.16 | convolution fusion | flops 335544320 | bytes 2686976 | tf_op jit(solution)/shard_map/dot_general | solution.py:214
  52.7 1.6 %collective-permute-start.11 = (f32[4,32,1024]{2,1,0:T(8,128)S(1)}, f32[4,32,1024]{2,1,0:T(8,128)S(1)}, u32[]{:S(2)}, u32[]{:S(2)}) collective-permute-start(f32[4,32,1024]{2,1,0:T(8,128)S(1)} %select_bitcast_fusion), channel_id=1, source_target_pairs={{0,2},{2,0},{4,6},{6,4},{8,10},{10,8},{12,14},{14,12},{1,3},{3,1},... | collective-permute-start | bytes 1572872 | tf_op jit(solution)/shard_map/ppermute | solution.py:23
  54.4 9.5 %collective-permute-done.11 = f32[4,32,1024]{2,1,0:T(8,128)S(1)} collective-permute-done((f32[4,32,1024]{2,1,0:T(8,128)S(1)}, f32[4,32,1024]{2,1,0:T(8,128)S(1)}, u32[]{:S(2)}, u32[]{:S(2)}) %collective-permute-start.11) | collective-permute-done | bytes 524320 | tf_op jit(solution)/shard_map/ppermute | solution.py:23
  64.0 0.1 fusion.47
  64.1 0.7 select_bitcast_fusion.2
  64.8 1.4 collective-permute-start.12
  66.3 0.3 fusion.109
  66.6 4.9 %collective-permute-done.12 = f32[2,32,1024]{2,1,0:T(8,128)} collective-permute-done((f32[2,32,1024]{2,1,0:T(8,128)}, f32[2,32,1024]{2,1,0:T(8,128)}, u32[]{:S(2)}, u32[]{:S(2)}) %collective-permute-start.12) | collective-permute-done | bytes 262176 | tf_op jit(solution)/shard_map/ppermute | solution.py:23
  71.5 1.0 fusion.61
  72.5 1.6 collective-permute-start.13
  74.1 5.8 %collective-permute-done.13 = f32[1,32,1024]{2,1,0:T(8,128)S(1)} collective-permute-done((f32[1,32,1024]{2,1,0:T(8,128)S(1)}, f32[1,32,1024]{2,1,0:T(8,128)S(1)}, u32[]{:S(2)}, u32[]{:S(2)}) %collective-permute-start.13) | collective-permute-done | bytes 131104 | tf_op jit(solution)/shard_map/ppermute | solution.py:23
  79.8 1.0 fusion.18
  80.8 0.2 all-gather.5.cloned.1.call-start
  81.1 7.6 %copy.170 = bf16[4096,4,128]{0,2,1:T(8,128)(2,1)} copy(bf16[4096,4,128]{2,1,0:T(4,128)(2,1)} %bitcast.205) | data formatting | bytes 8388608 | tf_op jit(solution)/shard_map/squeeze | solution.py:242
  89.1 0.2 multiply_cosine_fusion
  89.3 8.6 %all-gather.3.cloned.1.call-done = bf16[128,4096]{1,0:T(8,128)(2,1)} async-done(((bf16[128,1024]{1,0:T(8,128)(2,1)}), bf16[128,4096]{1,0:T(8,128)(2,1)}) %all-gather.3.cloned.1.call-update) | async-done | bytes 1048592 | tf_op jit(solution)/shard_map/all_gather | solution.py:229
  98.0 1.5 fusion.3
  99.5 3.8 %fusion.56 = f32[128,512]{0,1:S(1)} fusion(bf16[4096,512]{0,1:T(8,128)(2,1)} %bitcast.206, bf16[128,4096]{1,0:T(8,128)(2,1)} %all-gather.3.cloned.1.call-done, f32[4096]{0:T(1024)S(1)} %copy-done.7, f32[128]{0:T(128)S(1)} %add_rsqrt_fusion), kind=kOutput, calls=%fused_computation.61 | convolution fusion | flops 538968064 | bytes 5521920
  103.4 0.7 fusion.58
  104.1 0.1 select_reduce_fusion
  104.3 0.1 select_reduce_fusion.4
  104.6 1.0 compare_and_fusion
  105.6 21.4 %copy.171 = bf16[4096,4,2,128]{0,3,2,1:T(8,128)(2,1)} copy(bf16[4096,4,2,128]{3,2,1,0:T(2,128)(2,1)} %param.32) | data formatting | bytes 16777216 | tf_op jit(solution)/shard_map/optimization_barrier | solution.py:247
  127.0 5.9 %fusion.54 = f32[128,1024]{0,1:S(1)} fusion(bf16[4096,1024]{0,1:T(8,128)(2,1)} %bitcast.200, bf16[128,4096]{1,0:T(8,128)(2,1)S(1)} %copy-done.1, f32[4096]{0:T(1024)S(1)} %copy-done.7, f32[128]{0:T(128)} %copy-done.15), kind=kOutput, calls=%fused_computation.60 | convolution fusion | flops 1075838976 | bytes 9978368
  133.1 10.6 %all-gather.5.cloned.1.call-done = bf16[1024,4,128]{0,2,1:T(8,128)(2,1)} async-done(((bf16[128,4,128]{0,2,1:T(8,128)(2,1)}), bf16[1024,4,128]{0,2,1:T(8,128)(2,1)}) %all-gather.5.cloned.1.call-update) | async-done | bytes 1048592 | tf_op jit(solution)/shard_map/all_gather | solution.py:248
  143.7 2.9 %collective-permute-done.14 = bf16[1024,4,128]{0,2,1:T(8,128)(2,1)S(1)} collective-permute-done((bf16[1024,4,128]{0,2,1:T(8,128)(2,1)}, bf16[1024,4,128]{0,2,1:T(8,128)(2,1)S(1)}, u32[]{:S(2)}, u32[]{:S(2)}) %collective-permute-start.14) | collective-permute-done | bytes 1048608 | tf_op jit(solution)/shard_map/ppermute | solution.py:23
  146.5 2.2 %fusion.2 = (f32[4,2,128]{2,1,0:T(2,128)S(1)}, f32[4,1024,128,2]{2,1,3,0:T(8,128)S(1)}) fusion(pred[128,1024]{0,1:T(8,128)(4,1)} %compare_and_fusion, bf16[128,4,2,128]{0,3,2,1:T(8,128)(2,1)S(1)} %pad_maximum_fusion, bf16[1024,4,128]{0,2,1:T(8,128)(2,1)} %all-gather.5.cloned.1.call-done, bf16[1024,4,128]{0,2,1:T(8,128)(2,1)S(1)} %collective-permute-done.14, ...), kind=kOutput, calls=%fused_computation.5 | convolution fusion | flops 272104448 | bytes 6688769 | tf_op jit(solution)/shard_map/qkgd,nkd->kgqn/dot_general | solution.py:271
  148.8 0.9 fusion
  149.7 1.3 fusion.35
  151.0 0.9 copy.177
  (117 shorter events, 2.9 us)
Async XLA Ops:
  6.5 2.5 %copy-start = (bf16[1280,3,4,80]{0,3,2,1:T(8,128)(2,1)S(1)}, bf16[1280,3,4,80]{0,3,2,1:T(8,128)(2,1)}, u32[]{:S(2)}) copy-start(bf16[1280,3,4,80]{0,3,2,1:T(8,128)(2,1)} %param.20) | copy-start | bytes 7372804
  6.5 4.5 %copy-start.18 = (s32[128]{0:T(128)S(1)}, s32[128]{0:T(128)}, u32[]{:S(2)}) copy-start(s32[128]{0:T(128)} %param.26) | copy-start | bytes 1540
  6.5 7.6 %copy-start.13 = (s32[256]{0:T(256)S(1)}, s32[256]{0:T(256)}, u32[]{:S(2)}) copy-start(s32[256]{0:T(256)} %param.27) | copy-start | bytes 3076
  6.5 7.7 %copy-start.8 = (s32[8]{0:T(128)S(1)}, s32[8]{0:T(128)}, u32[]{:S(2)}) copy-start(s32[8]{0:T(128)} %param.28) | copy-start | bytes 100
  6.5 91.4 %all-gather.3.cloned.1.call-start = ((), (), s32[]{:S(2)}) async-start(), calls=%async_computation | async-start | bytes 1310720 | tf_op jit(solution)/shard_map/all_gather | solution.py:229
  9.1 10.4 %copy-start.19 = (s32[8,2]{0,1:T(2,128)S(1)}, s32[8,2]{0,1:T(2,128)}, u32[]{:S(2)}) copy-start(s32[8,2]{0,1:T(2,128)} %param.25) | copy-start | bytes 196
  11.0 14.2 %copy-start.10 = (f32[1280]{0:T(1024)S(1)}, f32[1280]{0:T(1024)}, u32[]{:S(2)}) copy-start(f32[1280]{0:T(1024)} %param.23) | copy-start | bytes 15364
  11.0 14.2 %copy-start.11 = (f32[1280]{0:T(1024)S(1)}, f32[1280]{0:T(1024)}, u32[]{:S(2)}) copy-start(f32[1280]{0:T(1024)} %param.22) | copy-start | bytes 15364
  11.0 0.7 copy-start.3
  13.5 1.9 %collective-permute-start = (f32[1,64,1280]{2,1,0:T(8,128)S(1)}, f32[1,64,1280]{2,1,0:T(8,128)}, u32[]{:S(2)}, u32[]{:S(2)}) collective-permute-start(f32[1,64,1280]{2,1,0:T(8,128)S(1)} %select_bitcast_fusion.1), channel_id=1, source_target_pairs={{0,1},{1,0},{2,3},{3,2},{4,5},{5,4},{6,7},{7,6},{8,9},{9,8},{10,11... | collective-permute-start | bytes 983048 | tf_op jit(solution)/shard_map/ppermute | solution.py:23
  16.5 7.4 %collective-permute-start.1 = (f32[1,32,1280]{2,1,0:T(8,128)S(1)}, f32[1,32,1280]{2,1,0:T(8,128)S(1)}, u32[]{:S(2)}, u32[]{:S(2)}) collective-permute-start(f32[1,32,1280]{2,1,0:T(8,128)S(1)} %select_bitcast_fusion.3), channel_id=1, source_target_pairs={{0,16},{16,0},{1,17},{17,1},{2,18},{18,2},{3,19},{19,3},{4,20},{20... | collective-permute-start | bytes 491528 | tf_op jit(solution)/shard_map/ppermute | solution.py:23
  19.5 12.2 %copy-start.16 = (pred[8]{0:T(512)(128)(4,1)}, pred[8]{0:T(512)(128)(4,1)S(1)}, u32[]{:S(2)}) copy-start(pred[8]{0:T(512)(128)(4,1)S(1)} %iota_compare_fusion.10) | copy-start | bytes 28
  25.4 4.5 %collective-permute-start.2 = (bf16[1,8,5120]{2,1,0:T(8,128)(2,1)S(1)}, bf16[1,8,5120]{2,1,0:T(8,128)(2,1)S(1)}, u32[]{:S(2)}, u32[]{:S(2)}) collective-permute-start(bf16[1,8,5120]{2,1,0:T(8,128)(2,1)S(1)} %broadcast_in_dim_reshape.2), channel_id=1, source_target_pairs={{0,16},{16,0},{1,17},{17,1},{2,18},{18,2},{3,19},{19,3},{4,20},{20... | collective-permute-start | bytes 245768 | tf_op jit(solution)/shard_map/ppermute | solution.py:23
  29.9 1.5 collective-permute-start.3
  32.4 10.1 %collective-permute-start.4 = (bf16[32,640]{1,0:T(8,128)(2,1)S(1)}, bf16[32,640]{1,0:T(8,128)(2,1)S(1)}, u32[]{:S(2)}, u32[]{:S(2)}) collective-permute-start(bf16[32,640]{1,0:T(8,128)(2,1)S(1)} %bitcast.232), channel_id=1, source_target_pairs={{0,2},{2,4},{4,6},{6,8},{8,10},{10,12},{12,14},{14,0},{1,3},{3,5},... | collective-permute-start | bytes 122888 | tf_op jit(solution)/shard_map/ppermute | solution.py:202
  34.2 9.7 %collective-permute-start.5 = (bf16[32,640]{1,0:T(8,128)(2,1)S(1)}, bf16[32,640]{1,0:T(8,128)(2,1)S(1)}, u32[]{:S(2)}, u32[]{:S(2)}) collective-permute-start(bf16[32,640]{1,0:T(8,128)(2,1)S(1)} %bitcast.231), channel_id=1, source_target_pairs={{0,4},{2,6},{4,8},{6,10},{8,12},{10,14},{12,0},{14,2},{1,5},{3,7},... | collective-permute-start | bytes 122888 | tf_op jit(solution)/shard_map/ppermute | solution.py:202
  35.9 9.7 %collective-permute-start.6 = (bf16[32,640]{1,0:T(8,128)(2,1)S(1)}, bf16[32,640]{1,0:T(8,128)(2,1)S(1)}, u32[]{:S(2)}, u32[]{:S(2)}) collective-permute-start(bf16[32,640]{1,0:T(8,128)(2,1)S(1)} %bitcast.222), channel_id=1, source_target_pairs={{0,6},{2,8},{4,10},{6,12},{8,14},{10,0},{12,2},{14,4},{1,7},{3,9},... | collective-permute-start | bytes 122888 | tf_op jit(solution)/shard_map/ppermute | solution.py:202
  38.5 7.2 %collective-permute-start.7 = (bf16[32,640]{1,0:T(8,128)(2,1)S(1)}, bf16[32,640]{1,0:T(8,128)(2,1)S(1)}, u32[]{:S(2)}, u32[]{:S(2)}) collective-permute-start(bf16[32,640]{1,0:T(8,128)(2,1)S(1)} %bitcast.224), channel_id=1, source_target_pairs={{0,8},{2,10},{4,12},{6,14},{8,0},{10,2},{12,4},{14,6},{1,9},{3,11}... | collective-permute-start | bytes 122888 | tf_op jit(solution)/shard_map/ppermute | solution.py:202
  39.8 6.0 %collective-permute-start.8 = (bf16[32,640]{1,0:T(8,128)(2,1)S(1)}, bf16[32,640]{1,0:T(8,128)(2,1)S(1)}, u32[]{:S(2)}, u32[]{:S(2)}) collective-permute-start(bf16[32,640]{1,0:T(8,128)(2,1)S(1)} %bitcast.226), channel_id=1, source_target_pairs={{0,10},{2,12},{4,14},{6,0},{8,2},{10,4},{12,6},{14,8},{1,11},{3,13... | collective-permute-start | bytes 122888 | tf_op jit(solution)/shard_map/ppermute | solution.py:202
  42.5 4.1 %collective-permute-start.9 = (bf16[32,640]{1,0:T(8,128)(2,1)S(1)}, bf16[32,640]{1,0:T(8,128)(2,1)S(1)}, u32[]{:S(2)}, u32[]{:S(2)}) collective-permute-start(bf16[32,640]{1,0:T(8,128)(2,1)S(1)} %bitcast.228), channel_id=1, source_target_pairs={{0,12},{2,14},{4,0},{6,2},{8,4},{10,6},{12,8},{14,10},{1,13},{3,15... | collective-permute-start | bytes 122888 | tf_op jit(solution)/shard_map/ppermute | solution.py:202
  43.9 4.0 %collective-permute-start.10 = (bf16[32,640]{1,0:T(8,128)(2,1)S(1)}, bf16[32,640]{1,0:T(8,128)(2,1)S(1)}, u32[]{:S(2)}, u32[]{:S(2)}) collective-permute-start(bf16[32,640]{1,0:T(8,128)(2,1)S(1)} %bitcast.220), channel_id=1, source_target_pairs={{0,14},{2,0},{4,2},{6,4},{8,6},{10,8},{12,10},{14,12},{1,15},{3,1}... | collective-permute-start | bytes 122888 | tf_op jit(solution)/shard_map/ppermute | solution.py:202
  50.5 15.7 %copy-start.14 = (s32[256]{0:T(256)S(1)}, s32[256]{0:T(256)}, u32[]{:S(2)}) copy-start(s32[256]{0:T(256)} %param.27) | copy-start | bytes 3076
  50.7 29.2 %copy-start.6 = (bf16[128,1024]{1,0:T(8,128)(2,1)S(1)}, bf16[128,1024]{1,0:T(8,128)(2,1)}, u32[]{:S(2)}) copy-start(bf16[128,1024]{1,0:T(8,128)(2,1)} %param.30) | copy-start | bytes 786436
  52.7 11.3 %collective-permute-start.11 = (f32[4,32,1024]{2,1,0:T(8,128)S(1)}, f32[4,32,1024]{2,1,0:T(8,128)S(1)}, u32[]{:S(2)}, u32[]{:S(2)}) collective-permute-start(f32[4,32,1024]{2,1,0:T(8,128)S(1)} %select_bitcast_fusion), channel_id=1, source_target_pairs={{0,2},{2,0},{4,6},{6,4},{8,10},{10,8},{12,14},{14,12},{1,3},{3,1},... | collective-permute-start | bytes 1572872 | tf_op jit(solution)/shard_map/ppermute | solution.py:23
  64.8 6.7 %collective-permute-start.12 = (f32[2,32,1024]{2,1,0:T(8,128)}, f32[2,32,1024]{2,1,0:T(8,128)}, u32[]{:S(2)}, u32[]{:S(2)}) collective-permute-start(f32[2,32,1024]{2,1,0:T(8,128)} %select_bitcast_fusion.2), channel_id=1, source_target_pairs={{0,4},{2,6},{4,0},{6,2},{8,12},{10,14},{12,8},{14,10},{1,5},{3,7},... | collective-permute-start | bytes 786440 | tf_op jit(solution)/shard_map/ppermute | solution.py:23
  72.5 7.3 %collective-permute-start.13 = (f32[1,32,1024]{2,1,0:T(8,128)S(1)}, f32[1,32,1024]{2,1,0:T(8,128)S(1)}, u32[]{:S(2)}, u32[]{:S(2)}) collective-permute-start(f32[1,32,1024]{2,1,0:T(8,128)S(1)} %select_bitcast_fusion.4), channel_id=1, source_target_pairs={{0,8},{2,10},{4,12},{6,14},{8,0},{10,2},{12,4},{14,6},{1,9},{3,11}... | collective-permute-start | bytes 393224 | tf_op jit(solution)/shard_map/ppermute | solution.py:23
  80.8 62.8 %all-gather.5.cloned.1.call-start = ((), (), s32[]{:S(2)}) async-start(), calls=%async_computation.1 | async-start | bytes 1179648 | tf_op jit(solution)/shard_map/all_gather | solution.py:248
  81.1 7.7 %copy-start.9 = (s32[8]{0:T(128)S(1)}, s32[8]{0:T(128)}, u32[]{:S(2)}) copy-start(s32[8]{0:T(128)} %param.28) | copy-start | bytes 100
  81.1 7.8 %copy-start.12 = (s32[1024]{0:T(1024)S(1)}, s32[1024]{0:T(1024)}, u32[]{:S(2)}) copy-start(s32[1024]{0:T(1024)} %param.29) | copy-start | bytes 12292
  81.1 18.4 %copy-start.7 = (f32[4096]{0:T(1024)S(1)}, f32[4096]{0:T(1024)}, u32[]{:S(2)}) copy-start(f32[4096]{0:T(1024)} %param.31) | copy-start | bytes 49156
  88.7 15.6 %copy-start.17 = (pred[8]{0:T(512)(128)(4,1)S(1)}, pred[8]{0:T(512)(128)(4,1)}, u32[]{:S(2)}) copy-start(pred[8]{0:T(512)(128)(4,1)} %copy-done.16) | copy-start | bytes 28
  89.3 15.3 %copy-start.4 = (f32[128,64]{0,1:T(8,128)}, f32[128,64]{0,1:T(8,128)S(1)}, u32[]{:S(2)}) copy-start(f32[128,64]{0,1:T(8,128)S(1)} %get-tuple-element.34) | copy-start | bytes 98308
  99.5 3.9 %copy-start.15 = (f32[128]{0:T(128)}, f32[128]{0:T(128)S(1)}, u32[]{:S(2)}) copy-start(f32[128]{0:T(128)S(1)} %add_rsqrt_fusion) | copy-start | bytes 1540
  105.6 21.4 %copy-start.1 = (bf16[128,4096]{1,0:T(8,128)(2,1)S(1)}, bf16[128,4096]{1,0:T(8,128)(2,1)}, u32[]{:S(2)}) copy-start(bf16[128,4096]{1,0:T(8,128)(2,1)} %all-gather.3.cloned.1.call-done) | copy-start | bytes 3145732
  127.0 5.9 %copy-start.5 = (f32[128,64]{0,1:T(8,128)S(1)}, f32[128,64]{0,1:T(8,128)}, u32[]{:S(2)}) copy-start(f32[128,64]{0,1:T(8,128)} %copy-done.4) | copy-start | bytes 98308
  132.9 15.9 %copy-start.2 = (pred[128,1024]{0,1:T(8,128)(4,1)S(1)}, pred[128,1024]{0,1:T(8,128)(4,1)}, u32[]{:S(2)}) copy-start(pred[128,1024]{0,1:T(8,128)(4,1)} %compare_and_fusion) | copy-start | bytes 393220
  143.7 6.0 %copy-start.20 = (bf16[1024,4,128]{0,2,1:T(8,128)(2,1)S(1)}, bf16[1024,4,128]{0,2,1:T(8,128)(2,1)}, u32[]{:S(2)}) copy-start(bf16[1024,4,128]{0,2,1:T(8,128)(2,1)} %all-gather.5.cloned.1.call-done) | copy-start | bytes 3145732
  143.7 2.9 %collective-permute-start.14 = (bf16[1024,4,128]{0,2,1:T(8,128)(2,1)}, bf16[1024,4,128]{0,2,1:T(8,128)(2,1)S(1)}, u32[]{:S(2)}, u32[]{:S(2)}) collective-permute-start(bf16[1024,4,128]{0,2,1:T(8,128)(2,1)} %all-gather.5.cloned.1.call-done), channel_id=1, source_target_pairs={{0,1},{1,0},{2,3},{3,2},{4,5},{5,4},{6,7},{7,6},{8,9},{9,8},{10,11... | collective-permute-start | bytes 3145736 | tf_op jit(solution)/shard_map/ppermute | solution.py:23
Sparse Core Ops, SparseCore 0:
  81.0 16.9 all-gather.2
  104.2 39.3 all-gather.4

commit v14 on v13

--- a/solution.py
+++ b/solution.py
@@ -212,9 +212,14 @@
         received.reshape(shards, shards, send_each, block_feats), (1, 0, 2, 3)
     ).reshape(shards * ICAP, block_feats)
     partial = jnp.dot(by_dest, merge_weight, preferred_element_type=jnp.float32)
-    incoming = halving_scatter(partial.reshape(shards, ICAP, -1), ctx_index, shards).astype(
-        jnp.bfloat16
-    )
+    partial = partial.reshape(shards, ICAP, -1)
+    summed = lax.dynamic_index_in_dim(partial, ctx_index, 0, keepdims=False)
+    for shift in range(1, shards):
+        outgoing = lax.dynamic_index_in_dim(partial, (ctx_index + shift) % shards, 0, keepdims=False)
+        summed = summed + lax.ppermute(
+            outgoing, "ctx", [(i, (i + shift) % shards) for i in range(shards)]
+        )
+    incoming = summed.astype(jnp.bfloat16)
     mine_live = ((owner_dev == ctx_index) & is_live).reshape(-1)
     column_of = (shard_ids[:, None] * send_each + rank_in).reshape(-1)
     row_hot = (

time: 160 us -> 157 us (0.981)
  waiting for transfers between devices: 52.4 us -> 45.9 us
  starting transfers between devices: 23 us -> 29.1 us
  other arithmetic: 13.7 us -> 11.8 us
    ppermute x8 -> x5, waiting for transfers between devices: 31.1 us -> 11.5 us  [swapped(): lax.ppermute(value, axis, [(i, i ^ 1 << stride) for i in range(lax.axis_s...]
    ppermute x7 -> x14, starting transfers between devices: 12.8 us -> 23.8 us  [local(): lax.ppermute(outgoing, 'ctx', [(i, (i + shift) % shards) for i in range(s...]
    all_gather x1, waiting for transfers between devices: 8.63 us -> 15.4 us  [local(): full_rows = lax.all_gather(embeds, ('vis', 'tp'), axis=1, tiled=True)]
    ppermute x7 -> x14, waiting for transfers between devices: 2 us -> 8.29 us  [local(): lax.ppermute(outgoing, 'ctx', [(i, (i + shift) % shards) for i in range(s...]
    ppermute x8 -> x5, starting transfers between devices: 9.86 us -> 5 us  [swapped(): lax.ppermute(value, axis, [(i, i ^ 1 << stride) for i in range(lax.axis_s...]
  transfers between devices with their start and end apart: 17 -> 21, of which waited for: 12 -> 11; matrix products, arithmetic and copies ran while one was open for 25% -> 26% of each run, Pallas kernels for 0% -> 0%
where the time goes in v14:
time: 157 us; the launch traced here: 156 us
  waiting for transfers between devices  45.9 us (29%)
  local copies, waits for them, and re-layouts  34.8 us (22%)
  starting transfers between devices  29.1 us (19%)
  matrix products  20.8 us (13%)
  between operations  14 us (9%)
  other arithmetic  11.8 us (8%)
    ppermute x14, starting transfers between devices, local(): lax.ppermute(outgoing, 'ctx', [(i, (i + shift) % shards) for i in range(s...  23.8 us
    optimization_barrier x1, local copies, waits for them, and re-layouts, local(): query_weights, own_half = lax.optimization_barrier((w_query, own_half))  21.4 us
    all_gather x1, waiting for transfers between devices, local(): full_rows = lax.all_gather(embeds, ('vis', 'tp'), axis=1, tiled=True)  15.4 us
    unnamed x3, matrix products  11.6 us
    ppermute x5, waiting for transfers between devices, swapped(): lax.ppermute(value, axis, [(i, i ^ 1 << stride) for i in range(lax.axis_s...  11.5 us
    all_gather x1, waiting for transfers between devices, local(): gathered = lax.all_gather(own_half, 'ctx', axis=0, tiled=True)  10.6 us
    ppermute x14, waiting for transfers between devices, local(): lax.ppermute(outgoing, 'ctx', [(i, (i + shift) % shards) for i in range(s...  8.29 us
    squeeze x1, local copies, waits for them, and re-layouts, local(): w_keyval[0]  7.6 us
  transfers between devices with their start and end apart: 21, of which 11 were waited for; matrix products, arithmetic and copies ran while one was open for 26% of the time, Pallas kernels for 0%

profile of v14, /device:TPU:0, one launch (start us, length us, event | category | flops | bytes accessed | tf_op | source)
XLA Modules:
  0.0 156.4 jit_solution(18284228772254314745)
XLA Ops:
  6.6 1.2 convert_reduce_fusion
  7.9 1.2 fusion.42
  9.1 1.9 %fusion.46 = f32[128,960]{0,1:S(1)} fusion(bf16[1280,960]{0,1:T(8,128)(2,1)S(1)} %bitcast.173, bf16[128,1280]{1,0:T(8,128)(2,1)} %param.17, f32[1280]{0:T(1024)} %param.19, f32[1280]{0:T(1024)} %param.18, f32[128]{0:T(128)S(1)} %add_rsqrt_fusion.2, f32[128]{0:T(128)S(1)} %broadcast_multiply_fusion.1), kind=kOutput, calls=%fused_computation.48 | convolution fusion | flops 315555840 | bytes 3288064
  11.2 0.3 fusion.110
  11.5 0.3 copy-done.3
  11.7 1.7 %fusion.22 = f32[128,1280,1]{1,0,2:T(8,128)S(1)} fusion(bf16[4,80,1280]{2,1,0:T(8,128)(2,1)} %param.21, f32[4,128,128]{1,2,0:T(8,128)S(1)} %get-tuple-element.45, f32[4,128]{1,0:T(4,128)S(1)} %get-tuple-element.44, bf16[128,3,4,80]{0,3,2,1:T(8,128)(2,1)} %copy-done.3, f32[128,4]{0,1:T(4,128)S(1)} %bitcast.206), kind=kOutput, calls=%fused_computation.29 | convolution fusion | flops 115556352 | bytes 1822720 | tf_op jit(solution)/shard_map/phd,hdf->pf/dot_general | solution.py:159
  13.5 0.6 collective-permute-start
  14.3 0.7 fusion.108
  15.0 0.7 fusion.59
  16.0 1.0 bitcast_add_fusion
  17.0 2.6 %collective-permute-start.1 = (f32[1,32,1280]{2,1,0:T(8,128)S(1)}, f32[1,32,1280]{2,1,0:T(8,128)S(1)}, u32[]{:S(2)}, u32[]{:S(2)}) collective-permute-start(f32[1,32,1280]{2,1,0:T(8,128)S(1)} %select_bitcast_fusion.1), channel_id=1, source_target_pairs={{0,16},{16,0},{1,17},{17,1},{2,18},{18,2},{3,19},{19,3},{4,20},{20... | collective-permute-start | bytes 491528 | tf_op jit(solution)/shard_map/ppermute | solution.py:23
  19.7 4.8 %collective-permute-done.1 = f32[1,32,1280]{2,1,0:T(8,128)S(1)} collective-permute-done((f32[1,32,1280]{2,1,0:T(8,128)S(1)}, f32[1,32,1280]{2,1,0:T(8,128)S(1)}, u32[]{:S(2)}, u32[]{:S(2)}) %collective-permute-start.1) | collective-permute-done | bytes 163872 | tf_op jit(solution)/shard_map/ppermute | solution.py:23
  24.4 1.0 fusion.107
  25.5 0.2 multiply_reduce_fusion
  25.7 0.1 add_convert_fusion.1
  25.9 1.8 %collective-permute-start.2 = (bf16[1,8,5120]{2,1,0:T(8,128)(2,1)S(1)}, bf16[1,8,5120]{2,1,0:T(8,128)(2,1)S(1)}, u32[]{:S(2)}, u32[]{:S(2)}) collective-permute-start(bf16[1,8,5120]{2,1,0:T(8,128)(2,1)S(1)} %broadcast_in_dim_reshape.2), channel_id=1, source_target_pairs={{0,16},{16,0},{1,17},{17,1},{2,18},{18,2},{3,19},{19,3},{4,20},{20... | collective-permute-start | bytes 245768 | tf_op jit(solution)/shard_map/ppermute | solution.py:23
  27.7 0.1 select_reduce_fusion.3
  27.9 2.5 %collective-permute-done.2 = bf16[1,8,5120]{2,1,0:T(8,128)(2,1)S(1)} collective-permute-done((bf16[1,8,5120]{2,1,0:T(8,128)(2,1)S(1)}, bf16[1,8,5120]{2,1,0:T(8,128)(2,1)S(1)}, u32[]{:S(2)}, u32[]{:S(2)}) %collective-permute-start.2) | collective-permute-done | bytes 81952 | tf_op jit(solution)/shard_map/ppermute | solution.py:23
  30.5 1.4 collective-permute-done.3
  31.9 0.2 convolution_convert_fusion
  32.2 0.7 constant_dynamic-slice_fusion
  32.9 1.8 %collective-permute-start.4 = (bf16[32,640]{1,0:T(8,128)(2,1)S(1)}, bf16[32,640]{1,0:T(8,128)(2,1)S(1)}, u32[]{:S(2)}, u32[]{:S(2)}) collective-permute-start(bf16[32,640]{1,0:T(8,128)(2,1)S(1)} %bitcast.204), channel_id=1, source_target_pairs={{0,2},{2,4},{4,6},{6,8},{8,10},{10,12},{12,14},{14,0},{1,3},{3,5},... | collective-permute-start | bytes 122888 | tf_op jit(solution)/shard_map/ppermute | solution.py:202
  34.7 1.6 %collective-permute-start.5 = (bf16[32,640]{1,0:T(8,128)(2,1)S(1)}, bf16[32,640]{1,0:T(8,128)(2,1)S(1)}, u32[]{:S(2)}, u32[]{:S(2)}) collective-permute-start(bf16[32,640]{1,0:T(8,128)(2,1)S(1)} %bitcast.203), channel_id=1, source_target_pairs={{0,4},{2,6},{4,8},{6,10},{8,12},{10,14},{12,0},{14,2},{1,5},{3,7},... | collective-permute-start | bytes 122888 | tf_op jit(solution)/shard_map/ppermute | solution.py:202
  36.4 2.6 %collective-permute-start.6 = (bf16[32,640]{1,0:T(8,128)(2,1)S(1)}, bf16[32,640]{1,0:T(8,128)(2,1)S(1)}, u32[]{:S(2)}, u32[]{:S(2)}) collective-permute-start(bf16[32,640]{1,0:T(8,128)(2,1)S(1)} %bitcast.194), channel_id=1, source_target_pairs={{0,6},{2,8},{4,10},{6,12},{8,14},{10,0},{12,2},{14,4},{1,7},{3,9},... | collective-permute-start | bytes 122888 | tf_op jit(solution)/shard_map/ppermute | solution.py:202
  39.0 1.3 collective-permute-start.7
  40.3 2.7 %collective-permute-start.8 = (bf16[32,640]{1,0:T(8,128)(2,1)S(1)}, bf16[32,640]{1,0:T(8,128)(2,1)S(1)}, u32[]{:S(2)}, u32[]{:S(2)}) collective-permute-start(bf16[32,640]{1,0:T(8,128)(2,1)S(1)} %bitcast.198), channel_id=1, source_target_pairs={{0,10},{2,12},{4,14},{6,0},{8,2},{10,4},{12,6},{14,8},{1,11},{3,13... | collective-permute-start | bytes 122888 | tf_op jit(solution)/shard_map/ppermute | solution.py:202
  43.0 1.4 collective-permute-start.9
  44.4 1.4 collective-permute-start.10
  46.4 0.7 collective-permute-done.9
  47.2 1.3 collective-permute-done.10
  48.5 2.1 %stack.41 = bf16[8,32,640]{2,0,1:T(8,128)(2,1)S(1)} concatenate(bf16[1,32,640]{2,0,1:T(2,128)(2,1)S(1)} %get-tuple-element.39, bf16[1,32,640]{2,0,1:T(2,128)(2,1)S(1)} %copy.122, bf16[1,32,640]{2,0,1:T(2,128)(2,1)S(1)} %copy.123, bf16[1,32,640]{2,0,1:T(2,128)(2,1)S(1)} %copy.124, bf16[1,32,640]{2,0,1:T(2,128)(2,1)S(1)} %copy.125, bf16[1,32,640]{2,0,1:T(2,128)(2,1)S(1)} %copy.126, ...), dimensions={0} | concatenate | bytes 655360 | tf_op jit(solution)/shard_map/stack | solution.py:204
  50.7 0.3 convolution_convert_fusion.1
  51.0 0.1 copy.129
  51.2 1.9 %fusion.12 = f32[8,32,1024]{2,1,0:T(8,128)S(1)} fusion(bf16[8,32,640]{2,1,0:T(8,128)(2,1)S(1)} %dot_general.50, bf16[640,1024]{1,0:T(8,128)(2,1)} %param.24), kind=kOutput, calls=%fused_computation.16 | convolution fusion | flops 335544320 | bytes 2686976 | tf_op jit(solution)/shard_map/dot_general | solution.py:214
  53.1 0.1 dynamic-slice_bitcast_fusion.6
  53.2 1.6 %collective-permute-start.11 = (f32[32,1024]{1,0:T(8,128)S(1)}, f32[32,1024]{1,0:T(8,128)S(1)}, u32[]{:S(2)}, u32[]{:S(2)}) collective-permute-start(f32[32,1024]{1,0:T(8,128)S(1)} %get-tuple-element.21), channel_id=1, source_target_pairs={{0,2},{2,4},{4,6},{6,8},{8,10},{10,12},{12,14},{14,0},{1,3},{3,5},... | collective-permute-start | bytes 393224 | tf_op jit(solution)/shard_map/ppermute | solution.py:219
  54.8 0.3 fusion.109
  55.1 2.4 %collective-permute-start.13 = (f32[32,1024]{1,0:T(8,128)S(1)}, f32[32,1024]{1,0:T(8,128)S(1)}, u32[]{:S(2)}, u32[]{:S(2)}) collective-permute-start(f32[32,1024]{1,0:T(8,128)S(1)} %get-tuple-element.26), channel_id=1, source_target_pairs={{0,6},{2,8},{4,10},{6,12},{8,14},{10,0},{12,2},{14,4},{1,7},{3,9},... | collective-permute-start | bytes 393224 | tf_op jit(solution)/shard_map/ppermute | solution.py:219
  57.5 2.1 %collective-permute-start.14 = (f32[32,1024]{1,0:T(8,128)S(1)}, f32[32,1024]{1,0:T(8,128)S(1)}, u32[]{:S(2)}, u32[]{:S(2)}) collective-permute-start(f32[32,1024]{1,0:T(8,128)S(1)} %get-tuple-element.25), channel_id=1, source_target_pairs={{0,8},{2,10},{4,12},{6,14},{8,0},{10,2},{12,4},{14,6},{1,9},{3,11}... | collective-permute-start | bytes 393224 | tf_op jit(solution)/shard_map/ppermute | solution.py:219
  59.5 3.1 %collective-permute-start.15 = (f32[32,1024]{1,0:T(8,128)S(1)}, f32[32,1024]{1,0:T(8,128)S(1)}, u32[]{:S(2)}, u32[]{:S(2)}) collective-permute-start(f32[32,1024]{1,0:T(8,128)S(1)} %get-tuple-element.24), channel_id=1, source_target_pairs={{0,10},{2,12},{4,14},{6,0},{8,2},{10,4},{12,6},{14,8},{1,11},{3,13... | collective-permute-start | bytes 393224 | tf_op jit(solution)/shard_map/ppermute | solution.py:219
  62.6 0.1 collective-permute-start.16
  62.7 0.3 collective-permute-done.12
  63.0 1.7 %collective-permute-start.17 = (f32[32,1024]{1,0:T(8,128)S(1)}, f32[32,1024]{1,0:T(8,128)S(1)}, u32[]{:S(2)}, u32[]{:S(2)}) collective-permute-start(f32[32,1024]{1,0:T(8,128)S(1)} %get-tuple-element.22), channel_id=1, source_target_pairs={{0,14},{2,0},{4,2},{6,4},{8,6},{10,8},{12,10},{14,12},{1,15},{3,1}... | collective-permute-start | bytes 393224 | tf_op jit(solution)/shard_map/ppermute | solution.py:219
  64.7 5.5 %collective-permute-done.13 = f32[32,1024]{1,0:T(8,128)S(1)} collective-permute-done((f32[32,1024]{1,0:T(8,128)S(1)}, f32[32,1024]{1,0:T(8,128)S(1)}, u32[]{:S(2)}, u32[]{:S(2)}) %collective-permute-start.13) | collective-permute-done | bytes 131104 | tf_op jit(solution)/shard_map/ppermute | solution.py:219
  70.2 0.6 collective-permute-done.14
  70.8 1.0 fusion.18
  71.8 0.2 all-gather.5.cloned.1.call-start
  72.0 7.6 %copy.130 = bf16[4096,4,128]{0,2,1:T(8,128)(2,1)} copy(bf16[4096,4,128]{2,1,0:T(4,128)(2,1)} %bitcast.177) | data formatting | bytes 8388608 | tf_op jit(solution)/shard_map/squeeze | solution.py:247
  80.0 0.2 multiply_cosine_fusion
  80.2 15.4 %all-gather.3.cloned.1.call-done = bf16[128,4096]{1,0:T(8,128)(2,1)} async-done(((bf16[128,1024]{1,0:T(8,128)(2,1)}), bf16[128,4096]{1,0:T(8,128)(2,1)}) %all-gather.3.cloned.1.call-update) | async-done | bytes 1048592 | tf_op jit(solution)/shard_map/all_gather | solution.py:234
  95.6 1.5 fusion.3
  97.2 3.8 %fusion.54 = f32[128,512]{0,1:S(1)} fusion(bf16[4096,512]{0,1:T(8,128)(2,1)} %bitcast.178, bf16[128,4096]{1,0:T(8,128)(2,1)} %all-gather.3.cloned.1.call-done, f32[4096]{0:T(1024)S(1)} %copy-done.7, f32[128]{0:T(128)S(1)} %add_rsqrt_fusion), kind=kOutput, calls=%fused_computation.57 | convolution fusion | flops 538968064 | bytes 5521920
  101.1 0.7 fusion.56
  101.8 0.1 select_reduce_fusion
  102.0 0.1 select_reduce_fusion.4
  102.3 1.0 compare_and_fusion
  103.3 21.4 %copy.131 = bf16[4096,4,2,128]{0,3,2,1:T(8,128)(2,1)} copy(bf16[4096,4,2,128]{3,2,1,0:T(2,128)(2,1)} %param.32) | data formatting | bytes 16777216 | tf_op jit(solution)/shard_map/optimization_barrier | solution.py:252
  124.7 5.9 %fusion.52 = f32[128,1024]{0,1:S(1)} fusion(bf16[4096,1024]{0,1:T(8,128)(2,1)} %bitcast.174, bf16[128,4096]{1,0:T(8,128)(2,1)S(1)} %copy-done.1, f32[4096]{0:T(1024)S(1)} %copy-done.7, f32[128]{0:T(128)} %copy-done.13), kind=kOutput, calls=%fused_computation.56 | convolution fusion | flops 1075838976 | bytes 9978368
  130.7 10.6 %all-gather.5.cloned.1.call-done = bf16[1024,4,128]{0,2,1:T(8,128)(2,1)} async-done(((bf16[128,4,128]{0,2,1:T(8,128)(2,1)}), bf16[1024,4,128]{0,2,1:T(8,128)(2,1)}) %all-gather.5.cloned.1.call-update) | async-done | bytes 1048592 | tf_op jit(solution)/shard_map/all_gather | solution.py:253
  141.3 2.9 %collective-permute-done.18 = bf16[1024,4,128]{0,2,1:T(8,128)(2,1)S(1)} collective-permute-done((bf16[1024,4,128]{0,2,1:T(8,128)(2,1)}, bf16[1024,4,128]{0,2,1:T(8,128)(2,1)S(1)}, u32[]{:S(2)}, u32[]{:S(2)}) %collective-permute-start.18) | collective-permute-done | bytes 1048608 | tf_op jit(solution)/shard_map/ppermute | solution.py:23
  144.2 2.2 %fusion.2 = (f32[4,2,128]{2,1,0:T(2,128)S(1)}, f32[4,1024,128,2]{2,1,3,0:T(8,128)S(1)}) fusion(pred[128,1024]{0,1:T(8,128)(4,1)} %compare_and_fusion, bf16[128,4,2,128]{0,3,2,1:T(8,128)(2,1)S(1)} %pad_maximum_fusion, bf16[1024,4,128]{0,2,1:T(8,128)(2,1)} %all-gather.5.cloned.1.call-done, bf16[1024,4,128]{0,2,1:T(8,128)(2,1)S(1)} %collective-permute-done.18, ...), kind=kOutput, calls=%fused_computation.5 | convolution fusion | flops 272104448 | bytes 6688769 | tf_op jit(solution)/shard_map/qkgd,nkd->kgqn/dot_general | solution.py:276
  146.5 0.9 fusion
  147.4 1.3 fusion.35
  148.6 0.9 copy.137
  (117 shorter events, 2.9 us)
Async XLA Ops:
  6.5 2.5 %copy-start = (bf16[1280,3,4,80]{0,3,2,1:T(8,128)(2,1)S(1)}, bf16[1280,3,4,80]{0,3,2,1:T(8,128)(2,1)}, u32[]{:S(2)}) copy-start(bf16[1280,3,4,80]{0,3,2,1:T(8,128)(2,1)} %param.20) | copy-start | bytes 7372804
  6.5 4.5 %copy-start.16 = (s32[128]{0:T(128)S(1)}, s32[128]{0:T(128)}, u32[]{:S(2)}) copy-start(s32[128]{0:T(128)} %param.26) | copy-start | bytes 1540
  6.5 7.6 %copy-start.12 = (s32[256]{0:T(256)S(1)}, s32[256]{0:T(256)}, u32[]{:S(2)}) copy-start(s32[256]{0:T(256)} %param.27) | copy-start | bytes 3076
  6.5 7.7 %copy-start.8 = (s32[8]{0:T(128)S(1)}, s32[8]{0:T(128)}, u32[]{:S(2)}) copy-start(s32[8]{0:T(128)} %param.28) | copy-start | bytes 100
  6.5 89.1 %all-gather.3.cloned.1.call-start = ((), (), s32[]{:S(2)}) async-start(), calls=%async_computation | async-start | bytes 1310720 | tf_op jit(solution)/shard_map/all_gather | solution.py:234
  6.6 9.2 %copy-start.17 = (s32[8,2]{0,1:T(2,128)S(1)}, s32[8,2]{0,1:T(2,128)}, u32[]{:S(2)}) copy-start(s32[8,2]{0,1:T(2,128)} %param.25) | copy-start | bytes 196
  11.0 14.7 %copy-start.9 = (f32[1280]{0:T(1024)S(1)}, f32[1280]{0:T(1024)}, u32[]{:S(2)}) copy-start(f32[1280]{0:T(1024)} %param.23) | copy-start | bytes 15364
  11.0 14.7 %copy-start.10 = (f32[1280]{0:T(1024)S(1)}, f32[1280]{0:T(1024)}, u32[]{:S(2)}) copy-start(f32[1280]{0:T(1024)} %param.22) | copy-start | bytes 15364
  11.0 0.7 copy-start.3
  13.5 2.4 %collective-permute-start = (f32[1,64,1280]{2,1,0:T(8,128)S(1)}, f32[1,64,1280]{2,1,0:T(8,128)}, u32[]{:S(2)}, u32[]{:S(2)}) collective-permute-start(f32[1,64,1280]{2,1,0:T(8,128)S(1)} %select_bitcast_fusion), channel_id=1, source_target_pairs={{0,1},{1,0},{2,3},{3,2},{4,5},{5,4},{6,7},{7,6},{8,9},{9,8},{10,11... | collective-permute-start | bytes 983048 | tf_op jit(solution)/shard_map/ppermute | solution.py:23
  17.0 7.4 %collective-permute-start.1 = (f32[1,32,1280]{2,1,0:T(8,128)S(1)}, f32[1,32,1280]{2,1,0:T(8,128)S(1)}, u32[]{:S(2)}, u32[]{:S(2)}) collective-permute-start(f32[1,32,1280]{2,1,0:T(8,128)S(1)} %select_bitcast_fusion.1), channel_id=1, source_target_pairs={{0,16},{16,0},{1,17},{17,1},{2,18},{18,2},{3,19},{19,3},{4,20},{20... | collective-permute-start | bytes 491528 | tf_op jit(solution)/shard_map/ppermute | solution.py:23
  19.7 24.8 %copy-start.14 = (pred[8]{0:T(512)(128)(4,1)}, pred[8]{0:T(512)(128)(4,1)S(1)}, u32[]{:S(2)}) copy-start(pred[8]{0:T(512)(128)(4,1)S(1)} %iota_compare_fusion.10) | copy-start | bytes 28
  25.9 4.5 %collective-permute-start.2 = (bf16[1,8,5120]{2,1,0:T(8,128)(2,1)S(1)}, bf16[1,8,5120]{2,1,0:T(8,128)(2,1)S(1)}, u32[]{:S(2)}, u32[]{:S(2)}) collective-permute-start(bf16[1,8,5120]{2,1,0:T(8,128)(2,1)S(1)} %broadcast_in_dim_reshape.2), channel_id=1, source_target_pairs={{0,16},{16,0},{1,17},{17,1},{2,18},{18,2},{3,19},{19,3},{4,20},{20... | collective-permute-start | bytes 245768 | tf_op jit(solution)/shard_map/ppermute | solution.py:23
  30.4 1.5 collective-permute-start.3
  32.9 10.1 %collective-permute-start.4 = (bf16[32,640]{1,0:T(8,128)(2,1)S(1)}, bf16[32,640]{1,0:T(8,128)(2,1)S(1)}, u32[]{:S(2)}, u32[]{:S(2)}) collective-permute-start(bf16[32,640]{1,0:T(8,128)(2,1)S(1)} %bitcast.204), channel_id=1, source_target_pairs={{0,2},{2,4},{4,6},{6,8},{8,10},{10,12},{12,14},{14,0},{1,3},{3,5},... | collective-permute-start | bytes 122888 | tf_op jit(solution)/shard_map/ppermute | solution.py:202
  34.7 9.7 %collective-permute-start.5 = (bf16[32,640]{1,0:T(8,128)(2,1)S(1)}, bf16[32,640]{1,0:T(8,128)(2,1)S(1)}, u32[]{:S(2)}, u32[]{:S(2)}) collective-permute-start(bf16[32,640]{1,0:T(8,128)(2,1)S(1)} %bitcast.203), channel_id=1, source_target_pairs={{0,4},{2,6},{4,8},{6,10},{8,12},{10,14},{12,0},{14,2},{1,5},{3,7},... | collective-permute-start | bytes 122888 | tf_op jit(solution)/shard_map/ppermute | solution.py:202
  36.4 9.8 %collective-permute-start.6 = (bf16[32,640]{1,0:T(8,128)(2,1)S(1)}, bf16[32,640]{1,0:T(8,128)(2,1)S(1)}, u32[]{:S(2)}, u32[]{:S(2)}) collective-permute-start(bf16[32,640]{1,0:T(8,128)(2,1)S(1)} %bitcast.194), channel_id=1, source_target_pairs={{0,6},{2,8},{4,10},{6,12},{8,14},{10,0},{12,2},{14,4},{1,7},{3,9},... | collective-permute-start | bytes 122888 | tf_op jit(solution)/shard_map/ppermute | solution.py:202
  39.0 7.3 %collective-permute-start.7 = (bf16[32,640]{1,0:T(8,128)(2,1)S(1)}, bf16[32,640]{1,0:T(8,128)(2,1)S(1)}, u32[]{:S(2)}, u32[]{:S(2)}) collective-permute-start(bf16[32,640]{1,0:T(8,128)(2,1)S(1)} %bitcast.196), channel_id=1, source_target_pairs={{0,8},{2,10},{4,12},{6,14},{8,0},{10,2},{12,4},{14,6},{1,9},{3,11}... | collective-permute-start | bytes 122888 | tf_op jit(solution)/shard_map/ppermute | solution.py:202
  40.3 6.0 %collective-permute-start.8 = (bf16[32,640]{1,0:T(8,128)(2,1)S(1)}, bf16[32,640]{1,0:T(8,128)(2,1)S(1)}, u32[]{:S(2)}, u32[]{:S(2)}) collective-permute-start(bf16[32,640]{1,0:T(8,128)(2,1)S(1)} %bitcast.198), channel_id=1, source_target_pairs={{0,10},{2,12},{4,14},{6,0},{8,2},{10,4},{12,6},{14,8},{1,11},{3,13... | collective-permute-start | bytes 122888 | tf_op jit(solution)/shard_map/ppermute | solution.py:202
  43.0 4.1 %collective-permute-start.9 = (bf16[32,640]{1,0:T(8,128)(2,1)S(1)}, bf16[32,640]{1,0:T(8,128)(2,1)S(1)}, u32[]{:S(2)}, u32[]{:S(2)}) collective-permute-start(bf16[32,640]{1,0:T(8,128)(2,1)S(1)} %bitcast.200), channel_id=1, source_target_pairs={{0,12},{2,14},{4,0},{6,2},{8,4},{10,6},{12,8},{14,10},{1,13},{3,15... | collective-permute-start | bytes 122888 | tf_op jit(solution)/shard_map/ppermute | solution.py:202
  44.4 4.0 %collective-permute-start.10 = (bf16[32,640]{1,0:T(8,128)(2,1)S(1)}, bf16[32,640]{1,0:T(8,128)(2,1)S(1)}, u32[]{:S(2)}, u32[]{:S(2)}) collective-permute-start(bf16[32,640]{1,0:T(8,128)(2,1)S(1)} %bitcast.192), channel_id=1, source_target_pairs={{0,14},{2,0},{4,2},{6,4},{8,6},{10,8},{12,10},{14,12},{1,15},{3,1}... | collective-permute-start | bytes 122888 | tf_op jit(solution)/shard_map/ppermute | solution.py:202
  50.6 20.1 %copy-start.6 = (bf16[128,1024]{1,0:T(8,128)(2,1)S(1)}, bf16[128,1024]{1,0:T(8,128)(2,1)}, u32[]{:S(2)}) copy-start(bf16[128,1024]{1,0:T(8,128)(2,1)} %param.30) | copy-start | bytes 786436
  53.2 9.4 %collective-permute-start.11 = (f32[32,1024]{1,0:T(8,128)S(1)}, f32[32,1024]{1,0:T(8,128)S(1)}, u32[]{:S(2)}, u32[]{:S(2)}) collective-permute-start(f32[32,1024]{1,0:T(8,128)S(1)} %get-tuple-element.21), channel_id=1, source_target_pairs={{0,2},{2,4},{4,6},{6,8},{8,10},{10,12},{12,14},{14,0},{1,3},{3,5},... | collective-permute-start | bytes 393224 | tf_op jit(solution)/shard_map/ppermute | solution.py:219
  54.8 8.2 %collective-permute-start.12 = (f32[32,1024]{1,0:T(8,128)S(1)}, f32[32,1024]{1,0:T(8,128)S(1)}, u32[]{:S(2)}, u32[]{:S(2)}) collective-permute-start(f32[32,1024]{1,0:T(8,128)S(1)} %get-tuple-element.27), channel_id=1, source_target_pairs={{0,4},{2,6},{4,8},{6,10},{8,12},{10,14},{12,0},{14,2},{1,5},{3,7},... | collective-permute-start | bytes 393224 | tf_op jit(solution)/shard_map/ppermute | solution.py:219
  55.1 15.1 %collective-permute-start.13 = (f32[32,1024]{1,0:T(8,128)S(1)}, f32[32,1024]{1,0:T(8,128)S(1)}, u32[]{:S(2)}, u32[]{:S(2)}) collective-permute-start(f32[32,1024]{1,0:T(8,128)S(1)} %get-tuple-element.26), channel_id=1, source_target_pairs={{0,6},{2,8},{4,10},{6,12},{8,14},{10,0},{12,2},{14,4},{1,7},{3,9},... | collective-permute-start | bytes 393224 | tf_op jit(solution)/shard_map/ppermute | solution.py:219
  57.5 13.3 %collective-permute-start.14 = (f32[32,1024]{1,0:T(8,128)S(1)}, f32[32,1024]{1,0:T(8,128)S(1)}, u32[]{:S(2)}, u32[]{:S(2)}) collective-permute-start(f32[32,1024]{1,0:T(8,128)S(1)} %get-tuple-element.25), channel_id=1, source_target_pairs={{0,8},{2,10},{4,12},{6,14},{8,0},{10,2},{12,4},{14,6},{1,9},{3,11}... | collective-permute-start | bytes 393224 | tf_op jit(solution)/shard_map/ppermute | solution.py:219
  59.5 11.2 %collective-permute-start.15 = (f32[32,1024]{1,0:T(8,128)S(1)}, f32[32,1024]{1,0:T(8,128)S(1)}, u32[]{:S(2)}, u32[]{:S(2)}) collective-permute-start(f32[32,1024]{1,0:T(8,128)S(1)} %get-tuple-element.24), channel_id=1, source_target_pairs={{0,10},{2,12},{4,14},{6,0},{8,2},{10,4},{12,6},{14,8},{1,11},{3,13... | collective-permute-start | bytes 393224 | tf_op jit(solution)/shard_map/ppermute | solution.py:219
  62.6 8.1 %collective-permute-start.16 = (f32[32,1024]{1,0:T(8,128)S(1)}, f32[32,1024]{1,0:T(8,128)S(1)}, u32[]{:S(2)}, u32[]{:S(2)}) collective-permute-start(f32[32,1024]{1,0:T(8,128)S(1)} %get-tuple-element.23), channel_id=1, source_target_pairs={{0,12},{2,14},{4,0},{6,2},{8,4},{10,6},{12,8},{14,10},{1,13},{3,15... | collective-permute-start | bytes 393224 | tf_op jit(solution)/shard_map/ppermute | solution.py:219
  63.0 7.8 %collective-permute-start.17 = (f32[32,1024]{1,0:T(8,128)S(1)}, f32[32,1024]{1,0:T(8,128)S(1)}, u32[]{:S(2)}, u32[]{:S(2)}) collective-permute-start(f32[32,1024]{1,0:T(8,128)S(1)} %get-tuple-element.22), channel_id=1, source_target_pairs={{0,14},{2,0},{4,2},{6,4},{8,6},{10,8},{12,10},{14,12},{1,15},{3,1}... | collective-permute-start | bytes 393224 | tf_op jit(solution)/shard_map/ppermute | solution.py:219
  71.8 69.6 %all-gather.5.cloned.1.call-start = ((), (), s32[]{:S(2)}) async-start(), calls=%async_computation.1 | async-start | bytes 1179648 | tf_op jit(solution)/shard_map/all_gather | solution.py:253
  72.0 7.7 %copy-start.11 = (s32[1024]{0:T(1024)S(1)}, s32[1024]{0:T(1024)}, u32[]{:S(2)}) copy-start(s32[1024]{0:T(1024)} %param.29) | copy-start | bytes 12292
  72.0 25.2 %copy-start.7 = (f32[4096]{0:T(1024)S(1)}, f32[4096]{0:T(1024)}, u32[]{:S(2)}) copy-start(f32[4096]{0:T(1024)} %param.31) | copy-start | bytes 49156
  79.6 22.4 %copy-start.15 = (pred[8]{0:T(512)(128)(4,1)S(1)}, pred[8]{0:T(512)(128)(4,1)}, u32[]{:S(2)}) copy-start(pred[8]{0:T(512)(128)(4,1)} %copy-done.14) | copy-start | bytes 28
  80.2 22.1 %copy-start.4 = (f32[128,64]{0,1:T(8,128)}, f32[128,64]{0,1:T(8,128)S(1)}, u32[]{:S(2)}) copy-start(f32[128,64]{0,1:T(8,128)S(1)} %get-tuple-element.41) | copy-start | bytes 98308
  97.2 5.1 %copy-start.13 = (f32[128]{0:T(128)}, f32[128]{0:T(128)S(1)}, u32[]{:S(2)}) copy-start(f32[128]{0:T(128)S(1)} %add_rsqrt_fusion) | copy-start | bytes 1540
  103.3 21.4 %copy-start.1 = (bf16[128,4096]{1,0:T(8,128)(2,1)S(1)}, bf16[128,4096]{1,0:T(8,128)(2,1)}, u32[]{:S(2)}) copy-start(bf16[128,4096]{1,0:T(8,128)(2,1)} %all-gather.3.cloned.1.call-done) | copy-start | bytes 3145732
  124.7 5.9 %copy-start.5 = (f32[128,64]{0,1:T(8,128)S(1)}, f32[128,64]{0,1:T(8,128)}, u32[]{:S(2)}) copy-start(f32[128,64]{0,1:T(8,128)} %copy-done.4) | copy-start | bytes 98308
  130.6 15.9 %copy-start.2 = (pred[128,1024]{0,1:T(8,128)(4,1)S(1)}, pred[128,1024]{0,1:T(8,128)(4,1)}, u32[]{:S(2)}) copy-start(pred[128,1024]{0,1:T(8,128)(4,1)} %compare_and_fusion) | copy-start | bytes 393220
  141.3 6.0 %copy-start.18 = (bf16[1024,4,128]{0,2,1:T(8,128)(2,1)S(1)}, bf16[1024,4,128]{0,2,1:T(8,128)(2,1)}, u32[]{:S(2)}) copy-start(bf16[1024,4,128]{0,2,1:T(8,128)(2,1)} %all-gather.5.cloned.1.call-done) | copy-start | bytes 3145732
  141.3 2.9 %collective-permute-start.18 = (bf16[1024,4,128]{0,2,1:T(8,128)(2,1)}, bf16[1024,4,128]{0,2,1:T(8,128)(2,1)S(1)}, u32[]{:S(2)}, u32[]{:S(2)}) collective-permute-start(bf16[1024,4,128]{0,2,1:T(8,128)(2,1)} %all-gather.5.cloned.1.call-done), channel_id=1, source_target_pairs={{0,1},{1,0},{2,3},{3,2},{4,5},{5,4},{6,7},{7,6},{8,9},{9,8},{10,11... | collective-permute-start | bytes 3145736 | tf_op jit(solution)/shard_map/ppermute | solution.py:23
Sparse Core Ops, SparseCore 0:
  71.9 23.7 all-gather.2
  101.9 39.3 all-gather.4

commit v15 on v14

--- a/solution.py
+++ b/solution.py
@@ -231,7 +231,20 @@
     is_image = jnp.sum(placing, axis=1) > 0.5
     image_part = jnp.dot(placing.astype(jnp.bfloat16), incoming, preferred_element_type=jnp.float32)
     embeds = jnp.where(is_image[:, None], image_part.astype(jnp.bfloat16), text_rows)
-    full_rows = lax.all_gather(embeds, ("vis", "tp"), axis=1, tiled=True)
+    group = vis_size * tp_size
+    group_index = vis_index * tp_size + tp_index
+    by_shift = [embeds]
+    for shift in range(1, group):
+        by_shift.append(
+            lax.ppermute(embeds, ("vis", "tp"), [(i, (i + shift) % group) for i in range(group)])
+        )
+    group_ids = jnp.arange(group, dtype=jnp.int32)
+    group_hot = (
+        group_ids[None, :] == (group_index - group_ids[:, None]) % group
+    ).astype(jnp.bfloat16)
+    full_rows = jnp.einsum(
+        "sk,ktc->tsc", group_hot, jnp.stack(by_shift, axis=0), preferred_element_type=jnp.float32
+    ).astype(jnp.bfloat16).reshape(TOK, -1)
     widened = full_rows.astype(jnp.float32)
     normed_rows = (
         widened

time: 157 us -> 161 us (1.025)
  waiting for transfers between devices: 45.9 us -> 36.4 us
  local copies, waits for them, and re-layouts: 34.8 us -> 42.5 us
  other arithmetic: 11.8 us -> 15 us
  matrix products: 20.8 us -> 22.9 us
    all_gather x1 -> x0, waiting for transfers between devices: 15.4 us -> none  [local(): full_rows = lax.all_gather(embeds, ('vis', 'tp'), axis=1, tiled=True)]
    ppermute x14, waiting for transfers between devices: 8.29 us -> 15.7 us  [local(): lax.ppermute(outgoing, 'ctx', [(i, (i + shift) % shards) for i in range(s...]
    unnamed x46 -> x40, local copies, waits for them, and re-layouts: 0.45 us -> 6.8 us
    all_gather x1, waiting for transfers between devices: 10.6 us -> 4.47 us  [local(): gathered = lax.all_gather(own_half, 'ctx', axis=0, tiled=True)]
    ppermute x0 -> x3, waiting for transfers between devices: none -> 4.84 us  [local(): lax.ppermute(embeds, ('vis', 'tp'), [(i, (i + shift) % group) for i in ra...]
    dot_general x0 -> x1, matrix products: none -> 2.26 us  [local(): jnp.einsum('sk,ktc->tsc', group_hot, jnp.stack(by_shift, axis=0), preferr...]
    ppermute x14, starting transfers between devices: 23.8 us -> 21.8 us  [local(): lax.ppermute(outgoing, 'ctx', [(i, (i + shift) % shards) for i in range(s...]
    unnamed x3, matrix products: 11.6 us -> 9.59 us
  transfers between devices with their start and end apart: 21 -> 23, of which waited for: 11 -> 11; matrix products, arithmetic and copies ran while one was open for 26% -> 30% of each run, Pallas kernels for 0% -> 0%
where the time goes in v15:
time: 161 us; the launch traced here: 160 us
  local copies, waits for them, and re-layouts  42.5 us (26%)
  waiting for transfers between devices  36.4 us (23%)
  starting transfers between devices  28.6 us (18%)
  matrix products  22.9 us (14%)
  other arithmetic  15 us (9%)
  between operations  14.1 us (9%)
    ppermute x14, starting transfers between devices, local(): lax.ppermute(outgoing, 'ctx', [(i, (i + shift) % shards) for i in range(s...  21.8 us
    optimization_barrier x1, local copies, waits for them, and re-layouts, local(): query_weights, own_half = lax.optimization_barrier((w_query, own_half))  21.3 us
    ppermute x14, waiting for transfers between devices, local(): lax.ppermute(outgoing, 'ctx', [(i, (i + shift) % shards) for i in range(s...  15.7 us
    ppermute x5, waiting for transfers between devices, swapped(): lax.ppermute(value, axis, [(i, i ^ 1 << stride) for i in range(lax.axis_s...  11.4 us
    unnamed x3, matrix products  9.59 us
    squeeze x1, local copies, waits for them, and re-layouts, local(): w_keyval[0]  7.59 us
    unnamed x40, local copies, waits for them, and re-layouts  6.8 us
    ppermute x5, starting transfers between devices, swapped(): lax.ppermute(value, axis, [(i, i ^ 1 << stride) for i in range(lax.axis_s...  5.01 us
  transfers between devices with their start and end apart: 23, of which 11 were waited for; matrix products, arithmetic and copies ran while one was open for 30% of the time, Pallas kernels for 0%

profile of v15, /device:TPU:0, one launch (start us, length us, event | category | flops | bytes accessed | tf_op | source)
XLA Modules:
  0.0 159.5 jit_solution(15276382769569105891)
XLA Ops:
  6.6 1.2 convert_reduce_fusion
  7.8 1.2 fusion.45
  9.0 0.8 broadcast_compare_fusion
  9.9 1.9 %fusion.49 = f32[128,960]{0,1:S(1)} fusion(bf16[1280,960]{0,1:T(8,128)(2,1)S(1)} %bitcast.192, bf16[128,1280]{1,0:T(8,128)(2,1)} %param.17, f32[1280]{0:T(1024)} %param.19, f32[1280]{0:T(1024)} %param.18, f32[128]{0:T(128)S(1)} %add_rsqrt_fusion.2, f32[128]{0:T(128)S(1)} %broadcast_multiply_fusion.1), kind=kOutput, calls=%fused_computation.54 | convolution fusion | flops 315555840 | bytes 3288064
  12.2 0.4 copy-done.3
  12.5 1.7 %fusion.21 = f32[128,1280,1]{1,0,2:T(8,128)S(1)} fusion(bf16[4,80,1280]{2,1,0:T(8,128)(2,1)} %param.21, f32[4,128,128]{1,2,0:T(8,128)S(1)} %get-tuple-element.45, f32[4,128]{1,0:T(4,128)S(1)} %get-tuple-element.44, bf16[128,3,4,80]{0,3,2,1:T(8,128)(2,1)} %copy-done.3, f32[128,4]{0,1:T(4,128)S(1)} %bitcast.232), kind=kOutput, calls=%fused_computation.30 | convolution fusion | flops 115556352 | bytes 1822720 | tf_op jit(solution)/shard_map/phd,hdf->pf/dot_general | solution.py:159
  14.3 0.6 collective-permute-start
  15.1 0.7 fusion.111
  15.8 0.7 fusion.58
  17.1 0.8 fusion.112
  17.9 1.0 bitcast_add_fusion
  19.0 2.6 %collective-permute-start.1 = (f32[1,32,1280]{2,1,0:T(8,128)S(1)}, f32[1,32,1280]{2,1,0:T(8,128)S(1)}, u32[]{:S(2)}, u32[]{:S(2)}) collective-permute-start(f32[1,32,1280]{2,1,0:T(8,128)S(1)} %select_bitcast_fusion.1), channel_id=1, source_target_pairs={{0,16},{16,0},{1,17},{17,1},{2,18},{18,2},{3,19},{19,3},{4,20},{20... | collective-permute-start | bytes 491528 | tf_op jit(solution)/shard_map/ppermute | solution.py:23
  21.6 4.8 %collective-permute-done.1 = f32[1,32,1280]{2,1,0:T(8,128)S(1)} collective-permute-done((f32[1,32,1280]{2,1,0:T(8,128)S(1)}, f32[1,32,1280]{2,1,0:T(8,128)S(1)}, u32[]{:S(2)}, u32[]{:S(2)}) %collective-permute-start.1) | collective-permute-done | bytes 163872 | tf_op jit(solution)/shard_map/ppermute | solution.py:23
  26.4 1.0 fusion.110
  27.8 1.8 %collective-permute-start.2 = (bf16[1,8,5120]{2,1,0:T(8,128)(2,1)S(1)}, bf16[1,8,5120]{2,1,0:T(8,128)(2,1)S(1)}, u32[]{:S(2)}, u32[]{:S(2)}) collective-permute-start(bf16[1,8,5120]{2,1,0:T(8,128)(2,1)S(1)} %broadcast_in_dim_reshape.2), channel_id=1, source_target_pairs={{0,16},{16,0},{1,17},{17,1},{2,18},{18,2},{3,19},{19,3},{4,20},{20... | collective-permute-start | bytes 245768 | tf_op jit(solution)/shard_map/ppermute | solution.py:23
  29.8 2.5 %collective-permute-done.2 = bf16[1,8,5120]{2,1,0:T(8,128)(2,1)S(1)} collective-permute-done((bf16[1,8,5120]{2,1,0:T(8,128)(2,1)S(1)}, bf16[1,8,5120]{2,1,0:T(8,128)(2,1)S(1)}, u32[]{:S(2)}, u32[]{:S(2)}) %collective-permute-start.2) | collective-permute-done | bytes 81952 | tf_op jit(solution)/shard_map/ppermute | solution.py:23
  32.6 1.2 collective-permute-done.3
  34.1 0.7 constant_dynamic-slice_fusion
  34.8 1.8 %collective-permute-start.4 = (bf16[32,640]{1,0:T(8,128)(2,1)S(1)}, bf16[32,640]{1,0:T(8,128)(2,1)S(1)}, u32[]{:S(2)}, u32[]{:S(2)}) collective-permute-start(bf16[32,640]{1,0:T(8,128)(2,1)S(1)} %bitcast.230), channel_id=1, source_target_pairs={{0,2},{2,4},{4,6},{6,8},{8,10},{10,12},{12,14},{14,0},{1,3},{3,5},... | collective-permute-start | bytes 122888 | tf_op jit(solution)/shard_map/ppermute | solution.py:202
  36.7 1.6 collective-permute-start.5
  38.2 0.7 select_reduce_fusion.5
  39.0 2.6 %collective-permute-start.6 = (bf16[32,640]{1,0:T(8,128)(2,1)S(1)}, bf16[32,640]{1,0:T(8,128)(2,1)S(1)}, u32[]{:S(2)}, u32[]{:S(2)}) collective-permute-start(bf16[32,640]{1,0:T(8,128)(2,1)S(1)} %bitcast.227), channel_id=1, source_target_pairs={{0,6},{2,8},{4,10},{6,12},{8,14},{10,0},{12,2},{14,4},{1,7},{3,9},... | collective-permute-start | bytes 122888 | tf_op jit(solution)/shard_map/ppermute | solution.py:202
  41.6 1.2 collective-permute-start.7
  42.8 2.6 %collective-permute-start.8 = (bf16[32,640]{1,0:T(8,128)(2,1)S(1)}, bf16[32,640]{1,0:T(8,128)(2,1)S(1)}, u32[]{:S(2)}, u32[]{:S(2)}) collective-permute-start(bf16[32,640]{1,0:T(8,128)(2,1)S(1)} %bitcast.219), channel_id=1, source_target_pairs={{0,10},{2,12},{4,14},{6,0},{8,2},{10,4},{12,6},{14,8},{1,11},{3,13... | collective-permute-start | bytes 122888 | tf_op jit(solution)/shard_map/ppermute | solution.py:202
  45.5 1.3 collective-permute-start.9
  46.8 1.4 collective-permute-start.10
  48.6 0.8 collective-permute-done.9
  49.5 1.3 collective-permute-done.10
  50.9 2.1 %stack.56 = bf16[8,32,640]{2,0,1:T(8,128)(2,1)S(1)} concatenate(bf16[1,32,640]{2,0,1:T(2,128)(2,1)S(1)} %get-tuple-element.39, bf16[1,32,640]{2,0,1:T(2,128)(2,1)S(1)} %copy.126, bf16[1,32,640]{2,0,1:T(2,128)(2,1)S(1)} %copy.127, bf16[1,32,640]{2,0,1:T(2,128)(2,1)S(1)} %copy.128, bf16[1,32,640]{2,0,1:T(2,128)(2,1)S(1)} %copy.129, bf16[1,32,640]{2,0,1:T(2,128)(2,1)S(1)} %copy.130, ...), dimensions={0} | concatenate | bytes 655360 | tf_op jit(solution)/shard_map/stack | solution.py:204
  53.0 0.3 convolution_convert_fusion.2
  53.5 0.8 dot_general.53
  54.3 2.0 %fusion.11 = f32[8,32,1024]{2,1,0:T(8,128)S(1)} fusion(bf16[8,32,640]{2,1,0:T(8,128)(2,1)} %dot_general.53, bf16[640,1024]{1,0:T(8,128)(2,1)} %param.24), kind=kOutput, calls=%fused_computation.17 | convolution fusion | flops 335544320 | bytes 2686976 | tf_op jit(solution)/shard_map/dot_general | solution.py:214
  56.3 0.8 dynamic-slice_bitcast_fusion.6
  57.1 1.5 collective-permute-start.11
  58.6 3.2 %collective-permute-start.17 = (f32[32,1024]{1,0:T(8,128)S(1)}, f32[32,1024]{1,0:T(8,128)S(1)}, u32[]{:S(2)}, u32[]{:S(2)}) collective-permute-start(f32[32,1024]{1,0:T(8,128)S(1)} %get-tuple-element.22), channel_id=1, source_target_pairs={{0,14},{2,0},{4,2},{6,4},{8,6},{10,8},{12,10},{14,12},{1,15},{3,1}... | collective-permute-start | bytes 393224 | tf_op jit(solution)/shard_map/ppermute | solution.py:219
  61.9 0.7 fusion.108
  62.7 4.2 %collective-permute-start.14 = (f32[32,1024]{1,0:T(8,128)}, f32[32,1024]{1,0:T(8,128)}, u32[]{:S(2)}, u32[]{:S(2)}) collective-permute-start(f32[32,1024]{1,0:T(8,128)} %get-tuple-element.25), channel_id=1, source_target_pairs={{0,8},{2,10},{4,12},{6,14},{8,0},{10,2},{12,4},{14,6},{1,9},{3,11}... | collective-permute-start | bytes 393224 | tf_op jit(solution)/shard_map/ppermute | solution.py:219
  67.0 0.6 copy-done.5
  67.6 0.6 copy-done.6
  68.3 1.2 broadcast_compare_fusion.1
  69.5 0.5 multiply_power_fusion
  70.0 1.5 collective-permute-done.15
  71.5 10.8 %collective-permute-done.14 = f32[32,1024]{1,0:T(8,128)} collective-permute-done((f32[32,1024]{1,0:T(8,128)}, f32[32,1024]{1,0:T(8,128)}, u32[]{:S(2)}, u32[]{:S(2)}) %collective-permute-start.14) | collective-permute-done | bytes 131104 | tf_op jit(solution)/shard_map/ppermute | solution.py:219
  82.3 1.3 collective-permute-done.13
  83.6 2.3 %fusion.17 = bf16[128,1024]{1,0:T(8,128)(2,1)} fusion(bf16[128,1024]{1,0:T(8,128)(2,1)} %param.30, pred[128]{0:T(512)(128)(4,1)} %broadcast_compare_fusion.1, f32[32,1024]{1,0:T(8,128)} %copy-done.6, f32[32,1024]{1,0:T(8,128)} %collective-permute-done.16, f32[32,1024]{1,0:T(8,128)} %collective-permute-done.15, f32[32,1024]{1,0:T(8,128)} %collective-permute-done.14, ...), kind=kOutput, calls=%fused_computation.24 | convolution fusion | flops 8912896 | bytes 1581188 | tf_op jit(solution)/shard_map/dot_general | solution.py:232
  85.8 1.6 collective-permute-start.19
  87.7 7.6 %copy.135 = bf16[4096,4,128]{0,2,1:T(8,128)(2,1)} copy(bf16[4096,4,128]{2,1,0:T(4,128)(2,1)} %bitcast.199) | data formatting | bytes 8388608 | tf_op jit(solution)/shard_map/squeeze | solution.py:260
  95.5 4.8 %collective-permute-done.19 = bf16[128,1024]{1,0:T(8,128)(2,1)S(1)} collective-permute-done((bf16[128,1024]{1,0:T(8,128)(2,1)}, bf16[128,1024]{1,0:T(8,128)(2,1)S(1)}, u32[]{:S(2)}, u32[]{:S(2)}) %collective-permute-start.19) | collective-permute-done | bytes 262176 | tf_op jit(solution)/shard_map/ppermute | solution.py:239
  100.4 1.1 pad_maximum_fusion
  101.5 2.3 %multiply_reduce_fusion = (f32[128]{0:T(128)S(1)}, f32[128,1024,4]{1,2,0:T(4,128)S(1)}) fusion(s32[4]{0:T(128)S(1)} %and_select_fusion.3, bf16[4,128,1024]{2,1,0:T(8,128)(2,1)S(1)} %pad_maximum_fusion), kind=kOutput, calls=%fused_computation.13 | convolution fusion | flops 6291344 | bytes 3146256 | tf_op jit(solution)/shard_map/sk,ktc->tsc/dot_general | solution.py:245
  103.7 0.6 fusion.5
  104.3 0.4 copy.160
  104.7 1.2 fusion.114
  106.0 0.7 fusion.55
  107.2 0.3 compare_and_fusion
  107.5 4.6 %copy.159 = f32[16,8,4,1024]{3,1,2,0:T(8,128)} copy(f32[16,8,4,1024]{3,2,1,0:T(4,128)} %bitcast.196) | data formatting | bytes 4194304
  112.2 21.3 %copy.136 = bf16[4096,4,2,128]{0,3,2,1:T(8,128)(2,1)} copy(bf16[4096,4,2,128]{3,2,1,0:T(2,128)(2,1)} %param.32) | data formatting | bytes 16777216 | tf_op jit(solution)/shard_map/optimization_barrier | solution.py:265
  133.5 6.5 %fusion.22 = f32[128,1024]{0,1:S(1)} fusion(bf16[4096,1024]{0,1:T(8,128)(2,1)} %bitcast.193, f32[128,4096]{1,0:T(8,128)} %bitcast.194, f32[4096]{0:T(1024)S(1)} %copy-done.4, f32[128]{0:T(128)S(1)} %add_rsqrt_fusion), kind=kOutput, calls=%fused_computation.31 | convolution fusion | flops 1075314688 | bytes 11026944
  140.0 4.5 %all-gather.2.cloned.1.call-done = bf16[1024,4,128]{0,2,1:T(8,128)(2,1)} async-done(((bf16[128,4,128]{0,2,1:T(8,128)(2,1)}), bf16[1024,4,128]{0,2,1:T(8,128)(2,1)}) %all-gather.2.cloned.1.call-update) | async-done | bytes 1048592 | tf_op jit(solution)/shard_map/all_gather | solution.py:266
  144.5 2.9 %collective-permute-done.21 = bf16[1024,4,128]{0,2,1:T(8,128)(2,1)S(1)} collective-permute-done((bf16[1024,4,128]{0,2,1:T(8,128)(2,1)}, bf16[1024,4,128]{0,2,1:T(8,128)(2,1)S(1)}, u32[]{:S(2)}, u32[]{:S(2)}) %collective-permute-start.21) | collective-permute-done | bytes 1048608 | tf_op jit(solution)/shard_map/ppermute | solution.py:23
  147.4 2.2 %fusion.2 = (f32[4,2,128]{2,1,0:T(2,128)S(1)}, f32[4,1024,128,2]{2,1,3,0:T(8,128)S(1)}) fusion(pred[128,1024]{0,1:T(8,128)(4,1)S(1)} %compare_and_fusion, bf16[128,4,2,128]{0,3,2,1:T(8,128)(2,1)S(1)} %pad_maximum_fusion.1, bf16[1024,4,128]{0,2,1:T(8,128)(2,1)} %all-gather.2.cloned.1.call-done, bf16[1024,4,128]{0,2,1:T(8,128)(2,1)S(1)} %collective-permute-done.21, ...), kind=kOutput, calls=%fused_computation.5 | convolution fusion | flops 272104448 | bytes 6688769 | tf_op jit(solution)/shard_map/qkgd,nkd->kgqn/dot_general | solution.py:289
  149.6 0.9 fusion
  150.5 1.3 fusion.38
  151.8 0.9 copy.142
  (118 shorter events, 4.3 us)
Async XLA Ops:
  6.5 3.3 %copy-start = (bf16[1280,3,4,80]{0,3,2,1:T(8,128)(2,1)S(1)}, bf16[1280,3,4,80]{0,3,2,1:T(8,128)(2,1)}, u32[]{:S(2)}) copy-start(bf16[1280,3,4,80]{0,3,2,1:T(8,128)(2,1)} %param.20) | copy-start | bytes 7372804
  6.5 8.3 %copy-start.11 = (s32[256]{0:T(256)S(1)}, s32[256]{0:T(256)}, u32[]{:S(2)}) copy-start(s32[256]{0:T(256)} %param.27) | copy-start | bytes 3076
  6.5 8.4 %copy-start.7 = (s32[8]{0:T(128)S(1)}, s32[8]{0:T(128)}, u32[]{:S(2)}) copy-start(s32[8]{0:T(128)} %param.28) | copy-start | bytes 100
  6.5 138.0 %all-gather.2.cloned.1.call-start = ((), (), s32[]{:S(2)}) async-start(), calls=%async_computation | async-start | bytes 1179648 | tf_op jit(solution)/shard_map/all_gather | solution.py:266
  6.6 10.0 %copy-start.12 = (s32[8,2]{0,1:T(2,128)S(1)}, s32[8,2]{0,1:T(2,128)}, u32[]{:S(2)}) copy-start(s32[8,2]{0,1:T(2,128)} %param.25) | copy-start | bytes 196
  11.8 15.9 %copy-start.8 = (f32[1280]{0:T(1024)S(1)}, f32[1280]{0:T(1024)}, u32[]{:S(2)}) copy-start(f32[1280]{0:T(1024)} %param.23) | copy-start | bytes 15364
  11.8 15.9 %copy-start.9 = (f32[1280]{0:T(1024)S(1)}, f32[1280]{0:T(1024)}, u32[]{:S(2)}) copy-start(f32[1280]{0:T(1024)} %param.22) | copy-start | bytes 15364
  11.8 0.7 copy-start.3
  14.3 3.6 %collective-permute-start = (f32[1,64,1280]{2,1,0:T(8,128)S(1)}, f32[1,64,1280]{2,1,0:T(8,128)}, u32[]{:S(2)}, u32[]{:S(2)}) collective-permute-start(f32[1,64,1280]{2,1,0:T(8,128)S(1)} %select_bitcast_fusion), channel_id=1, source_target_pairs={{0,1},{1,0},{2,3},{3,2},{4,5},{5,4},{6,7},{7,6},{8,9},{9,8},{10,11... | collective-permute-start | bytes 983048 | tf_op jit(solution)/shard_map/ppermute | solution.py:23
  19.0 7.4 %collective-permute-start.1 = (f32[1,32,1280]{2,1,0:T(8,128)S(1)}, f32[1,32,1280]{2,1,0:T(8,128)S(1)}, u32[]{:S(2)}, u32[]{:S(2)}) collective-permute-start(f32[1,32,1280]{2,1,0:T(8,128)S(1)} %select_bitcast_fusion.1), channel_id=1, source_target_pairs={{0,16},{16,0},{1,17},{17,1},{2,18},{18,2},{3,19},{19,3},{4,20},{20... | collective-permute-start | bytes 491528 | tf_op jit(solution)/shard_map/ppermute | solution.py:23
  27.8 4.5 %collective-permute-start.2 = (bf16[1,8,5120]{2,1,0:T(8,128)(2,1)S(1)}, bf16[1,8,5120]{2,1,0:T(8,128)(2,1)S(1)}, u32[]{:S(2)}, u32[]{:S(2)}) collective-permute-start(bf16[1,8,5120]{2,1,0:T(8,128)(2,1)S(1)} %broadcast_in_dim_reshape.2), channel_id=1, source_target_pairs={{0,16},{16,0},{1,17},{17,1},{2,18},{18,2},{3,19},{19,3},{4,20},{20... | collective-permute-start | bytes 245768 | tf_op jit(solution)/shard_map/ppermute | solution.py:23
  32.3 1.5 collective-permute-start.3
  34.8 10.6 %collective-permute-start.4 = (bf16[32,640]{1,0:T(8,128)(2,1)S(1)}, bf16[32,640]{1,0:T(8,128)(2,1)S(1)}, u32[]{:S(2)}, u32[]{:S(2)}) collective-permute-start(bf16[32,640]{1,0:T(8,128)(2,1)S(1)} %bitcast.230), channel_id=1, source_target_pairs={{0,2},{2,4},{4,6},{6,8},{8,10},{10,12},{12,14},{14,0},{1,3},{3,5},... | collective-permute-start | bytes 122888 | tf_op jit(solution)/shard_map/ppermute | solution.py:202
  36.7 10.1 %collective-permute-start.5 = (bf16[32,640]{1,0:T(8,128)(2,1)S(1)}, bf16[32,640]{1,0:T(8,128)(2,1)S(1)}, u32[]{:S(2)}, u32[]{:S(2)}) collective-permute-start(bf16[32,640]{1,0:T(8,128)(2,1)S(1)} %bitcast.222), channel_id=1, source_target_pairs={{0,4},{2,6},{4,8},{6,10},{8,12},{10,14},{12,0},{14,2},{1,5},{3,7},... | collective-permute-start | bytes 122888 | tf_op jit(solution)/shard_map/ppermute | solution.py:202
  39.0 9.4 %collective-permute-start.6 = (bf16[32,640]{1,0:T(8,128)(2,1)S(1)}, bf16[32,640]{1,0:T(8,128)(2,1)S(1)}, u32[]{:S(2)}, u32[]{:S(2)}) collective-permute-start(bf16[32,640]{1,0:T(8,128)(2,1)S(1)} %bitcast.227), channel_id=1, source_target_pairs={{0,6},{2,8},{4,10},{6,12},{8,14},{10,0},{12,2},{14,4},{1,7},{3,9},... | collective-permute-start | bytes 122888 | tf_op jit(solution)/shard_map/ppermute | solution.py:202
  41.6 6.9 %collective-permute-start.7 = (bf16[32,640]{1,0:T(8,128)(2,1)S(1)}, bf16[32,640]{1,0:T(8,128)(2,1)S(1)}, u32[]{:S(2)}, u32[]{:S(2)}) collective-permute-start(bf16[32,640]{1,0:T(8,128)(2,1)S(1)} %bitcast.223), channel_id=1, source_target_pairs={{0,8},{2,10},{4,12},{6,14},{8,0},{10,2},{12,4},{14,6},{1,9},{3,11}... | collective-permute-start | bytes 122888 | tf_op jit(solution)/shard_map/ppermute | solution.py:202
  42.8 5.7 %collective-permute-start.8 = (bf16[32,640]{1,0:T(8,128)(2,1)S(1)}, bf16[32,640]{1,0:T(8,128)(2,1)S(1)}, u32[]{:S(2)}, u32[]{:S(2)}) collective-permute-start(bf16[32,640]{1,0:T(8,128)(2,1)S(1)} %bitcast.219), channel_id=1, source_target_pairs={{0,10},{2,12},{4,14},{6,0},{8,2},{10,4},{12,6},{14,8},{1,11},{3,13... | collective-permute-start | bytes 122888 | tf_op jit(solution)/shard_map/ppermute | solution.py:202
  45.5 4.0 %collective-permute-start.9 = (bf16[32,640]{1,0:T(8,128)(2,1)S(1)}, bf16[32,640]{1,0:T(8,128)(2,1)S(1)}, u32[]{:S(2)}, u32[]{:S(2)}) collective-permute-start(bf16[32,640]{1,0:T(8,128)(2,1)S(1)} %bitcast.218), channel_id=1, source_target_pairs={{0,12},{2,14},{4,0},{6,2},{8,4},{10,6},{12,8},{14,10},{1,13},{3,15... | collective-permute-start | bytes 122888 | tf_op jit(solution)/shard_map/ppermute | solution.py:202
  46.8 4.0 %collective-permute-start.10 = (bf16[32,640]{1,0:T(8,128)(2,1)S(1)}, bf16[32,640]{1,0:T(8,128)(2,1)S(1)}, u32[]{:S(2)}, u32[]{:S(2)}) collective-permute-start(bf16[32,640]{1,0:T(8,128)(2,1)S(1)} %bitcast.217), channel_id=1, source_target_pairs={{0,14},{2,0},{4,2},{6,4},{8,6},{10,8},{12,10},{14,12},{1,15},{3,1}... | collective-permute-start | bytes 122888 | tf_op jit(solution)/shard_map/ppermute | solution.py:202
  53.0 34.6 %copy-start.10 = (s32[1024]{0:T(1024)S(1)}, s32[1024]{0:T(1024)}, u32[]{:S(2)}) copy-start(s32[1024]{0:T(1024)} %param.29) | copy-start | bytes 12292
  53.0 34.7 %copy-start.4 = (f32[4096]{0:T(1024)S(1)}, f32[4096]{0:T(1024)}, u32[]{:S(2)}) copy-start(f32[4096]{0:T(1024)} %param.31) | copy-start | bytes 49156
  57.1 9.8 %collective-permute-start.11 = (f32[32,1024]{1,0:T(8,128)S(1)}, f32[32,1024]{1,0:T(8,128)S(1)}, u32[]{:S(2)}, u32[]{:S(2)}) collective-permute-start(f32[32,1024]{1,0:T(8,128)S(1)} %get-tuple-element.21), channel_id=1, source_target_pairs={{0,2},{2,4},{4,6},{6,8},{8,10},{10,12},{12,14},{14,0},{1,3},{3,5},... | collective-permute-start | bytes 393224 | tf_op jit(solution)/shard_map/ppermute | solution.py:219
  58.6 8.3 %collective-permute-start.17 = (f32[32,1024]{1,0:T(8,128)S(1)}, f32[32,1024]{1,0:T(8,128)S(1)}, u32[]{:S(2)}, u32[]{:S(2)}) collective-permute-start(f32[32,1024]{1,0:T(8,128)S(1)} %get-tuple-element.22), channel_id=1, source_target_pairs={{0,14},{2,0},{4,2},{6,4},{8,6},{10,8},{12,10},{14,12},{1,15},{3,1}... | collective-permute-start | bytes 393224 | tf_op jit(solution)/shard_map/ppermute | solution.py:219
  62.6 7.5 %collective-permute-start.16 = (f32[32,1024]{1,0:T(8,128)}, f32[32,1024]{1,0:T(8,128)}, u32[]{:S(2)}, u32[]{:S(2)}) collective-permute-start(f32[32,1024]{1,0:T(8,128)} %get-tuple-element.23), channel_id=1, source_target_pairs={{0,12},{2,14},{4,0},{6,2},{8,4},{10,6},{12,8},{14,10},{1,13},{3,15... | collective-permute-start | bytes 393224 | tf_op jit(solution)/shard_map/ppermute | solution.py:219
  62.7 8.8 %collective-permute-start.15 = (f32[32,1024]{1,0:T(8,128)}, f32[32,1024]{1,0:T(8,128)}, u32[]{:S(2)}, u32[]{:S(2)}) collective-permute-start(f32[32,1024]{1,0:T(8,128)} %get-tuple-element.24), channel_id=1, source_target_pairs={{0,10},{2,12},{4,14},{6,0},{8,2},{10,4},{12,6},{14,8},{1,11},{3,13... | collective-permute-start | bytes 393224 | tf_op jit(solution)/shard_map/ppermute | solution.py:219
  62.7 19.6 %collective-permute-start.14 = (f32[32,1024]{1,0:T(8,128)}, f32[32,1024]{1,0:T(8,128)}, u32[]{:S(2)}, u32[]{:S(2)}) collective-permute-start(f32[32,1024]{1,0:T(8,128)} %get-tuple-element.25), channel_id=1, source_target_pairs={{0,8},{2,10},{4,12},{6,14},{8,0},{10,2},{12,4},{14,6},{1,9},{3,11}... | collective-permute-start | bytes 393224 | tf_op jit(solution)/shard_map/ppermute | solution.py:219
  66.9 0.6 copy-start.5
  66.9 16.6 %collective-permute-start.13 = (f32[32,1024]{1,0:T(8,128)}, f32[32,1024]{1,0:T(8,128)}, u32[]{:S(2)}, u32[]{:S(2)}) collective-permute-start(f32[32,1024]{1,0:T(8,128)} %get-tuple-element.26), channel_id=1, source_target_pairs={{0,6},{2,8},{4,10},{6,12},{8,14},{10,0},{12,2},{14,4},{1,7},{3,9},... | collective-permute-start | bytes 393224 | tf_op jit(solution)/shard_map/ppermute | solution.py:219
  67.6 0.7 copy-start.6
  68.2 15.3 %collective-permute-start.12 = (f32[32,1024]{1,0:T(8,128)}, f32[32,1024]{1,0:T(8,128)}, u32[]{:S(2)}, u32[]{:S(2)}) collective-permute-start(f32[32,1024]{1,0:T(8,128)} %get-tuple-element.27), channel_id=1, source_target_pairs={{0,4},{2,6},{4,8},{6,10},{8,12},{10,14},{12,0},{14,2},{1,5},{3,7},... | collective-permute-start | bytes 393224 | tf_op jit(solution)/shard_map/ppermute | solution.py:219
  85.8 9.7 %collective-permute-start.20 = (bf16[128,1024]{1,0:T(8,128)(2,1)}, bf16[128,1024]{1,0:T(8,128)(2,1)S(1)}, u32[]{:S(2)}, u32[]{:S(2)}) collective-permute-start(bf16[128,1024]{1,0:T(8,128)(2,1)} %fusion.17), channel_id=1, source_target_pairs={{0,17},{1,0},{16,1},{17,16},{2,19},{3,2},{18,3},{19,18},{4,21},{5,... | collective-permute-start | bytes 786440 | tf_op jit(solution)/shard_map/ppermute | solution.py:239
  85.8 14.5 %collective-permute-start.19 = (bf16[128,1024]{1,0:T(8,128)(2,1)}, bf16[128,1024]{1,0:T(8,128)(2,1)S(1)}, u32[]{:S(2)}, u32[]{:S(2)}) collective-permute-start(bf16[128,1024]{1,0:T(8,128)(2,1)} %fusion.17), channel_id=1, source_target_pairs={{0,16},{1,17},{16,0},{17,1},{2,18},{3,19},{18,2},{19,3},{4,20},{5,... | collective-permute-start | bytes 786440 | tf_op jit(solution)/shard_map/ppermute | solution.py:239
  87.4 13.0 %collective-permute-start.18 = (bf16[128,1024]{1,0:T(8,128)(2,1)}, bf16[128,1024]{1,0:T(8,128)(2,1)S(1)}, u32[]{:S(2)}, u32[]{:S(2)}) collective-permute-start(bf16[128,1024]{1,0:T(8,128)(2,1)} %fusion.17), channel_id=1, source_target_pairs={{0,1},{1,16},{16,17},{17,0},{2,3},{3,18},{18,19},{19,2},{4,5},{5,2... | collective-permute-start | bytes 786440 | tf_op jit(solution)/shard_map/ppermute | solution.py:239
  87.7 7.6 %copy-start.13 = (f32[64]{0:T(128)S(1)}, f32[64]{0:T(128)}, u32[]{:S(2)}) copy-start(f32[64]{0:T(128)} %multiply_power_fusion) | copy-start | bytes 772
  101.4 3.2 %copy-start.1 = (bf16[4096,4,128]{0,2,1:T(8,128)(2,1)S(1)}, bf16[4096,4,128]{0,2,1:T(8,128)(2,1)}, u32[]{:S(2)}) copy-start(bf16[4096,4,128]{0,2,1:T(8,128)(2,1)} %copy.135) | copy-start | bytes 12582916
  103.7 2.2 %copy-start.2 = (f32[128,1024,4]{1,2,0:T(4,128)}, f32[128,1024,4]{1,2,0:T(4,128)S(1)}, u32[]{:S(2)}) copy-start(f32[128,1024,4]{1,2,0:T(4,128)S(1)} %get-tuple-element.47) | copy-start | bytes 6291460
  144.5 6.0 %copy-start.14 = (bf16[1024,4,128]{0,2,1:T(8,128)(2,1)S(1)}, bf16[1024,4,128]{0,2,1:T(8,128)(2,1)}, u32[]{:S(2)}) copy-start(bf16[1024,4,128]{0,2,1:T(8,128)(2,1)} %all-gather.2.cloned.1.call-done) | copy-start | bytes 3145732
  144.5 2.9 %collective-permute-start.21 = (bf16[1024,4,128]{0,2,1:T(8,128)(2,1)}, bf16[1024,4,128]{0,2,1:T(8,128)(2,1)S(1)}, u32[]{:S(2)}, u32[]{:S(2)}) collective-permute-start(bf16[1024,4,128]{0,2,1:T(8,128)(2,1)} %all-gather.2.cloned.1.call-done), channel_id=1, source_target_pairs={{0,1},{1,0},{2,3},{3,2},{4,5},{5,4},{6,7},{7,6},{8,9},{9,8},{10,11... | collective-permute-start | bytes 3145736 | tf_op jit(solution)/shard_map/ppermute | solution.py:23
Sparse Core Ops, SparseCore 0:
  106.8 37.6 all-gather.1
